TPU v7x, 32 devices: a whole 2x2x4 slice. The times are simulated.
32 devices in a mesh: groups: 2 (over x), seq: 16 (over z, y, core).
Axes of the slice: x: 2, y: 2, z: 4, core: 2. Of those that a mesh axis runs over, the one named last changes fastest.
Arguments:
- hidden_in: bfloat16 [16384, 768], P(('groups', 'seq')), parts along dimension 0
- ln_gain: float32 [2, 768], replicated, may hold values from 0.5 to 1.5
- w_qkv: bfloat16 [2, 768, 2304], replicated
- w_out: bfloat16 [2, 768, 768], replicated, may hold values from -0.21875 to 0.21875
- final_gain: float32 [768], replicated, may hold values from 0.5 to 1.5
- w_heads: bfloat16 [768, 512], replicated
- actions: int32 [16384], P(('groups', 'seq')), parts along dimension 0, may hold values from 0 to 255
- propensity: int32 [16384], P(('groups', 'seq')), parts along dimension 0, may hold values from 1024 to 65535
- logged_reward: float32 [16384], P(('groups', 'seq')), parts along dimension 0, may hold values from -6 to 6
- switch_index: int32 [2], P('groups'), parts along dimension 0, may hold values from 2 to 9
Outputs:
- rewards: float32 [16384], P(('groups', 'seq')), parts along dimension 0
- dr_terms: float32 [16384], P(('groups', 'seq')), parts along dimension 0
There are 2 independent parts, one for each index of `groups`. A program takes and returns all parts, laid end to end along the dimension named above; an argument that names none is the same for every part. Nothing has to cross between parts.
All inputs are finite; a program needn't handle non-finite values.
Results may differ from a plain program's by a relative error of at most 0.03.
Values may be sent and summed in bfloat16 or wider, within the bound.
No kernel may reach another device: no remote copies, remote signals or barrier semaphores. Data moves between devices by JAX's collectives and lax.ppermute only.
A program may use at most 128 MiB of HBM per device.

v0:
```python
import jax
import jax.numpy as jnp
from jax import lax
from jax.sharding import PartitionSpec as P

HEADS = 12
HEAD = 64
HALF = 256
PROMPT = 256
ACTIONS = 256
LAYERS = 2


def with_halo(array, sides, width):
    for axis, dim in sides:
        count, length = (lax.axis_size(axis), array.shape[dim])
        up = [(i, (i + 1) % count) for i in range(count - 1)]
        down = [(j, i) for i, j in up]
        last = lax.slice_in_dim(array, length - width, length, axis=dim)
        leading = lax.slice_in_dim(array, 0, width, axis=dim)
        before = lax.ppermute(last, axis, up)
        after = lax.ppermute(leading, axis, down)
        array = jnp.concatenate([before, array, after], axis=dim)
    return array


def spread(block, axis, source):
    block = jnp.where(lax.axis_index(axis) == source, block, jnp.zeros_like(block))
    return lax.psum(block, axis)


def layer_norm(hidden_state, gain_row):
    values_f = hidden_state.astype(jnp.float32)
    row_mean = jnp.mean(values_f, axis=-1, keepdims=True)
    centred = values_f - row_mean
    row_var = jnp.mean(centred * centred, axis=-1, keepdims=True)
    return (centred * lax.rsqrt(row_var + 1e-05) * gain_row).astype(jnp.bfloat16)


def attend_block(
    query_block, key_block, value_block, prompt_keys, prompt_values, row_start, total_len
):
    block_rows = query_block.shape[0]
    band_width = key_block.shape[0]
    band_scores = jnp.einsum(
        "qhe,khe->hqk", query_block, key_block, preferred_element_type=jnp.float32
    )
    prompt_scores = jnp.einsum(
        "qhe,khe->hqk", query_block, prompt_keys, preferred_element_type=jnp.float32
    )
    query_pos = row_start + jnp.arange(block_rows, dtype=jnp.int32)
    key_pos = row_start - HALF + jnp.arange(band_width, dtype=jnp.int32)
    prompt_pos = jnp.arange(PROMPT, dtype=jnp.int32)
    band_mask = (
        (jnp.abs(key_pos[None, :] - query_pos[:, None]) <= HALF)
        & (key_pos[None, :] >= 0)
        & (key_pos[None, :] < total_len)
    )
    prompt_mask = jnp.abs(prompt_pos[None, :] - query_pos[:, None]) > HALF
    scores = jnp.concatenate(
        [
            jnp.where(prompt_mask[None], prompt_scores, -1e30),
            jnp.where(band_mask[None], band_scores, -1e30),
        ],
        axis=-1,
    )
    row_max = jnp.max(scores, axis=-1, keepdims=True)
    exps = jnp.exp(scores - row_max)
    attn_probs = (exps / jnp.sum(exps, axis=-1, keepdims=True)).astype(jnp.bfloat16)
    value_rows = jnp.concatenate([prompt_values, value_block], axis=0)
    attn_out = jnp.einsum(
        "hqk,khe->qhe", attn_probs, value_rows, preferred_element_type=jnp.float32
    )
    return attn_out.reshape(block_rows, HEADS * HEAD).astype(jnp.bfloat16)


def per_device(
    hidden_in,
    ln_gain,
    w_qkv,
    w_out,
    final_gain,
    w_heads,
    actions,
    propensity,
    logged_reward,
    switch_index,
):
    tok_rows = hidden_in.shape[0]
    feat_width = hidden_in.shape[1]
    seq_devices = lax.axis_size("seq")
    seq_place = lax.axis_index("seq")
    total_len = tok_rows * seq_devices
    first_pos = seq_place * tok_rows
    block_rows = min(256, tok_rows)
    block_count = tok_rows // block_rows
    hidden_state = hidden_in
    for layer_idx in range(LAYERS):
        normed = layer_norm(hidden_state, ln_gain[layer_idx])
        weights = w_qkv[layer_idx]
        projected = jnp.dot(normed, weights, preferred_element_type=jnp.float32)
        queries = (projected[:, :feat_width] * 0.125).astype(jnp.bfloat16)
        key_value = projected[:, feat_width:].astype(jnp.bfloat16)
        extended = with_halo(key_value, (("seq", 0),), HALF)
        prompt_kv = spread(key_value[:PROMPT], "seq", 0)
        query_heads = queries.reshape(tok_rows, HEADS, HEAD)
        band_keys = extended[:, :feat_width].reshape(-1, HEADS, HEAD)
        band_values = extended[:, feat_width:].reshape(-1, HEADS, HEAD)
        prompt_keys = prompt_kv[:, :feat_width].reshape(PROMPT, HEADS, HEAD)
        prompt_values = prompt_kv[:, feat_width:].reshape(PROMPT, HEADS, HEAD)

        def one_block(block_idx):
            local_start = block_idx * block_rows
            return attend_block(
                lax.dynamic_slice_in_dim(query_heads, local_start, block_rows),
                lax.dynamic_slice_in_dim(band_keys, local_start, block_rows + 2 * HALF),
                lax.dynamic_slice_in_dim(band_values, local_start, block_rows + 2 * HALF),
                prompt_keys,
                prompt_values,
                first_pos + local_start,
                total_len,
            )

        attended = lax.map(one_block, jnp.arange(block_count, dtype=jnp.int32)).reshape(
            tok_rows, feat_width
        )
        projection = jnp.dot(attended, w_out[layer_idx], preferred_element_type=jnp.float32)
        hidden_state = (hidden_state.astype(jnp.float32) + projection).astype(jnp.bfloat16)
    final = layer_norm(hidden_state, final_gain)
    head_out = jnp.dot(final, w_heads, preferred_element_type=jnp.float32)
    logits = head_out[:, :ACTIONS]
    reward_table = head_out[:, ACTIONS:]
    logit_max = jnp.max(logits, axis=-1, keepdims=True)
    exps = jnp.exp(logits - logit_max)
    policy = exps / jnp.sum(exps, axis=-1, keepdims=True)
    chosen = actions[:, None] == jnp.arange(ACTIONS, dtype=jnp.int32)[None, :]
    rewards = jnp.sum(jnp.where(chosen, reward_table, 0.0), axis=-1)
    chosen_prob = jnp.sum(jnp.where(chosen, policy, 0.0), axis=-1)
    direct = jnp.sum(policy * reward_table, axis=-1)
    logged_prob = propensity.astype(jnp.float32) / 65536.0
    cutoff = 0.5 * switch_index[0].astype(jnp.float32)
    dr_terms = direct + jnp.minimum(chosen_prob / logged_prob, cutoff) * (logged_reward - rewards)
    return (rewards, dr_terms)


def solution(mesh):
    placed = (
        P(("groups", "seq"), None),
        P(),
        P(),
        P(),
        P(),
        P(),
        P(("groups", "seq")),
        P(("groups", "seq")),
        P(("groups", "seq")),
        P("groups"),
    )
    return jax.shard_map(
        per_device,
        mesh=mesh,
        in_specs=placed,
        out_specs=(P(("groups", "seq")), P(("groups", "seq"))),
        check_vma=False,
    )
```

profile of v0, /device:TPU:20, one launch (start us, length us, event | category | flops | bytes accessed | tf_op | source)
XLA Modules:
  0.0 359.7 jit_solution(2516836620028198546)
XLA Ops:
  8.6 1.5 fusion.55
  11.5 6.5 %fusion.92 = (bf16[512,2304]{1,0:T(8,128)(2,1)S(1)}, f32[512,2304]{1,0:T(8,128)}) fusion(bf16[2,768,2304]{2,1,0:T(8,128)(2,1)} %param.16, bf16[512,768]{1,0:T(8,128)(2,1)} %param.14, f32[768]{0:T(1024)S(1)} %get-tuple-element.252, f32[512]{0:T(512)S(1)} %add_rsqrt_fusion.2, f32[512]{0:T(512)S(1)} %broadcast_multiply_fusion.2), kind=kOutput, calls=%fused_computation.135 | convolution fusion | flops 1815085056 | bytes 11410432 | tf_op jit(solution)/shard_map/dot_general | solution.py:101
  19.4 1.5 broadcast_select_fusion.3
  21.0 1.9 collective-permute-start.1
  22.9 2.4 collective-permute-start
  25.6 1.5 slice.105
  27.1 1.5 fusion.64
  29.8 91.5 %all-reduce.3.cloned.1.call-done = bf16[256,1536]{1,0:T(8,128)(2,1)} async-done(((bf16[256,1536]{1,0:T(8,128)(2,1)}), bf16[256,1536]{1,0:T(8,128)(2,1)}) %all-reduce.3.cloned.1.call-update) | async-done | bytes 786448 | tf_op jit(solution)/shard_map/psum | solution.py:29
  124.3 1.5 pad_maximum_fusion
  125.8 1.9 fusion.89
  127.7 1.7 copy.30
  129.4 2.6 copy.26
  133.5 45.4 %while.24 = (s32[]{:T(128)}, bf16[2,256,768]{2,1,0:T(8,128)(2,1)}, s32[2]{0:T(128)}, bf16[1024,12,64]{0,2,1:T(8,128)(2,1)}, bf16[256,12,64]{0,2,1:T(8,128)(2,1)}...) while((s32[]{:T(128)}, bf16[2,256,768]{2,1,0:T(8,128)(2,1)}, ...), condition=%wide.region_7.8_spmd, body=%wide.region_3.7_spmd.sunk | while | flops 838137088 | bytes 71819664 | solution.py:124
  138.0 2.3 fusion.120
  140.4 3.5 copy.46
  143.9 2.9 fusion.119
  146.8 2.9 fusion.121
  149.7 4.5 %fusion.122 = bf16[12,64,256]{2,1,0:T(8,128)(2,1)} fusion(f32[12,256,768]{2,1,0:T(8,128)S(1)} %get-tuple-element.438, f32[12,256,256]{2,1,0:T(8,128)S(1)} %copy-done.1, f32[12,256]{1,0:T(8,128)S(1)} %fusion.121, f32[12,256]{1,0:T(8,128)S(1)} %reduce_max.69, bf16[768,12,64]{0,2,1:T(8,128)(2,1)S(1)} %constant_dynamic-slice_fusion.4, ...), kind=kOutput, calls=%fused_computation.10.clone.1 | convolution fusion | flops 418578432 | bytes 14573568 | tf_op jit(solution)/shard_map/while/body/eval_jaxpr/hqk,khe->qhe/dot_general | solution.py:71
  160.7 2.4 fusion.120
  163.0 3.5 copy.46
  166.6 3.0 fusion.119
  169.6 2.9 fusion.121
  172.4 4.5 %fusion.122 = bf16[12,64,256]{2,1,0:T(8,128)(2,1)} fusion(f32[12,256,768]{2,1,0:T(8,128)S(1)} %get-tuple-element.438, f32[12,256,256]{2,1,0:T(8,128)S(1)} %copy-done.1, f32[12,256]{1,0:T(8,128)S(1)} %fusion.121, f32[12,256]{1,0:T(8,128)S(1)} %reduce_max.69, bf16[768,12,64]{0,2,1:T(8,128)(2,1)S(1)} %constant_dynamic-slice_fusion.4, ...), kind=kOutput, calls=%fused_computation.10.clone.1 | convolution fusion | flops 418578432 | bytes 14573568 | tf_op jit(solution)/shard_map/while/body/eval_jaxpr/hqk,khe->qhe/dot_general | solution.py:71
  178.9 2.6 convert_reduce_fusion
  181.9 6.3 %fusion.93 = (bf16[512,2304]{1,0:T(8,128)(2,1)S(1)}, f32[512,2304]{1,0:T(8,128)}) fusion(bf16[2,768,2304]{2,1,0:T(8,128)(2,1)} %param.16, bf16[512,768]{1,0:T(8,128)(2,1)S(1)} %get-tuple-element.318, f32[768]{0:T(1024)S(1)} %copy-done.13, f32[512]{0:T(512)S(1)} %add_rsqrt_fusion.1, f32[512]{0:T(512)S(1)} %broadcast_multiply_fusion.1), kind=kOutput, calls=%fused_computation.136 | convolution fusion | flops 1815085056 | bytes 11410432 | tf_op jit(solution)/shard_map/dot_general | solution.py:101
  188.1 1.4 copy-done.7
  189.6 1.5 broadcast_select_fusion.2
  191.1 1.9 collective-permute-start.3
  193.0 2.6 collective-permute-start.2
  196.3 1.5 slice.113
  197.8 1.5 fusion.63
  200.6 90.1 %all-reduce.5.cloned.1.call-done = bf16[256,1536]{1,0:T(8,128)(2,1)} async-done(((bf16[256,1536]{1,0:T(8,128)(2,1)}), bf16[256,1536]{1,0:T(8,128)(2,1)}) %all-reduce.5.cloned.1.call-update) | async-done | bytes 786448 | tf_op jit(solution)/shard_map/psum | solution.py:29
  293.7 1.5 pad_maximum_fusion.1
  295.2 1.9 fusion.88
  297.1 1.7 copy.36
  298.8 2.6 copy.32
  302.8 45.1 %while.25 = (s32[]{:T(128)}, bf16[2,256,768]{2,1,0:T(8,128)(2,1)}, s32[2]{0:T(128)}, bf16[1024,12,64]{0,2,1:T(8,128)(2,1)}, bf16[256,12,64]{0,2,1:T(8,128)(2,1)}...) while((s32[]{:T(128)}, bf16[2,256,768]{2,1,0:T(8,128)(2,1)}, ...), condition=%wide.region_15.16_spmd, body=%wide.region_11.15_spmd.sunk | while | flops 838137088 | bytes 71819664 | solution.py:124
  307.3 2.3 fusion.128
  309.6 3.5 copy.48
  313.1 2.9 fusion.127
  316.1 2.9 fusion.129
  318.9 4.5 %fusion.130 = bf16[12,64,256]{2,1,0:T(8,128)(2,1)} fusion(f32[12,256,768]{2,1,0:T(8,128)S(1)} %get-tuple-element.453, f32[12,256,256]{2,1,0:T(8,128)S(1)} %copy-done.2, f32[12,256]{1,0:T(8,128)S(1)} %fusion.129, f32[12,256]{1,0:T(8,128)S(1)} %reduce_max.72, bf16[768,12,64]{0,2,1:T(8,128)(2,1)S(1)} %constant_dynamic-slice_fusion.5, ...), kind=kOutput, calls=%fused_computation.38.clone.1 | convolution fusion | flops 418578432 | bytes 14573568 | tf_op jit(solution)/shard_map/while/body/eval_jaxpr/hqk,khe->qhe/dot_general | solution.py:71
  329.8 2.3 fusion.128
  332.1 3.5 copy.48
  335.7 3.0 fusion.127
  338.7 2.9 fusion.129
  341.5 4.5 %fusion.130 = bf16[12,64,256]{2,1,0:T(8,128)(2,1)} fusion(f32[12,256,768]{2,1,0:T(8,128)S(1)} %get-tuple-element.453, f32[12,256,256]{2,1,0:T(8,128)S(1)} %copy-done.2, f32[12,256]{1,0:T(8,128)S(1)} %fusion.129, f32[12,256]{1,0:T(8,128)S(1)} %reduce_max.72, bf16[768,12,64]{0,2,1:T(8,128)(2,1)S(1)} %constant_dynamic-slice_fusion.5, ...), kind=kOutput, calls=%fused_computation.38.clone.1 | convolution fusion | flops 418578432 | bytes 14573568 | tf_op jit(solution)/shard_map/while/body/eval_jaxpr/hqk,khe->qhe/dot_general | solution.py:71
  348.0 2.6 convert_reduce_fusion.2
  (126 shorter events, 41.5 us)
Async XLA Ops:
  7.2 343.8 %copy-start = (bf16[768,512]{1,0:T(8,128)(2,1)S(1)}, bf16[768,512]{1,0:T(8,128)(2,1)}, u32[]{:S(2)}) copy-start(bf16[768,512]{1,0:T(8,128)(2,1)} %param.19) | copy-start | bytes 2359300
  7.2 114.1 %all-reduce.3.cloned.1.call-start = ((), (), s32[]{:S(2)}) async-start(), calls=%async_computation | async-start | bytes 1572864 | tf_op jit(solution)/shard_map/psum | solution.py:29
  18.0 1.4 copy-start.8
  21.0 103.3 %collective-permute-start.1 = (bf16[256,1536]{1,0:T(8,128)(2,1)}, bf16[256,1536]{1,0:T(8,128)(2,1)}, u32[]{:S(2)}, u32[]{:S(2)}) collective-permute-start(bf16[256,1536]{1,0:T(8,128)(2,1)} %get-tuple-element.309), channel_id=1, source_target_pairs={{1,0},{2,1},{3,2},{4,3},{5,4},{6,5},{7,6},{8,7},{9,8},{10,9},{11,1... | collective-permute-start | bytes 2359304 | tf_op jit(solution)/shard_map/ppermute | solution.py:22
  22.9 101.4 %collective-permute-start = (bf16[256,1536]{1,0:T(8,128)(2,1)}, bf16[256,1536]{1,0:T(8,128)(2,1)}, u32[]{:S(2)}, u32[]{:S(2)}) collective-permute-start(bf16[256,1536]{1,0:T(8,128)(2,1)} %get-tuple-element.310), channel_id=1, source_target_pairs={{0,1},{1,2},{2,3},{3,4},{4,5},{5,6},{6,7},{7,8},{8,9},{9,10},{10,1... | collective-permute-start | bytes 2359304 | tf_op jit(solution)/shard_map/ppermute | solution.py:21
  25.3 265.4 %all-reduce.5.cloned.1.call-start = ((), (), s32[]{:S(2)}) async-start(), calls=%async_computation.1 | async-start | bytes 1572864 | tf_op jit(solution)/shard_map/psum | solution.py:29
  135.5 2.5 copy-start.4
  135.5 2.5 copy-start.6
  143.9 2.9 copy-start.1
  146.8 2.9 copy-start.11
  158.1 2.5 copy-start.4
  158.1 2.5 copy-start.6
  166.6 3.0 copy-start.1
  169.6 2.9 copy-start.11
  178.9 3.0 copy-start.13
  181.5 6.7 %copy-start.9 = (bf16[512,768]{1,0:T(8,128)(2,1)}, bf16[512,768]{1,0:T(8,128)(2,1)S(1)}, u32[]{:S(2)}) copy-start(bf16[512,768]{1,0:T(8,128)(2,1)S(1)} %get-tuple-element.318) | copy-start | bytes 2359300
  188.1 1.4 copy-start.7
  191.1 102.6 %collective-permute-start.3 = (bf16[256,1536]{1,0:T(8,128)(2,1)}, bf16[256,1536]{1,0:T(8,128)(2,1)}, u32[]{:S(2)}, u32[]{:S(2)}) collective-permute-start(bf16[256,1536]{1,0:T(8,128)(2,1)} %get-tuple-element.306), channel_id=1, source_target_pairs={{1,0},{2,1},{3,2},{4,3},{5,4},{6,5},{7,6},{8,7},{9,8},{10,9},{11,1... | collective-permute-start | bytes 2359304 | tf_op jit(solution)/shard_map/ppermute | solution.py:22
  193.0 100.7 %collective-permute-start.2 = (bf16[256,1536]{1,0:T(8,128)(2,1)}, bf16[256,1536]{1,0:T(8,128)(2,1)}, u32[]{:S(2)}, u32[]{:S(2)}) collective-permute-start(bf16[256,1536]{1,0:T(8,128)(2,1)} %get-tuple-element.307), channel_id=1, source_target_pairs={{0,1},{1,2},{2,3},{3,4},{4,5},{5,6},{6,7},{7,8},{8,9},{9,10},{10,1... | collective-permute-start | bytes 2359304 | tf_op jit(solution)/shard_map/ppermute | solution.py:21
  304.7 2.5 copy-start.3
  304.7 2.5 copy-start.5
  313.1 2.9 copy-start.2
  316.1 2.9 copy-start.10
  327.2 2.5 copy-start.3
  327.3 2.5 copy-start.5
  335.7 3.0 copy-start.2
  338.7 2.9 copy-start.10
  348.0 3.0 copy-start.17
  350.6 1.4 copy-start.14
  351.0 1.2 copy-start.15
  351.0 1.2 copy-start.16
  352.2 0.6 copy-start.12
Sparse Core Ops, SparseCore 0:
  25.5 95.7 all-reduce.2
  195.8 94.8 all-reduce.4
where the time goes:
time: 363 us; the launch traced here: 360 us
  waiting for transfers between devices  182 us (50%)
  local copies, waits for them, and re-layouts  63.7 us (18%)
  matrix products  57.6 us (16%)
  other arithmetic  29.6 us (8%)
  between operations  14.9 us (4%)
  starting transfers between devices  9.11 us (3%)
    psum x2, waiting for transfers between devices, spread(): return lax.psum(block, axis)  182 us
    dot_general x4, matrix products, attend_block(): jnp.einsum('hqk,khe->qhe', attn_probs, value_rows, preferred_element_type...  17.9 us
    select_n x4, local copies, waits for them, and re-layouts, attend_block(): jnp.where(prompt_mask[None], prompt_scores, -1e+30)  14.2 us
    dot_general x2, matrix products, per_device(): projected = jnp.dot(normed, weights, preferred_element_type=jnp.float32)  12.7 us
    dot_general x4, matrix products, attend_block(): jnp.einsum('qhe,khe->hqk', query_block, key_block, preferred_element_type...  11.7 us
    reduce_sum x4, other arithmetic, attend_block(): jnp.sum(exps, axis=-1, keepdims=True)  11.4 us
    dot_general x4, matrix products, attend_block(): jnp.einsum('qhe,khe->hqk', query_block, prompt_keys, preferred_element_ty...  9.38 us
    dynamic_update_slice x8, local copies, waits for them, and re-layouts, per_device(): lax.map(one_block, jnp.arange(block_count, dtype=jnp.int32))  7.84 us
  transfers between devices with their start and end apart: 6, of which 2 were waited for; matrix products, arithmetic and copies ran while one was open for 4% of the time, Pallas kernels for 0%

commit v1 on v0

--- a/solution.py
+++ b/solution.py
@@ -24,9 +24,55 @@
     return array
 
 
-def spread(block, axis, source):
-    block = jnp.where(lax.axis_index(axis) == source, block, jnp.zeros_like(block))
-    return lax.psum(block, axis)
+def tree_rounds(count):
+    def near(i):
+        out = [i ^ 1]
+        if count % 4 == 0:
+            out += [i + 4, i ^ 2, i - 4]
+        else:
+            out += [i + 2, i - 2]
+        return [j for j in out if 0 <= j < count]
+
+    holders = {0}
+    rounds = []
+    while len(holders) < count:
+        taken = set()
+        pairs = []
+        for i in sorted(holders):
+            for j in near(i):
+                if j not in holders and j not in taken:
+                    taken.add(j)
+                    pairs.append((i, j))
+        if not pairs:
+            for j in range(count):
+                if j not in holders:
+                    pairs.append((min(holders), j))
+                    taken.add(j)
+                    break
+        ops = []
+        for pair in pairs:
+            for op in ops:
+                if all(pair[0] != s for s, _ in op):
+                    op.append(pair)
+                    break
+            else:
+                ops.append([pair])
+        rounds.append(ops)
+        holders |= taken
+    return rounds
+
+
+def spread(block, axis):
+    place = lax.axis_index(axis)
+    block = jnp.where(place == 0, block, jnp.zeros_like(block))
+    for ops in tree_rounds(lax.axis_size(axis)):
+        received = block
+        for op in ops:
+            got = lax.ppermute(block, axis, op)
+            targets = jnp.array([t for _, t in op], dtype=jnp.int32)
+            received = jnp.where(jnp.any(place == targets), got, received)
+        block = received
+    return block
 
 
 def layer_norm(hidden_state, gain_row):
@@ -102,7 +148,12 @@
         queries = (projected[:, :feat_width] * 0.125).astype(jnp.bfloat16)
         key_value = projected[:, feat_width:].astype(jnp.bfloat16)
         extended = with_halo(key_value, (("seq", 0),), HALF)
-        prompt_kv = spread(key_value[:PROMPT], "seq", 0)
+        prompt_rows = spread(hidden_state[:PROMPT], "seq")
+        prompt_kv = jnp.dot(
+            layer_norm(prompt_rows, ln_gain[layer_idx]),
+            weights[:, feat_width:],
+            preferred_element_type=jnp.float32,
+        ).astype(jnp.bfloat16)
         query_heads = queries.reshape(tok_rows, HEADS, HEAD)
         band_keys = extended[:, :feat_width].reshape(-1, HEADS, HEAD)
         band_values = extended[:, feat_width:].reshape(-1, HEADS, HEAD)

time: 363 us -> 230 us (0.63)
  the two profiles are of different devices: /device:TPU:20 before, /device:TPU:12 now
where the time goes in v1:
time: 230 us; the launch traced here: 228 us
  local copies, waits for them, and re-layouts  67.6 us (29%)
  matrix products  67.4 us (29%)
  other arithmetic  35 us (15%)
  starting transfers between devices  27.9 us (12%)
  waiting for transfers between devices  25.5 us (11%)
  loops' own time  3.03 us (1%)
    dot_general x4, matrix products, attend_block(): jnp.einsum('hqk,khe->qhe', attn_probs, value_rows, preferred_element_type...  17.9 us
    ppermute x16, waiting for transfers between devices, spread(): got = lax.ppermute(block, axis, op)  17.7 us
    ppermute x16, starting transfers between devices, spread(): got = lax.ppermute(block, axis, op)  16.8 us
    select_n x4, local copies, waits for them, and re-layouts, attend_block(): jnp.where(prompt_mask[None], prompt_scores, -1e+30)  14.2 us
    dot_general x4, matrix products, attend_block(): jnp.einsum('qhe,khe->hqk', query_block, prompt_keys, preferred_element_ty...  13.9 us
    dot_general x2, matrix products, per_device(): projected = jnp.dot(normed, weights, preferred_element_type=jnp.float32)  12.8 us
    dot_general x4, matrix products, attend_block(): jnp.einsum('qhe,khe->hqk', query_block, key_block, preferred_element_type...  11.7 us
    reduce_sum x4, other arithmetic, attend_block(): jnp.sum(exps, axis=-1, keepdims=True)  11.4 us
  transfers between devices with their start and end apart: 20, of which 3 were waited for; matrix products, arithmetic and copies ran while one was open for 24% of the time, Pallas kernels for 0%

profile of v1, /device:TPU:12, one launch (start us, length us, event | category | flops | bytes accessed | tf_op | source)
XLA Modules:
  0.0 228.3 jit_solution(13469530345601683137)
XLA Ops:
  5.2 1.5 fusion.51
  8.1 6.6 %fusion.110 = (bf16[512,2304]{1,0:T(8,128)(2,1)S(1)}, f32[512,2304]{1,0:T(8,128)}) fusion(bf16[2,768,2304]{2,1,0:T(8,128)(2,1)} %param.32, bf16[512,768]{1,0:T(8,128)(2,1)} %param.30, f32[768]{0:T(1024)S(1)} %get-tuple-element.252, f32[512]{0:T(512)S(1)} %add_rsqrt_fusion.2, f32[512]{0:T(512)S(1)} %broadcast_multiply_fusion.2), kind=kOutput, calls=%fused_computation.176 | convolution fusion | flops 1815085056 | bytes 11410432 | tf_op jit(solution)/shard_map/dot_general | solution.py:147
  18.0 1.9 collective-permute-start
  19.9 3.6 %collective-permute-start.1 = (bf16[256,1536]{1,0:T(8,128)(2,1)}, bf16[256,1536]{1,0:T(8,128)(2,1)}, u32[]{:S(2)}, u32[]{:S(2)}) collective-permute-start(bf16[256,1536]{1,0:T(8,128)(2,1)} %get-tuple-element.314), channel_id=1, source_target_pairs={{1,0},{2,1},{3,2},{4,3},{5,4},{6,5},{7,6},{8,7},{9,8},{10,9},{11,1... | collective-permute-start | bytes 2359304 | tf_op jit(solution)/shard_map/ppermute | solution.py:22
  25.1 2.8 %collective-permute-start.7 = (bf16[256,768]{1,0:T(8,128)(2,1)S(1)}, bf16[256,768]{1,0:T(8,128)(2,1)S(1)}, u32[]{:S(2)}, u32[]{:S(2)}) collective-permute-start(bf16[256,768]{1,0:T(8,128)(2,1)S(1)} %select_select_fusion.2), channel_id=1, source_target_pairs={{3,7},{5,9},{6,10},{8,12},{19,23},{21,25},{22,26},{24,28}} | collective-permute-start | bytes 1179656 | tf_op jit(solution)/shard_map/ppermute | solution.py:71
  27.9 6.5 %slice_bitcast_fusion = (bf16[768,2304]{1,0:T(8,128)(2,1)}, bf16[768,2304]{1,0:T(8,128)(2,1)}) fusion(bf16[2,768,2304]{2,1,0:T(8,128)(2,1)} %param.32), kind=kLoop, calls=%fused_computation.56 | loop fusion | bytes 14155776 | tf_op jit(solution)/shard_map/squeeze | solution.py:146
  34.3 1.5 slice.121
  38.8 1.5 fusion.60
  43.8 1.5 pad_maximum_fusion
  45.3 1.9 fusion.105
  47.2 1.7 copy.46
  48.9 2.6 %copy.42 = bf16[1024,768]{0,1:T(8,128)(2,1)} copy(bf16[1024,768]{1,0:T(8,128)(2,1)} %get-tuple-element.310) | data formatting | bytes 3145728 | tf_op jit(solution)/shard_map/slice | solution.py:159
  51.9 2.5 %convolution_convert_fusion.1 = bf16[256,1536]{1,0:T(8,128)(2,1)S(1)} fusion(bf16[768,2304]{1,0:T(8,128)(2,1)} %get-tuple-element.306, bf16[256,768]{1,0:T(8,128)(2,1)S(1)} %get-tuple-element.292, f32[768]{0:T(1024)S(1)} %get-tuple-element.252, f32[256]{0:T(256)S(1)} %add_rsqrt_fusion.4, f32[256]{0:T(256)S(1)} %broadcast_multiply_fusion.4), kind=kOutput, calls=%fused_computation.61 | convolution fusion | flops 605356032 | bytes 3544064 | tf_op jit(solution)/shard_map/dot_general | solution.py:152
  57.9 47.7 %while.24 = (s32[]{:T(128)}, bf16[2,256,768]{2,1,0:T(8,128)(2,1)}, s32[2]{0:T(128)}, bf16[1024,12,64]{0,2,1:T(8,128)(2,1)}, bf16[256,12,64]{0,2,1:T(8,128)(2,1)}...) while((s32[]{:T(128)}, bf16[2,256,768]{2,1,0:T(8,128)(2,1)}, ...), condition=%wide.region_11.12_spmd, body=%wide.region_7.11_spmd.sunk | while | flops 838137088 | bytes 67101016 | solution.py:175
  62.4 3.5 %fusion.138 = (f32[12,256]{1,0:T(8,128)S(1)}, f32[12,256,256]{1,2,0:T(8,128)}) fusion(bf16[256,12,64]{0,2,1:T(8,128)(2,1)} %get-tuple-element.498, bf16[512,12,64]{0,2,1:T(8,128)(2,1)} %get-tuple-element.497, s32[]{:T(128)S(6)} %select_n.263, pred[256,256]{0,1:T(8,128)(4,1)S(1)} %abs_compare_fusion.6), kind=kOutput, calls=%fused_computation.166.clone.1 | convolution fusion | flops 102233088 | bytes 4009988 | tf_op jit(solution)/shard_map/while/body/eval_jaxpr/qhe,khe->hqk/dot_general | solution.py:94
  65.9 3.5 %copy.62 = f32[12,256,256]{2,1,0:T(8,128)} copy(f32[12,256,256]{1,2,0:T(8,128)} %get-tuple-element.443) | data formatting | bytes 6291456 | tf_op jit(solution)/shard_map/while/body/eval_jaxpr/jit(_where)/select_n | solution.py:108
  69.5 2.9 %fusion.137 = (f32[12,256]{1,0:T(8,128)S(1)}, f32[12,256,768]{2,1,0:T(8,128)S(1)}) fusion(bf16[1024,12,64]{0,2,1:T(8,128)(2,1)S(1)} %get-tuple-element.499, s32[]{:T(128)S(6)} %select_n.262, bf16[512,12,64]{0,2,1:T(8,128)(2,1)} %get-tuple-element.497, s32[]{:T(128)S(6)} %select_n.263, pred[256,768]{1,0:T(8,128)(4,1)} %fusion.136), kind=kOutput, calls=%fused_computation.167.clone.1 | convolution fusion | flops 306705408 | bytes 11218952 | tf_op jit(solution)/shard_map/while/body/eval_jaxpr/qhe,khe->hqk/dot_general | solution.py:91
  72.4 2.9 %fusion.139 = f32[12,256]{1,0:T(8,128)S(1)} fusion(f32[12,256,768]{2,1,0:T(8,128)S(1)} %get-tuple-element.442, f32[12,256,256]{2,1,0:T(8,128)S(1)} %copy-done.1, f32[12,256]{1,0:T(8,128)S(1)} %reduce_max.69), kind=kLoop, calls=%fused_computation.3.clone.1 | loop fusion | flops 9434112 | bytes 12607488 | tf_op jit(solution)/shard_map/while/body/eval_jaxpr/reduce_sum | solution.py:115
  75.3 4.5 %fusion.140 = bf16[12,64,256]{2,1,0:T(8,128)(2,1)} fusion(f32[12,256,768]{2,1,0:T(8,128)S(1)} %get-tuple-element.442, f32[12,256,256]{2,1,0:T(8,128)S(1)} %copy-done.1, f32[12,256]{1,0:T(8,128)S(1)} %fusion.139, f32[12,256]{1,0:T(8,128)S(1)} %reduce_max.69, bf16[768,12,64]{0,2,1:T(8,128)(2,1)S(1)} %constant_dynamic-slice_fusion.4, ...), kind=kOutput, calls=%fused_computation.10.clone.1 | convolution fusion | flops 418578432 | bytes 14573568 | tf_op jit(solution)/shard_map/while/body/eval_jaxpr/hqk,khe->qhe/dot_general | solution.py:117
  86.2 3.5 %fusion.138 = (f32[12,256]{1,0:T(8,128)S(1)}, f32[12,256,256]{1,2,0:T(8,128)}) fusion(bf16[256,12,64]{0,2,1:T(8,128)(2,1)} %get-tuple-element.498, bf16[512,12,64]{0,2,1:T(8,128)(2,1)} %get-tuple-element.497, s32[]{:T(128)S(6)} %select_n.263, pred[256,256]{0,1:T(8,128)(4,1)S(1)} %abs_compare_fusion.6), kind=kOutput, calls=%fused_computation.166.clone.1 | convolution fusion | flops 102233088 | bytes 4009988 | tf_op jit(solution)/shard_map/while/body/eval_jaxpr/qhe,khe->hqk/dot_general | solution.py:94
  89.8 3.5 %copy.62 = f32[12,256,256]{2,1,0:T(8,128)} copy(f32[12,256,256]{1,2,0:T(8,128)} %get-tuple-element.443) | data formatting | bytes 6291456 | tf_op jit(solution)/shard_map/while/body/eval_jaxpr/jit(_where)/select_n | solution.py:108
  93.3 3.0 %fusion.137 = (f32[12,256]{1,0:T(8,128)S(1)}, f32[12,256,768]{2,1,0:T(8,128)S(1)}) fusion(bf16[1024,12,64]{0,2,1:T(8,128)(2,1)S(1)} %get-tuple-element.499, s32[]{:T(128)S(6)} %select_n.262, bf16[512,12,64]{0,2,1:T(8,128)(2,1)} %get-tuple-element.497, s32[]{:T(128)S(6)} %select_n.263, pred[256,768]{1,0:T(8,128)(4,1)} %fusion.136), kind=kOutput, calls=%fused_computation.167.clone.1 | convolution fusion | flops 306705408 | bytes 11218952 | tf_op jit(solution)/shard_map/while/body/eval_jaxpr/qhe,khe->hqk/dot_general | solution.py:91
  96.3 2.9 %fusion.139 = f32[12,256]{1,0:T(8,128)S(1)} fusion(f32[12,256,768]{2,1,0:T(8,128)S(1)} %get-tuple-element.442, f32[12,256,256]{2,1,0:T(8,128)S(1)} %copy-done.1, f32[12,256]{1,0:T(8,128)S(1)} %reduce_max.69), kind=kLoop, calls=%fused_computation.3.clone.1 | loop fusion | flops 9434112 | bytes 12607488 | tf_op jit(solution)/shard_map/while/body/eval_jaxpr/reduce_sum | solution.py:115
  99.2 4.5 %fusion.140 = bf16[12,64,256]{2,1,0:T(8,128)(2,1)} fusion(f32[12,256,768]{2,1,0:T(8,128)S(1)} %get-tuple-element.442, f32[12,256,256]{2,1,0:T(8,128)S(1)} %copy-done.1, f32[12,256]{1,0:T(8,128)S(1)} %fusion.139, f32[12,256]{1,0:T(8,128)S(1)} %reduce_max.69, bf16[768,12,64]{0,2,1:T(8,128)(2,1)S(1)} %constant_dynamic-slice_fusion.4, ...), kind=kOutput, calls=%fused_computation.10.clone.1 | convolution fusion | flops 418578432 | bytes 14573568 | tf_op jit(solution)/shard_map/while/body/eval_jaxpr/hqk,khe->qhe/dot_general | solution.py:117
  105.6 2.6 %convert_reduce_fusion = (f32[512]{0:T(512)S(1)}, bf16[512,768]{1,0:T(8,128)(2,1)S(1)}) fusion(bf16[512,768]{1,0:T(8,128)(2,1)} %bitcast.69, bf16[2,768,768]{2,1,0:T(8,128)(2,1)} %param.33, bf16[512,768]{1,0:T(8,128)(2,1)} %param.30), kind=kOutput, calls=%fused_computation.64 | convolution fusion | flops 605945344 | bytes 3540992 | tf_op jit(solution)/shard_map/dot_general | solution.py:178
  112.8 6.3 %fusion.111 = (bf16[512,2304]{1,0:T(8,128)(2,1)S(1)}, f32[512,2304]{1,0:T(8,128)}) fusion(bf16[2,768,2304]{2,1,0:T(8,128)(2,1)} %param.32, bf16[512,768]{1,0:T(8,128)(2,1)S(1)} %get-tuple-element.322, f32[768]{0:T(1024)S(1)} %copy-done.10, f32[512]{0:T(512)S(1)} %add_rsqrt_fusion.1, f32[512]{0:T(512)S(1)} %broadcast_multiply_fusion.1), kind=kOutput, calls=%fused_computation.177 | convolution fusion | flops 1815085056 | bytes 11410432 | tf_op jit(solution)/shard_map/dot_general | solution.py:147
  119.1 17.5 %collective-permute-done.16 = bf16[256,768]{1,0:T(8,128)(2,1)S(1)} collective-permute-done((bf16[256,768]{1,0:T(8,128)(2,1)S(1)}, bf16[256,768]{1,0:T(8,128)(2,1)S(1)}, u32[]{:S(2)}, u32[]{:S(2)}) %collective-permute-start.16) | collective-permute-done | bytes 393248 | tf_op jit(solution)/shard_map/ppermute | solution.py:71
  139.9 1.9 collective-permute-start.10
  141.9 3.6 %collective-permute-start.11 = (bf16[256,1536]{1,0:T(8,128)(2,1)}, bf16[256,1536]{1,0:T(8,128)(2,1)}, u32[]{:S(2)}, u32[]{:S(2)}) collective-permute-start(bf16[256,1536]{1,0:T(8,128)(2,1)} %get-tuple-element.312), channel_id=1, source_target_pairs={{1,0},{2,1},{3,2},{4,3},{5,4},{6,5},{7,6},{8,7},{9,8},{10,9},{11,1... | collective-permute-start | bytes 2359304 | tf_op jit(solution)/shard_map/ppermute | solution.py:22
  148.3 1.5 slice.130
  149.8 1.5 fusion.59
  154.2 7.8 %collective-permute-done.10 = bf16[256,1536]{1,0:T(8,128)(2,1)} collective-permute-done((bf16[256,1536]{1,0:T(8,128)(2,1)}, bf16[256,1536]{1,0:T(8,128)(2,1)}, u32[]{:S(2)}, u32[]{:S(2)}) %collective-permute-start.10) | collective-permute-done | bytes 786464 | tf_op jit(solution)/shard_map/ppermute | solution.py:21
  163.5 1.9 fusion.104
  165.3 1.7 copy.52
  167.0 2.7 %copy.48 = bf16[1024,768]{0,1:T(8,128)(2,1)} copy(bf16[1024,768]{1,0:T(8,128)(2,1)} %get-tuple-element.308) | data formatting | bytes 3145728 | tf_op jit(solution)/shard_map/slice | solution.py:159
  170.2 2.5 %convolution_convert_fusion = bf16[256,1536]{1,0:T(8,128)(2,1)S(1)} fusion(bf16[768,2304]{1,0:T(8,128)(2,1)} %get-tuple-element.305, bf16[256,768]{1,0:T(8,128)(2,1)S(1)} %get-tuple-element.290, f32[768]{0:T(1024)S(1)} %copy-done.10, f32[256]{0:T(256)S(1)} %add_rsqrt_fusion.3, f32[256]{0:T(256)S(1)} %broadcast_multiply_fusion.3), kind=kOutput, calls=%fused_computation.60 | convolution fusion | flops 605356032 | bytes 3544064 | tf_op jit(solution)/shard_map/dot_general | solution.py:152
  176.1 47.4 %while.25 = (s32[]{:T(128)}, bf16[2,256,768]{2,1,0:T(8,128)(2,1)}, s32[2]{0:T(128)}, bf16[1024,12,64]{0,2,1:T(8,128)(2,1)}, bf16[256,12,64]{0,2,1:T(8,128)(2,1)}...) while((s32[]{:T(128)}, bf16[2,256,768]{2,1,0:T(8,128)(2,1)}, ...), condition=%wide.region_23.24_spmd, body=%wide.region_19.23_spmd.sunk | while | flops 838137088 | bytes 67101016 | solution.py:175
  180.5 3.5 %fusion.146 = (f32[12,256]{1,0:T(8,128)S(1)}, f32[12,256,256]{1,2,0:T(8,128)}) fusion(bf16[256,12,64]{0,2,1:T(8,128)(2,1)} %get-tuple-element.543, bf16[512,12,64]{0,2,1:T(8,128)(2,1)} %get-tuple-element.542, s32[]{:T(128)S(6)} %select_n.265, pred[256,256]{0,1:T(8,128)(4,1)S(1)} %abs_compare_fusion.7), kind=kOutput, calls=%fused_computation.168.clone.1 | convolution fusion | flops 102233088 | bytes 4009988 | tf_op jit(solution)/shard_map/while/body/eval_jaxpr/qhe,khe->hqk/dot_general | solution.py:94
  183.9 3.5 %copy.64 = f32[12,256,256]{2,1,0:T(8,128)} copy(f32[12,256,256]{1,2,0:T(8,128)} %get-tuple-element.458) | data formatting | bytes 6291456 | tf_op jit(solution)/shard_map/while/body/eval_jaxpr/jit(_where)/select_n | solution.py:108
  187.5 2.9 %fusion.145 = (f32[12,256]{1,0:T(8,128)S(1)}, f32[12,256,768]{2,1,0:T(8,128)S(1)}) fusion(bf16[1024,12,64]{0,2,1:T(8,128)(2,1)S(1)} %get-tuple-element.544, s32[]{:T(128)S(6)} %select_n.264, bf16[512,12,64]{0,2,1:T(8,128)(2,1)} %get-tuple-element.542, s32[]{:T(128)S(6)} %select_n.265, pred[256,768]{1,0:T(8,128)(4,1)} %fusion.144), kind=kOutput, calls=%fused_computation.169.clone.1 | convolution fusion | flops 306705408 | bytes 11218952 | tf_op jit(solution)/shard_map/while/body/eval_jaxpr/qhe,khe->hqk/dot_general | solution.py:91
  190.4 2.9 %fusion.147 = f32[12,256]{1,0:T(8,128)S(1)} fusion(f32[12,256,768]{2,1,0:T(8,128)S(1)} %get-tuple-element.457, f32[12,256,256]{2,1,0:T(8,128)S(1)} %copy-done.2, f32[12,256]{1,0:T(8,128)S(1)} %reduce_max.72), kind=kLoop, calls=%fused_computation.31.clone.1 | loop fusion | flops 9434112 | bytes 12607488 | tf_op jit(solution)/shard_map/while/body/eval_jaxpr/reduce_sum | solution.py:115
  193.3 4.5 %fusion.148 = bf16[12,64,256]{2,1,0:T(8,128)(2,1)} fusion(f32[12,256,768]{2,1,0:T(8,128)S(1)} %get-tuple-element.457, f32[12,256,256]{2,1,0:T(8,128)S(1)} %copy-done.2, f32[12,256]{1,0:T(8,128)S(1)} %fusion.147, f32[12,256]{1,0:T(8,128)S(1)} %reduce_max.72, bf16[768,12,64]{0,2,1:T(8,128)(2,1)S(1)} %constant_dynamic-slice_fusion.5, ...), kind=kOutput, calls=%fused_computation.38.clone.1 | convolution fusion | flops 418578432 | bytes 14573568 | tf_op jit(solution)/shard_map/while/body/eval_jaxpr/hqk,khe->qhe/dot_general | solution.py:117
  204.1 3.5 %fusion.146 = (f32[12,256]{1,0:T(8,128)S(1)}, f32[12,256,256]{1,2,0:T(8,128)}) fusion(bf16[256,12,64]{0,2,1:T(8,128)(2,1)} %get-tuple-element.543, bf16[512,12,64]{0,2,1:T(8,128)(2,1)} %get-tuple-element.542, s32[]{:T(128)S(6)} %select_n.265, pred[256,256]{0,1:T(8,128)(4,1)S(1)} %abs_compare_fusion.7), kind=kOutput, calls=%fused_computation.168.clone.1 | convolution fusion | flops 102233088 | bytes 4009988 | tf_op jit(solution)/shard_map/while/body/eval_jaxpr/qhe,khe->hqk/dot_general | solution.py:94
  207.6 3.5 %copy.64 = f32[12,256,256]{2,1,0:T(8,128)} copy(f32[12,256,256]{1,2,0:T(8,128)} %get-tuple-element.458) | data formatting | bytes 6291456 | tf_op jit(solution)/shard_map/while/body/eval_jaxpr/jit(_where)/select_n | solution.py:108
  211.1 3.0 %fusion.145 = (f32[12,256]{1,0:T(8,128)S(1)}, f32[12,256,768]{2,1,0:T(8,128)S(1)}) fusion(bf16[1024,12,64]{0,2,1:T(8,128)(2,1)S(1)} %get-tuple-element.544, s32[]{:T(128)S(6)} %select_n.264, bf16[512,12,64]{0,2,1:T(8,128)(2,1)} %get-tuple-element.542, s32[]{:T(128)S(6)} %select_n.265, pred[256,768]{1,0:T(8,128)(4,1)} %fusion.144), kind=kOutput, calls=%fused_computation.169.clone.1 | convolution fusion | flops 306705408 | bytes 11218952 | tf_op jit(solution)/shard_map/while/body/eval_jaxpr/qhe,khe->hqk/dot_general | solution.py:91
  214.1 2.9 %fusion.147 = f32[12,256]{1,0:T(8,128)S(1)} fusion(f32[12,256,768]{2,1,0:T(8,128)S(1)} %get-tuple-element.457, f32[12,256,256]{2,1,0:T(8,128)S(1)} %copy-done.2, f32[12,256]{1,0:T(8,128)S(1)} %reduce_max.72), kind=kLoop, calls=%fused_computation.31.clone.1 | loop fusion | flops 9434112 | bytes 12607488 | tf_op jit(solution)/shard_map/while/body/eval_jaxpr/reduce_sum | solution.py:115
  217.0 4.5 %fusion.148 = bf16[12,64,256]{2,1,0:T(8,128)(2,1)} fusion(f32[12,256,768]{2,1,0:T(8,128)S(1)} %get-tuple-element.457, f32[12,256,256]{2,1,0:T(8,128)S(1)} %copy-done.2, f32[12,256]{1,0:T(8,128)S(1)} %fusion.147, f32[12,256]{1,0:T(8,128)S(1)} %reduce_max.72, bf16[768,12,64]{0,2,1:T(8,128)(2,1)S(1)} %constant_dynamic-slice_fusion.5, ...), kind=kOutput, calls=%fused_computation.38.clone.1 | convolution fusion | flops 418578432 | bytes 14573568 | tf_op jit(solution)/shard_map/while/body/eval_jaxpr/hqk,khe->qhe/dot_general | solution.py:117
  223.4 2.6 %convert_reduce_fusion.2 = (f32[512]{0:T(512)S(1)}, bf16[512,768]{1,0:T(8,128)(2,1)S(1)}) fusion(bf16[512,768]{1,0:T(8,128)(2,1)} %bitcast.68, bf16[2,768,768]{2,1,0:T(8,128)(2,1)} %param.33, bf16[512,768]{1,0:T(8,128)(2,1)} %copy-done.6), kind=kOutput, calls=%fused_computation.71 | convolution fusion | flops 605945344 | bytes 3540992 | tf_op jit(solution)/shard_map/dot_general | solution.py:178
  (168 shorter events, 64.1 us)
Async XLA Ops:
  0.6 225.8 %copy-start = (bf16[768,512]{1,0:T(8,128)(2,1)S(1)}, bf16[768,512]{1,0:T(8,128)(2,1)}, u32[]{:S(2)}) copy-start(bf16[768,512]{1,0:T(8,128)(2,1)} %param.35) | copy-start | bytes 2359300
  1.8 12.9 %collective-permute-start.4 = (bf16[256,768]{1,0:T(8,128)(2,1)S(1)}, bf16[256,768]{1,0:T(8,128)(2,1)S(1)}, u32[]{:S(2)}, u32[]{:S(2)}) collective-permute-start(bf16[256,768]{1,0:T(8,128)(2,1)S(1)} %slice_select_fusion.1), channel_id=1, source_target_pairs={{0,1},{16,17}} | collective-permute-start | bytes 1179656 | tf_op jit(solution)/shard_map/ppermute | solution.py:71
  2.4 12.2 %collective-permute-start.3 = (bf16[256,768]{1,0:T(8,128)(2,1)S(1)}, bf16[256,768]{1,0:T(8,128)(2,1)S(1)}, u32[]{:S(2)}, u32[]{:S(2)}) collective-permute-start(bf16[256,768]{1,0:T(8,128)(2,1)S(1)} %slice_select_fusion.1), channel_id=1, source_target_pairs={{0,4},{16,20}} | collective-permute-start | bytes 1179656 | tf_op jit(solution)/shard_map/ppermute | solution.py:71
  3.1 11.5 %collective-permute-start.2 = (bf16[256,768]{1,0:T(8,128)(2,1)S(1)}, bf16[256,768]{1,0:T(8,128)(2,1)S(1)}, u32[]{:S(2)}, u32[]{:S(2)}) collective-permute-start(bf16[256,768]{1,0:T(8,128)(2,1)S(1)} %slice_select_fusion.1), channel_id=1, source_target_pairs={{0,2},{16,18}} | collective-permute-start | bytes 1179656 | tf_op jit(solution)/shard_map/ppermute | solution.py:71
  8.1 6.6 %copy-start.3 = (bf16[512,768]{1,0:T(8,128)(2,1)S(1)}, bf16[512,768]{1,0:T(8,128)(2,1)}, u32[]{:S(2)}) copy-start(bf16[512,768]{1,0:T(8,128)(2,1)} %param.30) | copy-start | bytes 2359300
  14.6 2.1 copy-start.4
  14.6 9.0 %copy-start.17 = (s32[3]{0:T(128)S(1)}, s32[3]{0:T(128)}, u32[]{:S(2)}) copy-start(s32[3]{0:T(128)} %constant.179.clone) | copy-start | bytes 40
  14.7 9.7 %collective-permute-start.6 = (bf16[256,768]{1,0:T(8,128)(2,1)S(1)}, bf16[256,768]{1,0:T(8,128)(2,1)S(1)}, u32[]{:S(2)}, u32[]{:S(2)}) collective-permute-start(bf16[256,768]{1,0:T(8,128)(2,1)S(1)} %select_select_fusion.3), channel_id=1, source_target_pairs={{1,5},{2,6},{4,8},{17,21},{18,22},{20,24}} | collective-permute-start | bytes 1179656 | tf_op jit(solution)/shard_map/ppermute | solution.py:71
  16.0 8.4 %collective-permute-start.5 = (bf16[256,768]{1,0:T(8,128)(2,1)S(1)}, bf16[256,768]{1,0:T(8,128)(2,1)S(1)}, u32[]{:S(2)}, u32[]{:S(2)}) collective-permute-start(bf16[256,768]{1,0:T(8,128)(2,1)S(1)} %select_select_fusion.3), channel_id=1, source_target_pairs={{1,3},{17,19}} | collective-permute-start | bytes 1179656 | tf_op jit(solution)/shard_map/ppermute | solution.py:71
  18.0 25.8 %collective-permute-start = (bf16[256,1536]{1,0:T(8,128)(2,1)}, bf16[256,1536]{1,0:T(8,128)(2,1)}, u32[]{:S(2)}, u32[]{:S(2)}) collective-permute-start(bf16[256,1536]{1,0:T(8,128)(2,1)} %get-tuple-element.313), channel_id=1, source_target_pairs={{0,1},{1,2},{2,3},{3,4},{4,5},{5,6},{6,7},{7,8},{8,9},{9,10},{10,1... | collective-permute-start | bytes 2359304 | tf_op jit(solution)/shard_map/ppermute | solution.py:21
  19.9 23.9 %collective-permute-start.1 = (bf16[256,1536]{1,0:T(8,128)(2,1)}, bf16[256,1536]{1,0:T(8,128)(2,1)}, u32[]{:S(2)}, u32[]{:S(2)}) collective-permute-start(bf16[256,1536]{1,0:T(8,128)(2,1)} %get-tuple-element.314), channel_id=1, source_target_pairs={{1,0},{2,1},{3,2},{4,3},{5,4},{6,5},{7,6},{8,7},{9,8},{10,9},{11,1... | collective-permute-start | bytes 2359304 | tf_op jit(solution)/shard_map/ppermute | solution.py:22
  25.1 11.5 %collective-permute-start.7 = (bf16[256,768]{1,0:T(8,128)(2,1)S(1)}, bf16[256,768]{1,0:T(8,128)(2,1)S(1)}, u32[]{:S(2)}, u32[]{:S(2)}) collective-permute-start(bf16[256,768]{1,0:T(8,128)(2,1)S(1)} %select_select_fusion.2), channel_id=1, source_target_pairs={{3,7},{5,9},{6,10},{8,12},{19,23},{21,25},{22,26},{24,28}} | collective-permute-start | bytes 1179656 | tf_op jit(solution)/shard_map/ppermute | solution.py:71
  34.3 1.5 copy-start.16
  35.9 5.6 %copy-start.15 = (s32[3]{0:T(128)S(1)}, s32[3]{0:T(128)}, u32[]{:S(2)}) copy-start(s32[3]{0:T(128)} %constant.182.clone) | copy-start | bytes 40
  37.3 4.9 %collective-permute-start.8 = (bf16[256,768]{1,0:T(8,128)(2,1)S(1)}, bf16[256,768]{1,0:T(8,128)(2,1)}, u32[]{:S(2)}, u32[]{:S(2)}) collective-permute-start(bf16[256,768]{1,0:T(8,128)(2,1)S(1)} %broadcast_select_fusion.5), channel_id=1, source_target_pairs={{7,11},{9,13},{10,14},{23,27},{25,29},{26,30}} | collective-permute-start | bytes 1179656 | tf_op jit(solution)/shard_map/ppermute | solution.py:71
  42.9 8.6 %collective-permute-start.9 = (bf16[256,768]{1,0:T(8,128)(2,1)S(1)}, bf16[256,768]{1,0:T(8,128)(2,1)S(1)}, u32[]{:S(2)}, u32[]{:S(2)}) collective-permute-start(bf16[256,768]{1,0:T(8,128)(2,1)S(1)} %broadcast_select_fusion.7), channel_id=1, source_target_pairs={{11,15},{27,31}} | collective-permute-start | bytes 1179656 | tf_op jit(solution)/shard_map/ppermute | solution.py:71
  69.5 2.9 %copy-start.1 = (f32[12,256,256]{2,1,0:T(8,128)S(1)}, f32[12,256,256]{2,1,0:T(8,128)}, u32[]{:S(2)}) copy-start(f32[12,256,256]{2,1,0:T(8,128)} %copy.62) | copy-start | bytes 9437188 | tf_op jit(solution)/shard_map/while
  72.4 2.9 %copy-start.8 = (bf16[256,12,64]{0,2,1:T(8,128)(2,1)S(1)}, bf16[256,12,64]{0,2,1:T(8,128)(2,1)}, u32[]{:S(2)}) copy-start(bf16[256,12,64]{0,2,1:T(8,128)(2,1)} %get-tuple-element.495) | copy-start | bytes 1179652 | tf_op jit(solution)/shard_map/while
  93.3 3.0 %copy-start.1 = (f32[12,256,256]{2,1,0:T(8,128)S(1)}, f32[12,256,256]{2,1,0:T(8,128)}, u32[]{:S(2)}) copy-start(f32[12,256,256]{2,1,0:T(8,128)} %copy.62) | copy-start | bytes 9437188 | tf_op jit(solution)/shard_map/while
  96.3 2.9 %copy-start.8 = (bf16[256,12,64]{0,2,1:T(8,128)(2,1)S(1)}, bf16[256,12,64]{0,2,1:T(8,128)(2,1)}, u32[]{:S(2)}) copy-start(bf16[256,12,64]{0,2,1:T(8,128)(2,1)} %get-tuple-element.495) | copy-start | bytes 1179652 | tf_op jit(solution)/shard_map/while
  105.6 7.2 %copy-start.10 = (f32[768]{0:T(1024)S(1)}, f32[768]{0:T(1024)}, u32[]{:S(2)}) copy-start(f32[768]{0:T(1024)} %get-tuple-element.251) | copy-start | bytes 9220
  108.2 10.9 %copy-start.6 = (bf16[512,768]{1,0:T(8,128)(2,1)}, bf16[512,768]{1,0:T(8,128)(2,1)S(1)}, u32[]{:S(2)}) copy-start(bf16[512,768]{1,0:T(8,128)(2,1)S(1)} %get-tuple-element.322) | copy-start | bytes 2359300
  108.3 2.5 %collective-permute-start.14 = (bf16[256,768]{1,0:T(8,128)(2,1)S(1)}, bf16[256,768]{1,0:T(8,128)(2,1)S(1)}, u32[]{:S(2)}, u32[]{:S(2)}) collective-permute-start(bf16[256,768]{1,0:T(8,128)(2,1)S(1)} %slice_select_fusion), channel_id=1, source_target_pairs={{0,1},{16,17}} | collective-permute-start | bytes 1179656 | tf_op jit(solution)/shard_map/ppermute | solution.py:71
  109.0 1.8 collective-permute-start.13
  109.6 1.1 collective-permute-start.12
  110.8 25.8 %collective-permute-start.16 = (bf16[256,768]{1,0:T(8,128)(2,1)S(1)}, bf16[256,768]{1,0:T(8,128)(2,1)S(1)}, u32[]{:S(2)}, u32[]{:S(2)}) collective-permute-start(bf16[256,768]{1,0:T(8,128)(2,1)S(1)} %select_select_fusion.1), channel_id=1, source_target_pairs={{1,5},{2,6},{4,8},{17,21},{18,22},{20,24}} | collective-permute-start | bytes 1179656 | tf_op jit(solution)/shard_map/ppermute | solution.py:71
  112.1 24.5 %collective-permute-start.15 = (bf16[256,768]{1,0:T(8,128)(2,1)S(1)}, bf16[256,768]{1,0:T(8,128)(2,1)S(1)}, u32[]{:S(2)}, u32[]{:S(2)}) collective-permute-start(bf16[256,768]{1,0:T(8,128)(2,1)S(1)} %select_select_fusion.1), channel_id=1, source_target_pairs={{1,3},{17,19}} | collective-permute-start | bytes 1179656 | tf_op jit(solution)/shard_map/ppermute | solution.py:71
  119.1 19.5 %copy-start.5 = (bf16[512,2304]{1,0:T(8,128)(2,1)}, bf16[512,2304]{1,0:T(8,128)(2,1)S(1)}, u32[]{:S(2)}) copy-start(bf16[512,2304]{1,0:T(8,128)(2,1)S(1)} %get-tuple-element.323) | copy-start | bytes 7077892
  137.3 8.2 %collective-permute-start.17 = (bf16[256,768]{1,0:T(8,128)(2,1)S(1)}, bf16[256,768]{1,0:T(8,128)(2,1)S(1)}, u32[]{:S(2)}, u32[]{:S(2)}) collective-permute-start(bf16[256,768]{1,0:T(8,128)(2,1)S(1)} %select_select_fusion), channel_id=1, source_target_pairs={{3,7},{5,9},{6,10},{8,12},{19,23},{21,25},{22,26},{24,28}} | collective-permute-start | bytes 1179656 | tf_op jit(solution)/shard_map/ppermute | solution.py:71
  139.9 22.0 %collective-permute-start.10 = (bf16[256,1536]{1,0:T(8,128)(2,1)}, bf16[256,1536]{1,0:T(8,128)(2,1)}, u32[]{:S(2)}, u32[]{:S(2)}) collective-permute-start(bf16[256,1536]{1,0:T(8,128)(2,1)} %get-tuple-element.311), channel_id=1, source_target_pairs={{0,1},{1,2},{2,3},{3,4},{4,5},{5,6},{6,7},{7,8},{8,9},{9,10},{10,1... | collective-permute-start | bytes 2359304 | tf_op jit(solution)/shard_map/ppermute | solution.py:21
  141.9 20.1 %collective-permute-start.11 = (bf16[256,1536]{1,0:T(8,128)(2,1)}, bf16[256,1536]{1,0:T(8,128)(2,1)}, u32[]{:S(2)}, u32[]{:S(2)}) collective-permute-start(bf16[256,1536]{1,0:T(8,128)(2,1)} %get-tuple-element.312), channel_id=1, source_target_pairs={{1,0},{2,1},{3,2},{4,3},{5,4},{6,5},{7,6},{8,7},{9,8},{10,9},{11,1... | collective-permute-start | bytes 2359304 | tf_op jit(solution)/shard_map/ppermute | solution.py:22
  146.2 6.3 %collective-permute-start.18 = (bf16[256,768]{1,0:T(8,128)(2,1)S(1)}, bf16[256,768]{1,0:T(8,128)(2,1)}, u32[]{:S(2)}, u32[]{:S(2)}) collective-permute-start(bf16[256,768]{1,0:T(8,128)(2,1)S(1)} %broadcast_select_fusion.4), channel_id=1, source_target_pairs={{7,11},{9,13},{10,14},{23,27},{25,29},{26,30}} | collective-permute-start | bytes 1179656 | tf_op jit(solution)/shard_map/ppermute | solution.py:71
  153.3 16.4 %collective-permute-start.19 = (bf16[256,768]{1,0:T(8,128)(2,1)S(1)}, bf16[256,768]{1,0:T(8,128)(2,1)S(1)}, u32[]{:S(2)}, u32[]{:S(2)}) collective-permute-start(bf16[256,768]{1,0:T(8,128)(2,1)S(1)} %broadcast_select_fusion.6), channel_id=1, source_target_pairs={{11,15},{27,31}} | collective-permute-start | bytes 1179656 | tf_op jit(solution)/shard_map/ppermute | solution.py:71
  187.5 2.9 %copy-start.2 = (f32[12,256,256]{2,1,0:T(8,128)S(1)}, f32[12,256,256]{2,1,0:T(8,128)}, u32[]{:S(2)}) copy-start(f32[12,256,256]{2,1,0:T(8,128)} %copy.64) | copy-start | bytes 9437188 | tf_op jit(solution)/shard_map/while
  190.4 2.9 %copy-start.7 = (bf16[256,12,64]{0,2,1:T(8,128)(2,1)S(1)}, bf16[256,12,64]{0,2,1:T(8,128)(2,1)}, u32[]{:S(2)}) copy-start(bf16[256,12,64]{0,2,1:T(8,128)(2,1)} %get-tuple-element.540) | copy-start | bytes 1179652 | tf_op jit(solution)/shard_map/while
  211.1 3.0 %copy-start.2 = (f32[12,256,256]{2,1,0:T(8,128)S(1)}, f32[12,256,256]{2,1,0:T(8,128)}, u32[]{:S(2)}) copy-start(f32[12,256,256]{2,1,0:T(8,128)} %copy.64) | copy-start | bytes 9437188 | tf_op jit(solution)/shard_map/while
  214.1 2.9 %copy-start.7 = (bf16[256,12,64]{0,2,1:T(8,128)(2,1)S(1)}, bf16[256,12,64]{0,2,1:T(8,128)(2,1)}, u32[]{:S(2)}) copy-start(bf16[256,12,64]{0,2,1:T(8,128)(2,1)} %get-tuple-element.540) | copy-start | bytes 1179652 | tf_op jit(solution)/shard_map/while
  223.4 3.0 %copy-start.14 = (f32[768]{0:T(1024)S(1)}, f32[768]{0:T(1024)}, u32[]{:S(2)}) copy-start(f32[768]{0:T(1024)} %param.34) | copy-start | bytes 9220
  226.0 1.4 copy-start.11
  226.0 1.6 copy-start.12
  226.0 1.6 copy-start.13
  227.7 0.6 copy-start.9

commit v2 on v1

--- a/solution.py
+++ b/solution.py
@@ -1,6 +1,8 @@
 import jax
 import jax.numpy as jnp
 from jax import lax
+from jax.experimental import pallas as pl
+from jax.experimental.pallas import tpu as pltpu
 from jax.sharding import PartitionSpec as P
 
 HEADS = 12
@@ -83,41 +85,80 @@
     return (centred * lax.rsqrt(row_var + 1e-05) * gain_row).astype(jnp.bfloat16)
 
 
-def attend_block(
-    query_block, key_block, value_block, prompt_keys, prompt_values, row_start, total_len
-):
-    block_rows = query_block.shape[0]
-    band_width = key_block.shape[0]
-    band_scores = jnp.einsum(
-        "qhe,khe->hqk", query_block, key_block, preferred_element_type=jnp.float32
-    )
-    prompt_scores = jnp.einsum(
-        "qhe,khe->hqk", query_block, prompt_keys, preferred_element_type=jnp.float32
-    )
-    query_pos = row_start + jnp.arange(block_rows, dtype=jnp.int32)
-    key_pos = row_start - HALF + jnp.arange(band_width, dtype=jnp.int32)
-    prompt_pos = jnp.arange(PROMPT, dtype=jnp.int32)
-    band_mask = (
-        (jnp.abs(key_pos[None, :] - query_pos[:, None]) <= HALF)
-        & (key_pos[None, :] >= 0)
-        & (key_pos[None, :] < total_len)
-    )
-    prompt_mask = jnp.abs(prompt_pos[None, :] - query_pos[:, None]) > HALF
-    scores = jnp.concatenate(
-        [
-            jnp.where(prompt_mask[None], prompt_scores, -1e30),
-            jnp.where(band_mask[None], band_scores, -1e30),
-        ],
-        axis=-1,
-    )
-    row_max = jnp.max(scores, axis=-1, keepdims=True)
-    exps = jnp.exp(scores - row_max)
-    attn_probs = (exps / jnp.sum(exps, axis=-1, keepdims=True)).astype(jnp.bfloat16)
-    value_rows = jnp.concatenate([prompt_values, value_block], axis=0)
-    attn_out = jnp.einsum(
-        "hqk,khe->qhe", attn_probs, value_rows, preferred_element_type=jnp.float32
-    )
-    return attn_out.reshape(block_rows, HEADS * HEAD).astype(jnp.bfloat16)
+QUERY_TILE = 128
+
+
+def attention_kernel(pos_ref, q_ref, band_ref, prompt_ref, out_ref):
+    tile = q_ref.shape[0]
+    width = tile + 2 * HALF
+    feat = q_ref.shape[1]
+    block = pl.program_id(0)
+    first = pos_ref[0]
+    total = pos_ref[1]
+    query_pos = first + block * tile + lax.broadcasted_iota(jnp.int32, (tile, 1), 0)
+    key_pos = first + block * tile - HALF + lax.broadcasted_iota(jnp.int32, (1, width), 1)
+    gap = key_pos - query_pos
+    band_ok = (gap >= -HALF) & (gap <= HALF) & (key_pos >= 0) & (key_pos < total)
+    prompt_pos = lax.broadcasted_iota(jnp.int32, (1, PROMPT), 1)
+    prompt_ok = jnp.abs(prompt_pos - query_pos) > HALF
+    start = pl.multiple_of(block * tile, tile)
+    contract = (((1,), (1,)), ((), ()))
+    for head in range(HEADS):
+        cols = slice(head * HEAD, (head + 1) * HEAD)
+        vcols = slice(feat + head * HEAD, feat + (head + 1) * HEAD)
+        query = q_ref[:, cols]
+        band_scores = lax.dot_general(
+            query, band_ref[pl.ds(start, width), cols], contract,
+            preferred_element_type=jnp.float32,
+        )
+        prompt_scores = lax.dot_general(
+            query, prompt_ref[:, cols], contract, preferred_element_type=jnp.float32
+        )
+        band_scores = jnp.where(band_ok, band_scores, -1e30)
+        prompt_scores = jnp.where(prompt_ok, prompt_scores, -1e30)
+        row_max = jnp.maximum(
+            jnp.max(band_scores, axis=1, keepdims=True),
+            jnp.max(prompt_scores, axis=1, keepdims=True),
+        )
+        band_exp = jnp.exp(band_scores - row_max)
+        prompt_exp = jnp.exp(prompt_scores - row_max)
+        denom = jnp.sum(band_exp, axis=1, keepdims=True) + jnp.sum(
+            prompt_exp, axis=1, keepdims=True
+        )
+        band_probs = (band_exp / denom).astype(jnp.bfloat16)
+        prompt_probs = (prompt_exp / denom).astype(jnp.bfloat16)
+        attn = jnp.dot(
+            band_probs, band_ref[pl.ds(start, width), vcols],
+            preferred_element_type=jnp.float32,
+        ) + jnp.dot(prompt_probs, prompt_ref[:, vcols], preferred_element_type=jnp.float32)
+        out_ref[:, cols] = attn.astype(out_ref.dtype)
+
+
+def attention(queries, band_kv, prompt_kv, first_pos, total_len):
+    rows, feat = queries.shape
+    tile = min(QUERY_TILE, rows)
+    pos = jnp.stack([first_pos, total_len]).astype(jnp.int32)
+    width = tile + 2 * HALF
+    flops = 4 * rows * (width + PROMPT) * feat
+    return pl.pallas_call(
+        attention_kernel,
+        out_shape=jax.ShapeDtypeStruct((rows, feat), jnp.bfloat16),
+        grid_spec=pltpu.PrefetchScalarGridSpec(
+            num_scalar_prefetch=1,
+            grid=(rows // tile,),
+            in_specs=[
+                pl.BlockSpec((tile, feat), lambda b, p: (b, 0)),
+                pl.BlockSpec(band_kv.shape, lambda b, p: (0, 0)),
+                pl.BlockSpec(prompt_kv.shape, lambda b, p: (0, 0)),
+            ],
+            out_specs=pl.BlockSpec((tile, feat), lambda b, p: (b, 0)),
+        ),
+        cost_estimate=pl.CostEstimate(
+            flops=flops,
+            transcendentals=rows * (width + PROMPT) * HEADS,
+            bytes_accessed=2 * (2 * queries.size + band_kv.size + prompt_kv.size),
+        ),
+    )(pos, queries, band_kv, prompt_kv)
 
 
 def per_device(
@@ -138,8 +179,6 @@
     seq_place = lax.axis_index("seq")
     total_len = tok_rows * seq_devices
     first_pos = seq_place * tok_rows
-    block_rows = min(256, tok_rows)
-    block_count = tok_rows // block_rows
     hidden_state = hidden_in
     for layer_idx in range(LAYERS):
         normed = layer_norm(hidden_state, ln_gain[layer_idx])
@@ -154,27 +193,7 @@
             weights[:, feat_width:],
             preferred_element_type=jnp.float32,
         ).astype(jnp.bfloat16)
-        query_heads = queries.reshape(tok_rows, HEADS, HEAD)
-        band_keys = extended[:, :feat_width].reshape(-1, HEADS, HEAD)
-        band_values = extended[:, feat_width:].reshape(-1, HEADS, HEAD)
-        prompt_keys = prompt_kv[:, :feat_width].reshape(PROMPT, HEADS, HEAD)
-        prompt_values = prompt_kv[:, feat_width:].reshape(PROMPT, HEADS, HEAD)
-
-        def one_block(block_idx):
-            local_start = block_idx * block_rows
-            return attend_block(
-                lax.dynamic_slice_in_dim(query_heads, local_start, block_rows),
-                lax.dynamic_slice_in_dim(band_keys, local_start, block_rows + 2 * HALF),
-                lax.dynamic_slice_in_dim(band_values, local_start, block_rows + 2 * HALF),
-                prompt_keys,
-                prompt_values,
-                first_pos + local_start,
-                total_len,
-            )
-
-        attended = lax.map(one_block, jnp.arange(block_count, dtype=jnp.int32)).reshape(
-            tok_rows, feat_width
-        )
+        attended = attention(queries, extended, prompt_kv, first_pos, total_len)
         projection = jnp.dot(attended, w_out[layer_idx], preferred_element_type=jnp.float32)
         hidden_state = (hidden_state.astype(jnp.float32) + projection).astype(jnp.bfloat16)
     final = layer_norm(hidden_state, final_gain)

time: 230 us -> 177 us (0.77)
  the two profiles are of different devices: /device:TPU:12 before, /device:TPU:20 now
where the time goes in v2:
time: 177 us
  Pallas kernels  54.8 us (31%)
  waiting for transfers between devices  44.2 us (25%)
  starting transfers between devices  24.9 us (14%)
  other arithmetic  22.6 us (13%)
  matrix products  19.5 us (11%)
  local copies, waits for them, and re-layouts  8.7 us (5%)
  between operations  1.85 us (1%)
    pallas_call x2, Pallas kernels, attention(): pl.pallas_call(attention_kernel, out_shape=jax.ShapeDtypeStruct((rows, fe...  54.8 us
    ppermute x16, waiting for transfers between devices, spread(): got = lax.ppermute(block, axis, op)  33.9 us
    ppermute x16, starting transfers between devices, spread(): got = lax.ppermute(block, axis, op)  13.7 us
    dot_general x2, matrix products, per_device(): projected = jnp.dot(normed, weights, preferred_element_type=jnp.float32)  10.4 us
    ppermute x2, waiting for transfers between devices, with_halo(): before = lax.ppermute(last, axis, up)  10.4 us
    ppermute x2, starting transfers between devices, with_halo(): after = lax.ppermute(leading, axis, down)  7.29 us
    squeeze x1, local copies, waits for them, and re-layouts, per_device(): weights = w_qkv[layer_idx]  6.46 us
    select_n x8, other arithmetic, spread(): received = jnp.where(jnp.any(place == targets), got, received)  5.19 us
  transfers between devices with their start and end apart: 20, of which 5 were waited for; matrix products, arithmetic and copies ran while one was open for 21% of the time, Pallas kernels for 0%

profile of v2, /device:TPU:20, one launch (start us, length us, event | category | flops | bytes accessed | tf_op | source)
XLA Modules:
  0.0 176.5 jit_solution(2532304796444416662)
XLA Ops:
  0.7 1.1 slice_select_fusion.1
  1.8 0.7 collective-permute-start.4
  2.5 0.7 collective-permute-start.3
  3.2 0.7 collective-permute-start.2
  3.9 1.3 convert_reduce_fusion.1
  5.2 1.5 fusion.11
  6.8 6.3 %fusion.62 = (bf16[512,2304]{1,0:T(8,128)(2,1)S(1)}, f32[512,2304]{1,0:T(8,128)}) fusion(bf16[2,768,2304]{2,1,0:T(8,128)(2,1)} %param.28, bf16[512,768]{1,0:T(8,128)(2,1)S(1)} %copy-done.1, f32[768]{0:T(1024)S(1)} %get-tuple-element.6, f32[512]{0:T(512)S(1)} %add_rsqrt_fusion.2, f32[512]{0:T(512)S(1)} %broadcast_multiply_fusion.2), kind=kOutput, calls=%fused_computation.113 | convolution fusion | flops 1815085056 | bytes 11410432 | tf_op jit(solution)/shard_map/dot_general | solution.py:186
  13.2 0.7 collective-permute-start.6
  13.8 0.7 collective-permute-start.5
  14.5 1.3 fusion.61
  15.8 1.9 %collective-permute-start = (bf16[256,1536]{1,0:T(8,128)(2,1)}, bf16[256,1536]{1,0:T(8,128)(2,1)}, u32[]{:S(2)}, u32[]{:S(2)}) collective-permute-start(bf16[256,1536]{1,0:T(8,128)(2,1)} %get-tuple-element.15), channel_id=1, source_target_pairs={{0,1},{1,2},{2,3},{3,4},{4,5},{5,6},{6,7},{7,8},{8,9},{9,10},{10,1... | collective-permute-start | bytes 2359304 | tf_op jit(solution)/shard_map/ppermute | solution.py:23
  17.7 3.6 %collective-permute-start.1 = (bf16[256,1536]{1,0:T(8,128)(2,1)}, bf16[256,1536]{1,0:T(8,128)(2,1)}, u32[]{:S(2)}, u32[]{:S(2)}) collective-permute-start(bf16[256,1536]{1,0:T(8,128)(2,1)} %get-tuple-element.16), channel_id=1, source_target_pairs={{1,0},{2,1},{3,2},{4,3},{5,4},{6,5},{7,6},{8,7},{9,8},{10,9},{11,1... | collective-permute-start | bytes 2359304 | tf_op jit(solution)/shard_map/ppermute | solution.py:24
  21.4 0.7 compare_reduce_fusion
  22.1 0.8 select_select_fusion.2
  22.9 1.4 collective-permute-start.7
  24.3 6.5 %slice_bitcast_fusion = (bf16[768,2304]{1,0:T(8,128)(2,1)}, bf16[768,2304]{1,0:T(8,128)(2,1)}) fusion(bf16[2,768,2304]{2,1,0:T(8,128)(2,1)} %param.28), kind=kLoop, calls=%fused_computation | loop fusion | bytes 14155776 | tf_op jit(solution)/shard_map/squeeze | solution.py:185
  31.4 0.7 compare_reduce_fusion.1
  32.1 2.1 %collective-permute-done.7 = bf16[256,768]{1,0:T(8,128)(2,1)} collective-permute-done((bf16[256,768]{1,0:T(8,128)(2,1)S(1)}, bf16[256,768]{1,0:T(8,128)(2,1)}, u32[]{:S(2)}, u32[]{:S(2)}) %collective-permute-start.7) | collective-permute-done | bytes 393248 | tf_op jit(solution)/shard_map/ppermute | solution.py:73
  34.2 1.7 broadcast_select_fusion.3
  35.9 1.3 collective-permute-start.8
  37.9 2.4 %fusion.20.q_ref = bf16[512,768]{1,0:T(8,128)(2,1)} fusion(f32[512,2304]{1,0:T(8,128)} %get-tuple-element.18), kind=kLoop, calls=%fused_computation.36 | loop fusion | flops 786432 | bytes 2359296 | tf_op jit(solution)/shard_map/convert_element_type | solution.py:187
  40.3 2.2 %collective-permute-done.8 = bf16[256,768]{1,0:T(8,128)(2,1)S(1)} collective-permute-done((bf16[256,768]{1,0:T(8,128)(2,1)S(1)}, bf16[256,768]{1,0:T(8,128)(2,1)S(1)}, u32[]{:S(2)}, u32[]{:S(2)}) %collective-permute-start.8) | collective-permute-done | bytes 393248 | tf_op jit(solution)/shard_map/ppermute | solution.py:73
  43.1 0.7 collective-permute-start.9
  44.4 3.1 %pad_maximum_fusion.band_ref = bf16[1024,1536]{1,0:T(8,128)(2,1)} fusion(bf16[256,1536]{1,0:T(8,128)(2,1)} %collective-permute-done.1, bf16[512,1536]{1,0:T(8,128)(2,1)S(1)} %slice.90, bf16[256,1536]{1,0:T(8,128)(2,1)} %collective-permute-done), kind=kLoop, calls=%fused_computation.2 | loop fusion | flops 9437184 | bytes 6291456 | tf_op jit(solution)/shard_map/concatenate | solution.py:25
  48.0 1.7 convolution_convert_fusion.1.prompt_ref
  49.7 27.4 %shard_map.257 = bf16[512,768]{1,0:T(8,128)(2,1)} custom-call(s32[2]{0:T(128)} %pad_add_fusion.pos_ref, bf16[512,768]{1,0:T(8,128)(2,1)} %fusion.20.q_ref, bf16[1024,1536]{1,0:T(8,128)(2,1)} %pad_maximum_fusion.band_ref, bf16[256,1536]{1,0:T(8,128)(2,1)} %convolution_convert_fusion.1.prompt_ref), custom_call_target="tpu_custom_call" | custom-call | flops 1409286144 | bytes 5505024 | tf_op jit(solution)/shard_map/pallas_call | solution.py:143
  77.1 2.4 %convert_reduce_fusion = (f32[512]{0:T(512)S(1)}, bf16[512,768]{1,0:T(8,128)(2,1)S(1)}) fusion(bf16[512,768]{1,0:T(8,128)(2,1)} %shard_map.257, bf16[2,768,768]{2,1,0:T(8,128)(2,1)} %param.29, bf16[512,768]{1,0:T(8,128)(2,1)S(1)} %copy-done.1), kind=kOutput, calls=%fused_computation.8 | convolution fusion | flops 605945344 | bytes 3540992 | tf_op jit(solution)/shard_map/dot_general | solution.py:197
  79.5 0.7 collective-permute-start.14
  80.2 0.7 collective-permute-start.13
  80.9 0.7 collective-permute-start.12
  81.7 0.9 collective-permute-start.16
  82.6 0.7 collective-permute-start.15
  83.7 0.7 select_select_fusion
  84.4 1.3 collective-permute-start.17
  85.7 4.1 %fusion.63 = (bf16[512,2304]{1,0:T(8,128)(2,1)S(1)}, f32[512,2304]{1,0:T(8,128)S(1)}) fusion(bf16[2,768,2304]{2,1,0:T(8,128)(2,1)} %param.28, bf16[512,768]{1,0:T(8,128)(2,1)S(1)} %get-tuple-element.20, f32[768]{0:T(1024)S(1)} %get-tuple-element.5, f32[512]{0:T(512)S(1)} %add_rsqrt_fusion.1, f32[512]{0:T(512)S(1)} %broadcast_multiply_fusion.1), kind=kOutput, calls=%fused_computation.114 | convolution fusion | flops 1815085056 | bytes 11410432 | tf_op jit(solution)/shard_map/dot_general | solution.py:186
  89.9 26.8 %collective-permute-done.17 = bf16[256,768]{1,0:T(8,128)(2,1)S(1)} collective-permute-done((bf16[256,768]{1,0:T(8,128)(2,1)S(1)}, bf16[256,768]{1,0:T(8,128)(2,1)S(1)}, u32[]{:S(2)}, u32[]{:S(2)}) %collective-permute-start.17) | collective-permute-done | bytes 393248 | tf_op jit(solution)/shard_map/ppermute | solution.py:73
  117.3 1.3 collective-permute-start.18
  118.7 1.9 %collective-permute-start.10 = (bf16[256,1536]{1,0:T(8,128)(2,1)S(1)}, bf16[256,1536]{1,0:T(8,128)(2,1)S(1)}, u32[]{:S(2)}, u32[]{:S(2)}) collective-permute-start(bf16[256,1536]{1,0:T(8,128)(2,1)S(1)} %get-tuple-element.13), channel_id=1, source_target_pairs={{0,1},{1,2},{2,3},{3,4},{4,5},{5,6},{6,7},{7,8},{8,9},{9,10},{10,1... | collective-permute-start | bytes 2359304 | tf_op jit(solution)/shard_map/ppermute | solution.py:23
  120.7 3.6 %collective-permute-start.11 = (bf16[256,1536]{1,0:T(8,128)(2,1)S(1)}, bf16[256,1536]{1,0:T(8,128)(2,1)S(1)}, u32[]{:S(2)}, u32[]{:S(2)}) collective-permute-start(bf16[256,1536]{1,0:T(8,128)(2,1)S(1)} %get-tuple-element.14), channel_id=1, source_target_pairs={{1,0},{2,1},{3,2},{4,3},{5,4},{6,5},{7,6},{8,7},{9,8},{10,9},{11,1... | collective-permute-start | bytes 2359304 | tf_op jit(solution)/shard_map/ppermute | solution.py:24
  125.0 2.7 %collective-permute-done.18 = bf16[256,768]{1,0:T(8,128)(2,1)S(1)} collective-permute-done((bf16[256,768]{1,0:T(8,128)(2,1)S(1)}, bf16[256,768]{1,0:T(8,128)(2,1)S(1)}, u32[]{:S(2)}, u32[]{:S(2)}) %collective-permute-start.18) | collective-permute-done | bytes 393248 | tf_op jit(solution)/shard_map/ppermute | solution.py:73
  128.3 0.7 collective-permute-start.19
  129.0 1.0 fusion.19.q_ref
  130.1 10.4 %collective-permute-done.10 = bf16[256,1536]{1,0:T(8,128)(2,1)S(1)} collective-permute-done((bf16[256,1536]{1,0:T(8,128)(2,1)S(1)}, bf16[256,1536]{1,0:T(8,128)(2,1)S(1)}, u32[]{:S(2)}, u32[]{:S(2)}) %collective-permute-start.10) | collective-permute-done | bytes 786464 | tf_op jit(solution)/shard_map/ppermute | solution.py:23
  140.5 1.8 %pad_maximum_fusion.1.band_ref = bf16[1024,1536]{1,0:T(8,128)(2,1)} fusion(bf16[256,1536]{1,0:T(8,128)(2,1)S(1)} %collective-permute-done.11, bf16[512,1536]{1,0:T(8,128)(2,1)S(1)} %slice.95, bf16[256,1536]{1,0:T(8,128)(2,1)S(1)} %collective-permute-done.10), kind=kLoop, calls=%fused_computation.3 | loop fusion | flops 9437184 | bytes 6291456 | tf_op jit(solution)/shard_map/concatenate | solution.py:25
  142.8 1.7 convolution_convert_fusion.prompt_ref
  144.5 27.4 %shard_map.258 = bf16[512,768]{1,0:T(8,128)(2,1)} custom-call(s32[2]{0:T(128)} %pad_add_fusion.pos_ref, bf16[512,768]{1,0:T(8,128)(2,1)} %fusion.19.q_ref, bf16[1024,1536]{1,0:T(8,128)(2,1)} %pad_maximum_fusion.1.band_ref, bf16[256,1536]{1,0:T(8,128)(2,1)} %convolution_convert_fusion.prompt_ref), custom_call_target="tpu_custom_call" | custom-call | flops 1409286144 | bytes 5505024 | tf_op jit(solution)/shard_map/pallas_call | solution.py:143
  171.9 2.4 %convert_reduce_fusion.2 = (f32[512]{0:T(512)S(1)}, bf16[512,768]{1,0:T(8,128)(2,1)S(1)}) fusion(bf16[512,768]{1,0:T(8,128)(2,1)} %shard_map.258, bf16[2,768,768]{2,1,0:T(8,128)(2,1)} %param.29, bf16[512,768]{1,0:T(8,128)(2,1)S(1)} %get-tuple-element.20), kind=kOutput, calls=%fused_computation.15 | convolution fusion | flops 605945344 | bytes 3540992 | tf_op jit(solution)/shard_map/dot_general | solution.py:197
  174.7 0.8 fusion.35
  (77 shorter events, 6.9 us)
Async XLA Ops:
  0.6 174.0 %copy-start = (bf16[768,512]{1,0:T(8,128)(2,1)S(1)}, bf16[768,512]{1,0:T(8,128)(2,1)}, u32[]{:S(2)}) copy-start(bf16[768,512]{1,0:T(8,128)(2,1)} %param.31) | copy-start | bytes 2359300
  0.6 6.1 %copy-start.1 = (bf16[512,768]{1,0:T(8,128)(2,1)S(1)}, bf16[512,768]{1,0:T(8,128)(2,1)}, u32[]{:S(2)}) copy-start(bf16[512,768]{1,0:T(8,128)(2,1)} %param.26) | copy-start | bytes 2359300
  0.7 6.1 %copy-start.7 = (f32[2,768]{1,0:T(2,128)S(1)}, f32[2,768]{1,0:T(2,128)}, u32[]{:S(2)}) copy-start(f32[2,768]{1,0:T(2,128)} %param.27) | copy-start | bytes 18436
  1.8 11.2 %collective-permute-start.4 = (bf16[256,768]{1,0:T(8,128)(2,1)S(1)}, bf16[256,768]{1,0:T(8,128)(2,1)S(1)}, u32[]{:S(2)}, u32[]{:S(2)}) collective-permute-start(bf16[256,768]{1,0:T(8,128)(2,1)S(1)} %slice_select_fusion.1), channel_id=1, source_target_pairs={{0,1},{16,17}} | collective-permute-start | bytes 1179656 | tf_op jit(solution)/shard_map/ppermute | solution.py:73
  2.5 10.5 %collective-permute-start.3 = (bf16[256,768]{1,0:T(8,128)(2,1)S(1)}, bf16[256,768]{1,0:T(8,128)(2,1)S(1)}, u32[]{:S(2)}, u32[]{:S(2)}) collective-permute-start(bf16[256,768]{1,0:T(8,128)(2,1)S(1)} %slice_select_fusion.1), channel_id=1, source_target_pairs={{0,4},{16,20}} | collective-permute-start | bytes 1179656 | tf_op jit(solution)/shard_map/ppermute | solution.py:73
  3.2 9.9 %collective-permute-start.2 = (bf16[256,768]{1,0:T(8,128)(2,1)S(1)}, bf16[256,768]{1,0:T(8,128)(2,1)S(1)}, u32[]{:S(2)}, u32[]{:S(2)}) collective-permute-start(bf16[256,768]{1,0:T(8,128)(2,1)S(1)} %slice_select_fusion.1), channel_id=1, source_target_pairs={{0,2},{16,18}} | collective-permute-start | bytes 1179656 | tf_op jit(solution)/shard_map/ppermute | solution.py:73
  13.0 2.8 %copy-start.2 = (bf16[512,2304]{1,0:T(8,128)(2,1)}, bf16[512,2304]{1,0:T(8,128)(2,1)S(1)}, u32[]{:S(2)}) copy-start(bf16[512,2304]{1,0:T(8,128)(2,1)S(1)} %get-tuple-element.17) | copy-start | bytes 7077892
  13.0 8.3 %copy-start.14 = (s32[3]{0:T(128)S(1)}, s32[3]{0:T(128)}, u32[]{:S(2)}) copy-start(s32[3]{0:T(128)} %constant.61.clone) | copy-start | bytes 40
  13.2 8.9 %collective-permute-start.6 = (bf16[256,768]{1,0:T(8,128)(2,1)S(1)}, bf16[256,768]{1,0:T(8,128)(2,1)S(1)}, u32[]{:S(2)}, u32[]{:S(2)}) collective-permute-start(bf16[256,768]{1,0:T(8,128)(2,1)S(1)} %select_select_fusion.3), channel_id=1, source_target_pairs={{1,5},{2,6},{4,8},{17,21},{18,22},{20,24}} | collective-permute-start | bytes 1179656 | tf_op jit(solution)/shard_map/ppermute | solution.py:73
  13.8 8.3 %collective-permute-start.5 = (bf16[256,768]{1,0:T(8,128)(2,1)S(1)}, bf16[256,768]{1,0:T(8,128)(2,1)S(1)}, u32[]{:S(2)}, u32[]{:S(2)}) collective-permute-start(bf16[256,768]{1,0:T(8,128)(2,1)S(1)} %select_select_fusion.3), channel_id=1, source_target_pairs={{1,3},{17,19}} | collective-permute-start | bytes 1179656 | tf_op jit(solution)/shard_map/ppermute | solution.py:73
  15.8 28.6 %collective-permute-start = (bf16[256,1536]{1,0:T(8,128)(2,1)}, bf16[256,1536]{1,0:T(8,128)(2,1)}, u32[]{:S(2)}, u32[]{:S(2)}) collective-permute-start(bf16[256,1536]{1,0:T(8,128)(2,1)} %get-tuple-element.15), channel_id=1, source_target_pairs={{0,1},{1,2},{2,3},{3,4},{4,5},{5,6},{6,7},{7,8},{8,9},{9,10},{10,1... | collective-permute-start | bytes 2359304 | tf_op jit(solution)/shard_map/ppermute | solution.py:23
  17.7 26.7 %collective-permute-start.1 = (bf16[256,1536]{1,0:T(8,128)(2,1)}, bf16[256,1536]{1,0:T(8,128)(2,1)}, u32[]{:S(2)}, u32[]{:S(2)}) collective-permute-start(bf16[256,1536]{1,0:T(8,128)(2,1)} %get-tuple-element.16), channel_id=1, source_target_pairs={{1,0},{2,1},{3,2},{4,3},{5,4},{6,5},{7,6},{8,7},{9,8},{10,9},{11,1... | collective-permute-start | bytes 2359304 | tf_op jit(solution)/shard_map/ppermute | solution.py:24
  22.9 7.9 %copy-start.3 = (bf16[512,2304]{1,0:T(8,128)(2,1)S(1)}, bf16[512,2304]{1,0:T(8,128)(2,1)}, u32[]{:S(2)}) copy-start(bf16[512,2304]{1,0:T(8,128)(2,1)} %copy-done.2) | copy-start | bytes 7077892
  22.9 11.4 %collective-permute-start.7 = (bf16[256,768]{1,0:T(8,128)(2,1)S(1)}, bf16[256,768]{1,0:T(8,128)(2,1)}, u32[]{:S(2)}, u32[]{:S(2)}) collective-permute-start(bf16[256,768]{1,0:T(8,128)(2,1)S(1)} %select_select_fusion.2), channel_id=1, source_target_pairs={{3,7},{5,9},{6,10},{8,12},{19,23},{21,25},{22,26},{24,28}} | collective-permute-start | bytes 1179656 | tf_op jit(solution)/shard_map/ppermute | solution.py:73
  30.8 0.7 copy-start.13
  30.8 6.5 %copy-start.12 = (s32[3]{0:T(128)S(1)}, s32[3]{0:T(128)}, u32[]{:S(2)}) copy-start(s32[3]{0:T(128)} %constant.64.clone) | copy-start | bytes 40
  35.9 6.6 %collective-permute-start.8 = (bf16[256,768]{1,0:T(8,128)(2,1)S(1)}, bf16[256,768]{1,0:T(8,128)(2,1)S(1)}, u32[]{:S(2)}, u32[]{:S(2)}) collective-permute-start(bf16[256,768]{1,0:T(8,128)(2,1)S(1)} %broadcast_select_fusion.3), channel_id=1, source_target_pairs={{7,11},{9,13},{10,14},{23,27},{25,29},{26,30}} | collective-permute-start | bytes 1179656 | tf_op jit(solution)/shard_map/ppermute | solution.py:73
  43.1 4.4 %collective-permute-start.9 = (bf16[256,768]{1,0:T(8,128)(2,1)S(1)}, bf16[256,768]{1,0:T(8,128)(2,1)S(1)}, u32[]{:S(2)}, u32[]{:S(2)}) collective-permute-start(bf16[256,768]{1,0:T(8,128)(2,1)S(1)} %broadcast_select_fusion.5), channel_id=1, source_target_pairs={{11,15},{27,31}} | collective-permute-start | bytes 1179656 | tf_op jit(solution)/shard_map/ppermute | solution.py:73
  44.4 3.6 %copy-start.5 = (bf16[768,2304]{1,0:T(8,128)(2,1)S(1)}, bf16[768,2304]{1,0:T(8,128)(2,1)}, u32[]{:S(2)}) copy-start(bf16[768,2304]{1,0:T(8,128)(2,1)} %get-tuple-element.12) | copy-start | bytes 10616836
  79.5 2.1 %collective-permute-start.14 = (bf16[256,768]{1,0:T(8,128)(2,1)S(1)}, bf16[256,768]{1,0:T(8,128)(2,1)S(1)}, u32[]{:S(2)}, u32[]{:S(2)}) collective-permute-start(bf16[256,768]{1,0:T(8,128)(2,1)S(1)} %slice_select_fusion), channel_id=1, source_target_pairs={{0,1},{16,17}} | collective-permute-start | bytes 1179656 | tf_op jit(solution)/shard_map/ppermute | solution.py:73
  80.2 1.4 collective-permute-start.13
  80.9 0.7 collective-permute-start.12
  81.7 1.9 %collective-permute-start.16 = (bf16[256,768]{1,0:T(8,128)(2,1)S(1)}, bf16[256,768]{1,0:T(8,128)(2,1)S(1)}, u32[]{:S(2)}, u32[]{:S(2)}) collective-permute-start(bf16[256,768]{1,0:T(8,128)(2,1)S(1)} %select_select_fusion.1), channel_id=1, source_target_pairs={{1,5},{2,6},{4,8},{17,21},{18,22},{20,24}} | collective-permute-start | bytes 1179656 | tf_op jit(solution)/shard_map/ppermute | solution.py:73
  82.6 1.1 collective-permute-start.15
  84.4 32.2 %collective-permute-start.17 = (bf16[256,768]{1,0:T(8,128)(2,1)S(1)}, bf16[256,768]{1,0:T(8,128)(2,1)S(1)}, u32[]{:S(2)}, u32[]{:S(2)}) collective-permute-start(bf16[256,768]{1,0:T(8,128)(2,1)S(1)} %select_select_fusion), channel_id=1, source_target_pairs={{3,7},{5,9},{6,10},{8,12},{19,23},{21,25},{22,26},{24,28}} | collective-permute-start | bytes 1179656 | tf_op jit(solution)/shard_map/ppermute | solution.py:73
  117.3 10.4 %collective-permute-start.18 = (bf16[256,768]{1,0:T(8,128)(2,1)S(1)}, bf16[256,768]{1,0:T(8,128)(2,1)S(1)}, u32[]{:S(2)}, u32[]{:S(2)}) collective-permute-start(bf16[256,768]{1,0:T(8,128)(2,1)S(1)} %broadcast_select_fusion.2), channel_id=1, source_target_pairs={{7,11},{9,13},{10,14},{23,27},{25,29},{26,30}} | collective-permute-start | bytes 1179656 | tf_op jit(solution)/shard_map/ppermute | solution.py:73
  118.7 21.7 %collective-permute-start.10 = (bf16[256,1536]{1,0:T(8,128)(2,1)S(1)}, bf16[256,1536]{1,0:T(8,128)(2,1)S(1)}, u32[]{:S(2)}, u32[]{:S(2)}) collective-permute-start(bf16[256,1536]{1,0:T(8,128)(2,1)S(1)} %get-tuple-element.13), channel_id=1, source_target_pairs={{0,1},{1,2},{2,3},{3,4},{4,5},{5,6},{6,7},{7,8},{8,9},{9,10},{10,1... | collective-permute-start | bytes 2359304 | tf_op jit(solution)/shard_map/ppermute | solution.py:23
  120.7 19.8 %collective-permute-start.11 = (bf16[256,1536]{1,0:T(8,128)(2,1)S(1)}, bf16[256,1536]{1,0:T(8,128)(2,1)S(1)}, u32[]{:S(2)}, u32[]{:S(2)}) collective-permute-start(bf16[256,1536]{1,0:T(8,128)(2,1)S(1)} %get-tuple-element.14), channel_id=1, source_target_pairs={{1,0},{2,1},{3,2},{4,3},{5,4},{6,5},{7,6},{8,7},{9,8},{10,9},{11,1... | collective-permute-start | bytes 2359304 | tf_op jit(solution)/shard_map/ppermute | solution.py:24
  128.3 14.0 %collective-permute-start.19 = (bf16[256,768]{1,0:T(8,128)(2,1)S(1)}, bf16[256,768]{1,0:T(8,128)(2,1)S(1)}, u32[]{:S(2)}, u32[]{:S(2)}) collective-permute-start(bf16[256,768]{1,0:T(8,128)(2,1)S(1)} %broadcast_select_fusion.4), channel_id=1, source_target_pairs={{11,15},{27,31}} | collective-permute-start | bytes 1179656 | tf_op jit(solution)/shard_map/ppermute | solution.py:73
  130.1 12.6 %copy-start.4 = (bf16[768,2304]{1,0:T(8,128)(2,1)S(1)}, bf16[768,2304]{1,0:T(8,128)(2,1)}, u32[]{:S(2)}) copy-start(bf16[768,2304]{1,0:T(8,128)(2,1)} %get-tuple-element.11) | copy-start | bytes 10616836
  171.9 2.8 %copy-start.11 = (f32[768]{0:T(1024)S(1)}, f32[768]{0:T(1024)}, u32[]{:S(2)}) copy-start(f32[768]{0:T(1024)} %param.30) | copy-start | bytes 9220
  174.3 1.4 copy-start.8
  174.7 1.2 copy-start.9
  174.7 1.2 copy-start.10
  175.9 0.6 copy-start.6

commit v3 on v2

--- a/solution.py
+++ b/solution.py
@@ -103,34 +103,45 @@
     prompt_ok = jnp.abs(prompt_pos - query_pos) > HALF
     start = pl.multiple_of(block * tile, tile)
     contract = (((1,), (1,)), ((), ()))
-    for head in range(HEADS):
-        cols = slice(head * HEAD, (head + 1) * HEAD)
-        vcols = slice(feat + head * HEAD, feat + (head + 1) * HEAD)
-        query = q_ref[:, cols]
-        band_scores = lax.dot_general(
-            query, band_ref[pl.ds(start, width), cols], contract,
-            preferred_element_type=jnp.float32,
-        )
-        prompt_scores = lax.dot_general(
-            query, prompt_ref[:, cols], contract, preferred_element_type=jnp.float32
-        )
-        band_scores = jnp.where(band_ok, band_scores, -1e30)
-        prompt_scores = jnp.where(prompt_ok, prompt_scores, -1e30)
-        row_max = jnp.maximum(
-            jnp.max(band_scores, axis=1, keepdims=True),
-            jnp.max(prompt_scores, axis=1, keepdims=True),
-        )
-        band_exp = jnp.exp(band_scores - row_max)
-        prompt_exp = jnp.exp(prompt_scores - row_max)
-        denom = jnp.sum(band_exp, axis=1, keepdims=True) + jnp.sum(
-            prompt_exp, axis=1, keepdims=True
-        )
-        band_probs = (band_exp / denom).astype(jnp.bfloat16)
-        prompt_probs = (prompt_exp / denom).astype(jnp.bfloat16)
-        attn = jnp.dot(
-            band_probs, band_ref[pl.ds(start, width), vcols],
-            preferred_element_type=jnp.float32,
-        ) + jnp.dot(prompt_probs, prompt_ref[:, vcols], preferred_element_type=jnp.float32)
+    pair = 2 * HEAD
+    low_lanes = lax.broadcasted_iota(jnp.int32, (1, pair), 1) < HEAD
+    for head_pair in range(HEADS // 2):
+        cols = slice(head_pair * pair, (head_pair + 1) * pair)
+        vcols = slice(feat + head_pair * pair, feat + (head_pair + 1) * pair)
+        query_two = q_ref[:, cols]
+        band_keys = band_ref[pl.ds(start, width), cols]
+        band_values = band_ref[pl.ds(start, width), vcols]
+        prompt_keys = prompt_ref[:, cols]
+        prompt_values = prompt_ref[:, vcols]
+        halves = []
+        for low in (True, False):
+            keep = low_lanes if low else jnp.logical_not(low_lanes)
+            query = jnp.where(keep, query_two, jnp.zeros_like(query_two))
+            band_scores = lax.dot_general(
+                query, band_keys, contract, preferred_element_type=jnp.float32
+            )
+            prompt_scores = lax.dot_general(
+                query, prompt_keys, contract, preferred_element_type=jnp.float32
+            )
+            band_scores = jnp.where(band_ok, band_scores, -1e30)
+            prompt_scores = jnp.where(prompt_ok, prompt_scores, -1e30)
+            row_max = jnp.maximum(
+                jnp.max(band_scores, axis=1, keepdims=True),
+                jnp.max(prompt_scores, axis=1, keepdims=True),
+            )
+            band_exp = jnp.exp(band_scores - row_max)
+            prompt_exp = jnp.exp(prompt_scores - row_max)
+            denom = jnp.sum(band_exp, axis=1, keepdims=True) + jnp.sum(
+                prompt_exp, axis=1, keepdims=True
+            )
+            scale = 1.0 / denom
+            band_probs = (band_exp * scale).astype(jnp.bfloat16)
+            prompt_probs = (prompt_exp * scale).astype(jnp.bfloat16)
+            halves.append(
+                jnp.dot(band_probs, band_values, preferred_element_type=jnp.float32)
+                + jnp.dot(prompt_probs, prompt_values, preferred_element_type=jnp.float32)
+            )
+        attn = jnp.where(low_lanes, halves[0], halves[1])
         out_ref[:, cols] = attn.astype(out_ref.dtype)
 
 

time: 177 us -> 176 us (level)
  no operation moved by 1% of the time
where the time goes in v3:
time: 176 us; the launch traced here: 175 us
  Pallas kernels  54 us (31%)
  waiting for transfers between devices  43.8 us (25%)
  starting transfers between devices  24.9 us (14%)
  other arithmetic  22.6 us (13%)
  matrix products  19.4 us (11%)
  local copies, waits for them, and re-layouts  8.7 us (5%)
  between operations  1.85 us (1%)
    pallas_call x2, Pallas kernels, attention(): pl.pallas_call(attention_kernel, out_shape=jax.ShapeDtypeStruct((rows, fe...  54 us
    ppermute x16, waiting for transfers between devices, spread(): got = lax.ppermute(block, axis, op)  32.8 us
    ppermute x16, starting transfers between devices, spread(): got = lax.ppermute(block, axis, op)  13.7 us
    ppermute x2, waiting for transfers between devices, with_halo(): before = lax.ppermute(last, axis, up)  11 us
    dot_general x2, matrix products, per_device(): projected = jnp.dot(normed, weights, preferred_element_type=jnp.float32)  10.4 us
    ppermute x2, starting transfers between devices, with_halo(): after = lax.ppermute(leading, axis, down)  7.29 us
    squeeze x1, local copies, waits for them, and re-layouts, per_device(): weights = w_qkv[layer_idx]  6.46 us
    select_n x8, other arithmetic, spread(): received = jnp.where(jnp.any(place == targets), got, received)  5.19 us
  transfers between devices with their start and end apart: 20, of which 5 were waited for; matrix products, arithmetic and copies ran while one was open for 21% of the time, Pallas kernels for 0%

profile of v3, /device:TPU:20, one launch (start us, length us, event | category | flops | bytes accessed | tf_op | source)
XLA Modules:
  0.0 175.3 jit_solution(17816969103978480670)
XLA Ops:
  0.7 1.1 slice_select_fusion.1
  1.8 0.7 collective-permute-start.4
  2.5 0.7 collective-permute-start.3
  3.2 0.7 collective-permute-start.2
  3.9 1.3 convert_reduce_fusion.1
  5.2 1.5 fusion.11
  6.8 6.3 %fusion.62 = (bf16[512,2304]{1,0:T(8,128)(2,1)S(1)}, f32[512,2304]{1,0:T(8,128)}) fusion(bf16[2,768,2304]{2,1,0:T(8,128)(2,1)} %param.28, bf16[512,768]{1,0:T(8,128)(2,1)S(1)} %copy-done.1, f32[768]{0:T(1024)S(1)} %get-tuple-element.6, f32[512]{0:T(512)S(1)} %add_rsqrt_fusion.2, f32[512]{0:T(512)S(1)} %broadcast_multiply_fusion.2), kind=kOutput, calls=%fused_computation.113 | convolution fusion | flops 1815085056 | bytes 11410432 | tf_op jit(solution)/shard_map/dot_general | solution.py:197
  13.2 0.7 collective-permute-start.6
  13.8 0.7 collective-permute-start.5
  14.5 1.3 fusion.61
  15.8 1.9 %collective-permute-start = (bf16[256,1536]{1,0:T(8,128)(2,1)}, bf16[256,1536]{1,0:T(8,128)(2,1)}, u32[]{:S(2)}, u32[]{:S(2)}) collective-permute-start(bf16[256,1536]{1,0:T(8,128)(2,1)} %get-tuple-element.15), channel_id=1, source_target_pairs={{0,1},{1,2},{2,3},{3,4},{4,5},{5,6},{6,7},{7,8},{8,9},{9,10},{10,1... | collective-permute-start | bytes 2359304 | tf_op jit(solution)/shard_map/ppermute | solution.py:23
  17.7 3.6 %collective-permute-start.1 = (bf16[256,1536]{1,0:T(8,128)(2,1)}, bf16[256,1536]{1,0:T(8,128)(2,1)}, u32[]{:S(2)}, u32[]{:S(2)}) collective-permute-start(bf16[256,1536]{1,0:T(8,128)(2,1)} %get-tuple-element.16), channel_id=1, source_target_pairs={{1,0},{2,1},{3,2},{4,3},{5,4},{6,5},{7,6},{8,7},{9,8},{10,9},{11,1... | collective-permute-start | bytes 2359304 | tf_op jit(solution)/shard_map/ppermute | solution.py:24
  21.4 0.7 compare_reduce_fusion
  22.1 0.8 select_select_fusion.2
  22.9 1.4 collective-permute-start.7
  24.3 6.5 %slice_bitcast_fusion = (bf16[768,2304]{1,0:T(8,128)(2,1)}, bf16[768,2304]{1,0:T(8,128)(2,1)}) fusion(bf16[2,768,2304]{2,1,0:T(8,128)(2,1)} %param.28), kind=kLoop, calls=%fused_computation | loop fusion | bytes 14155776 | tf_op jit(solution)/shard_map/squeeze | solution.py:196
  31.4 0.7 compare_reduce_fusion.1
  32.1 2.1 %collective-permute-done.7 = bf16[256,768]{1,0:T(8,128)(2,1)} collective-permute-done((bf16[256,768]{1,0:T(8,128)(2,1)S(1)}, bf16[256,768]{1,0:T(8,128)(2,1)}, u32[]{:S(2)}, u32[]{:S(2)}) %collective-permute-start.7) | collective-permute-done | bytes 393248 | tf_op jit(solution)/shard_map/ppermute | solution.py:73
  34.2 1.7 broadcast_select_fusion.3
  35.9 1.3 collective-permute-start.8
  37.9 2.4 %fusion.20.q_ref = bf16[512,768]{1,0:T(8,128)(2,1)} fusion(f32[512,2304]{1,0:T(8,128)} %get-tuple-element.18), kind=kLoop, calls=%fused_computation.36 | loop fusion | flops 786432 | bytes 2359296 | tf_op jit(solution)/shard_map/convert_element_type | solution.py:198
  40.3 2.2 %collective-permute-done.8 = bf16[256,768]{1,0:T(8,128)(2,1)S(1)} collective-permute-done((bf16[256,768]{1,0:T(8,128)(2,1)S(1)}, bf16[256,768]{1,0:T(8,128)(2,1)S(1)}, u32[]{:S(2)}, u32[]{:S(2)}) %collective-permute-start.8) | collective-permute-done | bytes 393248 | tf_op jit(solution)/shard_map/ppermute | solution.py:73
  43.1 0.7 collective-permute-start.9
  44.4 3.1 %pad_maximum_fusion.band_ref = bf16[1024,1536]{1,0:T(8,128)(2,1)} fusion(bf16[256,1536]{1,0:T(8,128)(2,1)} %collective-permute-done.1, bf16[512,1536]{1,0:T(8,128)(2,1)S(1)} %slice.90, bf16[256,1536]{1,0:T(8,128)(2,1)} %collective-permute-done), kind=kLoop, calls=%fused_computation.2 | loop fusion | flops 9437184 | bytes 6291456 | tf_op jit(solution)/shard_map/concatenate | solution.py:25
  48.0 1.7 convolution_convert_fusion.1.prompt_ref
  49.7 27.0 %shard_map.257 = bf16[512,768]{1,0:T(8,128)(2,1)} custom-call(s32[2]{0:T(128)} %pad_add_fusion.pos_ref, bf16[512,768]{1,0:T(8,128)(2,1)} %fusion.20.q_ref, bf16[1024,1536]{1,0:T(8,128)(2,1)} %pad_maximum_fusion.band_ref, bf16[256,1536]{1,0:T(8,128)(2,1)} %convolution_convert_fusion.1.prompt_ref), custom_call_target="tpu_custom_call" | custom-call | flops 1409286144 | bytes 5505024 | tf_op jit(solution)/shard_map/pallas_call | solution.py:154
  76.7 2.4 %convert_reduce_fusion = (f32[512]{0:T(512)S(1)}, bf16[512,768]{1,0:T(8,128)(2,1)S(1)}) fusion(bf16[512,768]{1,0:T(8,128)(2,1)} %shard_map.257, bf16[2,768,768]{2,1,0:T(8,128)(2,1)} %param.29, bf16[512,768]{1,0:T(8,128)(2,1)S(1)} %copy-done.1), kind=kOutput, calls=%fused_computation.8 | convolution fusion | flops 605945344 | bytes 3540992 | tf_op jit(solution)/shard_map/dot_general | solution.py:208
  79.1 0.7 collective-permute-start.14
  79.8 0.7 collective-permute-start.13
  80.5 0.7 collective-permute-start.12
  81.3 0.7 collective-permute-start.16
  82.0 0.7 collective-permute-start.15
  83.1 0.7 select_select_fusion
  83.8 1.5 collective-permute-start.17
  85.3 4.1 %fusion.63 = (bf16[512,2304]{1,0:T(8,128)(2,1)S(1)}, f32[512,2304]{1,0:T(8,128)S(1)}) fusion(bf16[2,768,2304]{2,1,0:T(8,128)(2,1)} %param.28, bf16[512,768]{1,0:T(8,128)(2,1)S(1)} %get-tuple-element.20, f32[768]{0:T(1024)S(1)} %get-tuple-element.5, f32[512]{0:T(512)S(1)} %add_rsqrt_fusion.1, f32[512]{0:T(512)S(1)} %broadcast_multiply_fusion.1), kind=kOutput, calls=%fused_computation.114 | convolution fusion | flops 1815085056 | bytes 11410432 | tf_op jit(solution)/shard_map/dot_general | solution.py:197
  89.5 26.3 %collective-permute-done.17 = bf16[256,768]{1,0:T(8,128)(2,1)S(1)} collective-permute-done((bf16[256,768]{1,0:T(8,128)(2,1)S(1)}, bf16[256,768]{1,0:T(8,128)(2,1)S(1)}, u32[]{:S(2)}, u32[]{:S(2)}) %collective-permute-start.17) | collective-permute-done | bytes 393248 | tf_op jit(solution)/shard_map/ppermute | solution.py:73
  116.4 1.3 collective-permute-start.18
  117.9 1.9 %collective-permute-start.10 = (bf16[256,1536]{1,0:T(8,128)(2,1)S(1)}, bf16[256,1536]{1,0:T(8,128)(2,1)S(1)}, u32[]{:S(2)}, u32[]{:S(2)}) collective-permute-start(bf16[256,1536]{1,0:T(8,128)(2,1)S(1)} %get-tuple-element.13), channel_id=1, source_target_pairs={{0,1},{1,2},{2,3},{3,4},{4,5},{5,6},{6,7},{7,8},{8,9},{9,10},{10,1... | collective-permute-start | bytes 2359304 | tf_op jit(solution)/shard_map/ppermute | solution.py:23
  119.8 3.6 %collective-permute-start.11 = (bf16[256,1536]{1,0:T(8,128)(2,1)S(1)}, bf16[256,1536]{1,0:T(8,128)(2,1)S(1)}, u32[]{:S(2)}, u32[]{:S(2)}) collective-permute-start(bf16[256,1536]{1,0:T(8,128)(2,1)S(1)} %get-tuple-element.14), channel_id=1, source_target_pairs={{1,0},{2,1},{3,2},{4,3},{5,4},{6,5},{7,6},{8,7},{9,8},{10,9},{11,1... | collective-permute-start | bytes 2359304 | tf_op jit(solution)/shard_map/ppermute | solution.py:24
  124.1 2.1 %collective-permute-done.18 = bf16[256,768]{1,0:T(8,128)(2,1)S(1)} collective-permute-done((bf16[256,768]{1,0:T(8,128)(2,1)S(1)}, bf16[256,768]{1,0:T(8,128)(2,1)S(1)}, u32[]{:S(2)}, u32[]{:S(2)}) %collective-permute-start.18) | collective-permute-done | bytes 393248 | tf_op jit(solution)/shard_map/ppermute | solution.py:73
  126.8 0.7 collective-permute-start.19
  127.5 1.0 fusion.19.q_ref
  128.6 11.0 %collective-permute-done.10 = bf16[256,1536]{1,0:T(8,128)(2,1)S(1)} collective-permute-done((bf16[256,1536]{1,0:T(8,128)(2,1)S(1)}, bf16[256,1536]{1,0:T(8,128)(2,1)S(1)}, u32[]{:S(2)}, u32[]{:S(2)}) %collective-permute-start.10) | collective-permute-done | bytes 786464 | tf_op jit(solution)/shard_map/ppermute | solution.py:23
  139.6 1.8 %pad_maximum_fusion.1.band_ref = bf16[1024,1536]{1,0:T(8,128)(2,1)} fusion(bf16[256,1536]{1,0:T(8,128)(2,1)S(1)} %collective-permute-done.11, bf16[512,1536]{1,0:T(8,128)(2,1)S(1)} %slice.95, bf16[256,1536]{1,0:T(8,128)(2,1)S(1)} %collective-permute-done.10), kind=kLoop, calls=%fused_computation.3 | loop fusion | flops 9437184 | bytes 6291456 | tf_op jit(solution)/shard_map/concatenate | solution.py:25
  141.9 1.7 convolution_convert_fusion.prompt_ref
  143.6 27.0 %shard_map.258 = bf16[512,768]{1,0:T(8,128)(2,1)} custom-call(s32[2]{0:T(128)} %pad_add_fusion.pos_ref, bf16[512,768]{1,0:T(8,128)(2,1)} %fusion.19.q_ref, bf16[1024,1536]{1,0:T(8,128)(2,1)} %pad_maximum_fusion.1.band_ref, bf16[256,1536]{1,0:T(8,128)(2,1)} %convolution_convert_fusion.prompt_ref), custom_call_target="tpu_custom_call" | custom-call | flops 1409286144 | bytes 5505024 | tf_op jit(solution)/shard_map/pallas_call | solution.py:154
  170.6 2.4 %convert_reduce_fusion.2 = (f32[512]{0:T(512)S(1)}, bf16[512,768]{1,0:T(8,128)(2,1)S(1)}) fusion(bf16[512,768]{1,0:T(8,128)(2,1)} %shard_map.258, bf16[2,768,768]{2,1,0:T(8,128)(2,1)} %param.29, bf16[512,768]{1,0:T(8,128)(2,1)S(1)} %get-tuple-element.20), kind=kOutput, calls=%fused_computation.15 | convolution fusion | flops 605945344 | bytes 3540992 | tf_op jit(solution)/shard_map/dot_general | solution.py:208
  173.5 0.8 fusion.35
  (77 shorter events, 6.9 us)
Async XLA Ops:
  0.6 172.8 %copy-start = (bf16[768,512]{1,0:T(8,128)(2,1)S(1)}, bf16[768,512]{1,0:T(8,128)(2,1)}, u32[]{:S(2)}) copy-start(bf16[768,512]{1,0:T(8,128)(2,1)} %param.31) | copy-start | bytes 2359300
  0.6 6.1 %copy-start.1 = (bf16[512,768]{1,0:T(8,128)(2,1)S(1)}, bf16[512,768]{1,0:T(8,128)(2,1)}, u32[]{:S(2)}) copy-start(bf16[512,768]{1,0:T(8,128)(2,1)} %param.26) | copy-start | bytes 2359300
  0.7 6.1 %copy-start.7 = (f32[2,768]{1,0:T(2,128)S(1)}, f32[2,768]{1,0:T(2,128)}, u32[]{:S(2)}) copy-start(f32[2,768]{1,0:T(2,128)} %param.27) | copy-start | bytes 18436
  1.8 11.2 %collective-permute-start.4 = (bf16[256,768]{1,0:T(8,128)(2,1)S(1)}, bf16[256,768]{1,0:T(8,128)(2,1)S(1)}, u32[]{:S(2)}, u32[]{:S(2)}) collective-permute-start(bf16[256,768]{1,0:T(8,128)(2,1)S(1)} %slice_select_fusion.1), channel_id=1, source_target_pairs={{0,1},{16,17}} | collective-permute-start | bytes 1179656 | tf_op jit(solution)/shard_map/ppermute | solution.py:73
  2.5 10.5 %collective-permute-start.3 = (bf16[256,768]{1,0:T(8,128)(2,1)S(1)}, bf16[256,768]{1,0:T(8,128)(2,1)S(1)}, u32[]{:S(2)}, u32[]{:S(2)}) collective-permute-start(bf16[256,768]{1,0:T(8,128)(2,1)S(1)} %slice_select_fusion.1), channel_id=1, source_target_pairs={{0,4},{16,20}} | collective-permute-start | bytes 1179656 | tf_op jit(solution)/shard_map/ppermute | solution.py:73
  3.2 9.9 %collective-permute-start.2 = (bf16[256,768]{1,0:T(8,128)(2,1)S(1)}, bf16[256,768]{1,0:T(8,128)(2,1)S(1)}, u32[]{:S(2)}, u32[]{:S(2)}) collective-permute-start(bf16[256,768]{1,0:T(8,128)(2,1)S(1)} %slice_select_fusion.1), channel_id=1, source_target_pairs={{0,2},{16,18}} | collective-permute-start | bytes 1179656 | tf_op jit(solution)/shard_map/ppermute | solution.py:73
  13.0 2.8 %copy-start.2 = (bf16[512,2304]{1,0:T(8,128)(2,1)}, bf16[512,2304]{1,0:T(8,128)(2,1)S(1)}, u32[]{:S(2)}) copy-start(bf16[512,2304]{1,0:T(8,128)(2,1)S(1)} %get-tuple-element.17) | copy-start | bytes 7077892
  13.0 8.3 %copy-start.14 = (s32[3]{0:T(128)S(1)}, s32[3]{0:T(128)}, u32[]{:S(2)}) copy-start(s32[3]{0:T(128)} %constant.61.clone) | copy-start | bytes 40
  13.2 8.9 %collective-permute-start.6 = (bf16[256,768]{1,0:T(8,128)(2,1)S(1)}, bf16[256,768]{1,0:T(8,128)(2,1)S(1)}, u32[]{:S(2)}, u32[]{:S(2)}) collective-permute-start(bf16[256,768]{1,0:T(8,128)(2,1)S(1)} %select_select_fusion.3), channel_id=1, source_target_pairs={{1,5},{2,6},{4,8},{17,21},{18,22},{20,24}} | collective-permute-start | bytes 1179656 | tf_op jit(solution)/shard_map/ppermute | solution.py:73
  13.8 8.3 %collective-permute-start.5 = (bf16[256,768]{1,0:T(8,128)(2,1)S(1)}, bf16[256,768]{1,0:T(8,128)(2,1)S(1)}, u32[]{:S(2)}, u32[]{:S(2)}) collective-permute-start(bf16[256,768]{1,0:T(8,128)(2,1)S(1)} %select_select_fusion.3), channel_id=1, source_target_pairs={{1,3},{17,19}} | collective-permute-start | bytes 1179656 | tf_op jit(solution)/shard_map/ppermute | solution.py:73
  15.8 28.6 %collective-permute-start = (bf16[256,1536]{1,0:T(8,128)(2,1)}, bf16[256,1536]{1,0:T(8,128)(2,1)}, u32[]{:S(2)}, u32[]{:S(2)}) collective-permute-start(bf16[256,1536]{1,0:T(8,128)(2,1)} %get-tuple-element.15), channel_id=1, source_target_pairs={{0,1},{1,2},{2,3},{3,4},{4,5},{5,6},{6,7},{7,8},{8,9},{9,10},{10,1... | collective-permute-start | bytes 2359304 | tf_op jit(solution)/shard_map/ppermute | solution.py:23
  17.7 26.7 %collective-permute-start.1 = (bf16[256,1536]{1,0:T(8,128)(2,1)}, bf16[256,1536]{1,0:T(8,128)(2,1)}, u32[]{:S(2)}, u32[]{:S(2)}) collective-permute-start(bf16[256,1536]{1,0:T(8,128)(2,1)} %get-tuple-element.16), channel_id=1, source_target_pairs={{1,0},{2,1},{3,2},{4,3},{5,4},{6,5},{7,6},{8,7},{9,8},{10,9},{11,1... | collective-permute-start | bytes 2359304 | tf_op jit(solution)/shard_map/ppermute | solution.py:24
  22.9 7.9 %copy-start.3 = (bf16[512,2304]{1,0:T(8,128)(2,1)S(1)}, bf16[512,2304]{1,0:T(8,128)(2,1)}, u32[]{:S(2)}) copy-start(bf16[512,2304]{1,0:T(8,128)(2,1)} %copy-done.2) | copy-start | bytes 7077892
  22.9 11.4 %collective-permute-start.7 = (bf16[256,768]{1,0:T(8,128)(2,1)S(1)}, bf16[256,768]{1,0:T(8,128)(2,1)}, u32[]{:S(2)}, u32[]{:S(2)}) collective-permute-start(bf16[256,768]{1,0:T(8,128)(2,1)S(1)} %select_select_fusion.2), channel_id=1, source_target_pairs={{3,7},{5,9},{6,10},{8,12},{19,23},{21,25},{22,26},{24,28}} | collective-permute-start | bytes 1179656 | tf_op jit(solution)/shard_map/ppermute | solution.py:73
  30.8 0.7 copy-start.13
  30.8 6.5 %copy-start.12 = (s32[3]{0:T(128)S(1)}, s32[3]{0:T(128)}, u32[]{:S(2)}) copy-start(s32[3]{0:T(128)} %constant.64.clone) | copy-start | bytes 40
  35.9 6.6 %collective-permute-start.8 = (bf16[256,768]{1,0:T(8,128)(2,1)S(1)}, bf16[256,768]{1,0:T(8,128)(2,1)S(1)}, u32[]{:S(2)}, u32[]{:S(2)}) collective-permute-start(bf16[256,768]{1,0:T(8,128)(2,1)S(1)} %broadcast_select_fusion.3), channel_id=1, source_target_pairs={{7,11},{9,13},{10,14},{23,27},{25,29},{26,30}} | collective-permute-start | bytes 1179656 | tf_op jit(solution)/shard_map/ppermute | solution.py:73
  43.1 4.4 %collective-permute-start.9 = (bf16[256,768]{1,0:T(8,128)(2,1)S(1)}, bf16[256,768]{1,0:T(8,128)(2,1)S(1)}, u32[]{:S(2)}, u32[]{:S(2)}) collective-permute-start(bf16[256,768]{1,0:T(8,128)(2,1)S(1)} %broadcast_select_fusion.5), channel_id=1, source_target_pairs={{11,15},{27,31}} | collective-permute-start | bytes 1179656 | tf_op jit(solution)/shard_map/ppermute | solution.py:73
  44.4 3.6 %copy-start.5 = (bf16[768,2304]{1,0:T(8,128)(2,1)S(1)}, bf16[768,2304]{1,0:T(8,128)(2,1)}, u32[]{:S(2)}) copy-start(bf16[768,2304]{1,0:T(8,128)(2,1)} %get-tuple-element.12) | copy-start | bytes 10616836
  79.1 2.1 %collective-permute-start.14 = (bf16[256,768]{1,0:T(8,128)(2,1)S(1)}, bf16[256,768]{1,0:T(8,128)(2,1)S(1)}, u32[]{:S(2)}, u32[]{:S(2)}) collective-permute-start(bf16[256,768]{1,0:T(8,128)(2,1)S(1)} %slice_select_fusion), channel_id=1, source_target_pairs={{0,1},{16,17}} | collective-permute-start | bytes 1179656 | tf_op jit(solution)/shard_map/ppermute | solution.py:73
  79.8 1.4 collective-permute-start.13
  80.5 0.7 collective-permute-start.12
  81.3 1.8 %collective-permute-start.16 = (bf16[256,768]{1,0:T(8,128)(2,1)S(1)}, bf16[256,768]{1,0:T(8,128)(2,1)S(1)}, u32[]{:S(2)}, u32[]{:S(2)}) collective-permute-start(bf16[256,768]{1,0:T(8,128)(2,1)S(1)} %select_select_fusion.1), channel_id=1, source_target_pairs={{1,5},{2,6},{4,8},{17,21},{18,22},{20,24}} | collective-permute-start | bytes 1179656 | tf_op jit(solution)/shard_map/ppermute | solution.py:73
  82.0 1.1 collective-permute-start.15
  83.8 31.9 %collective-permute-start.17 = (bf16[256,768]{1,0:T(8,128)(2,1)S(1)}, bf16[256,768]{1,0:T(8,128)(2,1)S(1)}, u32[]{:S(2)}, u32[]{:S(2)}) collective-permute-start(bf16[256,768]{1,0:T(8,128)(2,1)S(1)} %select_select_fusion), channel_id=1, source_target_pairs={{3,7},{5,9},{6,10},{8,12},{19,23},{21,25},{22,26},{24,28}} | collective-permute-start | bytes 1179656 | tf_op jit(solution)/shard_map/ppermute | solution.py:73
  116.4 9.8 %collective-permute-start.18 = (bf16[256,768]{1,0:T(8,128)(2,1)S(1)}, bf16[256,768]{1,0:T(8,128)(2,1)S(1)}, u32[]{:S(2)}, u32[]{:S(2)}) collective-permute-start(bf16[256,768]{1,0:T(8,128)(2,1)S(1)} %broadcast_select_fusion.2), channel_id=1, source_target_pairs={{7,11},{9,13},{10,14},{23,27},{25,29},{26,30}} | collective-permute-start | bytes 1179656 | tf_op jit(solution)/shard_map/ppermute | solution.py:73
  117.9 21.7 %collective-permute-start.10 = (bf16[256,1536]{1,0:T(8,128)(2,1)S(1)}, bf16[256,1536]{1,0:T(8,128)(2,1)S(1)}, u32[]{:S(2)}, u32[]{:S(2)}) collective-permute-start(bf16[256,1536]{1,0:T(8,128)(2,1)S(1)} %get-tuple-element.13), channel_id=1, source_target_pairs={{0,1},{1,2},{2,3},{3,4},{4,5},{5,6},{6,7},{7,8},{8,9},{9,10},{10,1... | collective-permute-start | bytes 2359304 | tf_op jit(solution)/shard_map/ppermute | solution.py:23
  119.8 19.8 %collective-permute-start.11 = (bf16[256,1536]{1,0:T(8,128)(2,1)S(1)}, bf16[256,1536]{1,0:T(8,128)(2,1)S(1)}, u32[]{:S(2)}, u32[]{:S(2)}) collective-permute-start(bf16[256,1536]{1,0:T(8,128)(2,1)S(1)} %get-tuple-element.14), channel_id=1, source_target_pairs={{1,0},{2,1},{3,2},{4,3},{5,4},{6,5},{7,6},{8,7},{9,8},{10,9},{11,1... | collective-permute-start | bytes 2359304 | tf_op jit(solution)/shard_map/ppermute | solution.py:24
  126.8 14.6 %collective-permute-start.19 = (bf16[256,768]{1,0:T(8,128)(2,1)S(1)}, bf16[256,768]{1,0:T(8,128)(2,1)S(1)}, u32[]{:S(2)}, u32[]{:S(2)}) collective-permute-start(bf16[256,768]{1,0:T(8,128)(2,1)S(1)} %broadcast_select_fusion.4), channel_id=1, source_target_pairs={{11,15},{27,31}} | collective-permute-start | bytes 1179656 | tf_op jit(solution)/shard_map/ppermute | solution.py:73
  128.6 13.3 %copy-start.4 = (bf16[768,2304]{1,0:T(8,128)(2,1)S(1)}, bf16[768,2304]{1,0:T(8,128)(2,1)}, u32[]{:S(2)}) copy-start(bf16[768,2304]{1,0:T(8,128)(2,1)} %get-tuple-element.11) | copy-start | bytes 10616836
  170.6 2.8 %copy-start.11 = (f32[768]{0:T(1024)S(1)}, f32[768]{0:T(1024)}, u32[]{:S(2)}) copy-start(f32[768]{0:T(1024)} %param.30) | copy-start | bytes 9220
  173.0 1.4 copy-start.8
  173.4 1.2 copy-start.9
  173.4 1.2 copy-start.10
  174.6 0.6 copy-start.6

commit v4 on v3

--- a/solution.py
+++ b/solution.py
@@ -1,3 +1,5 @@
+import functools
+
 import jax
 import jax.numpy as jnp
 from jax import lax
@@ -88,20 +90,20 @@
 QUERY_TILE = 128
 
 
-def attention_kernel(pos_ref, q_ref, band_ref, prompt_ref, out_ref):
+def attention_kernel(row0, pos_ref, q_ref, band_ref, prompt_ref, out_ref):
     tile = q_ref.shape[0]
     width = tile + 2 * HALF
     feat = q_ref.shape[1]
     block = pl.program_id(0)
     first = pos_ref[0]
     total = pos_ref[1]
-    query_pos = first + block * tile + lax.broadcasted_iota(jnp.int32, (tile, 1), 0)
-    key_pos = first + block * tile - HALF + lax.broadcasted_iota(jnp.int32, (1, width), 1)
+    query_pos = first + row0 + block * tile + lax.broadcasted_iota(jnp.int32, (tile, 1), 0)
+    key_pos = first + row0 + block * tile - HALF + lax.broadcasted_iota(jnp.int32, (1, width), 1)
     gap = key_pos - query_pos
     band_ok = (gap >= -HALF) & (gap <= HALF) & (key_pos >= 0) & (key_pos < total)
     prompt_pos = lax.broadcasted_iota(jnp.int32, (1, PROMPT), 1)
     prompt_ok = jnp.abs(prompt_pos - query_pos) > HALF
-    start = pl.multiple_of(block * tile, tile)
+    start = pl.multiple_of(row0 + block * tile, tile)
     contract = (((1,), (1,)), ((), ()))
     pair = 2 * HEAD
     low_lanes = lax.broadcasted_iota(jnp.int32, (1, pair), 1) < HEAD
@@ -145,20 +147,21 @@
         out_ref[:, cols] = attn.astype(out_ref.dtype)
 
 
-def attention(queries, band_kv, prompt_kv, first_pos, total_len):
-    rows, feat = queries.shape
-    tile = min(QUERY_TILE, rows)
+def attention(queries, band_kv, prompt_kv, first_pos, total_len, row0, count):
+    feat = queries.shape[1]
+    tile = min(QUERY_TILE, count)
     pos = jnp.stack([first_pos, total_len]).astype(jnp.int32)
     width = tile + 2 * HALF
-    flops = 4 * rows * (width + PROMPT) * feat
+    flops = 4 * count * (width + PROMPT) * feat
+    skip = row0 // tile
     return pl.pallas_call(
-        attention_kernel,
-        out_shape=jax.ShapeDtypeStruct((rows, feat), jnp.bfloat16),
+        functools.partial(attention_kernel, row0),
+        out_shape=jax.ShapeDtypeStruct((count, feat), jnp.bfloat16),
         grid_spec=pltpu.PrefetchScalarGridSpec(
             num_scalar_prefetch=1,
-            grid=(rows // tile,),
+            grid=(count // tile,),
             in_specs=[
-                pl.BlockSpec((tile, feat), lambda b, p: (b, 0)),
+                pl.BlockSpec((tile, feat), lambda b, p: (b + skip, 0)),
                 pl.BlockSpec(band_kv.shape, lambda b, p: (0, 0)),
                 pl.BlockSpec(prompt_kv.shape, lambda b, p: (0, 0)),
             ],
@@ -166,8 +169,8 @@
         ),
         cost_estimate=pl.CostEstimate(
             flops=flops,
-            transcendentals=rows * (width + PROMPT) * HEADS,
-            bytes_accessed=2 * (2 * queries.size + band_kv.size + prompt_kv.size),
+            transcendentals=count * (width + PROMPT) * HEADS,
+            bytes_accessed=2 * (2 * count * feat + band_kv.size + prompt_kv.size),
         ),
     )(pos, queries, band_kv, prompt_kv)
 
@@ -190,23 +193,42 @@
     seq_place = lax.axis_index("seq")
     total_len = tok_rows * seq_devices
     first_pos = seq_place * tok_rows
+    half_rows = tok_rows // 2
     hidden_state = hidden_in
+    prompt_source = hidden_in[:PROMPT]
     for layer_idx in range(LAYERS):
-        normed = layer_norm(hidden_state, ln_gain[layer_idx])
+        gain = ln_gain[layer_idx]
         weights = w_qkv[layer_idx]
-        projected = jnp.dot(normed, weights, preferred_element_type=jnp.float32)
-        queries = (projected[:, :feat_width] * 0.125).astype(jnp.bfloat16)
-        key_value = projected[:, feat_width:].astype(jnp.bfloat16)
-        extended = with_halo(key_value, (("seq", 0),), HALF)
-        prompt_rows = spread(hidden_state[:PROMPT], "seq")
+        extended = with_halo(hidden_state, (("seq", 0),), HALF)
+        prompt_rows = spread(prompt_source, "seq")
+        extended_normed = layer_norm(extended, gain)
+        band_kv = jnp.dot(
+            extended_normed, weights[:, feat_width:], preferred_element_type=jnp.float32
+        ).astype(jnp.bfloat16)
+        normed = extended_normed[HALF : HALF + tok_rows]
+        queries = (
+            jnp.dot(normed, weights[:, :feat_width], preferred_element_type=jnp.float32) * 0.125
+        ).astype(jnp.bfloat16)
         prompt_kv = jnp.dot(
-            layer_norm(prompt_rows, ln_gain[layer_idx]),
+            layer_norm(prompt_rows, gain),
             weights[:, feat_width:],
             preferred_element_type=jnp.float32,
         ).astype(jnp.bfloat16)
-        attended = attention(queries, extended, prompt_kv, first_pos, total_len)
-        projection = jnp.dot(attended, w_out[layer_idx], preferred_element_type=jnp.float32)
-        hidden_state = (hidden_state.astype(jnp.float32) + projection).astype(jnp.bfloat16)
+        parts = []
+        for row0 in (0, half_rows):
+            attended = attention(
+                queries, band_kv, prompt_kv, first_pos, total_len, row0, half_rows
+            )
+            projection = jnp.dot(
+                attended, w_out[layer_idx], preferred_element_type=jnp.float32
+            )
+            rows_in = hidden_state[row0 : row0 + half_rows].astype(jnp.float32)
+            parts.append((rows_in + projection).astype(jnp.bfloat16))
+        hidden_state = jnp.concatenate(parts, axis=0)
+        if half_rows >= PROMPT:
+            prompt_source = parts[0][:PROMPT]
+        else:
+            prompt_source = hidden_state[:PROMPT]
     final = layer_norm(hidden_state, final_gain)
     head_out = jnp.dot(final, w_heads, preferred_element_type=jnp.float32)
     logits = head_out[:, :ACTIONS]

time: 176 us -> 173 us (0.983)
  waiting for transfers between devices: 43.8 us -> 33.5 us
  Pallas kernels: 54 us -> 61.3 us
  other arithmetic: 22.6 us -> 18.1 us
  starting transfers between devices: 24.9 us -> 27.6 us
  matrix products: 19.4 us -> 21.9 us
    pallas_call x2 -> x4, Pallas kernels: 54 us -> 61.3 us  [attention(): pl.pallas_call(functools.partial(attention_kernel, row0), out_shape=jax.S...]
    ppermute x2, waiting for transfers between devices: 11 us -> 4.93 us  [with_halo(): before = lax.ppermute(last, axis, up)]
    concatenate x2 -> x0, other arithmetic: 4.88 us -> none  [with_halo(): array = jnp.concatenate([before, array, after], axis=dim)]
    ppermute x16, waiting for transfers between devices: 32.8 us -> 28.5 us  [spread(): got = lax.ppermute(block, axis, op)]
    ppermute x16, starting transfers between devices: 13.7 us -> 17.9 us  [spread(): got = lax.ppermute(block, axis, op)]
    ppermute x2, starting transfers between devices: 7.29 us -> 5.25 us  [with_halo(): after = lax.ppermute(leading, axis, down)]
    dot_general x2 -> x4, matrix products: 4.77 us -> 6.14 us  [per_device(): jnp.dot(attended, w_out[layer_idx], preferred_element_type=jnp.float32)]
    dot_general x4 -> x6, matrix products: 13.9 us -> 14.9 us  [the longest x2 8.1 us: per_device(): jnp.dot(extended_normed, weights[:, feat_width:], preferred_element_type=...]
  transfers between devices with their start and end apart: 20 -> 20, of which waited for: 5 -> 5; matrix products, arithmetic and copies ran while one was open for 21% -> 17% of each run, Pallas kernels for 0% -> 9%
where the time goes in v4:
time: 173 us; the launch traced here: 171 us
  Pallas kernels  61.3 us (35%)
  waiting for transfers between devices  33.5 us (19%)
  starting transfers between devices  27.6 us (16%)
  matrix products  21.9 us (13%)
  other arithmetic  18.1 us (10%)
  local copies, waits for them, and re-layouts  7.39 us (4%)
  between operations  1.82 us (1%)
    pallas_call x4, Pallas kernels, attention(): pl.pallas_call(functools.partial(attention_kernel, row0), out_shape=jax.S...  61.3 us
    ppermute x16, waiting for transfers between devices, spread(): got = lax.ppermute(block, axis, op)  28.5 us
    ppermute x16, starting transfers between devices, spread(): got = lax.ppermute(block, axis, op)  17.9 us
    dot_general x2, matrix products, per_device(): jnp.dot(extended_normed, weights[:, feat_width:], preferred_element_type=...  8.1 us
    squeeze x1, local copies, waits for them, and re-layouts, per_device(): weights = w_qkv[layer_idx]  6.35 us
    dot_general x4, matrix products, per_device(): jnp.dot(attended, w_out[layer_idx], preferred_element_type=jnp.float32)  6.14 us
    ppermute x2, starting transfers between devices, with_halo(): after = lax.ppermute(leading, axis, down)  5.25 us
    ppermute x2, waiting for transfers between devices, with_halo(): before = lax.ppermute(last, axis, up)  4.93 us
  transfers between devices with their start and end apart: 20, of which 5 were waited for; matrix products, arithmetic and copies ran while one was open for 17% of the time, Pallas kernels for 9%

profile of v4, /device:TPU:20, one launch (start us, length us, event | category | flops | bytes accessed | tf_op | source)
XLA Modules:
  0.0 171.5 jit_solution(18378927729346405974)
XLA Ops:
  0.7 2.0 %broadcast_select_fusion.3 = (bf16[256,768]{1,0:T(8,128)(2,1)S(1)}, bf16[256,768]{1,0:T(8,128)(2,1)}, bf16[256,768]{1,0:T(8,128)(2,1)S(1)}) fusion(pred[]{:T(512)S(6)} %eq.98, bf16[512,768]{1,0:T(8,128)(2,1)} %param.26), kind=kLoop, calls=%fused_computation.95 | loop fusion | flops 196608 | bytes 1966081 | tf_op jit(solution)/shard_map/jit(_where)/select_n | solution.py:71
  3.3 1.4 collective-permute-start.3
  4.8 1.4 collective-permute-start.4
  6.2 1.9 %collective-permute-start.1 = (bf16[256,768]{1,0:T(8,128)(2,1)}, bf16[256,768]{1,0:T(8,128)(2,1)S(1)}, u32[]{:S(2)}, u32[]{:S(2)}) collective-permute-start(bf16[256,768]{1,0:T(8,128)(2,1)} %get-tuple-element.14), channel_id=1, source_target_pairs={{1,0},{2,1},{3,2},{4,3},{5,4},{6,5},{7,6},{8,7},{9,8},{10,9},{11,1... | collective-permute-start | bytes 1179656 | tf_op jit(solution)/shard_map/ppermute | solution.py:26
  8.1 2.5 %collective-permute-start = (bf16[256,768]{1,0:T(8,128)(2,1)S(1)}, bf16[256,768]{1,0:T(8,128)(2,1)S(1)}, u32[]{:S(2)}, u32[]{:S(2)}) collective-permute-start(bf16[256,768]{1,0:T(8,128)(2,1)S(1)} %get-tuple-element.15), channel_id=1, source_target_pairs={{0,1},{1,2},{2,3},{3,4},{4,5},{5,6},{6,7},{7,8},{8,9},{9,10},{10,1... | collective-permute-start | bytes 1179656 | tf_op jit(solution)/shard_map/ppermute | solution.py:25
  10.7 6.4 %slice_bitcast_fusion.1 = (bf16[768,2304]{1,0:T(8,128)(2,1)}, bf16[768,2304]{1,0:T(8,128)(2,1)}) fusion(bf16[2,768,2304]{2,1,0:T(8,128)(2,1)} %param.28), kind=kLoop, calls=%fused_computation.11 | loop fusion | bytes 14155776 | tf_op jit(solution)/shard_map/squeeze | solution.py:201
  17.0 1.4 compare_reduce_fusion
  18.4 0.7 compare_reduce_fusion.1
  19.2 0.8 copy-done.4
  20.1 0.7 collective-permute-start.5
  20.8 1.4 collective-permute-start.6
  23.8 0.7 select_select_fusion.2
  24.5 1.3 collective-permute-start.7
  26.4 13.3 %collective-permute-done.7 = bf16[256,768]{1,0:T(8,128)(2,1)S(1)} collective-permute-done((bf16[256,768]{1,0:T(8,128)(2,1)S(1)}, bf16[256,768]{1,0:T(8,128)(2,1)S(1)}, u32[]{:S(2)}, u32[]{:S(2)}) %collective-permute-start.7) | collective-permute-done | bytes 393248 | tf_op jit(solution)/shard_map/ppermute | solution.py:75
  39.7 0.7 broadcast_select_fusion.5
  40.4 1.6 collective-permute-start.8
  42.0 1.9 %fusion.9 = bf16[1024,768]{1,0:T(8,128)(2,1)S(1)} fusion(f32[768]{0:T(1024)S(1)} %get-tuple-element.5, f32[1024]{0:T(1024)S(1)} %add_rsqrt_fusion.1, f32[1024]{0:T(1024)S(1)} %broadcast_multiply_fusion.1, bf16[256,768]{1,0:T(8,128)(2,1)S(1)} %collective-permute-done.1, bf16[512,768]{1,0:T(8,128)(2,1)S(1)} %copy-done.1, ...), kind=kLoop, calls=%fused_computation.17 | loop fusion | flops 7864320 | bytes 3156992 | tf_op jit(solution)/shard_map/convert_element_type | solution.py:87
  43.9 3.4 %collective-permute-done.8 = bf16[256,768]{1,0:T(8,128)(2,1)S(1)} collective-permute-done((bf16[256,768]{1,0:T(8,128)(2,1)S(1)}, bf16[256,768]{1,0:T(8,128)(2,1)S(1)}, u32[]{:S(2)}, u32[]{:S(2)}) %collective-permute-start.8) | collective-permute-done | bytes 393248 | tf_op jit(solution)/shard_map/ppermute | solution.py:75
  47.3 0.7 broadcast_select_fusion.7
  48.0 0.7 collective-permute-start.9
  48.7 4.1 %convolution_convert_fusion.1.band_ref = bf16[1024,1536]{1,0:T(8,128)(2,1)} fusion(bf16[1024,768]{1,0:T(8,128)(2,1)S(1)} %fusion.9, bf16[768,2304]{1,0:T(8,128)(2,1)S(1)} %copy-done.3), kind=kOutput, calls=%fused_computation.5 | convolution fusion | flops 2417491968 | bytes 7077888 | tf_op jit(solution)/shard_map/dot_general | solution.py:205
  52.8 1.7 multiply_convert_fusion.1.q_ref
  54.9 1.8 %convolution_convert_fusion.3.prompt_ref = bf16[256,1536]{1,0:T(8,128)(2,1)} fusion(bf16[768,2304]{1,0:T(8,128)(2,1)S(1)} %copy-done.3, bf16[256,768]{1,0:T(8,128)(2,1)S(1)} %get-tuple-element.10, f32[768]{0:T(1024)S(1)} %get-tuple-element.5, f32[256]{0:T(256)S(1)} %add_rsqrt_fusion.4, f32[256]{0:T(256)S(1)} %broadcast_multiply_fusion.4), kind=kOutput, calls=%fused_computation.19 | convolution fusion | flops 605356032 | bytes 3545088 | tf_op jit(solution)/shard_map/dot_general | solution.py:212
  56.7 15.3 %shard_map.257 = bf16[256,768]{1,0:T(8,128)(2,1)} custom-call(s32[2]{0:T(128)} %pad_add_fusion.pos_ref, bf16[512,768]{1,0:T(8,128)(2,1)} %multiply_convert_fusion.1.q_ref, bf16[1024,1536]{1,0:T(8,128)(2,1)} %convolution_convert_fusion.1.band_ref, bf16[256,1536]{1,0:T(8,128)(2,1)} %convolution_convert_fusion.3.prompt_ref), custom_call_target="tpu_custom_call" | custom-call | flops 704643072 | bytes 4718592 | tf_op jit(solution)/shard_map/pallas_call | solution.py:157
  71.9 1.9 %broadcast_select_fusion.2 = (bf16[256,768]{1,0:T(8,128)(2,1)S(1)}, bf16[256,768]{1,0:T(8,128)(2,1)S(1)}) fusion(pred[]{:T(512)S(6)} %eq.98, bf16[256,768]{1,0:T(8,128)(2,1)} %shard_map.257, bf16[2,768,768]{2,1,0:T(8,128)(2,1)} %param.29, bf16[512,768]{1,0:T(8,128)(2,1)S(1)} %copy-done.1), kind=kOutput, calls=%fused_computation.94 | convolution fusion | flops 302776320 | bytes 2752513 | tf_op jit(solution)/shard_map/dot_general | solution.py:222
  74.5 1.5 collective-permute-start.13
  76.0 1.4 collective-permute-start.14
  77.4 3.3 %collective-permute-start.11 = (bf16[256,768]{1,0:T(8,128)(2,1)S(1)}, bf16[256,768]{1,0:T(8,128)(2,1)S(1)}, u32[]{:S(2)}, u32[]{:S(2)}) collective-permute-start(bf16[256,768]{1,0:T(8,128)(2,1)S(1)} %get-tuple-element.17), channel_id=1, source_target_pairs={{1,0},{2,1},{3,2},{4,3},{5,4},{6,5},{7,6},{8,7},{9,8},{10,9},{11,1... | collective-permute-start | bytes 1179656 | tf_op jit(solution)/shard_map/ppermute | solution.py:26
  80.7 15.3 %shard_map.258 = bf16[256,768]{1,0:T(8,128)(2,1)} custom-call(s32[2]{0:T(128)} %pad_add_fusion.pos_ref, bf16[512,768]{1,0:T(8,128)(2,1)} %multiply_convert_fusion.1.q_ref, bf16[1024,1536]{1,0:T(8,128)(2,1)} %convolution_convert_fusion.1.band_ref, bf16[256,1536]{1,0:T(8,128)(2,1)} %convolution_convert_fusion.3.prompt_ref), custom_call_target="tpu_custom_call" | custom-call | flops 704643072 | bytes 4718592 | tf_op jit(solution)/shard_map/pallas_call | solution.py:157
  96.1 1.9 %fusion.20 = bf16[256,768]{1,0:T(8,128)(2,1)S(1)} fusion(bf16[256,768]{1,0:T(8,128)(2,1)} %shard_map.258, bf16[2,768,768]{2,1,0:T(8,128)(2,1)} %param.29, bf16[512,768]{1,0:T(8,128)(2,1)S(1)} %copy-done.1), kind=kOutput, calls=%fused_computation.40 | convolution fusion | flops 302579712 | bytes 2359296 | tf_op jit(solution)/shard_map/dot_general | solution.py:222
  97.9 1.9 %collective-permute-start.10 = (bf16[256,768]{1,0:T(8,128)(2,1)S(1)}, bf16[256,768]{1,0:T(8,128)(2,1)S(1)}, u32[]{:S(2)}, u32[]{:S(2)}) collective-permute-start(bf16[256,768]{1,0:T(8,128)(2,1)S(1)} %fusion.20), channel_id=1, source_target_pairs={{0,1},{1,2},{2,3},{3,4},{4,5},{5,6},{6,7},{7,8},{8,9},{9,10},{10,1... | collective-permute-start | bytes 1179656 | tf_op jit(solution)/shard_map/ppermute | solution.py:25
  100.8 0.7 collective-permute-start.16
  102.1 4.9 %collective-permute-done.10 = bf16[256,768]{1,0:T(8,128)(2,1)S(1)} collective-permute-done((bf16[256,768]{1,0:T(8,128)(2,1)S(1)}, bf16[256,768]{1,0:T(8,128)(2,1)S(1)}, u32[]{:S(2)}, u32[]{:S(2)}) %collective-permute-start.10) | collective-permute-done | bytes 393248 | tf_op jit(solution)/shard_map/ppermute | solution.py:25
  108.0 1.3 collective-permute-start.17
  110.0 7.7 %collective-permute-done.17 = bf16[256,768]{1,0:T(8,128)(2,1)S(1)} collective-permute-done((bf16[256,768]{1,0:T(8,128)(2,1)S(1)}, bf16[256,768]{1,0:T(8,128)(2,1)S(1)}, u32[]{:S(2)}, u32[]{:S(2)}) %collective-permute-start.17) | collective-permute-done | bytes 393248 | tf_op jit(solution)/shard_map/ppermute | solution.py:75
  117.7 0.7 broadcast_select_fusion.4
  118.4 1.6 collective-permute-start.18
  120.0 2.1 %fusion.6 = bf16[1024,768]{1,0:T(8,128)(2,1)S(1)} fusion(f32[768]{0:T(1024)S(1)} %get-tuple-element.6, f32[1024]{0:T(1024)S(1)} %add_rsqrt_fusion, f32[1024]{0:T(1024)S(1)} %broadcast_multiply_fusion, bf16[256,768]{1,0:T(8,128)(2,1)S(1)} %collective-permute-done.11, bf16[256,768]{1,0:T(8,128)(2,1)S(1)} %fusion.20, ...), kind=kLoop, calls=%fused_computation.14 | loop fusion | flops 9437184 | bytes 3156992 | tf_op jit(solution)/shard_map/convert_element_type | solution.py:87
  122.2 4.1 %collective-permute-done.18 = bf16[256,768]{1,0:T(8,128)(2,1)S(1)} collective-permute-done((bf16[256,768]{1,0:T(8,128)(2,1)S(1)}, bf16[256,768]{1,0:T(8,128)(2,1)S(1)}, u32[]{:S(2)}, u32[]{:S(2)}) %collective-permute-start.18) | collective-permute-done | bytes 393248 | tf_op jit(solution)/shard_map/ppermute | solution.py:75
  126.2 0.7 broadcast_select_fusion.6
  126.9 0.9 collective-permute-start.19
  127.9 4.0 %convolution_convert_fusion.band_ref = bf16[1024,1536]{1,0:T(8,128)(2,1)} fusion(bf16[1024,768]{1,0:T(8,128)(2,1)S(1)} %fusion.6, bf16[768,2304]{1,0:T(8,128)(2,1)S(1)} %copy-done.2), kind=kOutput, calls=%fused_computation.4 | convolution fusion | flops 2417491968 | bytes 7077888 | tf_op jit(solution)/shard_map/dot_general | solution.py:205
  131.9 1.7 multiply_convert_fusion.q_ref
  134.0 1.8 %convolution_convert_fusion.2.prompt_ref = bf16[256,1536]{1,0:T(8,128)(2,1)} fusion(bf16[768,2304]{1,0:T(8,128)(2,1)S(1)} %copy-done.2, bf16[256,768]{1,0:T(8,128)(2,1)S(1)} %get-tuple-element.8, f32[768]{0:T(1024)S(1)} %get-tuple-element.6, f32[256]{0:T(256)S(1)} %add_rsqrt_fusion.3, f32[256]{0:T(256)S(1)} %broadcast_multiply_fusion.3), kind=kOutput, calls=%fused_computation.18 | convolution fusion | flops 605356032 | bytes 3545088 | tf_op jit(solution)/shard_map/dot_general | solution.py:212
  135.8 15.3 %shard_map.260 = bf16[256,768]{1,0:T(8,128)(2,1)} custom-call(s32[2]{0:T(128)} %pad_add_fusion.pos_ref, bf16[512,768]{1,0:T(8,128)(2,1)} %multiply_convert_fusion.q_ref, bf16[1024,1536]{1,0:T(8,128)(2,1)} %convolution_convert_fusion.band_ref, bf16[256,1536]{1,0:T(8,128)(2,1)} %convolution_convert_fusion.2.prompt_ref), custom_call_target="tpu_custom_call" | custom-call | flops 704643072 | bytes 4718592 | tf_op jit(solution)/shard_map/pallas_call | solution.py:157
  151.1 15.4 %shard_map.259 = bf16[256,768]{1,0:T(8,128)(2,1)} custom-call(s32[2]{0:T(128)} %pad_add_fusion.pos_ref, bf16[512,768]{1,0:T(8,128)(2,1)} %multiply_convert_fusion.q_ref, bf16[1024,1536]{1,0:T(8,128)(2,1)} %convolution_convert_fusion.band_ref, bf16[256,1536]{1,0:T(8,128)(2,1)} %convolution_convert_fusion.2.prompt_ref), custom_call_target="tpu_custom_call" | custom-call | flops 704643072 | bytes 4718592 | tf_op jit(solution)/shard_map/pallas_call | solution.py:157
  166.5 1.9 %fusion.22 = bf16[256,768]{1,0:T(8,128)(2,1)S(1)} fusion(bf16[256,768]{1,0:T(8,128)(2,1)S(1)} %copy-done.15, bf16[2,768,768]{2,1,0:T(8,128)(2,1)} %param.29, bf16[256,768]{1,0:T(8,128)(2,1)S(1)} %fusion.20), kind=kOutput, calls=%fused_computation.42 | convolution fusion | flops 302579712 | bytes 2359296 | tf_op jit(solution)/shard_map/dot_general | solution.py:222
  169.7 0.8 fusion.43
  (80 shorter events, 9.2 us)
Async XLA Ops:
  0.6 169.0 %copy-start = (bf16[768,512]{1,0:T(8,128)(2,1)S(1)}, bf16[768,512]{1,0:T(8,128)(2,1)}, u32[]{:S(2)}) copy-start(bf16[768,512]{1,0:T(8,128)(2,1)} %param.31) | copy-start | bytes 2359300
  2.7 16.5 %collective-permute-start.2 = (bf16[256,768]{1,0:T(8,128)(2,1)S(1)}, bf16[256,768]{1,0:T(8,128)(2,1)S(1)}, u32[]{:S(2)}, u32[]{:S(2)}) collective-permute-start(bf16[256,768]{1,0:T(8,128)(2,1)S(1)} %get-tuple-element.13), channel_id=1, source_target_pairs={{0,2},{16,18}} | collective-permute-start | bytes 1179656 | tf_op jit(solution)/shard_map/ppermute | solution.py:75
  3.3 15.8 %collective-permute-start.3 = (bf16[256,768]{1,0:T(8,128)(2,1)S(1)}, bf16[256,768]{1,0:T(8,128)(2,1)}, u32[]{:S(2)}, u32[]{:S(2)}) collective-permute-start(bf16[256,768]{1,0:T(8,128)(2,1)S(1)} %get-tuple-element.13), channel_id=1, source_target_pairs={{0,4},{16,20}} | collective-permute-start | bytes 1179656 | tf_op jit(solution)/shard_map/ppermute | solution.py:75
  4.8 15.2 %collective-permute-start.4 = (bf16[256,768]{1,0:T(8,128)(2,1)S(1)}, bf16[256,768]{1,0:T(8,128)(2,1)}, u32[]{:S(2)}, u32[]{:S(2)}) collective-permute-start(bf16[256,768]{1,0:T(8,128)(2,1)S(1)} %get-tuple-element.13), channel_id=1, source_target_pairs={{0,1},{16,17}} | collective-permute-start | bytes 1179656 | tf_op jit(solution)/shard_map/ppermute | solution.py:75
  6.2 17.3 %collective-permute-start.1 = (bf16[256,768]{1,0:T(8,128)(2,1)}, bf16[256,768]{1,0:T(8,128)(2,1)S(1)}, u32[]{:S(2)}, u32[]{:S(2)}) collective-permute-start(bf16[256,768]{1,0:T(8,128)(2,1)} %get-tuple-element.14), channel_id=1, source_target_pairs={{1,0},{2,1},{3,2},{4,3},{5,4},{6,5},{7,6},{8,7},{9,8},{10,9},{11,1... | collective-permute-start | bytes 1179656 | tf_op jit(solution)/shard_map/ppermute | solution.py:26
  8.1 10.4 %copy-start.13 = (s32[4]{0:T(128)S(1)}, s32[4]{0:T(128)}, u32[]{:S(2)}) copy-start(s32[4]{0:T(128)} %constant.65.clone) | copy-start | bytes 52
  8.1 14.7 %copy-start.12 = (s32[3]{0:T(128)S(1)}, s32[3]{0:T(128)}, u32[]{:S(2)}) copy-start(s32[3]{0:T(128)} %constant.66.clone) | copy-start | bytes 40
  8.1 15.3 %copy-start.6 = (f32[2,768]{1,0:T(2,128)S(1)}, f32[2,768]{1,0:T(2,128)}, u32[]{:S(2)}) copy-start(f32[2,768]{1,0:T(2,128)} %param.27) | copy-start | bytes 18436
  8.1 15.3 %collective-permute-start = (bf16[256,768]{1,0:T(8,128)(2,1)S(1)}, bf16[256,768]{1,0:T(8,128)(2,1)S(1)}, u32[]{:S(2)}, u32[]{:S(2)}) collective-permute-start(bf16[256,768]{1,0:T(8,128)(2,1)S(1)} %get-tuple-element.15), channel_id=1, source_target_pairs={{0,1},{1,2},{2,3},{3,4},{4,5},{5,6},{6,7},{7,8},{8,9},{9,10},{10,1... | collective-permute-start | bytes 1179656 | tf_op jit(solution)/shard_map/ppermute | solution.py:25
  17.0 6.4 %copy-start.1 = (bf16[512,768]{1,0:T(8,128)(2,1)S(1)}, bf16[512,768]{1,0:T(8,128)(2,1)}, u32[]{:S(2)}) copy-start(bf16[512,768]{1,0:T(8,128)(2,1)} %param.26) | copy-start | bytes 2359300
  19.1 0.8 copy-start.4
  20.1 3.7 %collective-permute-start.5 = (bf16[256,768]{1,0:T(8,128)(2,1)S(1)}, bf16[256,768]{1,0:T(8,128)(2,1)S(1)}, u32[]{:S(2)}, u32[]{:S(2)}) collective-permute-start(bf16[256,768]{1,0:T(8,128)(2,1)S(1)} %select_select_fusion.3), channel_id=1, source_target_pairs={{1,3},{17,19}} | collective-permute-start | bytes 1179656 | tf_op jit(solution)/shard_map/ppermute | solution.py:75
  20.8 3.0 %collective-permute-start.6 = (bf16[256,768]{1,0:T(8,128)(2,1)S(1)}, bf16[256,768]{1,0:T(8,128)(2,1)}, u32[]{:S(2)}, u32[]{:S(2)}) collective-permute-start(bf16[256,768]{1,0:T(8,128)(2,1)S(1)} %select_select_fusion.3), channel_id=1, source_target_pairs={{1,5},{2,6},{4,8},{17,21},{18,22},{20,24}} | collective-permute-start | bytes 1179656 | tf_op jit(solution)/shard_map/ppermute | solution.py:75
  24.5 15.3 %collective-permute-start.7 = (bf16[256,768]{1,0:T(8,128)(2,1)S(1)}, bf16[256,768]{1,0:T(8,128)(2,1)S(1)}, u32[]{:S(2)}, u32[]{:S(2)}) collective-permute-start(bf16[256,768]{1,0:T(8,128)(2,1)S(1)} %select_select_fusion.2), channel_id=1, source_target_pairs={{3,7},{5,9},{6,10},{8,12},{19,23},{21,25},{22,26},{24,28}} | collective-permute-start | bytes 1179656 | tf_op jit(solution)/shard_map/ppermute | solution.py:75
  40.4 8.2 %copy-start.3 = (bf16[768,2304]{1,0:T(8,128)(2,1)S(1)}, bf16[768,2304]{1,0:T(8,128)(2,1)}, u32[]{:S(2)}) copy-start(bf16[768,2304]{1,0:T(8,128)(2,1)} %get-tuple-element.11) | copy-start | bytes 10616836
  40.4 6.8 %collective-permute-start.8 = (bf16[256,768]{1,0:T(8,128)(2,1)S(1)}, bf16[256,768]{1,0:T(8,128)(2,1)S(1)}, u32[]{:S(2)}, u32[]{:S(2)}) collective-permute-start(bf16[256,768]{1,0:T(8,128)(2,1)S(1)} %broadcast_select_fusion.5), channel_id=1, source_target_pairs={{7,11},{9,13},{10,14},{23,27},{25,29},{26,30}} | collective-permute-start | bytes 1179656 | tf_op jit(solution)/shard_map/ppermute | solution.py:75
  48.0 6.5 %collective-permute-start.9 = (bf16[256,768]{1,0:T(8,128)(2,1)S(1)}, bf16[256,768]{1,0:T(8,128)(2,1)S(1)}, u32[]{:S(2)}, u32[]{:S(2)}) collective-permute-start(bf16[256,768]{1,0:T(8,128)(2,1)S(1)} %broadcast_select_fusion.7), channel_id=1, source_target_pairs={{11,15},{27,31}} | collective-permute-start | bytes 1179656 | tf_op jit(solution)/shard_map/ppermute | solution.py:75
  73.8 26.1 %collective-permute-start.12 = (bf16[256,768]{1,0:T(8,128)(2,1)S(1)}, bf16[256,768]{1,0:T(8,128)(2,1)S(1)}, u32[]{:S(2)}, u32[]{:S(2)}) collective-permute-start(bf16[256,768]{1,0:T(8,128)(2,1)S(1)} %get-tuple-element.16), channel_id=1, source_target_pairs={{0,2},{16,18}} | collective-permute-start | bytes 1179656 | tf_op jit(solution)/shard_map/ppermute | solution.py:75
  74.5 25.4 %collective-permute-start.13 = (bf16[256,768]{1,0:T(8,128)(2,1)S(1)}, bf16[256,768]{1,0:T(8,128)(2,1)}, u32[]{:S(2)}, u32[]{:S(2)}) collective-permute-start(bf16[256,768]{1,0:T(8,128)(2,1)S(1)} %get-tuple-element.16), channel_id=1, source_target_pairs={{0,4},{16,20}} | collective-permute-start | bytes 1179656 | tf_op jit(solution)/shard_map/ppermute | solution.py:75
  76.0 23.9 %collective-permute-start.14 = (bf16[256,768]{1,0:T(8,128)(2,1)S(1)}, bf16[256,768]{1,0:T(8,128)(2,1)}, u32[]{:S(2)}, u32[]{:S(2)}) collective-permute-start(bf16[256,768]{1,0:T(8,128)(2,1)S(1)} %get-tuple-element.16), channel_id=1, source_target_pairs={{0,1},{16,17}} | collective-permute-start | bytes 1179656 | tf_op jit(solution)/shard_map/ppermute | solution.py:75
  77.4 24.7 %collective-permute-start.11 = (bf16[256,768]{1,0:T(8,128)(2,1)S(1)}, bf16[256,768]{1,0:T(8,128)(2,1)S(1)}, u32[]{:S(2)}, u32[]{:S(2)}) collective-permute-start(bf16[256,768]{1,0:T(8,128)(2,1)S(1)} %get-tuple-element.17), channel_id=1, source_target_pairs={{1,0},{2,1},{3,2},{4,3},{5,4},{6,5},{7,6},{8,7},{9,8},{10,9},{11,1... | collective-permute-start | bytes 1179656 | tf_op jit(solution)/shard_map/ppermute | solution.py:26
  97.9 9.1 %collective-permute-start.10 = (bf16[256,768]{1,0:T(8,128)(2,1)S(1)}, bf16[256,768]{1,0:T(8,128)(2,1)S(1)}, u32[]{:S(2)}, u32[]{:S(2)}) collective-permute-start(bf16[256,768]{1,0:T(8,128)(2,1)S(1)} %fusion.20), channel_id=1, source_target_pairs={{0,1},{1,2},{2,3},{3,4},{4,5},{5,6},{6,7},{7,8},{8,9},{9,10},{10,1... | collective-permute-start | bytes 1179656 | tf_op jit(solution)/shard_map/ppermute | solution.py:25
  100.1 7.3 %collective-permute-start.15 = (bf16[256,768]{1,0:T(8,128)(2,1)S(1)}, bf16[256,768]{1,0:T(8,128)(2,1)S(1)}, u32[]{:S(2)}, u32[]{:S(2)}) collective-permute-start(bf16[256,768]{1,0:T(8,128)(2,1)S(1)} %select_select_fusion.1), channel_id=1, source_target_pairs={{1,3},{17,19}} | collective-permute-start | bytes 1179656 | tf_op jit(solution)/shard_map/ppermute | solution.py:75
  100.8 6.6 %collective-permute-start.16 = (bf16[256,768]{1,0:T(8,128)(2,1)S(1)}, bf16[256,768]{1,0:T(8,128)(2,1)S(1)}, u32[]{:S(2)}, u32[]{:S(2)}) collective-permute-start(bf16[256,768]{1,0:T(8,128)(2,1)S(1)} %select_select_fusion.1), channel_id=1, source_target_pairs={{1,5},{2,6},{4,8},{17,21},{18,22},{20,24}} | collective-permute-start | bytes 1179656 | tf_op jit(solution)/shard_map/ppermute | solution.py:75
  108.0 9.7 %collective-permute-start.17 = (bf16[256,768]{1,0:T(8,128)(2,1)S(1)}, bf16[256,768]{1,0:T(8,128)(2,1)S(1)}, u32[]{:S(2)}, u32[]{:S(2)}) collective-permute-start(bf16[256,768]{1,0:T(8,128)(2,1)S(1)} %select_select_fusion), channel_id=1, source_target_pairs={{3,7},{5,9},{6,10},{8,12},{19,23},{21,25},{22,26},{24,28}} | collective-permute-start | bytes 1179656 | tf_op jit(solution)/shard_map/ppermute | solution.py:75
  118.4 9.4 %copy-start.2 = (bf16[768,2304]{1,0:T(8,128)(2,1)S(1)}, bf16[768,2304]{1,0:T(8,128)(2,1)}, u32[]{:S(2)}) copy-start(bf16[768,2304]{1,0:T(8,128)(2,1)} %get-tuple-element.12) | copy-start | bytes 10616836
  118.4 7.8 %collective-permute-start.18 = (bf16[256,768]{1,0:T(8,128)(2,1)S(1)}, bf16[256,768]{1,0:T(8,128)(2,1)S(1)}, u32[]{:S(2)}, u32[]{:S(2)}) collective-permute-start(bf16[256,768]{1,0:T(8,128)(2,1)S(1)} %broadcast_select_fusion.4), channel_id=1, source_target_pairs={{7,11},{9,13},{10,14},{23,27},{25,29},{26,30}} | collective-permute-start | bytes 1179656 | tf_op jit(solution)/shard_map/ppermute | solution.py:75
  126.9 6.6 %collective-permute-start.19 = (bf16[256,768]{1,0:T(8,128)(2,1)S(1)}, bf16[256,768]{1,0:T(8,128)(2,1)S(1)}, u32[]{:S(2)}, u32[]{:S(2)}) collective-permute-start(bf16[256,768]{1,0:T(8,128)(2,1)S(1)} %broadcast_select_fusion.6), channel_id=1, source_target_pairs={{11,15},{27,31}} | collective-permute-start | bytes 1179656 | tf_op jit(solution)/shard_map/ppermute | solution.py:75
  151.1 15.4 %copy-start.15 = (bf16[256,768]{1,0:T(8,128)(2,1)S(1)}, bf16[256,768]{1,0:T(8,128)(2,1)}, u32[]{:S(2)}) copy-start(bf16[256,768]{1,0:T(8,128)(2,1)} %shard_map.260) | copy-start | bytes 1179652
  166.5 2.0 %copy-start.10 = (bf16[2,768,768]{2,1,0:T(8,128)(2,1)S(1)}, bf16[2,768,768]{2,1,0:T(8,128)(2,1)}, u32[]{:S(2)}) copy-start(bf16[2,768,768]{2,1,0:T(8,128)(2,1)} %param.29) | copy-start | bytes 7077892
  166.5 2.1 %copy-start.14 = (bf16[256,768]{1,0:T(8,128)(2,1)S(1)}, bf16[256,768]{1,0:T(8,128)(2,1)}, u32[]{:S(2)}) copy-start(bf16[256,768]{1,0:T(8,128)(2,1)} %shard_map.259) | copy-start | bytes 1179652
  168.6 1.1 copy-start.11
  169.6 1.0 copy-start.7
  169.6 1.2 copy-start.8
  169.6 1.2 copy-start.9
  170.8 0.6 copy-start.5

commit v5 on v4

--- a/solution.py
+++ b/solution.py
@@ -88,62 +88,64 @@
 
 
 QUERY_TILE = 128
-
-
-def attention_kernel(row0, pos_ref, q_ref, band_ref, prompt_ref, out_ref):
+GROUP = 4
+
+
+def attention_kernel(row0, pos_ref, q_ref, *refs):
+    band_refs = refs[:-2]
+    prompt_ref, out_ref = refs[-2:]
     tile = q_ref.shape[0]
-    width = tile + 2 * HALF
+    width = tile * len(band_refs)
     feat = q_ref.shape[1]
+    lanes = GROUP * HEAD
     block = pl.program_id(0)
     first = pos_ref[0]
     total = pos_ref[1]
-    query_pos = first + row0 + block * tile + lax.broadcasted_iota(jnp.int32, (tile, 1), 0)
+    row_in_tile = lax.broadcasted_iota(jnp.int32, (GROUP * tile, 1), 0) % tile
+    query_pos = first + row0 + block * tile + row_in_tile
     key_pos = first + row0 + block * tile - HALF + lax.broadcasted_iota(jnp.int32, (1, width), 1)
     gap = key_pos - query_pos
     band_ok = (gap >= -HALF) & (gap <= HALF) & (key_pos >= 0) & (key_pos < total)
     prompt_pos = lax.broadcasted_iota(jnp.int32, (1, PROMPT), 1)
     prompt_ok = jnp.abs(prompt_pos - query_pos) > HALF
-    start = pl.multiple_of(row0 + block * tile, tile)
     contract = (((1,), (1,)), ((), ()))
-    pair = 2 * HEAD
-    low_lanes = lax.broadcasted_iota(jnp.int32, (1, pair), 1) < HEAD
-    for head_pair in range(HEADS // 2):
-        cols = slice(head_pair * pair, (head_pair + 1) * pair)
-        vcols = slice(feat + head_pair * pair, feat + (head_pair + 1) * pair)
-        query_two = q_ref[:, cols]
-        band_keys = band_ref[pl.ds(start, width), cols]
-        band_values = band_ref[pl.ds(start, width), vcols]
-        prompt_keys = prompt_ref[:, cols]
-        prompt_values = prompt_ref[:, vcols]
-        halves = []
-        for low in (True, False):
-            keep = low_lanes if low else jnp.logical_not(low_lanes)
-            query = jnp.where(keep, query_two, jnp.zeros_like(query_two))
-            band_scores = lax.dot_general(
-                query, band_keys, contract, preferred_element_type=jnp.float32
-            )
-            prompt_scores = lax.dot_general(
-                query, prompt_keys, contract, preferred_element_type=jnp.float32
-            )
-            band_scores = jnp.where(band_ok, band_scores, -1e30)
-            prompt_scores = jnp.where(prompt_ok, prompt_scores, -1e30)
-            row_max = jnp.maximum(
-                jnp.max(band_scores, axis=1, keepdims=True),
-                jnp.max(prompt_scores, axis=1, keepdims=True),
-            )
-            band_exp = jnp.exp(band_scores - row_max)
-            prompt_exp = jnp.exp(prompt_scores - row_max)
-            denom = jnp.sum(band_exp, axis=1, keepdims=True) + jnp.sum(
-                prompt_exp, axis=1, keepdims=True
-            )
-            scale = 1.0 / denom
-            band_probs = (band_exp * scale).astype(jnp.bfloat16)
-            prompt_probs = (prompt_exp * scale).astype(jnp.bfloat16)
-            halves.append(
-                jnp.dot(band_probs, band_values, preferred_element_type=jnp.float32)
-                + jnp.dot(prompt_probs, prompt_values, preferred_element_type=jnp.float32)
-            )
-        attn = jnp.where(low_lanes, halves[0], halves[1])
+    lane_head = lax.broadcasted_iota(jnp.int32, (1, lanes), 1) // HEAD
+    for group in range(feat // lanes):
+        cols = slice(group * lanes, (group + 1) * lanes)
+        vcols = slice(feat + group * lanes, feat + (group + 1) * lanes)
+        band_keys = jnp.concatenate([ref[:, cols] for ref in band_refs], axis=0)
+        band_values = jnp.concatenate([ref[:, vcols] for ref in band_refs], axis=0)
+        query = q_ref[:, cols]
+        stacked = jnp.concatenate(
+            [jnp.where(lane_head == j, query, jnp.zeros_like(query)) for j in range(GROUP)],
+            axis=0,
+        )
+        band_scores = lax.dot_general(
+            stacked, band_keys, contract, preferred_element_type=jnp.float32
+        )
+        prompt_scores = lax.dot_general(
+            stacked, prompt_ref[:, cols], contract, preferred_element_type=jnp.float32
+        )
+        band_scores = jnp.where(band_ok, band_scores, -1e30)
+        prompt_scores = jnp.where(prompt_ok, prompt_scores, -1e30)
+        row_max = jnp.maximum(
+            jnp.max(band_scores, axis=1, keepdims=True),
+            jnp.max(prompt_scores, axis=1, keepdims=True),
+        )
+        band_exp = jnp.exp(band_scores - row_max)
+        prompt_exp = jnp.exp(prompt_scores - row_max)
+        denom = jnp.sum(band_exp, axis=1, keepdims=True) + jnp.sum(
+            prompt_exp, axis=1, keepdims=True
+        )
+        scale = 1.0 / denom
+        band_probs = (band_exp * scale).astype(jnp.bfloat16)
+        prompt_probs = (prompt_exp * scale).astype(jnp.bfloat16)
+        mixed = jnp.dot(band_probs, band_values, preferred_element_type=jnp.float32) + jnp.dot(
+            prompt_probs, prompt_ref[:, vcols], preferred_element_type=jnp.float32
+        )
+        attn = mixed[:tile]
+        for j in range(1, GROUP):
+            attn = jnp.where(lane_head == j, mixed[j * tile : (j + 1) * tile], attn)
         out_ref[:, cols] = attn.astype(out_ref.dtype)
 
 
@@ -151,28 +153,31 @@
     feat = queries.shape[1]
     tile = min(QUERY_TILE, count)
     pos = jnp.stack([first_pos, total_len]).astype(jnp.int32)
-    width = tile + 2 * HALF
-    flops = 4 * count * (width + PROMPT) * feat
+    pieces = 1 + 2 * HALF // tile
+    width = tile * pieces
+    flops = 4 * count * (width + PROMPT) * feat * GROUP
     skip = row0 // tile
+    band_specs = [
+        pl.BlockSpec((tile, band_kv.shape[1]), lambda b, p, k=k: (b + skip + k, 0))
+        for k in range(pieces)
+    ]
     return pl.pallas_call(
         functools.partial(attention_kernel, row0),
         out_shape=jax.ShapeDtypeStruct((count, feat), jnp.bfloat16),
         grid_spec=pltpu.PrefetchScalarGridSpec(
             num_scalar_prefetch=1,
             grid=(count // tile,),
-            in_specs=[
-                pl.BlockSpec((tile, feat), lambda b, p: (b + skip, 0)),
-                pl.BlockSpec(band_kv.shape, lambda b, p: (0, 0)),
-                pl.BlockSpec(prompt_kv.shape, lambda b, p: (0, 0)),
-            ],
+            in_specs=[pl.BlockSpec((tile, feat), lambda b, p: (b + skip, 0))]
+            + band_specs
+            + [pl.BlockSpec(prompt_kv.shape, lambda b, p: (0, 0))],
             out_specs=pl.BlockSpec((tile, feat), lambda b, p: (b, 0)),
         ),
         cost_estimate=pl.CostEstimate(
             flops=flops,
             transcendentals=count * (width + PROMPT) * HEADS,
-            bytes_accessed=2 * (2 * count * feat + band_kv.size + prompt_kv.size),
+            bytes_accessed=2 * (2 * count * feat + pieces * count * band_kv.shape[1] + prompt_kv.size),
         ),
-    )(pos, queries, band_kv, prompt_kv)
+    )(pos, queries, *([band_kv] * pieces), prompt_kv)
 
 
 def per_device(

time: 173 us -> 154 us (0.89)
  Pallas kernels: 61.3 us -> 43 us
    pallas_call x4, Pallas kernels: 61.3 us -> 43 us  [attention(): pl.pallas_call(functools.partial(attention_kernel, row0), out_shape=jax.S...]
    ppermute x2, waiting for transfers between devices: 0.01 us -> 3.52 us  [with_halo(): after = lax.ppermute(leading, axis, down)]
    ppermute x2, waiting for transfers between devices: 4.93 us -> 1.76 us  [with_halo(): before = lax.ppermute(last, axis, up)]
  transfers between devices with their start and end apart: 20 -> 20, of which waited for: 5 -> 6; matrix products, arithmetic and copies ran while one was open for 17% -> 19% of each run, Pallas kernels for 9% -> 7%
where the time goes in v5:
time: 154 us; the launch traced here: 153 us
  Pallas kernels  43 us (28%)
  waiting for transfers between devices  34.1 us (22%)
  starting transfers between devices  26.7 us (17%)
  matrix products  21.9 us (14%)
  other arithmetic  17.8 us (12%)
  local copies, waits for them, and re-layouts  7.47 us (5%)
  between operations  1.85 us (1%)
    pallas_call x4, Pallas kernels, attention(): pl.pallas_call(functools.partial(attention_kernel, row0), out_shape=jax.S...  43 us
    ppermute x16, waiting for transfers between devices, spread(): got = lax.ppermute(block, axis, op)  28.8 us
    ppermute x16, starting transfers between devices, spread(): got = lax.ppermute(block, axis, op)  17.1 us
    dot_general x2, matrix products, per_device(): jnp.dot(extended_normed, weights[:, feat_width:], preferred_element_type=...  8.1 us
    squeeze x1, local copies, waits for them, and re-layouts, per_device(): weights = w_qkv[layer_idx]  6.35 us
    dot_general x4, matrix products, per_device(): jnp.dot(attended, w_out[layer_idx], preferred_element_type=jnp.float32)  6.14 us
    ppermute x2, starting transfers between devices, with_halo(): after = lax.ppermute(leading, axis, down)  5.07 us
    ppermute x2, starting transfers between devices, with_halo(): before = lax.ppermute(last, axis, up)  4.46 us
  transfers between devices with their start and end apart: 20, of which 6 were waited for; matrix products, arithmetic and copies ran while one was open for 19% of the time, Pallas kernels for 7%

profile of v5, /device:TPU:20, one launch (start us, length us, event | category | flops | bytes accessed | tf_op | source)
XLA Modules:
  0.0 152.8 jit_solution(2979128480001191000)
XLA Ops:
  0.7 2.0 %broadcast_select_fusion.3 = (bf16[256,768]{1,0:T(8,128)(2,1)S(1)}, bf16[256,768]{1,0:T(8,128)(2,1)}, bf16[256,768]{1,0:T(8,128)(2,1)S(1)}) fusion(pred[]{:T(512)S(6)} %eq.98, bf16[512,768]{1,0:T(8,128)(2,1)} %param.26), kind=kLoop, calls=%fused_computation.95 | loop fusion | flops 196608 | bytes 1966081 | tf_op jit(solution)/shard_map/jit(_where)/select_n | solution.py:71
  3.3 1.4 collective-permute-start.3
  4.8 1.4 collective-permute-start.4
  6.2 1.9 %collective-permute-start.1 = (bf16[256,768]{1,0:T(8,128)(2,1)}, bf16[256,768]{1,0:T(8,128)(2,1)S(1)}, u32[]{:S(2)}, u32[]{:S(2)}) collective-permute-start(bf16[256,768]{1,0:T(8,128)(2,1)} %get-tuple-element.14), channel_id=1, source_target_pairs={{1,0},{2,1},{3,2},{4,3},{5,4},{6,5},{7,6},{8,7},{9,8},{10,9},{11,1... | collective-permute-start | bytes 1179656 | tf_op jit(solution)/shard_map/ppermute | solution.py:26
  8.1 2.5 %collective-permute-start = (bf16[256,768]{1,0:T(8,128)(2,1)S(1)}, bf16[256,768]{1,0:T(8,128)(2,1)S(1)}, u32[]{:S(2)}, u32[]{:S(2)}) collective-permute-start(bf16[256,768]{1,0:T(8,128)(2,1)S(1)} %get-tuple-element.15), channel_id=1, source_target_pairs={{0,1},{1,2},{2,3},{3,4},{4,5},{5,6},{6,7},{7,8},{8,9},{9,10},{10,1... | collective-permute-start | bytes 1179656 | tf_op jit(solution)/shard_map/ppermute | solution.py:25
  10.7 6.4 %slice_bitcast_fusion.1 = (bf16[768,2304]{1,0:T(8,128)(2,1)}, bf16[768,2304]{1,0:T(8,128)(2,1)}) fusion(bf16[2,768,2304]{2,1,0:T(8,128)(2,1)} %param.28), kind=kLoop, calls=%fused_computation.11 | loop fusion | bytes 14155776 | tf_op jit(solution)/shard_map/squeeze | solution.py:206
  17.0 1.4 compare_reduce_fusion
  19.1 0.8 copy-done.4
  20.0 0.7 collective-permute-start.5
  20.7 1.4 collective-permute-start.6
  23.7 0.7 select_select_fusion.2
  24.5 1.3 collective-permute-start.7
  26.4 13.3 %collective-permute-done.7 = bf16[256,768]{1,0:T(8,128)(2,1)S(1)} collective-permute-done((bf16[256,768]{1,0:T(8,128)(2,1)S(1)}, bf16[256,768]{1,0:T(8,128)(2,1)S(1)}, u32[]{:S(2)}, u32[]{:S(2)}) %collective-permute-start.7) | collective-permute-done | bytes 393248 | tf_op jit(solution)/shard_map/ppermute | solution.py:75
  40.3 1.6 %collective-permute-start.8 = (bf16[256,768]{1,0:T(8,128)(2,1)S(1)}, bf16[256,768]{1,0:T(8,128)(2,1)S(1)}, u32[]{:S(2)}, u32[]{:S(2)}) collective-permute-start(bf16[256,768]{1,0:T(8,128)(2,1)S(1)} %broadcast_select_fusion.5), channel_id=1, source_target_pairs={{7,11},{9,13},{10,14},{23,27},{25,29},{26,30}} | collective-permute-start | bytes 1179656 | tf_op jit(solution)/shard_map/ppermute | solution.py:75
  41.9 1.9 %fusion.9 = bf16[1024,768]{1,0:T(8,128)(2,1)S(1)} fusion(f32[768]{0:T(1024)S(1)} %get-tuple-element.5, f32[1024]{0:T(1024)S(1)} %add_rsqrt_fusion.1, f32[1024]{0:T(1024)S(1)} %broadcast_multiply_fusion.1, bf16[256,768]{1,0:T(8,128)(2,1)S(1)} %collective-permute-done.1, bf16[512,768]{1,0:T(8,128)(2,1)S(1)} %copy-done.1, ...), kind=kLoop, calls=%fused_computation.17 | loop fusion | flops 7864320 | bytes 3156992 | tf_op jit(solution)/shard_map/convert_element_type | solution.py:87
  43.8 3.4 %collective-permute-done.8 = bf16[256,768]{1,0:T(8,128)(2,1)S(1)} collective-permute-done((bf16[256,768]{1,0:T(8,128)(2,1)S(1)}, bf16[256,768]{1,0:T(8,128)(2,1)S(1)}, u32[]{:S(2)}, u32[]{:S(2)}) %collective-permute-start.8) | collective-permute-done | bytes 393248 | tf_op jit(solution)/shard_map/ppermute | solution.py:75
  47.2 0.7 broadcast_select_fusion.7
  47.9 0.7 collective-permute-start.9
  48.6 4.1 %convolution_convert_fusion.1.refs_0_.refs_1_.refs_2_.refs_3_.refs_4_ = bf16[1024,1536]{1,0:T(8,128)(2,1)} fusion(bf16[1024,768]{1,0:T(8,128)(2,1)S(1)} %fusion.9, bf16[768,2304]{1,0:T(8,128)(2,1)S(1)} %copy-done.3), kind=kOutput, calls=%fused_computation.5 | convolution fusion | flops 2417491968 | bytes 7077888 | tf_op jit(solution)/shard_map/dot_general | solution.py:210
  52.7 1.7 %multiply_convert_fusion.1.q_ref = bf16[512,768]{1,0:T(8,128)(2,1)} fusion(bf16[768,2304]{1,0:T(8,128)(2,1)S(1)} %copy-done.3, bf16[1024,768]{1,0:T(8,128)(2,1)S(1)} %fusion.9), kind=kOutput, calls=%fused_computation.34 | convolution fusion | flops 604766208 | bytes 2752512 | tf_op jit(solution)/shard_map/dot_general | solution.py:215
  54.8 1.8 %convolution_convert_fusion.3.refs_5_ = bf16[256,1536]{1,0:T(8,128)(2,1)} fusion(bf16[768,2304]{1,0:T(8,128)(2,1)S(1)} %copy-done.3, bf16[256,768]{1,0:T(8,128)(2,1)S(1)} %get-tuple-element.10, f32[768]{0:T(1024)S(1)} %get-tuple-element.5, f32[256]{0:T(256)S(1)} %add_rsqrt_fusion.4, f32[256]{0:T(256)S(1)} %broadcast_multiply_fusion.4), kind=kOutput, calls=%fused_computation.19 | convolution fusion | flops 605356032 | bytes 3545088 | tf_op jit(solution)/shard_map/dot_general | solution.py:217
  56.5 10.7 %shard_map.257 = bf16[256,768]{1,0:T(8,128)(2,1)} custom-call(s32[2]{0:T(128)} %pad_add_fusion.pos_ref, bf16[512,768]{1,0:T(8,128)(2,1)} %multiply_convert_fusion.1.q_ref, bf16[1024,1536]{1,0:T(8,128)(2,1)} %convolution_convert_fusion.1.refs_0_.refs_1_.refs_2_.refs_3_.refs_4_, ...), custom_call_target="tpu_custom_call" | custom-call | flops 2818572288 | bytes 5505024 | tf_op jit(solution)/shard_map/pallas_call | solution.py:164
  67.2 1.9 %broadcast_select_fusion.2 = (bf16[256,768]{1,0:T(8,128)(2,1)S(1)}, bf16[256,768]{1,0:T(8,128)(2,1)S(1)}) fusion(pred[]{:T(512)S(6)} %eq.98, bf16[256,768]{1,0:T(8,128)(2,1)} %shard_map.257, bf16[2,768,768]{2,1,0:T(8,128)(2,1)} %param.29, bf16[512,768]{1,0:T(8,128)(2,1)S(1)} %copy-done.1), kind=kOutput, calls=%fused_computation.94 | convolution fusion | flops 302776320 | bytes 2752513 | tf_op jit(solution)/shard_map/dot_general | solution.py:227
  69.1 0.7 collective-permute-start.12
  69.8 0.7 collective-permute-start.13
  70.5 1.5 collective-permute-start.14
  72.0 10.7 %shard_map.258 = bf16[256,768]{1,0:T(8,128)(2,1)} custom-call(s32[2]{0:T(128)} %pad_add_fusion.pos_ref, bf16[512,768]{1,0:T(8,128)(2,1)} %multiply_convert_fusion.1.q_ref, bf16[1024,1536]{1,0:T(8,128)(2,1)} %convolution_convert_fusion.1.refs_0_.refs_1_.refs_2_.refs_3_.refs_4_, ...), custom_call_target="tpu_custom_call" | custom-call | flops 2818572288 | bytes 5505024 | tf_op jit(solution)/shard_map/pallas_call | solution.py:164
  82.7 3.2 %collective-permute-start.11 = (bf16[256,768]{1,0:T(8,128)(2,1)S(1)}, bf16[256,768]{1,0:T(8,128)(2,1)S(1)}, u32[]{:S(2)}, u32[]{:S(2)}) collective-permute-start(bf16[256,768]{1,0:T(8,128)(2,1)S(1)} %get-tuple-element.17), channel_id=1, source_target_pairs={{1,0},{2,1},{3,2},{4,3},{5,4},{6,5},{7,6},{8,7},{9,8},{10,9},{11,1... | collective-permute-start | bytes 1179656 | tf_op jit(solution)/shard_map/ppermute | solution.py:26
  85.8 1.9 %fusion.20 = bf16[256,768]{1,0:T(8,128)(2,1)S(1)} fusion(bf16[256,768]{1,0:T(8,128)(2,1)} %shard_map.258, bf16[2,768,768]{2,1,0:T(8,128)(2,1)} %param.29, bf16[512,768]{1,0:T(8,128)(2,1)S(1)} %copy-done.1), kind=kOutput, calls=%fused_computation.40 | convolution fusion | flops 302579712 | bytes 2359296 | tf_op jit(solution)/shard_map/dot_general | solution.py:227
  87.7 1.9 %collective-permute-start.10 = (bf16[256,768]{1,0:T(8,128)(2,1)S(1)}, bf16[256,768]{1,0:T(8,128)(2,1)S(1)}, u32[]{:S(2)}, u32[]{:S(2)}) collective-permute-start(bf16[256,768]{1,0:T(8,128)(2,1)S(1)} %fusion.20), channel_id=1, source_target_pairs={{0,1},{1,2},{2,3},{3,4},{4,5},{5,6},{6,7},{7,8},{8,9},{9,10},{10,1... | collective-permute-start | bytes 1179656 | tf_op jit(solution)/shard_map/ppermute | solution.py:25
  89.8 0.7 collective-permute-start.15
  91.8 3.5 %collective-permute-done.11 = bf16[256,768]{1,0:T(8,128)(2,1)S(1)} collective-permute-done((bf16[256,768]{1,0:T(8,128)(2,1)S(1)}, bf16[256,768]{1,0:T(8,128)(2,1)S(1)}, u32[]{:S(2)}, u32[]{:S(2)}) %collective-permute-start.11) | collective-permute-done | bytes 393248 | tf_op jit(solution)/shard_map/ppermute | solution.py:26
  95.3 1.8 %collective-permute-done.10 = bf16[256,768]{1,0:T(8,128)(2,1)S(1)} collective-permute-done((bf16[256,768]{1,0:T(8,128)(2,1)S(1)}, bf16[256,768]{1,0:T(8,128)(2,1)S(1)}, u32[]{:S(2)}, u32[]{:S(2)}) %collective-permute-start.10) | collective-permute-done | bytes 393248 | tf_op jit(solution)/shard_map/ppermute | solution.py:25
  97.4 0.7 select_select_fusion
  98.1 1.3 collective-permute-start.17
  100.1 7.9 %collective-permute-done.17 = bf16[256,768]{1,0:T(8,128)(2,1)S(1)} collective-permute-done((bf16[256,768]{1,0:T(8,128)(2,1)S(1)}, bf16[256,768]{1,0:T(8,128)(2,1)S(1)}, u32[]{:S(2)}, u32[]{:S(2)}) %collective-permute-start.17) | collective-permute-done | bytes 393248 | tf_op jit(solution)/shard_map/ppermute | solution.py:75
  108.6 1.6 %collective-permute-start.18 = (bf16[256,768]{1,0:T(8,128)(2,1)S(1)}, bf16[256,768]{1,0:T(8,128)(2,1)S(1)}, u32[]{:S(2)}, u32[]{:S(2)}) collective-permute-start(bf16[256,768]{1,0:T(8,128)(2,1)S(1)} %broadcast_select_fusion.4), channel_id=1, source_target_pairs={{7,11},{9,13},{10,14},{23,27},{25,29},{26,30}} | collective-permute-start | bytes 1179656 | tf_op jit(solution)/shard_map/ppermute | solution.py:75
  110.2 2.1 %fusion.6 = bf16[1024,768]{1,0:T(8,128)(2,1)S(1)} fusion(f32[768]{0:T(1024)S(1)} %get-tuple-element.6, f32[1024]{0:T(1024)S(1)} %add_rsqrt_fusion, f32[1024]{0:T(1024)S(1)} %broadcast_multiply_fusion, bf16[256,768]{1,0:T(8,128)(2,1)S(1)} %collective-permute-done.11, bf16[256,768]{1,0:T(8,128)(2,1)S(1)} %fusion.20, ...), kind=kLoop, calls=%fused_computation.14 | loop fusion | flops 9437184 | bytes 3156992 | tf_op jit(solution)/shard_map/convert_element_type | solution.py:87
  112.3 4.2 %collective-permute-done.18 = bf16[256,768]{1,0:T(8,128)(2,1)S(1)} collective-permute-done((bf16[256,768]{1,0:T(8,128)(2,1)S(1)}, bf16[256,768]{1,0:T(8,128)(2,1)S(1)}, u32[]{:S(2)}, u32[]{:S(2)}) %collective-permute-start.18) | collective-permute-done | bytes 393248 | tf_op jit(solution)/shard_map/ppermute | solution.py:75
  116.6 0.7 broadcast_select_fusion.6
  117.3 0.9 collective-permute-start.19
  118.2 4.0 %convolution_convert_fusion.refs_0_.refs_1_.refs_2_.refs_3_.refs_4_ = bf16[1024,1536]{1,0:T(8,128)(2,1)} fusion(bf16[1024,768]{1,0:T(8,128)(2,1)S(1)} %fusion.6, bf16[768,2304]{1,0:T(8,128)(2,1)S(1)} %copy-done.2), kind=kOutput, calls=%fused_computation.4 | convolution fusion | flops 2417491968 | bytes 7077888 | tf_op jit(solution)/shard_map/dot_general | solution.py:210
  122.2 1.7 %multiply_convert_fusion.q_ref = bf16[512,768]{1,0:T(8,128)(2,1)} fusion(bf16[768,2304]{1,0:T(8,128)(2,1)S(1)} %copy-done.2, bf16[1024,768]{1,0:T(8,128)(2,1)S(1)} %fusion.6), kind=kOutput, calls=%fused_computation.33 | convolution fusion | flops 604766208 | bytes 2752512 | tf_op jit(solution)/shard_map/dot_general | solution.py:215
  124.3 1.8 %convolution_convert_fusion.2.refs_5_ = bf16[256,1536]{1,0:T(8,128)(2,1)} fusion(bf16[768,2304]{1,0:T(8,128)(2,1)S(1)} %copy-done.2, bf16[256,768]{1,0:T(8,128)(2,1)S(1)} %get-tuple-element.8, f32[768]{0:T(1024)S(1)} %get-tuple-element.6, f32[256]{0:T(256)S(1)} %add_rsqrt_fusion.3, f32[256]{0:T(256)S(1)} %broadcast_multiply_fusion.3), kind=kOutput, calls=%fused_computation.18 | convolution fusion | flops 605356032 | bytes 3545088 | tf_op jit(solution)/shard_map/dot_general | solution.py:217
  126.1 10.8 %shard_map.260 = bf16[256,768]{1,0:T(8,128)(2,1)} custom-call(s32[2]{0:T(128)} %pad_add_fusion.pos_ref, bf16[512,768]{1,0:T(8,128)(2,1)} %multiply_convert_fusion.q_ref, bf16[1024,1536]{1,0:T(8,128)(2,1)} %convolution_convert_fusion.refs_0_.refs_1_.refs_2_.refs_3_.refs_4_, bf16[1024,1536]{1,0:T(8,128)(2,1)} %convolution_convert_fusion.refs_0_.refs_1_.refs_2_.refs_3_.refs_4_, ...), custom_call_target="tpu_custom_call" | custom-call | flops 2818572288 | bytes 5505024 | tf_op jit(solution)/shard_map/pallas_call | solution.py:164
  136.9 10.8 %shard_map.259 = bf16[256,768]{1,0:T(8,128)(2,1)} custom-call(s32[2]{0:T(128)} %pad_add_fusion.pos_ref, bf16[512,768]{1,0:T(8,128)(2,1)} %multiply_convert_fusion.q_ref, bf16[1024,1536]{1,0:T(8,128)(2,1)} %convolution_convert_fusion.refs_0_.refs_1_.refs_2_.refs_3_.refs_4_, bf16[1024,1536]{1,0:T(8,128)(2,1)} %convolution_convert_fusion.refs_0_.refs_1_.refs_2_.refs_3_.refs_4_, ...), custom_call_target="tpu_custom_call" | custom-call | flops 2818572288 | bytes 5505024 | tf_op jit(solution)/shard_map/pallas_call | solution.py:164
  147.7 1.9 %fusion.22 = bf16[256,768]{1,0:T(8,128)(2,1)S(1)} fusion(bf16[256,768]{1,0:T(8,128)(2,1)S(1)} %copy-done.6, bf16[2,768,768]{2,1,0:T(8,128)(2,1)} %param.29, bf16[256,768]{1,0:T(8,128)(2,1)S(1)} %fusion.20), kind=kOutput, calls=%fused_computation.42 | convolution fusion | flops 302579712 | bytes 2359296 | tf_op jit(solution)/shard_map/dot_general | solution.py:227
  150.9 0.8 fusion.43
  (80 shorter events, 9.7 us)
Async XLA Ops:
  0.6 150.3 %copy-start = (bf16[768,512]{1,0:T(8,128)(2,1)S(1)}, bf16[768,512]{1,0:T(8,128)(2,1)}, u32[]{:S(2)}) copy-start(bf16[768,512]{1,0:T(8,128)(2,1)} %param.31) | copy-start | bytes 2359300
  2.7 16.4 %collective-permute-start.2 = (bf16[256,768]{1,0:T(8,128)(2,1)S(1)}, bf16[256,768]{1,0:T(8,128)(2,1)S(1)}, u32[]{:S(2)}, u32[]{:S(2)}) collective-permute-start(bf16[256,768]{1,0:T(8,128)(2,1)S(1)} %get-tuple-element.13), channel_id=1, source_target_pairs={{0,2},{16,18}} | collective-permute-start | bytes 1179656 | tf_op jit(solution)/shard_map/ppermute | solution.py:75
  3.3 15.8 %collective-permute-start.3 = (bf16[256,768]{1,0:T(8,128)(2,1)S(1)}, bf16[256,768]{1,0:T(8,128)(2,1)}, u32[]{:S(2)}, u32[]{:S(2)}) collective-permute-start(bf16[256,768]{1,0:T(8,128)(2,1)S(1)} %get-tuple-element.13), channel_id=1, source_target_pairs={{0,4},{16,20}} | collective-permute-start | bytes 1179656 | tf_op jit(solution)/shard_map/ppermute | solution.py:75
  4.8 15.1 %collective-permute-start.4 = (bf16[256,768]{1,0:T(8,128)(2,1)S(1)}, bf16[256,768]{1,0:T(8,128)(2,1)}, u32[]{:S(2)}, u32[]{:S(2)}) collective-permute-start(bf16[256,768]{1,0:T(8,128)(2,1)S(1)} %get-tuple-element.13), channel_id=1, source_target_pairs={{0,1},{16,17}} | collective-permute-start | bytes 1179656 | tf_op jit(solution)/shard_map/ppermute | solution.py:75
  6.2 17.2 %collective-permute-start.1 = (bf16[256,768]{1,0:T(8,128)(2,1)}, bf16[256,768]{1,0:T(8,128)(2,1)S(1)}, u32[]{:S(2)}, u32[]{:S(2)}) collective-permute-start(bf16[256,768]{1,0:T(8,128)(2,1)} %get-tuple-element.14), channel_id=1, source_target_pairs={{1,0},{2,1},{3,2},{4,3},{5,4},{6,5},{7,6},{8,7},{9,8},{10,9},{11,1... | collective-permute-start | bytes 1179656 | tf_op jit(solution)/shard_map/ppermute | solution.py:26
  8.1 10.4 %copy-start.15 = (s32[4]{0:T(128)S(1)}, s32[4]{0:T(128)}, u32[]{:S(2)}) copy-start(s32[4]{0:T(128)} %constant.65.clone) | copy-start | bytes 52
  8.1 14.6 %copy-start.14 = (s32[3]{0:T(128)S(1)}, s32[3]{0:T(128)}, u32[]{:S(2)}) copy-start(s32[3]{0:T(128)} %constant.66.clone) | copy-start | bytes 40
  8.1 15.3 %copy-start.8 = (f32[2,768]{1,0:T(2,128)S(1)}, f32[2,768]{1,0:T(2,128)}, u32[]{:S(2)}) copy-start(f32[2,768]{1,0:T(2,128)} %param.27) | copy-start | bytes 18436
  8.1 15.3 %collective-permute-start = (bf16[256,768]{1,0:T(8,128)(2,1)S(1)}, bf16[256,768]{1,0:T(8,128)(2,1)S(1)}, u32[]{:S(2)}, u32[]{:S(2)}) collective-permute-start(bf16[256,768]{1,0:T(8,128)(2,1)S(1)} %get-tuple-element.15), channel_id=1, source_target_pairs={{0,1},{1,2},{2,3},{3,4},{4,5},{5,6},{6,7},{7,8},{8,9},{9,10},{10,1... | collective-permute-start | bytes 1179656 | tf_op jit(solution)/shard_map/ppermute | solution.py:25
  17.0 6.4 %copy-start.1 = (bf16[512,768]{1,0:T(8,128)(2,1)S(1)}, bf16[512,768]{1,0:T(8,128)(2,1)}, u32[]{:S(2)}) copy-start(bf16[512,768]{1,0:T(8,128)(2,1)} %param.26) | copy-start | bytes 2359300
  19.1 0.8 copy-start.4
  20.0 3.7 %collective-permute-start.5 = (bf16[256,768]{1,0:T(8,128)(2,1)S(1)}, bf16[256,768]{1,0:T(8,128)(2,1)S(1)}, u32[]{:S(2)}, u32[]{:S(2)}) collective-permute-start(bf16[256,768]{1,0:T(8,128)(2,1)S(1)} %select_select_fusion.3), channel_id=1, source_target_pairs={{1,3},{17,19}} | collective-permute-start | bytes 1179656 | tf_op jit(solution)/shard_map/ppermute | solution.py:75
  20.7 3.0 %collective-permute-start.6 = (bf16[256,768]{1,0:T(8,128)(2,1)S(1)}, bf16[256,768]{1,0:T(8,128)(2,1)}, u32[]{:S(2)}, u32[]{:S(2)}) collective-permute-start(bf16[256,768]{1,0:T(8,128)(2,1)S(1)} %select_select_fusion.3), channel_id=1, source_target_pairs={{1,5},{2,6},{4,8},{17,21},{18,22},{20,24}} | collective-permute-start | bytes 1179656 | tf_op jit(solution)/shard_map/ppermute | solution.py:75
  24.5 15.3 %collective-permute-start.7 = (bf16[256,768]{1,0:T(8,128)(2,1)S(1)}, bf16[256,768]{1,0:T(8,128)(2,1)S(1)}, u32[]{:S(2)}, u32[]{:S(2)}) collective-permute-start(bf16[256,768]{1,0:T(8,128)(2,1)S(1)} %select_select_fusion.2), channel_id=1, source_target_pairs={{3,7},{5,9},{6,10},{8,12},{19,23},{21,25},{22,26},{24,28}} | collective-permute-start | bytes 1179656 | tf_op jit(solution)/shard_map/ppermute | solution.py:75
  40.3 8.2 %copy-start.3 = (bf16[768,2304]{1,0:T(8,128)(2,1)S(1)}, bf16[768,2304]{1,0:T(8,128)(2,1)}, u32[]{:S(2)}) copy-start(bf16[768,2304]{1,0:T(8,128)(2,1)} %get-tuple-element.11) | copy-start | bytes 10616836
  40.3 6.8 %collective-permute-start.8 = (bf16[256,768]{1,0:T(8,128)(2,1)S(1)}, bf16[256,768]{1,0:T(8,128)(2,1)S(1)}, u32[]{:S(2)}, u32[]{:S(2)}) collective-permute-start(bf16[256,768]{1,0:T(8,128)(2,1)S(1)} %broadcast_select_fusion.5), channel_id=1, source_target_pairs={{7,11},{9,13},{10,14},{23,27},{25,29},{26,30}} | collective-permute-start | bytes 1179656 | tf_op jit(solution)/shard_map/ppermute | solution.py:75
  47.9 6.5 %collective-permute-start.9 = (bf16[256,768]{1,0:T(8,128)(2,1)S(1)}, bf16[256,768]{1,0:T(8,128)(2,1)S(1)}, u32[]{:S(2)}, u32[]{:S(2)}) collective-permute-start(bf16[256,768]{1,0:T(8,128)(2,1)S(1)} %broadcast_select_fusion.7), channel_id=1, source_target_pairs={{11,15},{27,31}} | collective-permute-start | bytes 1179656 | tf_op jit(solution)/shard_map/ppermute | solution.py:75
  69.1 20.5 %collective-permute-start.12 = (bf16[256,768]{1,0:T(8,128)(2,1)S(1)}, bf16[256,768]{1,0:T(8,128)(2,1)S(1)}, u32[]{:S(2)}, u32[]{:S(2)}) collective-permute-start(bf16[256,768]{1,0:T(8,128)(2,1)S(1)} %get-tuple-element.16), channel_id=1, source_target_pairs={{0,2},{16,18}} | collective-permute-start | bytes 1179656 | tf_op jit(solution)/shard_map/ppermute | solution.py:75
  69.8 19.9 %collective-permute-start.13 = (bf16[256,768]{1,0:T(8,128)(2,1)S(1)}, bf16[256,768]{1,0:T(8,128)(2,1)S(1)}, u32[]{:S(2)}, u32[]{:S(2)}) collective-permute-start(bf16[256,768]{1,0:T(8,128)(2,1)S(1)} %get-tuple-element.16), channel_id=1, source_target_pairs={{0,4},{16,20}} | collective-permute-start | bytes 1179656 | tf_op jit(solution)/shard_map/ppermute | solution.py:75
  70.5 19.2 %collective-permute-start.14 = (bf16[256,768]{1,0:T(8,128)(2,1)S(1)}, bf16[256,768]{1,0:T(8,128)(2,1)}, u32[]{:S(2)}, u32[]{:S(2)}) collective-permute-start(bf16[256,768]{1,0:T(8,128)(2,1)S(1)} %get-tuple-element.16), channel_id=1, source_target_pairs={{0,1},{16,17}} | collective-permute-start | bytes 1179656 | tf_op jit(solution)/shard_map/ppermute | solution.py:75
  82.7 12.7 %collective-permute-start.11 = (bf16[256,768]{1,0:T(8,128)(2,1)S(1)}, bf16[256,768]{1,0:T(8,128)(2,1)S(1)}, u32[]{:S(2)}, u32[]{:S(2)}) collective-permute-start(bf16[256,768]{1,0:T(8,128)(2,1)S(1)} %get-tuple-element.17), channel_id=1, source_target_pairs={{1,0},{2,1},{3,2},{4,3},{5,4},{6,5},{7,6},{8,7},{9,8},{10,9},{11,1... | collective-permute-start | bytes 1179656 | tf_op jit(solution)/shard_map/ppermute | solution.py:26
  87.7 9.4 %collective-permute-start.10 = (bf16[256,768]{1,0:T(8,128)(2,1)S(1)}, bf16[256,768]{1,0:T(8,128)(2,1)S(1)}, u32[]{:S(2)}, u32[]{:S(2)}) collective-permute-start(bf16[256,768]{1,0:T(8,128)(2,1)S(1)} %fusion.20), channel_id=1, source_target_pairs={{0,1},{1,2},{2,3},{3,4},{4,5},{5,6},{6,7},{7,8},{8,9},{9,10},{10,1... | collective-permute-start | bytes 1179656 | tf_op jit(solution)/shard_map/ppermute | solution.py:25
  89.8 7.6 %collective-permute-start.15 = (bf16[256,768]{1,0:T(8,128)(2,1)S(1)}, bf16[256,768]{1,0:T(8,128)(2,1)S(1)}, u32[]{:S(2)}, u32[]{:S(2)}) collective-permute-start(bf16[256,768]{1,0:T(8,128)(2,1)S(1)} %select_select_fusion.1), channel_id=1, source_target_pairs={{1,3},{17,19}} | collective-permute-start | bytes 1179656 | tf_op jit(solution)/shard_map/ppermute | solution.py:75
  90.5 6.9 %collective-permute-start.16 = (bf16[256,768]{1,0:T(8,128)(2,1)S(1)}, bf16[256,768]{1,0:T(8,128)(2,1)S(1)}, u32[]{:S(2)}, u32[]{:S(2)}) collective-permute-start(bf16[256,768]{1,0:T(8,128)(2,1)S(1)} %select_select_fusion.1), channel_id=1, source_target_pairs={{1,5},{2,6},{4,8},{17,21},{18,22},{20,24}} | collective-permute-start | bytes 1179656 | tf_op jit(solution)/shard_map/ppermute | solution.py:75
  98.1 9.8 %collective-permute-start.17 = (bf16[256,768]{1,0:T(8,128)(2,1)S(1)}, bf16[256,768]{1,0:T(8,128)(2,1)S(1)}, u32[]{:S(2)}, u32[]{:S(2)}) collective-permute-start(bf16[256,768]{1,0:T(8,128)(2,1)S(1)} %select_select_fusion), channel_id=1, source_target_pairs={{3,7},{5,9},{6,10},{8,12},{19,23},{21,25},{22,26},{24,28}} | collective-permute-start | bytes 1179656 | tf_op jit(solution)/shard_map/ppermute | solution.py:75
  108.6 9.6 %copy-start.2 = (bf16[768,2304]{1,0:T(8,128)(2,1)S(1)}, bf16[768,2304]{1,0:T(8,128)(2,1)}, u32[]{:S(2)}) copy-start(bf16[768,2304]{1,0:T(8,128)(2,1)} %get-tuple-element.12) | copy-start | bytes 10616836
  108.6 8.0 %collective-permute-start.18 = (bf16[256,768]{1,0:T(8,128)(2,1)S(1)}, bf16[256,768]{1,0:T(8,128)(2,1)S(1)}, u32[]{:S(2)}, u32[]{:S(2)}) collective-permute-start(bf16[256,768]{1,0:T(8,128)(2,1)S(1)} %broadcast_select_fusion.4), channel_id=1, source_target_pairs={{7,11},{9,13},{10,14},{23,27},{25,29},{26,30}} | collective-permute-start | bytes 1179656 | tf_op jit(solution)/shard_map/ppermute | solution.py:75
  117.3 6.6 %collective-permute-start.19 = (bf16[256,768]{1,0:T(8,128)(2,1)S(1)}, bf16[256,768]{1,0:T(8,128)(2,1)S(1)}, u32[]{:S(2)}, u32[]{:S(2)}) collective-permute-start(bf16[256,768]{1,0:T(8,128)(2,1)S(1)} %broadcast_select_fusion.6), channel_id=1, source_target_pairs={{11,15},{27,31}} | collective-permute-start | bytes 1179656 | tf_op jit(solution)/shard_map/ppermute | solution.py:75
  136.9 10.8 %copy-start.6 = (bf16[256,768]{1,0:T(8,128)(2,1)S(1)}, bf16[256,768]{1,0:T(8,128)(2,1)}, u32[]{:S(2)}) copy-start(bf16[256,768]{1,0:T(8,128)(2,1)} %shard_map.260) | copy-start | bytes 1179652
  147.7 1.9 %copy-start.5 = (bf16[256,768]{1,0:T(8,128)(2,1)S(1)}, bf16[256,768]{1,0:T(8,128)(2,1)}, u32[]{:S(2)}) copy-start(bf16[256,768]{1,0:T(8,128)(2,1)} %shard_map.259) | copy-start | bytes 1179652
  147.7 2.2 %copy-start.12 = (bf16[2,768,768]{2,1,0:T(8,128)(2,1)S(1)}, bf16[2,768,768]{2,1,0:T(8,128)(2,1)}, u32[]{:S(2)}) copy-start(bf16[2,768,768]{2,1,0:T(8,128)(2,1)} %param.29) | copy-start | bytes 7077892
  149.8 1.1 copy-start.13
  150.9 1.0 copy-start.9
  150.9 1.2 copy-start.10
  150.9 1.2 copy-start.11
  152.1 0.6 copy-start.7

commit v6 on v5

--- a/solution.py
+++ b/solution.py
@@ -91,9 +91,23 @@
 GROUP = 4
 
 
-def attention_kernel(row0, pos_ref, q_ref, *refs):
+def stack_heads(query, lane_head):
+    return jnp.concatenate(
+        [jnp.where(lane_head == j, query, jnp.zeros_like(query)) for j in range(GROUP)],
+        axis=0,
+    )
+
+
+def to_lanes(stacked, lane_head, tile):
+    out = stacked[:tile]
+    for j in range(1, GROUP):
+        out = jnp.where(lane_head == j, stacked[j * tile : (j + 1) * tile], out)
+    return out
+
+
+def band_kernel(row0, pos_ref, q_ref, *refs):
     band_refs = refs[:-2]
-    prompt_ref, out_ref = refs[-2:]
+    out_ref, lse_ref = refs[-2:]
     tile = q_ref.shape[0]
     width = tile * len(band_refs)
     feat = q_ref.shape[1]
@@ -106,6 +120,35 @@
     key_pos = first + row0 + block * tile - HALF + lax.broadcasted_iota(jnp.int32, (1, width), 1)
     gap = key_pos - query_pos
     band_ok = (gap >= -HALF) & (gap <= HALF) & (key_pos >= 0) & (key_pos < total)
+    contract = (((1,), (1,)), ((), ()))
+    lane_head = lax.broadcasted_iota(jnp.int32, (1, lanes), 1) // HEAD
+    for group in range(feat // lanes):
+        cols = slice(group * lanes, (group + 1) * lanes)
+        vcols = slice(feat + group * lanes, feat + (group + 1) * lanes)
+        band_keys = jnp.concatenate([ref[:, cols] for ref in band_refs], axis=0)
+        band_values = jnp.concatenate([ref[:, vcols] for ref in band_refs], axis=0)
+        stacked = stack_heads(q_ref[:, cols], lane_head)
+        scores = lax.dot_general(stacked, band_keys, contract, preferred_element_type=jnp.float32)
+        scores = jnp.where(band_ok, scores, -1e30)
+        row_max = jnp.max(scores, axis=1, keepdims=True)
+        exps = jnp.exp(scores - row_max)
+        denom = jnp.sum(exps, axis=1, keepdims=True)
+        mixed = jnp.dot(exps.astype(jnp.bfloat16), band_values, preferred_element_type=jnp.float32)
+        mixed = mixed * (1.0 / denom)
+        out_ref[:, cols] = to_lanes(mixed, lane_head, tile)
+        lse_ref[:, cols] = to_lanes(
+            jnp.broadcast_to(row_max + jnp.log(denom), mixed.shape), lane_head, tile
+        )
+
+
+def prompt_kernel(row0, pos_ref, q_ref, prompt_ref, band_out_ref, lse_ref, out_ref):
+    tile = q_ref.shape[0]
+    feat = q_ref.shape[1]
+    lanes = GROUP * HEAD
+    block = pl.program_id(0)
+    first = pos_ref[0]
+    row_in_tile = lax.broadcasted_iota(jnp.int32, (GROUP * tile, 1), 0) % tile
+    query_pos = first + row0 + block * tile + row_in_tile
     prompt_pos = lax.broadcasted_iota(jnp.int32, (1, PROMPT), 1)
     prompt_ok = jnp.abs(prompt_pos - query_pos) > HALF
     contract = (((1,), (1,)), ((), ()))
@@ -113,40 +156,28 @@
     for group in range(feat // lanes):
         cols = slice(group * lanes, (group + 1) * lanes)
         vcols = slice(feat + group * lanes, feat + (group + 1) * lanes)
-        band_keys = jnp.concatenate([ref[:, cols] for ref in band_refs], axis=0)
-        band_values = jnp.concatenate([ref[:, vcols] for ref in band_refs], axis=0)
-        query = q_ref[:, cols]
-        stacked = jnp.concatenate(
-            [jnp.where(lane_head == j, query, jnp.zeros_like(query)) for j in range(GROUP)],
-            axis=0,
-        )
-        band_scores = lax.dot_general(
-            stacked, band_keys, contract, preferred_element_type=jnp.float32
-        )
-        prompt_scores = lax.dot_general(
+        stacked = stack_heads(q_ref[:, cols], lane_head)
+        scores = lax.dot_general(
             stacked, prompt_ref[:, cols], contract, preferred_element_type=jnp.float32
         )
-        band_scores = jnp.where(band_ok, band_scores, -1e30)
-        prompt_scores = jnp.where(prompt_ok, prompt_scores, -1e30)
-        row_max = jnp.maximum(
-            jnp.max(band_scores, axis=1, keepdims=True),
-            jnp.max(prompt_scores, axis=1, keepdims=True),
+        scores = jnp.where(prompt_ok, scores, -1e30)
+        row_max = jnp.max(scores, axis=1, keepdims=True)
+        exps = jnp.exp(scores - row_max)
+        denom = jnp.sum(exps, axis=1, keepdims=True)
+        mixed = jnp.dot(
+            exps.astype(jnp.bfloat16), prompt_ref[:, vcols], preferred_element_type=jnp.float32
         )
-        band_exp = jnp.exp(band_scores - row_max)
-        prompt_exp = jnp.exp(prompt_scores - row_max)
-        denom = jnp.sum(band_exp, axis=1, keepdims=True) + jnp.sum(
-            prompt_exp, axis=1, keepdims=True
+        prompt_acc = to_lanes(mixed, lane_head, tile)
+        prompt_max = to_lanes(jnp.broadcast_to(row_max, mixed.shape), lane_head, tile)
+        prompt_sum = to_lanes(jnp.broadcast_to(denom, mixed.shape), lane_head, tile)
+        band_lse = lse_ref[:, cols]
+        top = jnp.maximum(band_lse, prompt_max)
+        band_weight = jnp.exp(band_lse - top)
+        prompt_weight = jnp.exp(prompt_max - top)
+        merged = (band_out_ref[:, cols] * band_weight + prompt_acc * prompt_weight) / (
+            band_weight + prompt_sum * prompt_weight
         )
-        scale = 1.0 / denom
-        band_probs = (band_exp * scale).astype(jnp.bfloat16)
-        prompt_probs = (prompt_exp * scale).astype(jnp.bfloat16)
-        mixed = jnp.dot(band_probs, band_values, preferred_element_type=jnp.float32) + jnp.dot(
-            prompt_probs, prompt_ref[:, vcols], preferred_element_type=jnp.float32
-        )
-        attn = mixed[:tile]
-        for j in range(1, GROUP):
-            attn = jnp.where(lane_head == j, mixed[j * tile : (j + 1) * tile], attn)
-        out_ref[:, cols] = attn.astype(out_ref.dtype)
+        out_ref[:, cols] = merged.astype(out_ref.dtype)
 
 
 def attention(queries, band_kv, prompt_kv, first_pos, total_len, row0, count):
@@ -155,29 +186,46 @@
     pos = jnp.stack([first_pos, total_len]).astype(jnp.int32)
     pieces = 1 + 2 * HALF // tile
     width = tile * pieces
-    flops = 4 * count * (width + PROMPT) * feat * GROUP
     skip = row0 // tile
     band_specs = [
         pl.BlockSpec((tile, band_kv.shape[1]), lambda b, p, k=k: (b + skip + k, 0))
         for k in range(pieces)
     ]
+    row_spec = pl.BlockSpec((tile, feat), lambda b, p: (b, 0))
+    q_spec = pl.BlockSpec((tile, feat), lambda b, p: (b + skip, 0))
+    band_out, band_lse = pl.pallas_call(
+        functools.partial(band_kernel, row0),
+        out_shape=(
+            jax.ShapeDtypeStruct((count, feat), jnp.float32),
+            jax.ShapeDtypeStruct((count, feat), jnp.float32),
+        ),
+        grid_spec=pltpu.PrefetchScalarGridSpec(
+            num_scalar_prefetch=1,
+            grid=(count // tile,),
+            in_specs=[q_spec] + band_specs,
+            out_specs=(row_spec, row_spec),
+        ),
+        cost_estimate=pl.CostEstimate(
+            flops=4 * count * width * feat * GROUP,
+            transcendentals=count * width * HEADS,
+            bytes_accessed=2 * count * feat + 2 * pieces * count * band_kv.shape[1] + 8 * count * feat,
+        ),
+    )(pos, queries, *([band_kv] * pieces))
     return pl.pallas_call(
-        functools.partial(attention_kernel, row0),
+        functools.partial(prompt_kernel, row0),
         out_shape=jax.ShapeDtypeStruct((count, feat), jnp.bfloat16),
         grid_spec=pltpu.PrefetchScalarGridSpec(
             num_scalar_prefetch=1,
             grid=(count // tile,),
-            in_specs=[pl.BlockSpec((tile, feat), lambda b, p: (b + skip, 0))]
-            + band_specs
-            + [pl.BlockSpec(prompt_kv.shape, lambda b, p: (0, 0))],
-            out_specs=pl.BlockSpec((tile, feat), lambda b, p: (b, 0)),
+            in_specs=[q_spec, pl.BlockSpec(prompt_kv.shape, lambda b, p: (0, 0)), row_spec, row_spec],
+            out_specs=row_spec,
         ),
         cost_estimate=pl.CostEstimate(
-            flops=flops,
-            transcendentals=count * (width + PROMPT) * HEADS,
-            bytes_accessed=2 * (2 * count * feat + pieces * count * band_kv.shape[1] + prompt_kv.size),
-        ),
-    )(pos, queries, *([band_kv] * pieces), prompt_kv)
+            flops=4 * count * PROMPT * feat * GROUP,
+            transcendentals=count * PROMPT * HEADS,
+            bytes_accessed=4 * count * feat + 2 * prompt_kv.size + 8 * count * feat,
+        ),
+    )(pos, queries, prompt_kv, band_out, band_lse)
 
 
 def per_device(

time: 154 us -> 162 us (1.052)
  Pallas kernels: 43 us -> 56 us
  waiting for transfers between devices: 34.1 us -> 25.7 us
  matrix products: 21.9 us -> 26.6 us
    pallas_call x4 -> x8, Pallas kernels: 43 us -> 56 us  [the longest x4 34.7 us: attention(): pl.pallas_call(functools.partial(band_kernel, row0), out_shape=(jax.Shape...]
    ppermute x16, waiting for transfers between devices: 28.8 us -> 20.7 us  [spread(): got = lax.ppermute(block, axis, op)]
    ppermute x2, waiting for transfers between devices: 3.52 us -> 0.01 us  [with_halo(): after = lax.ppermute(leading, axis, down)]
    dot_general x2, matrix products: 3.51 us -> 6.82 us  [per_device(): jnp.dot(layer_norm(prompt_rows, gain), weights[:, feat_width:], preferred...]
    ppermute x2, waiting for transfers between devices: 1.76 us -> 4.99 us  [with_halo(): before = lax.ppermute(last, axis, up)]
  transfers between devices with their start and end apart: 20 -> 20, of which waited for: 6 -> 5; matrix products, arithmetic and copies ran while one was open for 19% -> 18% of each run, Pallas kernels for 7% -> 25%
where the time goes in v6:
time: 162 us; the launch traced here: 160 us
  Pallas kernels  56 us (35%)
  starting transfers between devices  27.6 us (17%)
  matrix products  26.6 us (16%)
  waiting for transfers between devices  25.7 us (16%)
  other arithmetic  16.2 us (10%)
  local copies, waits for them, and re-layouts  6.45 us (4%)
  between operations  1.86 us (1%)
    pallas_call x4, Pallas kernels, attention(): pl.pallas_call(functools.partial(band_kernel, row0), out_shape=(jax.Shape...  34.7 us
    pallas_call x4, Pallas kernels, attention(): pl.pallas_call(functools.partial(prompt_kernel, row0), out_shape=jax.Shap...  21.3 us
    ppermute x16, waiting for transfers between devices, spread(): got = lax.ppermute(block, axis, op)  20.7 us
    ppermute x16, starting transfers between devices, spread(): got = lax.ppermute(block, axis, op)  18 us
    dot_general x2, matrix products, per_device(): jnp.dot(extended_normed, weights[:, feat_width:], preferred_element_type=...  8.12 us
    dot_general x4, matrix products, per_device(): jnp.dot(attended, w_out[layer_idx], preferred_element_type=jnp.float32)  7.51 us
    dot_general x2, matrix products, per_device(): jnp.dot(layer_norm(prompt_rows, gain), weights[:, feat_width:], preferred...  6.82 us
    squeeze x1, local copies, waits for them, and re-layouts, per_device(): weights = w_qkv[layer_idx]  6.35 us
  transfers between devices with their start and end apart: 20, of which 5 were waited for; matrix products, arithmetic and copies ran while one was open for 18% of the time, Pallas kernels for 25%

profile of v6, /device:TPU:20, one launch (start us, length us, event | category | flops | bytes accessed | tf_op | source)
XLA Modules:
  0.0 160.3 jit_solution(14421411406794103946)
XLA Ops:
  0.7 1.3 broadcast_select_fusion.3
  1.9 1.4 collective-permute-start.2
  3.3 1.4 collective-permute-start.3
  4.7 1.4 collective-permute-start.4
  6.1 1.9 %collective-permute-start.1 = (bf16[256,768]{1,0:T(8,128)(2,1)S(1)}, bf16[256,768]{1,0:T(8,128)(2,1)S(1)}, u32[]{:S(2)}, u32[]{:S(2)}) collective-permute-start(bf16[256,768]{1,0:T(8,128)(2,1)S(1)} %get-tuple-element.30), channel_id=1, source_target_pairs={{1,0},{2,1},{3,2},{4,3},{5,4},{6,5},{7,6},{8,7},{9,8},{10,9},{11,1... | collective-permute-start | bytes 1179656 | tf_op jit(solution)/shard_map/ppermute | solution.py:26
  8.1 2.5 %collective-permute-start = (bf16[256,768]{1,0:T(8,128)(2,1)S(1)}, bf16[256,768]{1,0:T(8,128)(2,1)S(1)}, u32[]{:S(2)}, u32[]{:S(2)}) collective-permute-start(bf16[256,768]{1,0:T(8,128)(2,1)S(1)} %get-tuple-element.31), channel_id=1, source_target_pairs={{0,1},{1,2},{2,3},{3,4},{4,5},{5,6},{6,7},{7,8},{8,9},{9,10},{10,1... | collective-permute-start | bytes 1179656 | tf_op jit(solution)/shard_map/ppermute | solution.py:25
  10.7 6.4 %slice_bitcast_fusion.1 = (bf16[768,2304]{1,0:T(8,128)(2,1)}, bf16[768,2304]{1,0:T(8,128)(2,1)}) fusion(bf16[2,768,2304]{2,1,0:T(8,128)(2,1)} %param.28), kind=kLoop, calls=%fused_computation.11 | loop fusion | bytes 14155776 | tf_op jit(solution)/shard_map/squeeze | solution.py:254
  17.0 0.7 compare_reduce_fusion
  19.8 0.7 collective-permute-start.5
  20.4 0.7 collective-permute-start.6
  22.8 1.6 collective-permute-start.7
  24.4 1.9 %fusion.9 = bf16[1024,768]{1,0:T(8,128)(2,1)S(1)} fusion(f32[768]{0:T(1024)S(1)} %get-tuple-element.21, f32[1024]{0:T(1024)S(1)} %add_rsqrt_fusion.1, f32[1024]{0:T(1024)S(1)} %broadcast_multiply_fusion.1, bf16[256,768]{1,0:T(8,128)(2,1)S(1)} %collective-permute-done.1, bf16[512,768]{1,0:T(8,128)(2,1)S(1)} %copy-done.1, ...), kind=kLoop, calls=%fused_computation.17 | loop fusion | flops 7864320 | bytes 3156992 | tf_op jit(solution)/shard_map/convert_element_type | solution.py:87
  26.2 12.3 %collective-permute-done.7 = bf16[256,768]{1,0:T(8,128)(2,1)S(1)} collective-permute-done((bf16[256,768]{1,0:T(8,128)(2,1)S(1)}, bf16[256,768]{1,0:T(8,128)(2,1)S(1)}, u32[]{:S(2)}, u32[]{:S(2)}) %collective-permute-start.7) | collective-permute-done | bytes 393248 | tf_op jit(solution)/shard_map/ppermute | solution.py:75
  39.2 1.3 collective-permute-start.8
  40.5 4.1 %convolution_convert_fusion.1.refs_0_.refs_1_.refs_2_.refs_3_.refs_4_ = bf16[1024,1536]{1,0:T(8,128)(2,1)} fusion(bf16[1024,768]{1,0:T(8,128)(2,1)S(1)} %fusion.9, bf16[768,2304]{1,0:T(8,128)(2,1)S(1)} %copy-done.3), kind=kOutput, calls=%fused_computation.5 | convolution fusion | flops 2417491968 | bytes 7077888 | tf_op jit(solution)/shard_map/dot_general | solution.py:258
  44.6 1.2 collective-permute-done.8
  46.4 0.9 collective-permute-start.9
  47.3 1.7 %multiply_convert_fusion.1.q_ref = bf16[512,768]{1,0:T(8,128)(2,1)} fusion(bf16[768,2304]{1,0:T(8,128)(2,1)S(1)} %copy-done.3, bf16[1024,768]{1,0:T(8,128)(2,1)S(1)} %fusion.9), kind=kOutput, calls=%fused_computation.34 | convolution fusion | flops 604766208 | bytes 2752512 | tf_op jit(solution)/shard_map/dot_general | solution.py:263
  49.0 8.6 %shard_map.257 = (f32[256,768]{1,0:T(8,128)}, f32[256,768]{1,0:T(8,128)}) custom-call(s32[2]{0:T(128)} %pad_add_fusion.pos_ref, bf16[512,768]{1,0:T(8,128)(2,1)} %multiply_convert_fusion.1.q_ref, bf16[1024,1536]{1,0:T(8,128)(2,1)} %convolution_convert_fusion.1.refs_0_.refs_1_.refs_2_.refs_3_.refs_4_, ...), custom_call_target="tpu_custom_call" | custom-call | flops 2013265920 | bytes 5898240 | tf_op jit(solution)/shard_map/pallas_call | solution.py:196
  57.6 8.8 %shard_map.259 = (f32[256,768]{1,0:T(8,128)}, f32[256,768]{1,0:T(8,128)}) custom-call(s32[2]{0:T(128)} %pad_add_fusion.pos_ref, bf16[512,768]{1,0:T(8,128)(2,1)} %multiply_convert_fusion.1.q_ref, bf16[1024,1536]{1,0:T(8,128)(2,1)} %convolution_convert_fusion.1.refs_0_.refs_1_.refs_2_.refs_3_.refs_4_, ...), custom_call_target="tpu_custom_call" | custom-call | flops 2013265920 | bytes 5898240 | tf_op jit(solution)/shard_map/pallas_call | solution.py:196
  66.9 3.4 %convolution_convert_fusion.3.prompt_ref = bf16[256,1536]{1,0:T(8,128)(2,1)} fusion(bf16[768,2304]{1,0:T(8,128)(2,1)} %get-tuple-element.27, bf16[256,768]{1,0:T(8,128)(2,1)S(1)} %get-tuple-element.26, f32[768]{0:T(1024)S(1)} %get-tuple-element.21, f32[256]{0:T(256)S(1)} %add_rsqrt_fusion.4, f32[256]{0:T(256)S(1)} %broadcast_multiply_fusion.4), kind=kOutput, calls=%fused_computation.19 | convolution fusion | flops 605356032 | bytes 3544064 | tf_op jit(solution)/shard_map/dot_general | solution.py:265
  70.3 5.3 %shard_map.258 = bf16[256,768]{1,0:T(8,128)(2,1)} custom-call(s32[2]{0:T(128)} %pad_add_fusion.pos_ref, bf16[512,768]{1,0:T(8,128)(2,1)} %multiply_convert_fusion.1.q_ref, bf16[256,1536]{1,0:T(8,128)(2,1)} %convolution_convert_fusion.3.prompt_ref, f32[256,768]{1,0:T(8,128)} %get-tuple-element.10.band_out_ref, f32[256,768]{1,0:T(8,128)} %get-tuple-element.11.lse_ref), custom_call_target="tpu_custom_call" | custom-call | flops 805306368 | bytes 3145728 | tf_op jit(solution)/shard_map/pallas_call | solution.py:214
  75.6 1.9 %broadcast_select_fusion.2 = (bf16[256,768]{1,0:T(8,128)(2,1)S(1)}, bf16[256,768]{1,0:T(8,128)(2,1)S(1)}) fusion(pred[]{:T(512)S(6)} %eq.98, bf16[256,768]{1,0:T(8,128)(2,1)} %shard_map.258, bf16[2,768,768]{2,1,0:T(8,128)(2,1)} %param.29, bf16[512,768]{1,0:T(8,128)(2,1)S(1)} %copy-done.1), kind=kOutput, calls=%fused_computation.94 | convolution fusion | flops 302776320 | bytes 2752513 | tf_op jit(solution)/shard_map/dot_general | solution.py:275
  77.5 0.7 collective-permute-start.12
  78.2 1.4 collective-permute-start.13
  79.6 1.5 collective-permute-start.14
  81.0 3.2 %collective-permute-start.11 = (bf16[256,768]{1,0:T(8,128)(2,1)S(1)}, bf16[256,768]{1,0:T(8,128)(2,1)S(1)}, u32[]{:S(2)}, u32[]{:S(2)}) collective-permute-start(bf16[256,768]{1,0:T(8,128)(2,1)S(1)} %get-tuple-element.33), channel_id=1, source_target_pairs={{1,0},{2,1},{3,2},{4,3},{5,4},{6,5},{7,6},{8,7},{9,8},{10,9},{11,1... | collective-permute-start | bytes 1179656 | tf_op jit(solution)/shard_map/ppermute | solution.py:26
  84.2 5.3 %shard_map.260 = bf16[256,768]{1,0:T(8,128)(2,1)} custom-call(s32[2]{0:T(128)} %pad_add_fusion.pos_ref, bf16[512,768]{1,0:T(8,128)(2,1)} %multiply_convert_fusion.1.q_ref, bf16[256,1536]{1,0:T(8,128)(2,1)} %convolution_convert_fusion.3.prompt_ref, f32[256,768]{1,0:T(8,128)} %get-tuple-element.12.band_out_ref, f32[256,768]{1,0:T(8,128)} %get-tuple-element.13.lse_ref), custom_call_target="tpu_custom_call" | custom-call | flops 805306368 | bytes 3145728 | tf_op jit(solution)/shard_map/pallas_call | solution.py:214
  89.5 1.9 %fusion.20 = bf16[256,768]{1,0:T(8,128)(2,1)S(1)} fusion(bf16[256,768]{1,0:T(8,128)(2,1)} %shard_map.260, bf16[2,768,768]{2,1,0:T(8,128)(2,1)} %param.29, bf16[512,768]{1,0:T(8,128)(2,1)S(1)} %copy-done.1), kind=kOutput, calls=%fused_computation.40 | convolution fusion | flops 302579712 | bytes 2359296 | tf_op jit(solution)/shard_map/dot_general | solution.py:275
  91.4 1.9 %collective-permute-start.10 = (bf16[256,768]{1,0:T(8,128)(2,1)S(1)}, bf16[256,768]{1,0:T(8,128)(2,1)S(1)}, u32[]{:S(2)}, u32[]{:S(2)}) collective-permute-start(bf16[256,768]{1,0:T(8,128)(2,1)S(1)} %fusion.20), channel_id=1, source_target_pairs={{0,1},{1,2},{2,3},{3,4},{4,5},{5,6},{6,7},{7,8},{8,9},{9,10},{10,1... | collective-permute-start | bytes 1179656 | tf_op jit(solution)/shard_map/ppermute | solution.py:25
  94.1 0.7 collective-permute-start.15
  94.8 0.7 collective-permute-start.16
  95.5 5.0 %collective-permute-done.10 = bf16[256,768]{1,0:T(8,128)(2,1)S(1)} collective-permute-done((bf16[256,768]{1,0:T(8,128)(2,1)S(1)}, bf16[256,768]{1,0:T(8,128)(2,1)S(1)}, u32[]{:S(2)}, u32[]{:S(2)}) %collective-permute-start.10) | collective-permute-done | bytes 393248 | tf_op jit(solution)/shard_map/ppermute | solution.py:25
  102.1 1.8 %collective-permute-start.17 = (bf16[256,768]{1,0:T(8,128)(2,1)S(1)}, bf16[256,768]{1,0:T(8,128)(2,1)S(1)}, u32[]{:S(2)}, u32[]{:S(2)}) collective-permute-start(bf16[256,768]{1,0:T(8,128)(2,1)S(1)} %select_select_fusion), channel_id=1, source_target_pairs={{3,7},{5,9},{6,10},{8,12},{19,23},{21,25},{22,26},{24,28}} | collective-permute-start | bytes 1179656 | tf_op jit(solution)/shard_map/ppermute | solution.py:75
  103.9 2.1 %fusion.6 = bf16[1024,768]{1,0:T(8,128)(2,1)S(1)} fusion(f32[768]{0:T(1024)S(1)} %get-tuple-element.22, f32[1024]{0:T(1024)S(1)} %add_rsqrt_fusion, f32[1024]{0:T(1024)S(1)} %broadcast_multiply_fusion, bf16[256,768]{1,0:T(8,128)(2,1)S(1)} %collective-permute-done.11, bf16[256,768]{1,0:T(8,128)(2,1)S(1)} %fusion.20, ...), kind=kLoop, calls=%fused_computation.14 | loop fusion | flops 9437184 | bytes 3156992 | tf_op jit(solution)/shard_map/convert_element_type | solution.py:87
  106.1 6.0 %collective-permute-done.17 = bf16[256,768]{1,0:T(8,128)(2,1)S(1)} collective-permute-done((bf16[256,768]{1,0:T(8,128)(2,1)S(1)}, bf16[256,768]{1,0:T(8,128)(2,1)S(1)}, u32[]{:S(2)}, u32[]{:S(2)}) %collective-permute-start.17) | collective-permute-done | bytes 393248 | tf_op jit(solution)/shard_map/ppermute | solution.py:75
  112.7 1.3 collective-permute-start.18
  114.0 4.1 %convolution_convert_fusion.refs_0_.refs_1_.refs_2_.refs_3_.refs_4_ = bf16[1024,1536]{1,0:T(8,128)(2,1)} fusion(bf16[1024,768]{1,0:T(8,128)(2,1)S(1)} %fusion.6, bf16[768,2304]{1,0:T(8,128)(2,1)S(1)} %copy-done.2), kind=kOutput, calls=%fused_computation.4 | convolution fusion | flops 2417491968 | bytes 7077888 | tf_op jit(solution)/shard_map/dot_general | solution.py:258
  118.1 1.2 collective-permute-done.18
  120.6 1.7 %multiply_convert_fusion.q_ref = bf16[512,768]{1,0:T(8,128)(2,1)} fusion(bf16[768,2304]{1,0:T(8,128)(2,1)S(1)} %copy-done.2, bf16[1024,768]{1,0:T(8,128)(2,1)S(1)} %fusion.6), kind=kOutput, calls=%fused_computation.33 | convolution fusion | flops 604766208 | bytes 2752512 | tf_op jit(solution)/shard_map/dot_general | solution.py:263
  122.3 8.6 %shard_map.263 = (f32[256,768]{1,0:T(8,128)}, f32[256,768]{1,0:T(8,128)}) custom-call(s32[2]{0:T(128)} %pad_add_fusion.pos_ref, bf16[512,768]{1,0:T(8,128)(2,1)} %multiply_convert_fusion.q_ref, bf16[1024,1536]{1,0:T(8,128)(2,1)} %convolution_convert_fusion.refs_0_.refs_1_.refs_2_.refs_3_.refs_4_, ...), custom_call_target="tpu_custom_call" | custom-call | flops 2013265920 | bytes 5898240 | tf_op jit(solution)/shard_map/pallas_call | solution.py:196
  130.9 8.6 %shard_map.261 = (f32[256,768]{1,0:T(8,128)}, f32[256,768]{1,0:T(8,128)}) custom-call(s32[2]{0:T(128)} %pad_add_fusion.pos_ref, bf16[512,768]{1,0:T(8,128)(2,1)} %multiply_convert_fusion.q_ref, bf16[1024,1536]{1,0:T(8,128)(2,1)} %convolution_convert_fusion.refs_0_.refs_1_.refs_2_.refs_3_.refs_4_, ...), custom_call_target="tpu_custom_call" | custom-call | flops 2013265920 | bytes 5898240 | tf_op jit(solution)/shard_map/pallas_call | solution.py:196
  140.0 3.4 %convolution_convert_fusion.2.prompt_ref = bf16[256,1536]{1,0:T(8,128)(2,1)} fusion(bf16[768,2304]{1,0:T(8,128)(2,1)} %get-tuple-element.28, bf16[256,768]{1,0:T(8,128)(2,1)S(1)} %get-tuple-element.24, f32[768]{0:T(1024)S(1)} %get-tuple-element.22, f32[256]{0:T(256)S(1)} %add_rsqrt_fusion.3, f32[256]{0:T(256)S(1)} %broadcast_multiply_fusion.3), kind=kOutput, calls=%fused_computation.18 | convolution fusion | flops 605356032 | bytes 3544064 | tf_op jit(solution)/shard_map/dot_general | solution.py:265
  143.5 5.3 %shard_map.264 = bf16[256,768]{1,0:T(8,128)(2,1)} custom-call(s32[2]{0:T(128)} %pad_add_fusion.pos_ref, bf16[512,768]{1,0:T(8,128)(2,1)} %multiply_convert_fusion.q_ref, bf16[256,1536]{1,0:T(8,128)(2,1)} %convolution_convert_fusion.2.prompt_ref, f32[256,768]{1,0:T(8,128)} %get-tuple-element.16.band_out_ref, f32[256,768]{1,0:T(8,128)} %get-tuple-element.17.lse_ref), custom_call_target="tpu_custom_call" | custom-call | flops 805306368 | bytes 3145728 | tf_op jit(solution)/shard_map/pallas_call | solution.py:214
  148.8 1.9 %fusion.22 = bf16[256,768]{1,0:T(8,128)(2,1)S(1)} fusion(bf16[256,768]{1,0:T(8,128)(2,1)} %shard_map.264, bf16[2,768,768]{2,1,0:T(8,128)(2,1)} %param.29, bf16[256,768]{1,0:T(8,128)(2,1)S(1)} %fusion.20), kind=kOutput, calls=%fused_computation.42 | convolution fusion | flops 302579712 | bytes 2359296 | tf_op jit(solution)/shard_map/dot_general | solution.py:275
  150.7 5.3 %shard_map.262 = bf16[256,768]{1,0:T(8,128)(2,1)} custom-call(s32[2]{0:T(128)} %pad_add_fusion.pos_ref, bf16[512,768]{1,0:T(8,128)(2,1)} %multiply_convert_fusion.q_ref, bf16[256,1536]{1,0:T(8,128)(2,1)} %convolution_convert_fusion.2.prompt_ref, f32[256,768]{1,0:T(8,128)} %get-tuple-element.14.band_out_ref, f32[256,768]{1,0:T(8,128)} %get-tuple-element.15.lse_ref), custom_call_target="tpu_custom_call" | custom-call | flops 805306368 | bytes 3145728 | tf_op jit(solution)/shard_map/pallas_call | solution.py:214
  156.0 1.9 %fusion.21 = bf16[256,768]{1,0:T(8,128)(2,1)S(1)} fusion(bf16[256,768]{1,0:T(8,128)(2,1)} %shard_map.262, bf16[2,768,768]{2,1,0:T(8,128)(2,1)} %param.29, bf16[256,768]{1,0:T(8,128)(2,1)S(1)} %get-tuple-element.33), kind=kOutput, calls=%fused_computation.41 | convolution fusion | flops 302579712 | bytes 2359296 | tf_op jit(solution)/shard_map/dot_general | solution.py:275
  158.5 0.8 fusion.43
  (78 shorter events, 11.0 us)
Async XLA Ops:
  0.6 157.8 %copy-start = (bf16[768,512]{1,0:T(8,128)(2,1)S(1)}, bf16[768,512]{1,0:T(8,128)(2,1)}, u32[]{:S(2)}) copy-start(bf16[768,512]{1,0:T(8,128)(2,1)} %param.31) | copy-start | bytes 2359300
  1.9 17.7 %collective-permute-start.2 = (bf16[256,768]{1,0:T(8,128)(2,1)S(1)}, bf16[256,768]{1,0:T(8,128)(2,1)}, u32[]{:S(2)}, u32[]{:S(2)}) collective-permute-start(bf16[256,768]{1,0:T(8,128)(2,1)S(1)} %get-tuple-element.29), channel_id=1, source_target_pairs={{0,2},{16,18}} | collective-permute-start | bytes 1179656 | tf_op jit(solution)/shard_map/ppermute | solution.py:75
  3.3 16.3 %collective-permute-start.3 = (bf16[256,768]{1,0:T(8,128)(2,1)S(1)}, bf16[256,768]{1,0:T(8,128)(2,1)}, u32[]{:S(2)}, u32[]{:S(2)}) collective-permute-start(bf16[256,768]{1,0:T(8,128)(2,1)S(1)} %get-tuple-element.29), channel_id=1, source_target_pairs={{0,4},{16,20}} | collective-permute-start | bytes 1179656 | tf_op jit(solution)/shard_map/ppermute | solution.py:75
  4.7 14.9 %collective-permute-start.4 = (bf16[256,768]{1,0:T(8,128)(2,1)S(1)}, bf16[256,768]{1,0:T(8,128)(2,1)}, u32[]{:S(2)}, u32[]{:S(2)}) collective-permute-start(bf16[256,768]{1,0:T(8,128)(2,1)S(1)} %get-tuple-element.29), channel_id=1, source_target_pairs={{0,1},{16,17}} | collective-permute-start | bytes 1179656 | tf_op jit(solution)/shard_map/ppermute | solution.py:75
  6.1 15.0 %collective-permute-start.1 = (bf16[256,768]{1,0:T(8,128)(2,1)S(1)}, bf16[256,768]{1,0:T(8,128)(2,1)S(1)}, u32[]{:S(2)}, u32[]{:S(2)}) collective-permute-start(bf16[256,768]{1,0:T(8,128)(2,1)S(1)} %get-tuple-element.30), channel_id=1, source_target_pairs={{1,0},{2,1},{3,2},{4,3},{5,4},{6,5},{7,6},{8,7},{9,8},{10,9},{11,1... | collective-permute-start | bytes 1179656 | tf_op jit(solution)/shard_map/ppermute | solution.py:26
  8.1 8.9 %copy-start.12 = (s32[3]{0:T(128)S(1)}, s32[3]{0:T(128)}, u32[]{:S(2)}) copy-start(s32[3]{0:T(128)} %constant.63.clone) | copy-start | bytes 40
  8.1 9.6 %copy-start.11 = (s32[4]{0:T(128)S(1)}, s32[4]{0:T(128)}, u32[]{:S(2)}) copy-start(s32[4]{0:T(128)} %constant.65.clone) | copy-start | bytes 52
  8.1 10.3 %copy-start.10 = (s32[3]{0:T(128)S(1)}, s32[3]{0:T(128)}, u32[]{:S(2)}) copy-start(s32[3]{0:T(128)} %constant.66.clone) | copy-start | bytes 40
  8.1 11.5 %copy-start.5 = (f32[2,768]{1,0:T(2,128)S(1)}, f32[2,768]{1,0:T(2,128)}, u32[]{:S(2)}) copy-start(f32[2,768]{1,0:T(2,128)} %param.27) | copy-start | bytes 18436
  8.1 13.0 %collective-permute-start = (bf16[256,768]{1,0:T(8,128)(2,1)S(1)}, bf16[256,768]{1,0:T(8,128)(2,1)S(1)}, u32[]{:S(2)}, u32[]{:S(2)}) collective-permute-start(bf16[256,768]{1,0:T(8,128)(2,1)S(1)} %get-tuple-element.31), channel_id=1, source_target_pairs={{0,1},{1,2},{2,3},{3,4},{4,5},{5,6},{6,7},{7,8},{8,9},{9,10},{10,1... | collective-permute-start | bytes 1179656 | tf_op jit(solution)/shard_map/ppermute | solution.py:25
  17.0 4.2 %copy-start.1 = (bf16[512,768]{1,0:T(8,128)(2,1)S(1)}, bf16[512,768]{1,0:T(8,128)(2,1)}, u32[]{:S(2)}) copy-start(bf16[512,768]{1,0:T(8,128)(2,1)} %param.26) | copy-start | bytes 2359300
  19.8 2.3 %collective-permute-start.5 = (bf16[256,768]{1,0:T(8,128)(2,1)S(1)}, bf16[256,768]{1,0:T(8,128)(2,1)S(1)}, u32[]{:S(2)}, u32[]{:S(2)}) collective-permute-start(bf16[256,768]{1,0:T(8,128)(2,1)S(1)} %select_select_fusion.3), channel_id=1, source_target_pairs={{1,3},{17,19}} | collective-permute-start | bytes 1179656 | tf_op jit(solution)/shard_map/ppermute | solution.py:75
  20.4 1.6 %collective-permute-start.6 = (bf16[256,768]{1,0:T(8,128)(2,1)S(1)}, bf16[256,768]{1,0:T(8,128)(2,1)S(1)}, u32[]{:S(2)}, u32[]{:S(2)}) collective-permute-start(bf16[256,768]{1,0:T(8,128)(2,1)S(1)} %select_select_fusion.3), channel_id=1, source_target_pairs={{1,5},{2,6},{4,8},{17,21},{18,22},{20,24}} | collective-permute-start | bytes 1179656 | tf_op jit(solution)/shard_map/ppermute | solution.py:75
  22.8 17.7 %copy-start.3 = (bf16[768,2304]{1,0:T(8,128)(2,1)S(1)}, bf16[768,2304]{1,0:T(8,128)(2,1)}, u32[]{:S(2)}) copy-start(bf16[768,2304]{1,0:T(8,128)(2,1)} %get-tuple-element.27) | copy-start | bytes 10616836
  22.8 15.8 %collective-permute-start.7 = (bf16[256,768]{1,0:T(8,128)(2,1)S(1)}, bf16[256,768]{1,0:T(8,128)(2,1)S(1)}, u32[]{:S(2)}, u32[]{:S(2)}) collective-permute-start(bf16[256,768]{1,0:T(8,128)(2,1)S(1)} %select_select_fusion.2), channel_id=1, source_target_pairs={{3,7},{5,9},{6,10},{8,12},{19,23},{21,25},{22,26},{24,28}} | collective-permute-start | bytes 1179656 | tf_op jit(solution)/shard_map/ppermute | solution.py:75
  39.2 6.6 %collective-permute-start.8 = (bf16[256,768]{1,0:T(8,128)(2,1)S(1)}, bf16[256,768]{1,0:T(8,128)(2,1)S(1)}, u32[]{:S(2)}, u32[]{:S(2)}) collective-permute-start(bf16[256,768]{1,0:T(8,128)(2,1)S(1)} %broadcast_select_fusion.5), channel_id=1, source_target_pairs={{7,11},{9,13},{10,14},{23,27},{25,29},{26,30}} | collective-permute-start | bytes 1179656 | tf_op jit(solution)/shard_map/ppermute | solution.py:75
  46.4 20.0 %collective-permute-start.9 = (bf16[256,768]{1,0:T(8,128)(2,1)S(1)}, bf16[256,768]{1,0:T(8,128)(2,1)S(1)}, u32[]{:S(2)}, u32[]{:S(2)}) collective-permute-start(bf16[256,768]{1,0:T(8,128)(2,1)S(1)} %broadcast_select_fusion.7), channel_id=1, source_target_pairs={{11,15},{27,31}} | collective-permute-start | bytes 1179656 | tf_op jit(solution)/shard_map/ppermute | solution.py:75
  77.5 16.5 %collective-permute-start.12 = (bf16[256,768]{1,0:T(8,128)(2,1)S(1)}, bf16[256,768]{1,0:T(8,128)(2,1)S(1)}, u32[]{:S(2)}, u32[]{:S(2)}) collective-permute-start(bf16[256,768]{1,0:T(8,128)(2,1)S(1)} %get-tuple-element.32), channel_id=1, source_target_pairs={{0,2},{16,18}} | collective-permute-start | bytes 1179656 | tf_op jit(solution)/shard_map/ppermute | solution.py:75
  78.2 15.8 %collective-permute-start.13 = (bf16[256,768]{1,0:T(8,128)(2,1)S(1)}, bf16[256,768]{1,0:T(8,128)(2,1)}, u32[]{:S(2)}, u32[]{:S(2)}) collective-permute-start(bf16[256,768]{1,0:T(8,128)(2,1)S(1)} %get-tuple-element.32), channel_id=1, source_target_pairs={{0,4},{16,20}} | collective-permute-start | bytes 1179656 | tf_op jit(solution)/shard_map/ppermute | solution.py:75
  79.6 14.4 %collective-permute-start.14 = (bf16[256,768]{1,0:T(8,128)(2,1)S(1)}, bf16[256,768]{1,0:T(8,128)(2,1)}, u32[]{:S(2)}, u32[]{:S(2)}) collective-permute-start(bf16[256,768]{1,0:T(8,128)(2,1)S(1)} %get-tuple-element.32), channel_id=1, source_target_pairs={{0,1},{16,17}} | collective-permute-start | bytes 1179656 | tf_op jit(solution)/shard_map/ppermute | solution.py:75
  81.0 14.5 %collective-permute-start.11 = (bf16[256,768]{1,0:T(8,128)(2,1)S(1)}, bf16[256,768]{1,0:T(8,128)(2,1)S(1)}, u32[]{:S(2)}, u32[]{:S(2)}) collective-permute-start(bf16[256,768]{1,0:T(8,128)(2,1)S(1)} %get-tuple-element.33), channel_id=1, source_target_pairs={{1,0},{2,1},{3,2},{4,3},{5,4},{6,5},{7,6},{8,7},{9,8},{10,9},{11,1... | collective-permute-start | bytes 1179656 | tf_op jit(solution)/shard_map/ppermute | solution.py:26
  91.4 9.1 %collective-permute-start.10 = (bf16[256,768]{1,0:T(8,128)(2,1)S(1)}, bf16[256,768]{1,0:T(8,128)(2,1)S(1)}, u32[]{:S(2)}, u32[]{:S(2)}) collective-permute-start(bf16[256,768]{1,0:T(8,128)(2,1)S(1)} %fusion.20), channel_id=1, source_target_pairs={{0,1},{1,2},{2,3},{3,4},{4,5},{5,6},{6,7},{7,8},{8,9},{9,10},{10,1... | collective-permute-start | bytes 1179656 | tf_op jit(solution)/shard_map/ppermute | solution.py:25
  94.1 7.3 %collective-permute-start.15 = (bf16[256,768]{1,0:T(8,128)(2,1)S(1)}, bf16[256,768]{1,0:T(8,128)(2,1)S(1)}, u32[]{:S(2)}, u32[]{:S(2)}) collective-permute-start(bf16[256,768]{1,0:T(8,128)(2,1)S(1)} %select_select_fusion.1), channel_id=1, source_target_pairs={{1,3},{17,19}} | collective-permute-start | bytes 1179656 | tf_op jit(solution)/shard_map/ppermute | solution.py:75
  94.8 6.6 %collective-permute-start.16 = (bf16[256,768]{1,0:T(8,128)(2,1)S(1)}, bf16[256,768]{1,0:T(8,128)(2,1)S(1)}, u32[]{:S(2)}, u32[]{:S(2)}) collective-permute-start(bf16[256,768]{1,0:T(8,128)(2,1)S(1)} %select_select_fusion.1), channel_id=1, source_target_pairs={{1,5},{2,6},{4,8},{17,21},{18,22},{20,24}} | collective-permute-start | bytes 1179656 | tf_op jit(solution)/shard_map/ppermute | solution.py:75
  102.1 11.9 %copy-start.2 = (bf16[768,2304]{1,0:T(8,128)(2,1)S(1)}, bf16[768,2304]{1,0:T(8,128)(2,1)}, u32[]{:S(2)}) copy-start(bf16[768,2304]{1,0:T(8,128)(2,1)} %get-tuple-element.28) | copy-start | bytes 10616836
  102.1 9.9 %collective-permute-start.17 = (bf16[256,768]{1,0:T(8,128)(2,1)S(1)}, bf16[256,768]{1,0:T(8,128)(2,1)S(1)}, u32[]{:S(2)}, u32[]{:S(2)}) collective-permute-start(bf16[256,768]{1,0:T(8,128)(2,1)S(1)} %select_select_fusion), channel_id=1, source_target_pairs={{3,7},{5,9},{6,10},{8,12},{19,23},{21,25},{22,26},{24,28}} | collective-permute-start | bytes 1179656 | tf_op jit(solution)/shard_map/ppermute | solution.py:75
  112.7 6.6 %collective-permute-start.18 = (bf16[256,768]{1,0:T(8,128)(2,1)S(1)}, bf16[256,768]{1,0:T(8,128)(2,1)S(1)}, u32[]{:S(2)}, u32[]{:S(2)}) collective-permute-start(bf16[256,768]{1,0:T(8,128)(2,1)S(1)} %broadcast_select_fusion.4), channel_id=1, source_target_pairs={{7,11},{9,13},{10,14},{23,27},{25,29},{26,30}} | collective-permute-start | bytes 1179656 | tf_op jit(solution)/shard_map/ppermute | solution.py:75
  119.9 19.7 %collective-permute-start.19 = (bf16[256,768]{1,0:T(8,128)(2,1)S(1)}, bf16[256,768]{1,0:T(8,128)(2,1)S(1)}, u32[]{:S(2)}, u32[]{:S(2)}) collective-permute-start(bf16[256,768]{1,0:T(8,128)(2,1)S(1)} %broadcast_select_fusion.6), channel_id=1, source_target_pairs={{11,15},{27,31}} | collective-permute-start | bytes 1179656 | tf_op jit(solution)/shard_map/ppermute | solution.py:75
  156.0 2.5 %copy-start.9 = (f32[768]{0:T(1024)S(1)}, f32[768]{0:T(1024)}, u32[]{:S(2)}) copy-start(f32[768]{0:T(1024)} %param.30) | copy-start | bytes 9220
  158.4 1.0 copy-start.6
  158.5 1.2 copy-start.7
  158.5 1.2 copy-start.8
  159.7 0.6 copy-start.4

commit v7 on v5

--- a/solution.py
+++ b/solution.py
@@ -29,40 +29,18 @@
 
 
 def tree_rounds(count):
-    def near(i):
-        out = [i ^ 1]
-        if count % 4 == 0:
-            out += [i + 4, i ^ 2, i - 4]
-        else:
-            out += [i + 2, i - 2]
-        return [j for j in out if 0 <= j < count]
-
-    holders = {0}
+    if count & (count - 1) == 0:
+        bits = []
+        step = count // 2
+        while step:
+            bits.append(step)
+            step //= 2
+        return [[[(i, i + bit) for i in range(0, count, 2 * bit)]] for bit in bits]
     rounds = []
-    while len(holders) < count:
-        taken = set()
-        pairs = []
-        for i in sorted(holders):
-            for j in near(i):
-                if j not in holders and j not in taken:
-                    taken.add(j)
-                    pairs.append((i, j))
-        if not pairs:
-            for j in range(count):
-                if j not in holders:
-                    pairs.append((min(holders), j))
-                    taken.add(j)
-                    break
-        ops = []
-        for pair in pairs:
-            for op in ops:
-                if all(pair[0] != s for s, _ in op):
-                    op.append(pair)
-                    break
-            else:
-                ops.append([pair])
-        rounds.append(ops)
-        holders |= taken
+    held = 1
+    while held < count:
+        rounds.append([[(i, i + held) for i in range(min(held, count - held))]])
+        held *= 2
     return rounds
 
 

time: 154 us -> 134 us (0.87)
  starting transfers between devices: 26.7 us -> 18.4 us
  waiting for transfers between devices: 34.1 us -> 26.2 us
  other arithmetic: 17.8 us -> 15.9 us
    ppermute x16 -> x8, waiting for transfers between devices: 28.8 us -> 19.8 us  [spread(): got = lax.ppermute(block, axis, op)]
    ppermute x16 -> x8, starting transfers between devices: 17.1 us -> 9.75 us  [spread(): got = lax.ppermute(block, axis, op)]
    ppermute x2, waiting for transfers between devices: 1.76 us -> 6.13 us  [with_halo(): before = lax.ppermute(last, axis, up)]
    ppermute x2, waiting for transfers between devices: 3.52 us -> 0.26 us  [with_halo(): after = lax.ppermute(leading, axis, down)]
    select_n x8 -> x6, other arithmetic: 4.27 us -> 2.51 us  [spread(): received = jnp.where(jnp.any(place == targets), got, received)]
  transfers between devices with their start and end apart: 20 -> 12, of which waited for: 6 -> 4; matrix products, arithmetic and copies ran while one was open for 19% -> 20% of each run, Pallas kernels for 7% -> 0%
where the time goes in v7:
time: 134 us; the launch traced here: 133 us
  Pallas kernels  43.1 us (32%)
  waiting for transfers between devices  26.2 us (20%)
  matrix products  20.5 us (15%)
  starting transfers between devices  18.4 us (14%)
  other arithmetic  15.9 us (12%)
  local copies, waits for them, and re-layouts  6.69 us (5%)
  between operations  1.8 us (1%)
    pallas_call x4, Pallas kernels, attention(): pl.pallas_call(functools.partial(attention_kernel, row0), out_shape=jax.S...  43.1 us
    ppermute x8, waiting for transfers between devices, spread(): got = lax.ppermute(block, axis, op)  19.8 us
    ppermute x8, starting transfers between devices, spread(): got = lax.ppermute(block, axis, op)  9.75 us
    dot_general x2, matrix products, per_device(): jnp.dot(extended_normed, weights[:, feat_width:], preferred_element_type=...  8.11 us
    squeeze x1, local copies, waits for them, and re-layouts, per_device(): weights = w_qkv[layer_idx]  6.35 us
    ppermute x2, waiting for transfers between devices, with_halo(): before = lax.ppermute(last, axis, up)  6.13 us
    ppermute x2, starting transfers between devices, with_halo(): before = lax.ppermute(last, axis, up)  4.81 us
    dot_general x4, matrix products, per_device(): jnp.dot(attended, w_out[layer_idx], preferred_element_type=jnp.float32)  4.77 us
  transfers between devices with their start and end apart: 12, of which 4 were waited for; matrix products, arithmetic and copies ran while one was open for 20% of the time, Pallas kernels for 0%

profile of v7, /device:TPU:20, one launch (start us, length us, event | category | flops | bytes accessed | tf_op | source)
XLA Modules:
  0.0 132.7 jit_solution(8078940871765311609)
XLA Ops:
  0.7 1.3 broadcast_select_fusion.3
  1.9 1.9 %collective-permute-start.1 = (bf16[256,768]{1,0:T(8,128)(2,1)S(1)}, bf16[256,768]{1,0:T(8,128)(2,1)S(1)}, u32[]{:S(2)}, u32[]{:S(2)}) collective-permute-start(bf16[256,768]{1,0:T(8,128)(2,1)S(1)} %get-tuple-element.14), channel_id=1, source_target_pairs={{1,0},{2,1},{3,2},{4,3},{5,4},{6,5},{7,6},{8,7},{9,8},{10,9},{11,1... | collective-permute-start | bytes 1179656 | tf_op jit(solution)/shard_map/ppermute | solution.py:26
  3.8 2.4 %collective-permute-start = (bf16[256,768]{1,0:T(8,128)(2,1)S(1)}, bf16[256,768]{1,0:T(8,128)(2,1)S(1)}, u32[]{:S(2)}, u32[]{:S(2)}) collective-permute-start(bf16[256,768]{1,0:T(8,128)(2,1)S(1)} %get-tuple-element.15), channel_id=1, source_target_pairs={{0,1},{1,2},{2,3},{3,4},{4,5},{5,6},{6,7},{7,8},{8,9},{9,10},{10,1... | collective-permute-start | bytes 1179656 | tf_op jit(solution)/shard_map/ppermute | solution.py:25
  6.3 1.6 %collective-permute-start.2 = (bf16[256,768]{1,0:T(8,128)(2,1)S(1)}, bf16[256,768]{1,0:T(8,128)(2,1)}, u32[]{:S(2)}, u32[]{:S(2)}) collective-permute-start(bf16[256,768]{1,0:T(8,128)(2,1)S(1)} %get-tuple-element.13), channel_id=1, source_target_pairs={{0,8},{16,24}} | collective-permute-start | bytes 1179656 | tf_op jit(solution)/shard_map/ppermute | solution.py:53
  7.9 6.3 %slice_bitcast_fusion.1 = (bf16[768,2304]{1,0:T(8,128)(2,1)}, bf16[768,2304]{1,0:T(8,128)(2,1)}) fusion(bf16[2,768,2304]{2,1,0:T(8,128)(2,1)} %param.20), kind=kLoop, calls=%fused_computation.11 | loop fusion | bytes 14155776 | tf_op jit(solution)/shard_map/squeeze | solution.py:184
  14.2 0.6 compare_reduce_fusion
  14.9 0.6 compare_reduce_fusion.1
  15.5 0.7 compare_reduce_fusion.2
  16.2 0.6 pad_add_fusion.pos_ref
  16.9 0.7 collective-permute-start.3
  17.9 0.6 fusion.7
  18.5 0.6 broadcast_select_fusion.5
  19.1 1.6 %collective-permute-start.4 = (bf16[256,768]{1,0:T(8,128)(2,1)S(1)}, bf16[256,768]{1,0:T(8,128)(2,1)S(1)}, u32[]{:S(2)}, u32[]{:S(2)}) collective-permute-start(bf16[256,768]{1,0:T(8,128)(2,1)S(1)} %broadcast_select_fusion.5), channel_id=1, source_target_pairs={{0,2},{4,6},{8,10},{12,14},{16,18},{20,22},{24,26},{28,30}} | collective-permute-start | bytes 1179656 | tf_op jit(solution)/shard_map/ppermute | solution.py:53
  20.7 1.9 %fusion.9 = bf16[1024,768]{1,0:T(8,128)(2,1)S(1)} fusion(f32[768]{0:T(1024)S(1)} %get-tuple-element.5, f32[1024]{0:T(1024)S(1)} %add_rsqrt_fusion.1, f32[1024]{0:T(1024)S(1)} %broadcast_multiply_fusion.1, bf16[256,768]{1,0:T(8,128)(2,1)S(1)} %collective-permute-done.1, bf16[512,768]{1,0:T(8,128)(2,1)S(1)} %copy-done.1, ...), kind=kLoop, calls=%fused_computation.17 | loop fusion | flops 7864320 | bytes 3156992 | tf_op jit(solution)/shard_map/convert_element_type | solution.py:65
  22.6 11.8 %collective-permute-done.4 = bf16[256,768]{1,0:T(8,128)(2,1)S(1)} collective-permute-done((bf16[256,768]{1,0:T(8,128)(2,1)S(1)}, bf16[256,768]{1,0:T(8,128)(2,1)S(1)}, u32[]{:S(2)}, u32[]{:S(2)}) %collective-permute-start.4) | collective-permute-done | bytes 393248 | tf_op jit(solution)/shard_map/ppermute | solution.py:53
  34.4 0.6 broadcast_select_fusion.7
  35.0 1.5 %collective-permute-start.5 = (bf16[256,768]{1,0:T(8,128)(2,1)S(1)}, bf16[256,768]{1,0:T(8,128)(2,1)S(1)}, u32[]{:S(2)}, u32[]{:S(2)}) collective-permute-start(bf16[256,768]{1,0:T(8,128)(2,1)S(1)} %broadcast_select_fusion.7), channel_id=1, source_target_pairs={{0,1},{2,3},{4,5},{6,7},{8,9},{10,11},{12,13},{14,15},{16,17},{18,... | collective-permute-start | bytes 1179656 | tf_op jit(solution)/shard_map/ppermute | solution.py:53
  36.5 4.1 %convolution_convert_fusion.1.refs_0_.refs_1_.refs_2_.refs_3_.refs_4_ = bf16[1024,1536]{1,0:T(8,128)(2,1)} fusion(bf16[1024,768]{1,0:T(8,128)(2,1)S(1)} %fusion.9, bf16[768,2304]{1,0:T(8,128)(2,1)S(1)} %copy-done.3), kind=kOutput, calls=%fused_computation.5 | convolution fusion | flops 2417491968 | bytes 7077888 | tf_op jit(solution)/shard_map/dot_general | solution.py:188
  40.6 1.7 %multiply_convert_fusion.1.q_ref = bf16[512,768]{1,0:T(8,128)(2,1)} fusion(bf16[768,2304]{1,0:T(8,128)(2,1)S(1)} %copy-done.3, bf16[1024,768]{1,0:T(8,128)(2,1)S(1)} %fusion.9), kind=kOutput, calls=%fused_computation.34 | convolution fusion | flops 604766208 | bytes 2752512 | tf_op jit(solution)/shard_map/dot_general | solution.py:193
  42.3 0.9 convert_reduce_fusion.4
  43.4 1.8 %convolution_convert_fusion.3.refs_5_ = bf16[256,1536]{1,0:T(8,128)(2,1)} fusion(bf16[768,2304]{1,0:T(8,128)(2,1)S(1)} %copy-done.3, bf16[256,768]{1,0:T(8,128)(2,1)S(1)} %get-tuple-element.10, f32[768]{0:T(1024)S(1)} %get-tuple-element.5, f32[256]{0:T(256)S(1)} %add_rsqrt_fusion.4, f32[256]{0:T(256)S(1)} %broadcast_multiply_fusion.4), kind=kOutput, calls=%fused_computation.19 | convolution fusion | flops 605356032 | bytes 3545088 | tf_op jit(solution)/shard_map/dot_general | solution.py:195
  45.2 10.7 %shard_map.185 = bf16[256,768]{1,0:T(8,128)(2,1)} custom-call(s32[2]{0:T(128)} %pad_add_fusion.pos_ref, bf16[512,768]{1,0:T(8,128)(2,1)} %multiply_convert_fusion.1.q_ref, bf16[1024,1536]{1,0:T(8,128)(2,1)} %convolution_convert_fusion.1.refs_0_.refs_1_.refs_2_.refs_3_.refs_4_, ...), custom_call_target="tpu_custom_call" | custom-call | flops 2818572288 | bytes 5505024 | tf_op jit(solution)/shard_map/pallas_call | solution.py:142
  55.9 10.8 %shard_map.186 = bf16[256,768]{1,0:T(8,128)(2,1)} custom-call(s32[2]{0:T(128)} %pad_add_fusion.pos_ref, bf16[512,768]{1,0:T(8,128)(2,1)} %multiply_convert_fusion.1.q_ref, bf16[1024,1536]{1,0:T(8,128)(2,1)} %convolution_convert_fusion.1.refs_0_.refs_1_.refs_2_.refs_3_.refs_4_, ...), custom_call_target="tpu_custom_call" | custom-call | flops 2818572288 | bytes 5505024 | tf_op jit(solution)/shard_map/pallas_call | solution.py:142
  66.7 1.9 %broadcast_select_fusion.2 = (bf16[256,768]{1,0:T(8,128)(2,1)S(1)}, bf16[256,768]{1,0:T(8,128)(2,1)S(1)}) fusion(pred[]{:T(512)S(6)} %eq.68, bf16[256,768]{1,0:T(8,128)(2,1)S(1)} %copy-done.6, bf16[2,768,768]{2,1,0:T(8,128)(2,1)} %param.21, bf16[512,768]{1,0:T(8,128)(2,1)S(1)} %copy-done.1), kind=kOutput, calls=%fused_computation.90 | convolution fusion | flops 302776320 | bytes 2752513 | tf_op jit(solution)/shard_map/dot_general | solution.py:205
  68.6 1.9 %collective-permute-start.7 = (bf16[256,768]{1,0:T(8,128)(2,1)S(1)}, bf16[256,768]{1,0:T(8,128)(2,1)S(1)}, u32[]{:S(2)}, u32[]{:S(2)}) collective-permute-start(bf16[256,768]{1,0:T(8,128)(2,1)S(1)} %get-tuple-element.17), channel_id=1, source_target_pairs={{1,0},{2,1},{3,2},{4,3},{5,4},{6,5},{7,6},{8,7},{9,8},{10,9},{11,1... | collective-permute-start | bytes 1179656 | tf_op jit(solution)/shard_map/ppermute | solution.py:26
  70.6 0.7 collective-permute-start.8
  71.3 0.5 fusion.20
  71.8 2.4 %collective-permute-start.6 = (bf16[256,768]{1,0:T(8,128)(2,1)S(1)}, bf16[256,768]{1,0:T(8,128)(2,1)S(1)}, u32[]{:S(2)}, u32[]{:S(2)}) collective-permute-start(bf16[256,768]{1,0:T(8,128)(2,1)S(1)} %fusion.20), channel_id=1, source_target_pairs={{0,1},{1,2},{2,3},{3,4},{4,5},{5,6},{6,7},{7,8},{8,9},{9,10},{10,1... | collective-permute-start | bytes 1179656 | tf_op jit(solution)/shard_map/ppermute | solution.py:25
  74.9 0.7 collective-permute-start.9
  75.8 6.1 %collective-permute-done.6 = bf16[256,768]{1,0:T(8,128)(2,1)S(1)} collective-permute-done((bf16[256,768]{1,0:T(8,128)(2,1)S(1)}, bf16[256,768]{1,0:T(8,128)(2,1)S(1)}, u32[]{:S(2)}, u32[]{:S(2)}) %collective-permute-start.6) | collective-permute-done | bytes 393248 | tf_op jit(solution)/shard_map/ppermute | solution.py:25
  82.2 0.6 fusion.4
  82.9 0.6 broadcast_select_fusion.4
  83.5 1.8 %collective-permute-start.10 = (bf16[256,768]{1,0:T(8,128)(2,1)S(1)}, bf16[256,768]{1,0:T(8,128)(2,1)S(1)}, u32[]{:S(2)}, u32[]{:S(2)}) collective-permute-start(bf16[256,768]{1,0:T(8,128)(2,1)S(1)} %broadcast_select_fusion.4), channel_id=1, source_target_pairs={{0,2},{4,6},{8,10},{12,14},{16,18},{20,22},{24,26},{28,30}} | collective-permute-start | bytes 1179656 | tf_op jit(solution)/shard_map/ppermute | solution.py:53
  85.3 2.1 %fusion.6 = bf16[1024,768]{1,0:T(8,128)(2,1)S(1)} fusion(f32[768]{0:T(1024)S(1)} %get-tuple-element.6, f32[1024]{0:T(1024)S(1)} %add_rsqrt_fusion, f32[1024]{0:T(1024)S(1)} %broadcast_multiply_fusion, bf16[256,768]{1,0:T(8,128)(2,1)S(1)} %collective-permute-done.7, bf16[256,768]{1,0:T(8,128)(2,1)S(1)} %fusion.20, bf16[256,768]{1,0:T(8,128)(2,1)S(1)} %get-tuple-element.17, ...), kind=kLoop, calls=%fused_computation.14 | loop fusion | flops 9437184 | bytes 3156992 | tf_op jit(solution)/shard_map/convert_element_type | solution.py:65
  87.4 8.0 %collective-permute-done.10 = bf16[256,768]{1,0:T(8,128)(2,1)S(1)} collective-permute-done((bf16[256,768]{1,0:T(8,128)(2,1)S(1)}, bf16[256,768]{1,0:T(8,128)(2,1)S(1)}, u32[]{:S(2)}, u32[]{:S(2)}) %collective-permute-start.10) | collective-permute-done | bytes 393248 | tf_op jit(solution)/shard_map/ppermute | solution.py:53
  95.5 0.6 broadcast_select_fusion.6
  96.1 1.3 collective-permute-start.11
  97.4 4.0 %convolution_convert_fusion.refs_0_.refs_1_.refs_2_.refs_3_.refs_4_ = bf16[1024,1536]{1,0:T(8,128)(2,1)} fusion(bf16[1024,768]{1,0:T(8,128)(2,1)S(1)} %fusion.6, bf16[768,2304]{1,0:T(8,128)(2,1)S(1)} %copy-done.2), kind=kOutput, calls=%fused_computation.4 | convolution fusion | flops 2417491968 | bytes 7077888 | tf_op jit(solution)/shard_map/dot_general | solution.py:188
  101.4 1.7 %multiply_convert_fusion.q_ref = bf16[512,768]{1,0:T(8,128)(2,1)} fusion(bf16[768,2304]{1,0:T(8,128)(2,1)S(1)} %copy-done.2, bf16[1024,768]{1,0:T(8,128)(2,1)S(1)} %fusion.6), kind=kOutput, calls=%fused_computation.33 | convolution fusion | flops 604766208 | bytes 2752512 | tf_op jit(solution)/shard_map/dot_general | solution.py:193
  103.1 0.9 convert_reduce_fusion.3
  104.2 1.8 %convolution_convert_fusion.2.refs_5_ = bf16[256,1536]{1,0:T(8,128)(2,1)} fusion(bf16[768,2304]{1,0:T(8,128)(2,1)S(1)} %copy-done.2, bf16[256,768]{1,0:T(8,128)(2,1)S(1)} %get-tuple-element.8, f32[768]{0:T(1024)S(1)} %get-tuple-element.6, f32[256]{0:T(256)S(1)} %add_rsqrt_fusion.3, f32[256]{0:T(256)S(1)} %broadcast_multiply_fusion.3), kind=kOutput, calls=%fused_computation.18 | convolution fusion | flops 605356032 | bytes 3545088 | tf_op jit(solution)/shard_map/dot_general | solution.py:195
  106.0 10.8 %shard_map.188 = bf16[256,768]{1,0:T(8,128)(2,1)} custom-call(s32[2]{0:T(128)} %pad_add_fusion.pos_ref, bf16[512,768]{1,0:T(8,128)(2,1)} %multiply_convert_fusion.q_ref, bf16[1024,1536]{1,0:T(8,128)(2,1)} %convolution_convert_fusion.refs_0_.refs_1_.refs_2_.refs_3_.refs_4_, bf16[1024,1536]{1,0:T(8,128)(2,1)} %convolution_convert_fusion.refs_0_.refs_1_.refs_2_.refs_3_.refs_4_, ...), custom_call_target="tpu_custom_call" | custom-call | flops 2818572288 | bytes 5505024 | tf_op jit(solution)/shard_map/pallas_call | solution.py:142
  116.8 10.8 %shard_map.187 = bf16[256,768]{1,0:T(8,128)(2,1)} custom-call(s32[2]{0:T(128)} %pad_add_fusion.pos_ref, bf16[512,768]{1,0:T(8,128)(2,1)} %multiply_convert_fusion.q_ref, bf16[1024,1536]{1,0:T(8,128)(2,1)} %convolution_convert_fusion.refs_0_.refs_1_.refs_2_.refs_3_.refs_4_, bf16[1024,1536]{1,0:T(8,128)(2,1)} %convolution_convert_fusion.refs_0_.refs_1_.refs_2_.refs_3_.refs_4_, ...), custom_call_target="tpu_custom_call" | custom-call | flops 2818572288 | bytes 5505024 | tf_op jit(solution)/shard_map/pallas_call | solution.py:142
  127.6 1.9 %fusion.22 = bf16[256,768]{1,0:T(8,128)(2,1)S(1)} fusion(bf16[256,768]{1,0:T(8,128)(2,1)S(1)} %copy-done.7, bf16[2,768,768]{2,1,0:T(8,128)(2,1)} %param.21, bf16[256,768]{1,0:T(8,128)(2,1)S(1)} %fusion.20), kind=kOutput, calls=%fused_computation.42 | convolution fusion | flops 302579712 | bytes 2359296 | tf_op jit(solution)/shard_map/dot_general | solution.py:205
  129.7 0.5 fusion.21
  130.4 0.4 fusion.16
  130.8 0.8 fusion.43
  132.1 0.6 multiply_add_fusion
  (68 shorter events, 2.4 us)
Async XLA Ops:
  0.6 130.2 %copy-start = (bf16[768,512]{1,0:T(8,128)(2,1)S(1)}, bf16[768,512]{1,0:T(8,128)(2,1)}, u32[]{:S(2)}) copy-start(bf16[768,512]{1,0:T(8,128)(2,1)} %param.23) | copy-start | bytes 2359300
  1.9 15.7 %collective-permute-start.1 = (bf16[256,768]{1,0:T(8,128)(2,1)S(1)}, bf16[256,768]{1,0:T(8,128)(2,1)S(1)}, u32[]{:S(2)}, u32[]{:S(2)}) collective-permute-start(bf16[256,768]{1,0:T(8,128)(2,1)S(1)} %get-tuple-element.14), channel_id=1, source_target_pairs={{1,0},{2,1},{3,2},{4,3},{5,4},{6,5},{7,6},{8,7},{9,8},{10,9},{11,1... | collective-permute-start | bytes 1179656 | tf_op jit(solution)/shard_map/ppermute | solution.py:26
  3.8 13.7 %collective-permute-start = (bf16[256,768]{1,0:T(8,128)(2,1)S(1)}, bf16[256,768]{1,0:T(8,128)(2,1)S(1)}, u32[]{:S(2)}, u32[]{:S(2)}) collective-permute-start(bf16[256,768]{1,0:T(8,128)(2,1)S(1)} %get-tuple-element.15), channel_id=1, source_target_pairs={{0,1},{1,2},{2,3},{3,4},{4,5},{5,6},{6,7},{7,8},{8,9},{9,10},{10,1... | collective-permute-start | bytes 1179656 | tf_op jit(solution)/shard_map/ppermute | solution.py:25
  6.3 8.0 %copy-start.18 = (s32[2]{0:T(128)S(1)}, s32[2]{0:T(128)}, u32[]{:S(2)}) copy-start(s32[2]{0:T(128)} %constant.53.clone) | copy-start | bytes 28
  6.3 8.6 %copy-start.17 = (s32[4]{0:T(128)S(1)}, s32[4]{0:T(128)}, u32[]{:S(2)}) copy-start(s32[4]{0:T(128)} %constant.54.clone) | copy-start | bytes 52
  6.3 9.2 %copy-start.16 = (s32[8]{0:T(128)S(1)}, s32[8]{0:T(128)}, u32[]{:S(2)}) copy-start(s32[8]{0:T(128)} %constant.55.clone) | copy-start | bytes 100
  6.3 10.5 %copy-start.9 = (f32[2,768]{1,0:T(2,128)S(1)}, f32[2,768]{1,0:T(2,128)}, u32[]{:S(2)}) copy-start(f32[2,768]{1,0:T(2,128)} %param.19) | copy-start | bytes 18436
  6.3 11.3 %copy-start.1 = (bf16[512,768]{1,0:T(8,128)(2,1)S(1)}, bf16[512,768]{1,0:T(8,128)(2,1)}, u32[]{:S(2)}) copy-start(bf16[512,768]{1,0:T(8,128)(2,1)} %param.18) | copy-start | bytes 2359300
  6.3 10.5 %collective-permute-start.2 = (bf16[256,768]{1,0:T(8,128)(2,1)S(1)}, bf16[256,768]{1,0:T(8,128)(2,1)}, u32[]{:S(2)}, u32[]{:S(2)}) collective-permute-start(bf16[256,768]{1,0:T(8,128)(2,1)S(1)} %get-tuple-element.13), channel_id=1, source_target_pairs={{0,8},{16,24}} | collective-permute-start | bytes 1179656 | tf_op jit(solution)/shard_map/ppermute | solution.py:53
  16.9 1.6 %collective-permute-start.3 = (bf16[256,768]{1,0:T(8,128)(2,1)S(1)}, bf16[256,768]{1,0:T(8,128)(2,1)S(1)}, u32[]{:S(2)}, u32[]{:S(2)}) collective-permute-start(bf16[256,768]{1,0:T(8,128)(2,1)S(1)} %broadcast_select_fusion.1), channel_id=1, source_target_pairs={{0,4},{8,12},{16,20},{24,28}} | collective-permute-start | bytes 1179656 | tf_op jit(solution)/shard_map/ppermute | solution.py:53
  19.1 17.4 %copy-start.3 = (bf16[768,2304]{1,0:T(8,128)(2,1)S(1)}, bf16[768,2304]{1,0:T(8,128)(2,1)}, u32[]{:S(2)}) copy-start(bf16[768,2304]{1,0:T(8,128)(2,1)} %get-tuple-element.11) | copy-start | bytes 10616836
  19.1 15.3 %collective-permute-start.4 = (bf16[256,768]{1,0:T(8,128)(2,1)S(1)}, bf16[256,768]{1,0:T(8,128)(2,1)S(1)}, u32[]{:S(2)}, u32[]{:S(2)}) collective-permute-start(bf16[256,768]{1,0:T(8,128)(2,1)S(1)} %broadcast_select_fusion.5), channel_id=1, source_target_pairs={{0,2},{4,6},{8,10},{12,14},{16,18},{20,22},{24,26},{28,30}} | collective-permute-start | bytes 1179656 | tf_op jit(solution)/shard_map/ppermute | solution.py:53
  35.0 7.3 %collective-permute-start.5 = (bf16[256,768]{1,0:T(8,128)(2,1)S(1)}, bf16[256,768]{1,0:T(8,128)(2,1)S(1)}, u32[]{:S(2)}, u32[]{:S(2)}) collective-permute-start(bf16[256,768]{1,0:T(8,128)(2,1)S(1)} %broadcast_select_fusion.7), channel_id=1, source_target_pairs={{0,1},{2,3},{4,5},{6,7},{8,9},{10,11},{12,13},{14,15},{16,17},{18,... | collective-permute-start | bytes 1179656 | tf_op jit(solution)/shard_map/ppermute | solution.py:53
  55.8 10.8 %copy-start.6 = (bf16[256,768]{1,0:T(8,128)(2,1)S(1)}, bf16[256,768]{1,0:T(8,128)(2,1)}, u32[]{:S(2)}) copy-start(bf16[256,768]{1,0:T(8,128)(2,1)} %shard_map.185) | copy-start | bytes 1179652
  66.7 4.6 %copy-start.4 = (bf16[256,768]{1,0:T(8,128)(2,1)S(1)}, bf16[256,768]{1,0:T(8,128)(2,1)}, u32[]{:S(2)}) copy-start(bf16[256,768]{1,0:T(8,128)(2,1)} %shard_map.186) | copy-start | bytes 1179652
  66.7 4.6 %copy-start.13 = (bf16[2,768,768]{2,1,0:T(8,128)(2,1)S(1)}, bf16[2,768,768]{2,1,0:T(8,128)(2,1)}, u32[]{:S(2)}) copy-start(bf16[2,768,768]{2,1,0:T(8,128)(2,1)} %param.21) | copy-start | bytes 7077892
  68.6 7.2 %collective-permute-start.7 = (bf16[256,768]{1,0:T(8,128)(2,1)S(1)}, bf16[256,768]{1,0:T(8,128)(2,1)S(1)}, u32[]{:S(2)}, u32[]{:S(2)}) collective-permute-start(bf16[256,768]{1,0:T(8,128)(2,1)S(1)} %get-tuple-element.17), channel_id=1, source_target_pairs={{1,0},{2,1},{3,2},{4,3},{5,4},{6,5},{7,6},{8,7},{9,8},{10,9},{11,1... | collective-permute-start | bytes 1179656 | tf_op jit(solution)/shard_map/ppermute | solution.py:26
  70.6 4.3 %collective-permute-start.8 = (bf16[256,768]{1,0:T(8,128)(2,1)S(1)}, bf16[256,768]{1,0:T(8,128)(2,1)S(1)}, u32[]{:S(2)}, u32[]{:S(2)}) collective-permute-start(bf16[256,768]{1,0:T(8,128)(2,1)S(1)} %get-tuple-element.16), channel_id=1, source_target_pairs={{0,8},{16,24}} | collective-permute-start | bytes 1179656 | tf_op jit(solution)/shard_map/ppermute | solution.py:53
  71.8 10.2 %collective-permute-start.6 = (bf16[256,768]{1,0:T(8,128)(2,1)S(1)}, bf16[256,768]{1,0:T(8,128)(2,1)S(1)}, u32[]{:S(2)}, u32[]{:S(2)}) collective-permute-start(bf16[256,768]{1,0:T(8,128)(2,1)S(1)} %fusion.20), channel_id=1, source_target_pairs={{0,1},{1,2},{2,3},{3,4},{4,5},{5,6},{6,7},{7,8},{8,9},{9,10},{10,1... | collective-permute-start | bytes 1179656 | tf_op jit(solution)/shard_map/ppermute | solution.py:25
  74.9 8.0 %collective-permute-start.9 = (bf16[256,768]{1,0:T(8,128)(2,1)S(1)}, bf16[256,768]{1,0:T(8,128)(2,1)S(1)}, u32[]{:S(2)}, u32[]{:S(2)}) collective-permute-start(bf16[256,768]{1,0:T(8,128)(2,1)S(1)} %broadcast_select_fusion), channel_id=1, source_target_pairs={{0,4},{8,12},{16,20},{24,28}} | collective-permute-start | bytes 1179656 | tf_op jit(solution)/shard_map/ppermute | solution.py:53
  83.5 13.9 %copy-start.2 = (bf16[768,2304]{1,0:T(8,128)(2,1)S(1)}, bf16[768,2304]{1,0:T(8,128)(2,1)}, u32[]{:S(2)}) copy-start(bf16[768,2304]{1,0:T(8,128)(2,1)} %get-tuple-element.12) | copy-start | bytes 10616836
  83.5 11.9 %collective-permute-start.10 = (bf16[256,768]{1,0:T(8,128)(2,1)S(1)}, bf16[256,768]{1,0:T(8,128)(2,1)S(1)}, u32[]{:S(2)}, u32[]{:S(2)}) collective-permute-start(bf16[256,768]{1,0:T(8,128)(2,1)S(1)} %broadcast_select_fusion.4), channel_id=1, source_target_pairs={{0,2},{4,6},{8,10},{12,14},{16,18},{20,22},{24,26},{28,30}} | collective-permute-start | bytes 1179656 | tf_op jit(solution)/shard_map/ppermute | solution.py:53
  96.1 7.0 %collective-permute-start.11 = (bf16[256,768]{1,0:T(8,128)(2,1)S(1)}, bf16[256,768]{1,0:T(8,128)(2,1)S(1)}, u32[]{:S(2)}, u32[]{:S(2)}) collective-permute-start(bf16[256,768]{1,0:T(8,128)(2,1)S(1)} %broadcast_select_fusion.6), channel_id=1, source_target_pairs={{0,1},{2,3},{4,5},{6,7},{8,9},{10,11},{12,13},{14,15},{16,17},{18,... | collective-permute-start | bytes 1179656 | tf_op jit(solution)/shard_map/ppermute | solution.py:53
  116.7 10.8 %copy-start.7 = (bf16[256,768]{1,0:T(8,128)(2,1)S(1)}, bf16[256,768]{1,0:T(8,128)(2,1)}, u32[]{:S(2)}) copy-start(bf16[256,768]{1,0:T(8,128)(2,1)} %shard_map.188) | copy-start | bytes 1179652
  127.6 1.9 %copy-start.5 = (bf16[256,768]{1,0:T(8,128)(2,1)S(1)}, bf16[256,768]{1,0:T(8,128)(2,1)}, u32[]{:S(2)}) copy-start(bf16[256,768]{1,0:T(8,128)(2,1)} %shard_map.187) | copy-start | bytes 1179652
  127.6 2.2 %copy-start.14 = (bf16[2,768,768]{2,1,0:T(8,128)(2,1)S(1)}, bf16[2,768,768]{2,1,0:T(8,128)(2,1)}, u32[]{:S(2)}) copy-start(bf16[2,768,768]{2,1,0:T(8,128)(2,1)} %param.21) | copy-start | bytes 7077892
  129.7 1.1 copy-start.15
  130.8 1.0 copy-start.10
  130.8 1.2 copy-start.11
  130.8 1.2 copy-start.12
  132.0 0.6 copy-start.8

commit v8 on v7

--- a/solution.py
+++ b/solution.py
@@ -65,7 +65,7 @@
     return (centred * lax.rsqrt(row_var + 1e-05) * gain_row).astype(jnp.bfloat16)
 
 
-QUERY_TILE = 128
+QUERY_TILE = 256
 GROUP = 4
 
 
@@ -176,7 +176,6 @@
     seq_place = lax.axis_index("seq")
     total_len = tok_rows * seq_devices
     first_pos = seq_place * tok_rows
-    half_rows = tok_rows // 2
     hidden_state = hidden_in
     prompt_source = hidden_in[:PROMPT]
     for layer_idx in range(LAYERS):
@@ -197,21 +196,10 @@
             weights[:, feat_width:],
             preferred_element_type=jnp.float32,
         ).astype(jnp.bfloat16)
-        parts = []
-        for row0 in (0, half_rows):
-            attended = attention(
-                queries, band_kv, prompt_kv, first_pos, total_len, row0, half_rows
-            )
-            projection = jnp.dot(
-                attended, w_out[layer_idx], preferred_element_type=jnp.float32
-            )
-            rows_in = hidden_state[row0 : row0 + half_rows].astype(jnp.float32)
-            parts.append((rows_in + projection).astype(jnp.bfloat16))
-        hidden_state = jnp.concatenate(parts, axis=0)
-        if half_rows >= PROMPT:
-            prompt_source = parts[0][:PROMPT]
-        else:
-            prompt_source = hidden_state[:PROMPT]
+        attended = attention(queries, band_kv, prompt_kv, first_pos, total_len, 0, tok_rows)
+        projection = jnp.dot(attended, w_out[layer_idx], preferred_element_type=jnp.float32)
+        hidden_state = (hidden_state.astype(jnp.float32) + projection).astype(jnp.bfloat16)
+        prompt_source = hidden_state[:PROMPT]
     final = layer_norm(hidden_state, final_gain)
     head_out = jnp.dot(final, w_heads, preferred_element_type=jnp.float32)
     logits = head_out[:, :ACTIONS]

time: 134 us -> 128 us (0.955)
  the two profiles are of different devices: /device:TPU:20 before, /device:TPU:0 now
where the time goes in v8:
time: 128 us
  Pallas kernels  37.1 us (29%)
  starting transfers between devices  30.8 us (24%)
  matrix products  20.4 us (16%)
  other arithmetic  15.6 us (12%)
  waiting for transfers between devices  15.6 us (12%)
  local copies, waits for them, and re-layouts  6.55 us (5%)
  between operations  1.72 us (1%)
    pallas_call x2, Pallas kernels, attention(): pl.pallas_call(functools.partial(attention_kernel, row0), out_shape=jax.S...  37.1 us
    ppermute x8, starting transfers between devices, spread(): got = lax.ppermute(block, axis, op)  22.1 us
    ppermute x8, waiting for transfers between devices, spread(): got = lax.ppermute(block, axis, op)  15.6 us
    dot_general x2, matrix products, per_device(): jnp.dot(extended_normed, weights[:, feat_width:], preferred_element_type=...  8.11 us
    squeeze x1, local copies, waits for them, and re-layouts, per_device(): weights = w_qkv[layer_idx]  6.45 us
    ppermute x2, starting transfers between devices, with_halo(): before = lax.ppermute(last, axis, up)  6.11 us
    dot_general x2, matrix products, per_device(): jnp.dot(attended, w_out[layer_idx], preferred_element_type=jnp.float32)  4.68 us
    convert_element_type x2, other arithmetic, layer_norm(): (centred * lax.rsqrt(row_var + 1e-05) * gain_row).astype(jnp.bfloat16)  3.75 us
  transfers between devices with their start and end apart: 12, of which 5 were waited for; matrix products, arithmetic and copies ran while one was open for 20% of the time, Pallas kernels for 0%

profile of v8, /device:TPU:0, one launch (start us, length us, event | category | flops | bytes accessed | tf_op | source)
XLA Modules:
  0.0 127.8 jit_solution(17838432910410468479)
XLA Ops:
  0.7 1.3 broadcast_select_fusion.3
  1.9 1.3 %collective-permute-start.1 = (bf16[256,768]{1,0:T(8,128)(2,1)S(1)}, bf16[256,768]{1,0:T(8,128)(2,1)S(1)}, u32[]{:S(2)}, u32[]{:S(2)}) collective-permute-start(bf16[256,768]{1,0:T(8,128)(2,1)S(1)} %get-tuple-element.18), channel_id=1, source_target_pairs={{1,0},{2,1},{3,2},{4,3},{5,4},{6,5},{7,6},{8,7},{9,8},{10,9},{11,1... | collective-permute-start | bytes 1179656 | tf_op jit(solution)/shard_map/ppermute | solution.py:26
  3.2 3.1 %collective-permute-start = (bf16[256,768]{1,0:T(8,128)(2,1)S(1)}, bf16[256,768]{1,0:T(8,128)(2,1)S(1)}, u32[]{:S(2)}, u32[]{:S(2)}) collective-permute-start(bf16[256,768]{1,0:T(8,128)(2,1)S(1)} %get-tuple-element.17), channel_id=1, source_target_pairs={{0,1},{1,2},{2,3},{3,4},{4,5},{5,6},{6,7},{7,8},{8,9},{9,10},{10,1... | collective-permute-start | bytes 1179656 | tf_op jit(solution)/shard_map/ppermute | solution.py:25
  6.3 7.2 %collective-permute-start.2 = (bf16[256,768]{1,0:T(8,128)(2,1)S(1)}, bf16[256,768]{1,0:T(8,128)(2,1)}, u32[]{:S(2)}, u32[]{:S(2)}) collective-permute-start(bf16[256,768]{1,0:T(8,128)(2,1)S(1)} %get-tuple-element.16), channel_id=1, source_target_pairs={{0,8},{16,24}} | collective-permute-start | bytes 1179656 | tf_op jit(solution)/shard_map/ppermute | solution.py:53
  13.5 6.4 %slice_bitcast_fusion = (bf16[768,2304]{1,0:T(8,128)(2,1)}, bf16[768,2304]{1,0:T(8,128)(2,1)}) fusion(bf16[2,768,2304]{2,1,0:T(8,128)(2,1)} %param.20), kind=kLoop, calls=%fused_computation.10 | loop fusion | bytes 14155776 | tf_op jit(solution)/shard_map/squeeze | solution.py:183
  20.0 0.6 compare_reduce_fusion
  20.6 0.6 compare_reduce_fusion.1
  21.2 0.7 compare_reduce_fusion.2
  21.9 0.6 pad_add_fusion.pos_ref
  22.6 1.3 %collective-permute-start.3 = (bf16[256,768]{1,0:T(8,128)(2,1)S(1)}, bf16[256,768]{1,0:T(8,128)(2,1)S(1)}, u32[]{:S(2)}, u32[]{:S(2)}) collective-permute-start(bf16[256,768]{1,0:T(8,128)(2,1)S(1)} %broadcast_select_fusion.1), channel_id=1, source_target_pairs={{0,4},{8,12},{16,20},{24,28}} | collective-permute-start | bytes 1179656 | tf_op jit(solution)/shard_map/ppermute | solution.py:53
  24.0 0.3 convert_reduce_fusion.1
  24.2 0.6 fusion.7
  24.9 4.3 %collective-permute-done.3 = bf16[256,768]{1,0:T(8,128)(2,1)S(1)} collective-permute-done((bf16[256,768]{1,0:T(8,128)(2,1)S(1)}, bf16[256,768]{1,0:T(8,128)(2,1)S(1)}, u32[]{:S(2)}, u32[]{:S(2)}) %collective-permute-start.3) | collective-permute-done | bytes 393248 | tf_op jit(solution)/shard_map/ppermute | solution.py:53
  29.2 0.6 broadcast_select_fusion.5
  29.8 1.6 %collective-permute-start.4 = (bf16[256,768]{1,0:T(8,128)(2,1)S(1)}, bf16[256,768]{1,0:T(8,128)(2,1)S(1)}, u32[]{:S(2)}, u32[]{:S(2)}) collective-permute-start(bf16[256,768]{1,0:T(8,128)(2,1)S(1)} %broadcast_select_fusion.5), channel_id=1, source_target_pairs={{0,2},{4,6},{8,10},{12,14},{16,18},{20,22},{24,26},{28,30}} | collective-permute-start | bytes 1179656 | tf_op jit(solution)/shard_map/ppermute | solution.py:53
  31.4 1.9 %fusion.9 = bf16[1024,768]{1,0:T(8,128)(2,1)S(1)} fusion(f32[768]{0:T(1024)S(1)} %get-tuple-element.6, f32[1024]{0:T(1024)S(1)} %add_rsqrt_fusion.1, f32[1024]{0:T(1024)S(1)} %broadcast_multiply_fusion.1, bf16[256,768]{1,0:T(8,128)(2,1)S(1)} %collective-permute-done.1, bf16[512,768]{1,0:T(8,128)(2,1)S(1)} %copy-done.1, ...), kind=kLoop, calls=%fused_computation.17 | loop fusion | flops 7864320 | bytes 3156992 | tf_op jit(solution)/shard_map/convert_element_type | solution.py:65
  33.3 3.4 %collective-permute-done.4 = bf16[256,768]{1,0:T(8,128)(2,1)S(1)} collective-permute-done((bf16[256,768]{1,0:T(8,128)(2,1)S(1)}, bf16[256,768]{1,0:T(8,128)(2,1)S(1)}, u32[]{:S(2)}, u32[]{:S(2)}) %collective-permute-start.4) | collective-permute-done | bytes 393248 | tf_op jit(solution)/shard_map/ppermute | solution.py:53
  36.6 0.6 broadcast_select_fusion.7
  37.2 1.5 %collective-permute-start.5 = (bf16[256,768]{1,0:T(8,128)(2,1)S(1)}, bf16[256,768]{1,0:T(8,128)(2,1)S(1)}, u32[]{:S(2)}, u32[]{:S(2)}) collective-permute-start(bf16[256,768]{1,0:T(8,128)(2,1)S(1)} %broadcast_select_fusion.7), channel_id=1, source_target_pairs={{0,1},{2,3},{4,5},{6,7},{8,9},{10,11},{12,13},{14,15},{16,17},{18,... | collective-permute-start | bytes 1179656 | tf_op jit(solution)/shard_map/ppermute | solution.py:53
  38.7 4.1 %convolution_convert_fusion.1.refs_0_.refs_1_.refs_2_ = bf16[1024,1536]{1,0:T(8,128)(2,1)} fusion(bf16[1024,768]{1,0:T(8,128)(2,1)S(1)} %fusion.9, bf16[768,2304]{1,0:T(8,128)(2,1)S(1)} %copy-done.3), kind=kOutput, calls=%fused_computation.5 | convolution fusion | flops 2417491968 | bytes 7077888 | tf_op jit(solution)/shard_map/dot_general | solution.py:187
  42.8 1.7 %multiply_convert_fusion.1.q_ref = bf16[512,768]{1,0:T(8,128)(2,1)} fusion(bf16[768,2304]{1,0:T(8,128)(2,1)S(1)} %copy-done.3, bf16[1024,768]{1,0:T(8,128)(2,1)S(1)} %fusion.9), kind=kOutput, calls=%fused_computation.36 | convolution fusion | flops 604766208 | bytes 2752512 | tf_op jit(solution)/shard_map/dot_general | solution.py:192
  44.5 0.9 convert_reduce_fusion.4
  45.6 1.8 %convolution_convert_fusion.3.refs_3_ = bf16[256,1536]{1,0:T(8,128)(2,1)} fusion(bf16[768,2304]{1,0:T(8,128)(2,1)S(1)} %copy-done.3, bf16[256,768]{1,0:T(8,128)(2,1)S(1)} %get-tuple-element.10, f32[768]{0:T(1024)S(1)} %get-tuple-element.6, f32[256]{0:T(256)S(1)} %add_rsqrt_fusion.4, f32[256]{0:T(256)S(1)} %broadcast_multiply_fusion.4), kind=kOutput, calls=%fused_computation.19 | convolution fusion | flops 605356032 | bytes 3545088 | tf_op jit(solution)/shard_map/dot_general | solution.py:194
  47.4 18.6 %shard_map.185 = bf16[512,768]{1,0:T(8,128)(2,1)} custom-call(s32[2]{0:T(128)} %pad_add_fusion.pos_ref, bf16[512,768]{1,0:T(8,128)(2,1)} %multiply_convert_fusion.1.q_ref, bf16[1024,1536]{1,0:T(8,128)(2,1)} %convolution_convert_fusion.1.refs_0_.refs_1_.refs_2_, bf16[1024,1536]{1,0:T(8,128)(2,1)} %convolution_convert_fusion.1.refs_0_.refs_1_.refs_2_, ...), custom_call_target="tpu_custom_call" | custom-call | flops 6442450944 | bytes 7077888 | tf_op jit(solution)/shard_map/pallas_call | solution.py:142
  66.0 2.3 %add_convert_fusion.1 = bf16[512,768]{1,0:T(8,128)(2,1)S(1)} fusion(bf16[512,768]{1,0:T(8,128)(2,1)S(1)} %copy-done.1, bf16[512,768]{1,0:T(8,128)(2,1)} %shard_map.185, bf16[2,768,768]{2,1,0:T(8,128)(2,1)} %param.21), kind=kOutput, calls=%fused_computation.35 | convolution fusion | flops 605159424 | bytes 3538944 | tf_op jit(solution)/shard_map/dot_general | solution.py:200
  68.4 2.9 %collective-permute-start.8 = (bf16[256,768]{1,0:T(8,128)(2,1)S(1)}, bf16[256,768]{1,0:T(8,128)(2,1)S(1)}, u32[]{:S(2)}, u32[]{:S(2)}) collective-permute-start(bf16[256,768]{1,0:T(8,128)(2,1)S(1)} %get-tuple-element.13), channel_id=1, source_target_pairs={{0,8},{16,24}} | collective-permute-start | bytes 1179656 | tf_op jit(solution)/shard_map/ppermute | solution.py:53
  71.2 1.3 %collective-permute-start.7 = (bf16[256,768]{1,0:T(8,128)(2,1)S(1)}, bf16[256,768]{1,0:T(8,128)(2,1)S(1)}, u32[]{:S(2)}, u32[]{:S(2)}) collective-permute-start(bf16[256,768]{1,0:T(8,128)(2,1)S(1)} %get-tuple-element.14), channel_id=1, source_target_pairs={{1,0},{2,1},{3,2},{4,3},{5,4},{6,5},{7,6},{8,7},{9,8},{10,9},{11,1... | collective-permute-start | bytes 1179656 | tf_op jit(solution)/shard_map/ppermute | solution.py:26
  72.5 3.1 %collective-permute-start.6 = (bf16[256,768]{1,0:T(8,128)(2,1)S(1)}, bf16[256,768]{1,0:T(8,128)(2,1)S(1)}, u32[]{:S(2)}, u32[]{:S(2)}) collective-permute-start(bf16[256,768]{1,0:T(8,128)(2,1)S(1)} %get-tuple-element.15), channel_id=1, source_target_pairs={{0,1},{1,2},{2,3},{3,4},{4,5},{5,6},{6,7},{7,8},{8,9},{9,10},{10,1... | collective-permute-start | bytes 1179656 | tf_op jit(solution)/shard_map/ppermute | solution.py:25
  76.5 2.0 %collective-permute-start.9 = (bf16[256,768]{1,0:T(8,128)(2,1)S(1)}, bf16[256,768]{1,0:T(8,128)(2,1)S(1)}, u32[]{:S(2)}, u32[]{:S(2)}) collective-permute-start(bf16[256,768]{1,0:T(8,128)(2,1)S(1)} %broadcast_select_fusion), channel_id=1, source_target_pairs={{0,4},{8,12},{16,20},{24,28}} | collective-permute-start | bytes 1179656 | tf_op jit(solution)/shard_map/ppermute | solution.py:53
  78.5 0.3 convert_reduce_fusion
  78.8 0.6 fusion.4
  79.5 4.3 %collective-permute-done.9 = bf16[256,768]{1,0:T(8,128)(2,1)S(1)} collective-permute-done((bf16[256,768]{1,0:T(8,128)(2,1)S(1)}, bf16[256,768]{1,0:T(8,128)(2,1)S(1)}, u32[]{:S(2)}, u32[]{:S(2)}) %collective-permute-start.9) | collective-permute-done | bytes 393248 | tf_op jit(solution)/shard_map/ppermute | solution.py:53
  83.8 0.6 broadcast_select_fusion.4
  84.4 4.2 %collective-permute-start.10 = (bf16[256,768]{1,0:T(8,128)(2,1)S(1)}, bf16[256,768]{1,0:T(8,128)(2,1)S(1)}, u32[]{:S(2)}, u32[]{:S(2)}) collective-permute-start(bf16[256,768]{1,0:T(8,128)(2,1)S(1)} %broadcast_select_fusion.4), channel_id=1, source_target_pairs={{0,2},{4,6},{8,10},{12,14},{16,18},{20,22},{24,26},{28,30}} | collective-permute-start | bytes 1179656 | tf_op jit(solution)/shard_map/ppermute | solution.py:53
  88.6 1.9 %fusion.6 = bf16[1024,768]{1,0:T(8,128)(2,1)S(1)} fusion(f32[768]{0:T(1024)S(1)} %get-tuple-element.5, f32[1024]{0:T(1024)S(1)} %add_rsqrt_fusion, f32[1024]{0:T(1024)S(1)} %broadcast_multiply_fusion, bf16[256,768]{1,0:T(8,128)(2,1)S(1)} %collective-permute-done.7, bf16[512,768]{1,0:T(8,128)(2,1)S(1)} %add_convert_fusion.1, ...), kind=kLoop, calls=%fused_computation.14 | loop fusion | flops 7864320 | bytes 3156992 | tf_op jit(solution)/shard_map/convert_element_type | solution.py:65
  90.5 3.4 %collective-permute-done.10 = bf16[256,768]{1,0:T(8,128)(2,1)S(1)} collective-permute-done((bf16[256,768]{1,0:T(8,128)(2,1)S(1)}, bf16[256,768]{1,0:T(8,128)(2,1)S(1)}, u32[]{:S(2)}, u32[]{:S(2)}) %collective-permute-start.10) | collective-permute-done | bytes 393248 | tf_op jit(solution)/shard_map/ppermute | solution.py:53
  93.9 0.6 broadcast_select_fusion.6
  94.5 1.5 %collective-permute-start.11 = (bf16[256,768]{1,0:T(8,128)(2,1)S(1)}, bf16[256,768]{1,0:T(8,128)(2,1)S(1)}, u32[]{:S(2)}, u32[]{:S(2)}) collective-permute-start(bf16[256,768]{1,0:T(8,128)(2,1)S(1)} %broadcast_select_fusion.6), channel_id=1, source_target_pairs={{0,1},{2,3},{4,5},{6,7},{8,9},{10,11},{12,13},{14,15},{16,17},{18,... | collective-permute-start | bytes 1179656 | tf_op jit(solution)/shard_map/ppermute | solution.py:53
  96.0 4.0 %convolution_convert_fusion.refs_0_.refs_1_.refs_2_ = bf16[1024,1536]{1,0:T(8,128)(2,1)} fusion(bf16[1024,768]{1,0:T(8,128)(2,1)S(1)} %fusion.6, bf16[768,2304]{1,0:T(8,128)(2,1)S(1)} %copy-done.2), kind=kOutput, calls=%fused_computation.4 | convolution fusion | flops 2417491968 | bytes 7077888 | tf_op jit(solution)/shard_map/dot_general | solution.py:187
  100.0 1.7 %multiply_convert_fusion.q_ref = bf16[512,768]{1,0:T(8,128)(2,1)} fusion(bf16[768,2304]{1,0:T(8,128)(2,1)S(1)} %copy-done.2, bf16[1024,768]{1,0:T(8,128)(2,1)S(1)} %fusion.6), kind=kOutput, calls=%fused_computation.34 | convolution fusion | flops 604766208 | bytes 2752512 | tf_op jit(solution)/shard_map/dot_general | solution.py:192
  101.7 0.9 convert_reduce_fusion.3
  102.6 0.2 fusion.29
  102.9 1.8 %convolution_convert_fusion.2.refs_3_ = bf16[256,1536]{1,0:T(8,128)(2,1)} fusion(bf16[768,2304]{1,0:T(8,128)(2,1)S(1)} %copy-done.2, bf16[256,768]{1,0:T(8,128)(2,1)S(1)} %get-tuple-element.8, f32[768]{0:T(1024)S(1)} %get-tuple-element.5, f32[256]{0:T(256)S(1)} %add_rsqrt_fusion.3, f32[256]{0:T(256)S(1)} %broadcast_multiply_fusion.3), kind=kOutput, calls=%fused_computation.18 | convolution fusion | flops 605356032 | bytes 3545088 | tf_op jit(solution)/shard_map/dot_general | solution.py:194
  104.6 18.6 %shard_map.186 = bf16[512,768]{1,0:T(8,128)(2,1)} custom-call(s32[2]{0:T(128)} %pad_add_fusion.pos_ref, bf16[512,768]{1,0:T(8,128)(2,1)} %multiply_convert_fusion.q_ref, bf16[1024,1536]{1,0:T(8,128)(2,1)} %convolution_convert_fusion.refs_0_.refs_1_.refs_2_, bf16[1024,1536]{1,0:T(8,128)(2,1)} %convolution_convert_fusion.refs_0_.refs_1_.refs_2_, ...), custom_call_target="tpu_custom_call" | custom-call | flops 6442450944 | bytes 7077888 | tf_op jit(solution)/shard_map/pallas_call | solution.py:142
  123.2 2.4 %convert_reduce_fusion.2 = (f32[512]{0:T(512)S(1)}, bf16[512,768]{1,0:T(8,128)(2,1)S(1)}) fusion(bf16[512,768]{1,0:T(8,128)(2,1)} %shard_map.186, bf16[2,768,768]{2,1,0:T(8,128)(2,1)} %param.21, bf16[512,768]{1,0:T(8,128)(2,1)S(1)} %add_convert_fusion.1), kind=kOutput, calls=%fused_computation.25 | convolution fusion | flops 605945344 | bytes 3540992 | tf_op jit(solution)/shard_map/dot_general | solution.py:200
  125.6 0.4 fusion.16
  126.0 0.8 fusion.35
  127.2 0.6 multiply_add_fusion
  (52 shorter events, 1.3 us)
Async XLA Ops:
  0.6 125.3 %copy-start = (bf16[768,512]{1,0:T(8,128)(2,1)S(1)}, bf16[768,512]{1,0:T(8,128)(2,1)}, u32[]{:S(2)}) copy-start(bf16[768,512]{1,0:T(8,128)(2,1)} %param.23) | copy-start | bytes 2359300
  1.9 22.0 %collective-permute-start.1 = (bf16[256,768]{1,0:T(8,128)(2,1)S(1)}, bf16[256,768]{1,0:T(8,128)(2,1)S(1)}, u32[]{:S(2)}, u32[]{:S(2)}) collective-permute-start(bf16[256,768]{1,0:T(8,128)(2,1)S(1)} %get-tuple-element.18), channel_id=1, source_target_pairs={{1,0},{2,1},{3,2},{4,3},{5,4},{6,5},{7,6},{8,7},{9,8},{10,9},{11,1... | collective-permute-start | bytes 1179656 | tf_op jit(solution)/shard_map/ppermute | solution.py:26
  3.2 20.7 %collective-permute-start = (bf16[256,768]{1,0:T(8,128)(2,1)S(1)}, bf16[256,768]{1,0:T(8,128)(2,1)S(1)}, u32[]{:S(2)}, u32[]{:S(2)}) collective-permute-start(bf16[256,768]{1,0:T(8,128)(2,1)S(1)} %get-tuple-element.17), channel_id=1, source_target_pairs={{0,1},{1,2},{2,3},{3,4},{4,5},{5,6},{6,7},{7,8},{8,9},{9,10},{10,1... | collective-permute-start | bytes 1179656 | tf_op jit(solution)/shard_map/ppermute | solution.py:25
  6.3 13.7 %copy-start.12 = (s32[2]{0:T(128)S(1)}, s32[2]{0:T(128)}, u32[]{:S(2)}) copy-start(s32[2]{0:T(128)} %constant.53.clone) | copy-start | bytes 28
  6.3 14.3 %copy-start.11 = (s32[4]{0:T(128)S(1)}, s32[4]{0:T(128)}, u32[]{:S(2)}) copy-start(s32[4]{0:T(128)} %constant.54.clone) | copy-start | bytes 52
  6.3 14.9 %copy-start.10 = (s32[8]{0:T(128)S(1)}, s32[8]{0:T(128)}, u32[]{:S(2)}) copy-start(s32[8]{0:T(128)} %constant.55.clone) | copy-start | bytes 100
  6.3 16.2 %copy-start.5 = (f32[2,768]{1,0:T(2,128)S(1)}, f32[2,768]{1,0:T(2,128)}, u32[]{:S(2)}) copy-start(f32[2,768]{1,0:T(2,128)} %param.19) | copy-start | bytes 18436
  6.3 17.6 %copy-start.1 = (bf16[512,768]{1,0:T(8,128)(2,1)S(1)}, bf16[512,768]{1,0:T(8,128)(2,1)}, u32[]{:S(2)}) copy-start(bf16[512,768]{1,0:T(8,128)(2,1)} %param.18) | copy-start | bytes 2359300
  6.3 16.2 %collective-permute-start.2 = (bf16[256,768]{1,0:T(8,128)(2,1)S(1)}, bf16[256,768]{1,0:T(8,128)(2,1)}, u32[]{:S(2)}, u32[]{:S(2)}) collective-permute-start(bf16[256,768]{1,0:T(8,128)(2,1)S(1)} %get-tuple-element.16), channel_id=1, source_target_pairs={{0,8},{16,24}} | collective-permute-start | bytes 1179656 | tf_op jit(solution)/shard_map/ppermute | solution.py:53
  22.6 6.6 %collective-permute-start.3 = (bf16[256,768]{1,0:T(8,128)(2,1)S(1)}, bf16[256,768]{1,0:T(8,128)(2,1)S(1)}, u32[]{:S(2)}, u32[]{:S(2)}) collective-permute-start(bf16[256,768]{1,0:T(8,128)(2,1)S(1)} %broadcast_select_fusion.1), channel_id=1, source_target_pairs={{0,4},{8,12},{16,20},{24,28}} | collective-permute-start | bytes 1179656 | tf_op jit(solution)/shard_map/ppermute | solution.py:53
  29.8 8.9 %copy-start.3 = (bf16[768,2304]{1,0:T(8,128)(2,1)S(1)}, bf16[768,2304]{1,0:T(8,128)(2,1)}, u32[]{:S(2)}) copy-start(bf16[768,2304]{1,0:T(8,128)(2,1)} %get-tuple-element.12) | copy-start | bytes 10616836
  29.8 6.8 %collective-permute-start.4 = (bf16[256,768]{1,0:T(8,128)(2,1)S(1)}, bf16[256,768]{1,0:T(8,128)(2,1)S(1)}, u32[]{:S(2)}, u32[]{:S(2)}) collective-permute-start(bf16[256,768]{1,0:T(8,128)(2,1)S(1)} %broadcast_select_fusion.5), channel_id=1, source_target_pairs={{0,2},{4,6},{8,10},{12,14},{16,18},{20,22},{24,26},{28,30}} | collective-permute-start | bytes 1179656 | tf_op jit(solution)/shard_map/ppermute | solution.py:53
  37.2 7.3 %collective-permute-start.5 = (bf16[256,768]{1,0:T(8,128)(2,1)S(1)}, bf16[256,768]{1,0:T(8,128)(2,1)S(1)}, u32[]{:S(2)}, u32[]{:S(2)}) collective-permute-start(bf16[256,768]{1,0:T(8,128)(2,1)S(1)} %broadcast_select_fusion.7), channel_id=1, source_target_pairs={{0,1},{2,3},{4,5},{6,7},{8,9},{10,11},{12,13},{14,15},{16,17},{18,... | collective-permute-start | bytes 1179656 | tf_op jit(solution)/shard_map/ppermute | solution.py:53
  68.4 8.1 %collective-permute-start.8 = (bf16[256,768]{1,0:T(8,128)(2,1)S(1)}, bf16[256,768]{1,0:T(8,128)(2,1)S(1)}, u32[]{:S(2)}, u32[]{:S(2)}) collective-permute-start(bf16[256,768]{1,0:T(8,128)(2,1)S(1)} %get-tuple-element.13), channel_id=1, source_target_pairs={{0,8},{16,24}} | collective-permute-start | bytes 1179656 | tf_op jit(solution)/shard_map/ppermute | solution.py:53
  71.2 7.3 %collective-permute-start.7 = (bf16[256,768]{1,0:T(8,128)(2,1)S(1)}, bf16[256,768]{1,0:T(8,128)(2,1)S(1)}, u32[]{:S(2)}, u32[]{:S(2)}) collective-permute-start(bf16[256,768]{1,0:T(8,128)(2,1)S(1)} %get-tuple-element.14), channel_id=1, source_target_pairs={{1,0},{2,1},{3,2},{4,3},{5,4},{6,5},{7,6},{8,7},{9,8},{10,9},{11,1... | collective-permute-start | bytes 1179656 | tf_op jit(solution)/shard_map/ppermute | solution.py:26
  72.5 6.0 %collective-permute-start.6 = (bf16[256,768]{1,0:T(8,128)(2,1)S(1)}, bf16[256,768]{1,0:T(8,128)(2,1)S(1)}, u32[]{:S(2)}, u32[]{:S(2)}) collective-permute-start(bf16[256,768]{1,0:T(8,128)(2,1)S(1)} %get-tuple-element.15), channel_id=1, source_target_pairs={{0,1},{1,2},{2,3},{3,4},{4,5},{5,6},{6,7},{7,8},{8,9},{9,10},{10,1... | collective-permute-start | bytes 1179656 | tf_op jit(solution)/shard_map/ppermute | solution.py:25
  76.5 7.2 %collective-permute-start.9 = (bf16[256,768]{1,0:T(8,128)(2,1)S(1)}, bf16[256,768]{1,0:T(8,128)(2,1)S(1)}, u32[]{:S(2)}, u32[]{:S(2)}) collective-permute-start(bf16[256,768]{1,0:T(8,128)(2,1)S(1)} %broadcast_select_fusion), channel_id=1, source_target_pairs={{0,4},{8,12},{16,20},{24,28}} | collective-permute-start | bytes 1179656 | tf_op jit(solution)/shard_map/ppermute | solution.py:53
  84.4 11.6 %copy-start.2 = (bf16[768,2304]{1,0:T(8,128)(2,1)S(1)}, bf16[768,2304]{1,0:T(8,128)(2,1)}, u32[]{:S(2)}) copy-start(bf16[768,2304]{1,0:T(8,128)(2,1)} %get-tuple-element.11) | copy-start | bytes 10616836
  84.4 9.5 %collective-permute-start.10 = (bf16[256,768]{1,0:T(8,128)(2,1)S(1)}, bf16[256,768]{1,0:T(8,128)(2,1)S(1)}, u32[]{:S(2)}, u32[]{:S(2)}) collective-permute-start(bf16[256,768]{1,0:T(8,128)(2,1)S(1)} %broadcast_select_fusion.4), channel_id=1, source_target_pairs={{0,2},{4,6},{8,10},{12,14},{16,18},{20,22},{24,26},{28,30}} | collective-permute-start | bytes 1179656 | tf_op jit(solution)/shard_map/ppermute | solution.py:53
  94.5 7.2 %collective-permute-start.11 = (bf16[256,768]{1,0:T(8,128)(2,1)S(1)}, bf16[256,768]{1,0:T(8,128)(2,1)S(1)}, u32[]{:S(2)}, u32[]{:S(2)}) collective-permute-start(bf16[256,768]{1,0:T(8,128)(2,1)S(1)} %broadcast_select_fusion.6), channel_id=1, source_target_pairs={{0,1},{2,3},{4,5},{6,7},{8,9},{10,11},{12,13},{14,15},{16,17},{18,... | collective-permute-start | bytes 1179656 | tf_op jit(solution)/shard_map/ppermute | solution.py:53
  123.2 2.8 %copy-start.9 = (f32[768]{0:T(1024)S(1)}, f32[768]{0:T(1024)}, u32[]{:S(2)}) copy-start(f32[768]{0:T(1024)} %param.22) | copy-start | bytes 9220
  125.6 1.4 %copy-start.6 = (s32[512]{0:T(512)S(1)}, s32[512]{0:T(512)}, u32[]{:S(2)}) copy-start(s32[512]{0:T(512)} %param.24) | copy-start | bytes 6148
  126.0 1.2 copy-start.7
  126.0 1.2 copy-start.8
  127.2 0.6 copy-start.4

commit v9 on v8

--- a/solution.py
+++ b/solution.py
@@ -158,6 +158,36 @@
     )(pos, queries, *([band_kv] * pieces), prompt_kv)
 
 
+PROJ_COLS = 256
+
+
+def projection_kernel(scale, x_ref, w_ref, out_ref):
+    product = jnp.dot(x_ref[...], w_ref[...], preferred_element_type=jnp.float32)
+    if scale != 1.0:
+        product = product * scale
+    out_ref[...] = product.astype(out_ref.dtype)
+
+
+def project(rows, weights, layer, col0, cols, scale):
+    count, depth = rows.shape
+    first_block = col0 // PROJ_COLS
+    return pl.pallas_call(
+        functools.partial(projection_kernel, scale),
+        out_shape=jax.ShapeDtypeStruct((count, cols), jnp.bfloat16),
+        grid=(cols // PROJ_COLS,),
+        in_specs=[
+            pl.BlockSpec((count, depth), lambda j: (0, 0)),
+            pl.BlockSpec((None, depth, PROJ_COLS), lambda j: (layer, 0, j + first_block)),
+        ],
+        out_specs=pl.BlockSpec((count, PROJ_COLS), lambda j: (0, j)),
+        cost_estimate=pl.CostEstimate(
+            flops=2 * count * depth * cols,
+            transcendentals=0,
+            bytes_accessed=2 * (count * depth + depth * cols + count * cols),
+        ),
+    )(rows, weights)
+
+
 def per_device(
     hidden_in,
     ln_gain,
@@ -180,22 +210,15 @@
     prompt_source = hidden_in[:PROMPT]
     for layer_idx in range(LAYERS):
         gain = ln_gain[layer_idx]
-        weights = w_qkv[layer_idx]
         extended = with_halo(hidden_state, (("seq", 0),), HALF)
         prompt_rows = spread(prompt_source, "seq")
         extended_normed = layer_norm(extended, gain)
-        band_kv = jnp.dot(
-            extended_normed, weights[:, feat_width:], preferred_element_type=jnp.float32
-        ).astype(jnp.bfloat16)
+        band_kv = project(extended_normed, w_qkv, layer_idx, feat_width, 2 * feat_width, 1.0)
         normed = extended_normed[HALF : HALF + tok_rows]
-        queries = (
-            jnp.dot(normed, weights[:, :feat_width], preferred_element_type=jnp.float32) * 0.125
-        ).astype(jnp.bfloat16)
-        prompt_kv = jnp.dot(
-            layer_norm(prompt_rows, gain),
-            weights[:, feat_width:],
-            preferred_element_type=jnp.float32,
-        ).astype(jnp.bfloat16)
+        queries = project(normed, w_qkv, layer_idx, 0, feat_width, 0.125)
+        prompt_kv = project(
+            layer_norm(prompt_rows, gain), w_qkv, layer_idx, feat_width, 2 * feat_width, 1.0
+        )
         attended = attention(queries, band_kv, prompt_kv, first_pos, total_len, 0, tok_rows)
         projection = jnp.dot(attended, w_out[layer_idx], preferred_element_type=jnp.float32)
         hidden_state = (hidden_state.astype(jnp.float32) + projection).astype(jnp.bfloat16)

time: 128 us -> 154 us (1.20)
  the two profiles are of different devices: /device:TPU:0 before, /device:TPU:20 now
where the time goes in v9:
time: 154 us; the launch traced here: 152 us
  Pallas kernels  70.1 us (46%)
  waiting for transfers between devices  31.7 us (21%)
  other arithmetic  21.1 us (14%)
  starting transfers between devices  18.2 us (12%)
  matrix products  5.48 us (4%)
  local copies, waits for them, and re-layouts  3.89 us (3%)
  between operations  1.65 us (1%)
    pallas_call x2, Pallas kernels, attention(): pl.pallas_call(functools.partial(attention_kernel, row0), out_shape=jax.S...  37.1 us
    pallas_call x6, Pallas kernels, project(): pl.pallas_call(functools.partial(projection_kernel, scale), out_shape=jax...  33 us
    ppermute x8, waiting for transfers between devices, spread(): got = lax.ppermute(block, axis, op)  21.8 us
    ppermute x8, starting transfers between devices, spread(): got = lax.ppermute(block, axis, op)  9.58 us
    ppermute x2, waiting for transfers between devices, with_halo(): after = lax.ppermute(leading, axis, down)  5.67 us
    convert_element_type x4, other arithmetic, layer_norm(): (centred * lax.rsqrt(row_var + 1e-05) * gain_row).astype(jnp.bfloat16)  5.34 us
    ppermute x2, starting transfers between devices, with_halo(): before = lax.ppermute(last, axis, up)  4.81 us
    dot_general x2, matrix products, per_device(): jnp.dot(attended, w_out[layer_idx], preferred_element_type=jnp.float32)  4.68 us
  transfers between devices with their start and end apart: 12, of which 5 were waited for; matrix products, arithmetic and copies ran while one was open for 8% of the time, Pallas kernels for 15%

profile of v9, /device:TPU:20, one launch (start us, length us, event | category | flops | bytes accessed | tf_op | source)
XLA Modules:
  0.0 152.2 jit_solution(5041517233918720315)
XLA Ops:
  0.7 1.3 broadcast_select_fusion.3
  2.0 1.9 %collective-permute-start.1 = (bf16[256,768]{1,0:T(8,128)(2,1)S(1)}, bf16[256,768]{1,0:T(8,128)(2,1)S(1)}, u32[]{:S(2)}, u32[]{:S(2)}) collective-permute-start(bf16[256,768]{1,0:T(8,128)(2,1)S(1)} %get-tuple-element.16), channel_id=1, source_target_pairs={{1,0},{2,1},{3,2},{4,3},{5,4},{6,5},{7,6},{8,7},{9,8},{10,9},{11,1... | collective-permute-start | bytes 1179656 | tf_op jit(solution)/shard_map/ppermute | solution.py:26
  3.9 2.4 %collective-permute-start = (bf16[256,768]{1,0:T(8,128)(2,1)S(1)}, bf16[256,768]{1,0:T(8,128)(2,1)S(1)}, u32[]{:S(2)}, u32[]{:S(2)}) collective-permute-start(bf16[256,768]{1,0:T(8,128)(2,1)S(1)} %get-tuple-element.15), channel_id=1, source_target_pairs={{0,1},{1,2},{2,3},{3,4},{4,5},{5,6},{6,7},{7,8},{8,9},{9,10},{10,1... | collective-permute-start | bytes 1179656 | tf_op jit(solution)/shard_map/ppermute | solution.py:25
  6.3 1.4 collective-permute-start.2
  7.7 1.3 compare_reduce_fusion
  9.0 1.4 compare_reduce_fusion.1
  10.4 0.8 slice_reduce_fusion.1
  11.2 1.3 compare_reduce_fusion.2
  12.6 0.7 collective-permute-start.3
  13.8 2.3 %collective-permute-done = bf16[256,768]{1,0:T(8,128)(2,1)S(1)} collective-permute-done((bf16[256,768]{1,0:T(8,128)(2,1)S(1)}, bf16[256,768]{1,0:T(8,128)(2,1)S(1)}, u32[]{:S(2)}, u32[]{:S(2)}) %collective-permute-start) | collective-permute-done | bytes 393248 | tf_op jit(solution)/shard_map/ppermute | solution.py:25
  16.5 0.7 broadcast_select_fusion.5
  17.2 1.3 collective-permute-start.4
  18.5 0.6 fusion.7
  19.1 14.1 %collective-permute-done.4 = bf16[256,768]{1,0:T(8,128)(2,1)S(1)} collective-permute-done((bf16[256,768]{1,0:T(8,128)(2,1)S(1)}, bf16[256,768]{1,0:T(8,128)(2,1)S(1)}, u32[]{:S(2)}, u32[]{:S(2)}) %collective-permute-start.4) | collective-permute-done | bytes 393248 | tf_op jit(solution)/shard_map/ppermute | solution.py:53
  33.2 1.4 broadcast_select_fusion.7
  34.6 2.0 %collective-permute-start.5 = (bf16[256,768]{1,0:T(8,128)(2,1)}, bf16[256,768]{1,0:T(8,128)(2,1)}, u32[]{:S(2)}, u32[]{:S(2)}) collective-permute-start(bf16[256,768]{1,0:T(8,128)(2,1)} %broadcast_select_fusion.7), channel_id=1, source_target_pairs={{0,1},{2,3},{4,5},{6,7},{8,9},{10,11},{12,13},{14,15},{16,17},{18,... | collective-permute-start | bytes 1179656 | tf_op jit(solution)/shard_map/ppermute | solution.py:53
  36.7 1.5 fusion.9.x_ref
  38.2 1.0 slice.50.x_ref
  39.2 3.9 %shard_map.185.q_ref = bf16[512,768]{1,0:T(8,128)(2,1)} custom-call(bf16[512,768]{1,0:T(8,128)(2,1)} %slice.50.x_ref, bf16[2,768,2304]{2,1,0:T(8,128)(2,1)} %w_ref.11), custom_call_target="tpu_custom_call" | custom-call | flops 603979776 | bytes 2752512 | tf_op jit(solution)/shard_map/pallas_call | solution.py:174
  43.1 7.2 %shard_map.186.refs_0_.refs_1_.refs_2_ = bf16[1024,1536]{1,0:T(8,128)(2,1)} custom-call(bf16[1024,768]{1,0:T(8,128)(2,1)} %copy-done.2, bf16[2,768,2304]{2,1,0:T(8,128)(2,1)} %w_ref.11), custom_call_target="tpu_custom_call" | custom-call | flops 2415919104 | bytes 7077888 | tf_op jit(solution)/shard_map/pallas_call | solution.py:174
  50.3 1.8 %convert_reduce_fusion.4 = (f32[256]{0:T(256)S(1)}, bf16[256,768]{1,0:T(8,128)(2,1)S(1)}) fusion(bf16[256,768]{1,0:T(8,128)(2,1)} %collective-permute-done.5, bf16[256,768]{1,0:T(8,128)(2,1)} %broadcast_select_fusion.7, pred[]{:T(512)} %compare_reduce_fusion.2), kind=kLoop, calls=%fused_computation.32 | loop fusion | flops 589568 | bytes 1180673 | tf_op jit(solution)/shard_map/reduce_sum | solution.py:62
  52.3 1.0 fusion.28.x_ref
  53.3 5.4 %shard_map.187.refs_3_ = bf16[256,1536]{1,0:T(8,128)(2,1)} custom-call(bf16[256,768]{1,0:T(8,128)(2,1)} %fusion.28.x_ref, bf16[2,768,2304]{2,1,0:T(8,128)(2,1)} %w_ref.11), custom_call_target="tpu_custom_call" | custom-call | flops 603979776 | bytes 3538944 | tf_op jit(solution)/shard_map/pallas_call | solution.py:174
  58.7 18.6 %shard_map.188 = bf16[512,768]{1,0:T(8,128)(2,1)} custom-call(s32[2]{0:T(128)} %pad_add_fusion.pos_ref, bf16[512,768]{1,0:T(8,128)(2,1)} %shard_map.185.q_ref, bf16[1024,1536]{1,0:T(8,128)(2,1)} %shard_map.186.refs_0_.refs_1_.refs_2_, bf16[1024,1536]{1,0:T(8,128)(2,1)} %shard_map.186.refs_0_.refs_1_.refs_2_, ...), custom_call_target="tpu_custom_call" | custom-call | flops 6442450944 | bytes 7077888 | tf_op jit(solution)/shard_map/pallas_call | solution.py:142
  77.3 2.3 %add_convert_fusion.1 = bf16[512,768]{1,0:T(8,128)(2,1)S(1)} fusion(bf16[512,768]{1,0:T(8,128)(2,1)S(1)} %copy-done.1, bf16[512,768]{1,0:T(8,128)(2,1)} %shard_map.188, bf16[2,768,768]{2,1,0:T(8,128)(2,1)} %param.21), kind=kOutput, calls=%fused_computation.24 | convolution fusion | flops 605159424 | bytes 3538944 | tf_op jit(solution)/shard_map/dot_general | solution.py:223
  79.7 0.7 collective-permute-start.8
  80.4 1.9 %collective-permute-start.7 = (bf16[256,768]{1,0:T(8,128)(2,1)S(1)}, bf16[256,768]{1,0:T(8,128)(2,1)S(1)}, u32[]{:S(2)}, u32[]{:S(2)}) collective-permute-start(bf16[256,768]{1,0:T(8,128)(2,1)S(1)} %get-tuple-element.12), channel_id=1, source_target_pairs={{1,0},{2,1},{3,2},{4,3},{5,4},{6,5},{7,6},{8,7},{9,8},{10,9},{11,1... | collective-permute-start | bytes 1179656 | tf_op jit(solution)/shard_map/ppermute | solution.py:26
  82.3 2.4 %collective-permute-start.6 = (bf16[256,768]{1,0:T(8,128)(2,1)S(1)}, bf16[256,768]{1,0:T(8,128)(2,1)S(1)}, u32[]{:S(2)}, u32[]{:S(2)}) collective-permute-start(bf16[256,768]{1,0:T(8,128)(2,1)S(1)} %get-tuple-element.13), channel_id=1, source_target_pairs={{0,1},{1,2},{2,3},{3,4},{4,5},{5,6},{6,7},{7,8},{8,9},{9,10},{10,1... | collective-permute-start | bytes 1179656 | tf_op jit(solution)/shard_map/ppermute | solution.py:25
  84.8 0.7 collective-permute-start.9
  86.1 5.7 %collective-permute-done.7 = bf16[256,768]{1,0:T(8,128)(2,1)S(1)} collective-permute-done((bf16[256,768]{1,0:T(8,128)(2,1)S(1)}, bf16[256,768]{1,0:T(8,128)(2,1)S(1)}, u32[]{:S(2)}, u32[]{:S(2)}) %collective-permute-start.7) | collective-permute-done | bytes 393248 | tf_op jit(solution)/shard_map/ppermute | solution.py:26
  91.8 1.9 %collective-permute-done.6 = bf16[256,768]{1,0:T(8,128)(2,1)S(1)} collective-permute-done((bf16[256,768]{1,0:T(8,128)(2,1)S(1)}, bf16[256,768]{1,0:T(8,128)(2,1)S(1)}, u32[]{:S(2)}, u32[]{:S(2)}) %collective-permute-start.6) | collective-permute-done | bytes 393248 | tf_op jit(solution)/shard_map/ppermute | solution.py:25
  94.0 0.7 broadcast_select_fusion.4
  94.7 1.3 collective-permute-start.10
  96.0 0.6 fusion.4
  96.6 7.7 %collective-permute-done.10 = bf16[256,768]{1,0:T(8,128)(2,1)S(1)} collective-permute-done((bf16[256,768]{1,0:T(8,128)(2,1)S(1)}, bf16[256,768]{1,0:T(8,128)(2,1)S(1)}, u32[]{:S(2)}, u32[]{:S(2)}) %collective-permute-start.10) | collective-permute-done | bytes 393248 | tf_op jit(solution)/shard_map/ppermute | solution.py:53
  104.4 0.7 broadcast_select_fusion.6
  105.0 1.5 collective-permute-start.11
  106.5 1.9 %fusion.6.x_ref = bf16[1024,768]{1,0:T(8,128)(2,1)S(1)} fusion(f32[768]{0:T(1024)S(1)} %get-tuple-element.5, f32[1024]{0:T(1024)S(1)} %add_rsqrt_fusion, f32[1024]{0:T(1024)S(1)} %broadcast_multiply_fusion, bf16[256,768]{1,0:T(8,128)(2,1)S(1)} %collective-permute-done.7, bf16[512,768]{1,0:T(8,128)(2,1)S(1)} %add_convert_fusion.1, ...), kind=kLoop, calls=%fused_computation.10 | loop fusion | flops 7864320 | bytes 3156992 | tf_op jit(solution)/shard_map/convert_element_type | solution.py:65
  108.4 1.1 copy-done.3
  109.6 0.9 slice.53.x_ref
  110.5 3.9 %shard_map.189.q_ref = bf16[512,768]{1,0:T(8,128)(2,1)} custom-call(bf16[512,768]{1,0:T(8,128)(2,1)} %slice.53.x_ref, bf16[2,768,2304]{2,1,0:T(8,128)(2,1)} %w_ref.11), custom_call_target="tpu_custom_call" | custom-call | flops 603979776 | bytes 2752512 | tf_op jit(solution)/shard_map/pallas_call | solution.py:174
  114.3 7.2 %shard_map.190.refs_0_.refs_1_.refs_2_ = bf16[1024,1536]{1,0:T(8,128)(2,1)} custom-call(bf16[1024,768]{1,0:T(8,128)(2,1)} %copy-done.3, bf16[2,768,2304]{2,1,0:T(8,128)(2,1)} %w_ref.11), custom_call_target="tpu_custom_call" | custom-call | flops 2415919104 | bytes 7077888 | tf_op jit(solution)/shard_map/pallas_call | solution.py:174
  121.6 0.8 convert_reduce_fusion.3
  122.6 1.0 fusion.25.x_ref
  123.6 5.4 %shard_map.191.refs_3_ = bf16[256,1536]{1,0:T(8,128)(2,1)} custom-call(bf16[256,768]{1,0:T(8,128)(2,1)} %fusion.25.x_ref, bf16[2,768,2304]{2,1,0:T(8,128)(2,1)} %w_ref.11), custom_call_target="tpu_custom_call" | custom-call | flops 603979776 | bytes 3538944 | tf_op jit(solution)/shard_map/pallas_call | solution.py:174
  129.0 18.6 %shard_map.192 = bf16[512,768]{1,0:T(8,128)(2,1)} custom-call(s32[2]{0:T(128)} %pad_add_fusion.pos_ref, bf16[512,768]{1,0:T(8,128)(2,1)} %shard_map.189.q_ref, bf16[1024,1536]{1,0:T(8,128)(2,1)} %shard_map.190.refs_0_.refs_1_.refs_2_, bf16[1024,1536]{1,0:T(8,128)(2,1)} %shard_map.190.refs_0_.refs_1_.refs_2_, ...), custom_call_target="tpu_custom_call" | custom-call | flops 6442450944 | bytes 7077888 | tf_op jit(solution)/shard_map/pallas_call | solution.py:142
  147.5 2.4 %convert_reduce_fusion.2 = (f32[512]{0:T(512)S(1)}, bf16[512,768]{1,0:T(8,128)(2,1)S(1)}) fusion(bf16[512,768]{1,0:T(8,128)(2,1)} %shard_map.192, bf16[2,768,768]{2,1,0:T(8,128)(2,1)} %param.21, bf16[512,768]{1,0:T(8,128)(2,1)S(1)} %add_convert_fusion.1), kind=kOutput, calls=%fused_computation.15 | convolution fusion | flops 605945344 | bytes 3540992 | tf_op jit(solution)/shard_map/dot_general | solution.py:223
  150.4 0.8 fusion.29
  (49 shorter events, 3.3 us)
Async XLA Ops:
  0.6 149.7 %copy-start = (bf16[768,512]{1,0:T(8,128)(2,1)S(1)}, bf16[768,512]{1,0:T(8,128)(2,1)}, u32[]{:S(2)}) copy-start(bf16[768,512]{1,0:T(8,128)(2,1)} %param.23) | copy-start | bytes 2359300
  0.6 15.6 %copy-start.1 = (bf16[512,768]{1,0:T(8,128)(2,1)S(1)}, bf16[512,768]{1,0:T(8,128)(2,1)}, u32[]{:S(2)}) copy-start(bf16[512,768]{1,0:T(8,128)(2,1)} %param.18) | copy-start | bytes 2359300
  2.0 11.9 %collective-permute-start.1 = (bf16[256,768]{1,0:T(8,128)(2,1)S(1)}, bf16[256,768]{1,0:T(8,128)(2,1)S(1)}, u32[]{:S(2)}, u32[]{:S(2)}) collective-permute-start(bf16[256,768]{1,0:T(8,128)(2,1)S(1)} %get-tuple-element.16), channel_id=1, source_target_pairs={{1,0},{2,1},{3,2},{4,3},{5,4},{6,5},{7,6},{8,7},{9,8},{10,9},{11,1... | collective-permute-start | bytes 1179656 | tf_op jit(solution)/shard_map/ppermute | solution.py:26
  3.9 12.3 %collective-permute-start = (bf16[256,768]{1,0:T(8,128)(2,1)S(1)}, bf16[256,768]{1,0:T(8,128)(2,1)S(1)}, u32[]{:S(2)}, u32[]{:S(2)}) collective-permute-start(bf16[256,768]{1,0:T(8,128)(2,1)S(1)} %get-tuple-element.15), channel_id=1, source_target_pairs={{0,1},{1,2},{2,3},{3,4},{4,5},{5,6},{6,7},{7,8},{8,9},{9,10},{10,1... | collective-permute-start | bytes 1179656 | tf_op jit(solution)/shard_map/ppermute | solution.py:25
  6.3 6.2 %collective-permute-start.2 = (bf16[256,768]{1,0:T(8,128)(2,1)S(1)}, bf16[256,768]{1,0:T(8,128)(2,1)}, u32[]{:S(2)}, u32[]{:S(2)}) collective-permute-start(bf16[256,768]{1,0:T(8,128)(2,1)S(1)} %get-tuple-element.14), channel_id=1, source_target_pairs={{0,8},{16,24}} | collective-permute-start | bytes 1179656 | tf_op jit(solution)/shard_map/ppermute | solution.py:53
  12.6 3.9 %collective-permute-start.3 = (bf16[256,768]{1,0:T(8,128)(2,1)S(1)}, bf16[256,768]{1,0:T(8,128)(2,1)S(1)}, u32[]{:S(2)}, u32[]{:S(2)}) collective-permute-start(bf16[256,768]{1,0:T(8,128)(2,1)S(1)} %broadcast_select_fusion.1), channel_id=1, source_target_pairs={{0,4},{8,12},{16,20},{24,28}} | collective-permute-start | bytes 1179656 | tf_op jit(solution)/shard_map/ppermute | solution.py:53
  16.2 20.5 %copy-start.4 = (bf16[256,768]{1,0:T(8,128)(2,1)}, bf16[256,768]{1,0:T(8,128)(2,1)S(1)}, u32[]{:S(2)}) copy-start(bf16[256,768]{1,0:T(8,128)(2,1)S(1)} %collective-permute-done) | copy-start | bytes 1179652
  17.2 16.0 %collective-permute-start.4 = (bf16[256,768]{1,0:T(8,128)(2,1)S(1)}, bf16[256,768]{1,0:T(8,128)(2,1)S(1)}, u32[]{:S(2)}, u32[]{:S(2)}) collective-permute-start(bf16[256,768]{1,0:T(8,128)(2,1)S(1)} %broadcast_select_fusion.5), channel_id=1, source_target_pairs={{0,2},{4,6},{8,10},{12,14},{16,18},{20,22},{24,26},{28,30}} | collective-permute-start | bytes 1179656 | tf_op jit(solution)/shard_map/ppermute | solution.py:53
  34.6 15.7 %collective-permute-start.5 = (bf16[256,768]{1,0:T(8,128)(2,1)}, bf16[256,768]{1,0:T(8,128)(2,1)}, u32[]{:S(2)}, u32[]{:S(2)}) collective-permute-start(bf16[256,768]{1,0:T(8,128)(2,1)} %broadcast_select_fusion.7), channel_id=1, source_target_pairs={{0,1},{2,3},{4,5},{6,7},{8,9},{10,11},{12,13},{14,15},{16,17},{18,... | collective-permute-start | bytes 1179656 | tf_op jit(solution)/shard_map/ppermute | solution.py:53
  38.2 4.9 %copy-start.2 = (bf16[1024,768]{1,0:T(8,128)(2,1)}, bf16[1024,768]{1,0:T(8,128)(2,1)S(1)}, u32[]{:S(2)}) copy-start(bf16[1024,768]{1,0:T(8,128)(2,1)S(1)} %fusion.9.x_ref) | copy-start | bytes 4718596
  79.7 5.0 %collective-permute-start.8 = (bf16[256,768]{1,0:T(8,128)(2,1)S(1)}, bf16[256,768]{1,0:T(8,128)(2,1)S(1)}, u32[]{:S(2)}, u32[]{:S(2)}) collective-permute-start(bf16[256,768]{1,0:T(8,128)(2,1)S(1)} %get-tuple-element.11), channel_id=1, source_target_pairs={{0,8},{16,24}} | collective-permute-start | bytes 1179656 | tf_op jit(solution)/shard_map/ppermute | solution.py:53
  80.4 11.4 %collective-permute-start.7 = (bf16[256,768]{1,0:T(8,128)(2,1)S(1)}, bf16[256,768]{1,0:T(8,128)(2,1)S(1)}, u32[]{:S(2)}, u32[]{:S(2)}) collective-permute-start(bf16[256,768]{1,0:T(8,128)(2,1)S(1)} %get-tuple-element.12), channel_id=1, source_target_pairs={{1,0},{2,1},{3,2},{4,3},{5,4},{6,5},{7,6},{8,7},{9,8},{10,9},{11,1... | collective-permute-start | bytes 1179656 | tf_op jit(solution)/shard_map/ppermute | solution.py:26
  82.3 11.4 %collective-permute-start.6 = (bf16[256,768]{1,0:T(8,128)(2,1)S(1)}, bf16[256,768]{1,0:T(8,128)(2,1)S(1)}, u32[]{:S(2)}, u32[]{:S(2)}) collective-permute-start(bf16[256,768]{1,0:T(8,128)(2,1)S(1)} %get-tuple-element.13), channel_id=1, source_target_pairs={{0,1},{1,2},{2,3},{3,4},{4,5},{5,6},{6,7},{7,8},{8,9},{9,10},{10,1... | collective-permute-start | bytes 1179656 | tf_op jit(solution)/shard_map/ppermute | solution.py:25
  84.8 9.2 %collective-permute-start.9 = (bf16[256,768]{1,0:T(8,128)(2,1)S(1)}, bf16[256,768]{1,0:T(8,128)(2,1)S(1)}, u32[]{:S(2)}, u32[]{:S(2)}) collective-permute-start(bf16[256,768]{1,0:T(8,128)(2,1)S(1)} %broadcast_select_fusion), channel_id=1, source_target_pairs={{0,4},{8,12},{16,20},{24,28}} | collective-permute-start | bytes 1179656 | tf_op jit(solution)/shard_map/ppermute | solution.py:53
  94.7 9.7 %collective-permute-start.10 = (bf16[256,768]{1,0:T(8,128)(2,1)S(1)}, bf16[256,768]{1,0:T(8,128)(2,1)S(1)}, u32[]{:S(2)}, u32[]{:S(2)}) collective-permute-start(bf16[256,768]{1,0:T(8,128)(2,1)S(1)} %broadcast_select_fusion.4), channel_id=1, source_target_pairs={{0,2},{4,6},{8,10},{12,14},{16,18},{20,22},{24,26},{28,30}} | collective-permute-start | bytes 1179656 | tf_op jit(solution)/shard_map/ppermute | solution.py:53
  105.0 16.5 %collective-permute-start.11 = (bf16[256,768]{1,0:T(8,128)(2,1)S(1)}, bf16[256,768]{1,0:T(8,128)(2,1)S(1)}, u32[]{:S(2)}, u32[]{:S(2)}) collective-permute-start(bf16[256,768]{1,0:T(8,128)(2,1)S(1)} %broadcast_select_fusion.6), channel_id=1, source_target_pairs={{0,1},{2,3},{4,5},{6,7},{8,9},{10,11},{12,13},{14,15},{16,17},{18,... | collective-permute-start | bytes 1179656 | tf_op jit(solution)/shard_map/ppermute | solution.py:53
  108.4 1.1 copy-start.3
  147.5 2.8 %copy-start.9 = (f32[768]{0:T(1024)S(1)}, f32[768]{0:T(1024)}, u32[]{:S(2)}) copy-start(f32[768]{0:T(1024)} %param.22) | copy-start | bytes 9220
  149.9 1.4 copy-start.6
  149.9 1.6 %copy-start.7 = (f32[512]{0:T(512)S(1)}, f32[512]{0:T(512)}, u32[]{:S(2)}) copy-start(f32[512]{0:T(512)} %param.26) | copy-start | bytes 6148
  149.9 1.6 %copy-start.8 = (s32[512]{0:T(512)S(1)}, s32[512]{0:T(512)}, u32[]{:S(2)}) copy-start(s32[512]{0:T(512)} %param.25) | copy-start | bytes 6148
  151.6 0.6 copy-start.5

commit v10 on v8

--- a/solution.py
+++ b/solution.py
@@ -79,8 +79,7 @@
     block = pl.program_id(0)
     first = pos_ref[0]
     total = pos_ref[1]
-    row_in_tile = lax.broadcasted_iota(jnp.int32, (GROUP * tile, 1), 0) % tile
-    query_pos = first + row0 + block * tile + row_in_tile
+    query_pos = first + row0 + block * tile + lax.broadcasted_iota(jnp.int32, (tile, 1), 0)
     key_pos = first + row0 + block * tile - HALF + lax.broadcasted_iota(jnp.int32, (1, width), 1)
     gap = key_pos - query_pos
     band_ok = (gap >= -HALF) & (gap <= HALF) & (key_pos >= 0) & (key_pos < total)
@@ -100,27 +99,27 @@
         )
         band_scores = lax.dot_general(
             stacked, band_keys, contract, preferred_element_type=jnp.float32
-        )
+        ).reshape(GROUP, tile, width)
         prompt_scores = lax.dot_general(
             stacked, prompt_ref[:, cols], contract, preferred_element_type=jnp.float32
-        )
-        band_scores = jnp.where(band_ok, band_scores, -1e30)
-        prompt_scores = jnp.where(prompt_ok, prompt_scores, -1e30)
+        ).reshape(GROUP, tile, PROMPT)
+        band_scores = jnp.where(band_ok[None], band_scores, -1e30)
+        prompt_scores = jnp.where(prompt_ok[None], prompt_scores, -1e30)
         row_max = jnp.maximum(
-            jnp.max(band_scores, axis=1, keepdims=True),
-            jnp.max(prompt_scores, axis=1, keepdims=True),
+            jnp.max(band_scores, axis=2, keepdims=True),
+            jnp.max(prompt_scores, axis=2, keepdims=True),
         )
         band_exp = jnp.exp(band_scores - row_max)
         prompt_exp = jnp.exp(prompt_scores - row_max)
-        denom = jnp.sum(band_exp, axis=1, keepdims=True) + jnp.sum(
-            prompt_exp, axis=1, keepdims=True
-        )
-        scale = 1.0 / denom
-        band_probs = (band_exp * scale).astype(jnp.bfloat16)
-        prompt_probs = (prompt_exp * scale).astype(jnp.bfloat16)
+        denom = jnp.sum(band_exp, axis=2, keepdims=True) + jnp.sum(
+            prompt_exp, axis=2, keepdims=True
+        )
+        band_probs = band_exp.astype(jnp.bfloat16).reshape(GROUP * tile, width)
+        prompt_probs = prompt_exp.astype(jnp.bfloat16).reshape(GROUP * tile, PROMPT)
         mixed = jnp.dot(band_probs, band_values, preferred_element_type=jnp.float32) + jnp.dot(
             prompt_probs, prompt_ref[:, vcols], preferred_element_type=jnp.float32
         )
+        mixed = mixed * (1.0 / denom.reshape(GROUP * tile, 1))
         attn = mixed[:tile]
         for j in range(1, GROUP):
             attn = jnp.where(lane_head == j, mixed[j * tile : (j + 1) * tile], attn)

time: 128 us -> 122 us (0.953)
  Pallas kernels: 37.1 us -> 31.3 us
    pallas_call x2, Pallas kernels: 37.1 us -> 31.3 us  [attention(): pl.pallas_call(functools.partial(attention_kernel, row0), out_shape=jax.S...]
  transfers between devices with their start and end apart: 12 -> 12, of which waited for: 5 -> 5; matrix products, arithmetic and copies ran while one was open for 20% -> 21% of each run, Pallas kernels for 0% -> 0%
where the time goes in v10:
time: 122 us
  Pallas kernels  31.3 us (26%)
  starting transfers between devices  30.8 us (25%)
  matrix products  20.4 us (17%)
  other arithmetic  15.6 us (13%)
  waiting for transfers between devices  15.6 us (13%)
  local copies, waits for them, and re-layouts  6.55 us (5%)
  between operations  1.72 us (1%)
    pallas_call x2, Pallas kernels, attention(): pl.pallas_call(functools.partial(attention_kernel, row0), out_shape=jax.S...  31.3 us
    ppermute x8, starting transfers between devices, spread(): got = lax.ppermute(block, axis, op)  22.1 us
    ppermute x8, waiting for transfers between devices, spread(): got = lax.ppermute(block, axis, op)  15.6 us
    dot_general x2, matrix products, per_device(): jnp.dot(extended_normed, weights[:, feat_width:], preferred_element_type=...  8.1 us
    squeeze x1, local copies, waits for them, and re-layouts, per_device(): weights = w_qkv[layer_idx]  6.45 us
    ppermute x2, starting transfers between devices, with_halo(): before = lax.ppermute(last, axis, up)  6.11 us
    dot_general x2, matrix products, per_device(): jnp.dot(attended, w_out[layer_idx], preferred_element_type=jnp.float32)  4.68 us
    convert_element_type x2, other arithmetic, layer_norm(): (centred * lax.rsqrt(row_var + 1e-05) * gain_row).astype(jnp.bfloat16)  3.75 us
  transfers between devices with their start and end apart: 12, of which 5 were waited for; matrix products, arithmetic and copies ran while one was open for 21% of the time, Pallas kernels for 0%

profile of v10, /device:TPU:0, one launch (start us, length us, event | category | flops | bytes accessed | tf_op | source)
XLA Modules:
  0.0 122.0 jit_solution(10708899824933495381)
XLA Ops:
  0.7 1.3 %broadcast_select_fusion.3 = (bf16[256,768]{1,0:T(8,128)(2,1)S(1)}, bf16[256,768]{1,0:T(8,128)(2,1)S(1)}, bf16[256,768]{1,0:T(8,128)(2,1)S(1)}) fusion(pred[]{:T(512)S(6)} %eq.68, bf16[512,768]{1,0:T(8,128)(2,1)} %param.18), kind=kLoop, calls=%fused_computation.80 | loop fusion | flops 196608 | bytes 1966081 | tf_op jit(solution)/shard_map/jit(_where)/select_n | solution.py:49
  1.9 1.3 %collective-permute-start.1 = (bf16[256,768]{1,0:T(8,128)(2,1)S(1)}, bf16[256,768]{1,0:T(8,128)(2,1)S(1)}, u32[]{:S(2)}, u32[]{:S(2)}) collective-permute-start(bf16[256,768]{1,0:T(8,128)(2,1)S(1)} %get-tuple-element.18), channel_id=1, source_target_pairs={{1,0},{2,1},{3,2},{4,3},{5,4},{6,5},{7,6},{8,7},{9,8},{10,9},{11,1... | collective-permute-start | bytes 1179656 | tf_op jit(solution)/shard_map/ppermute | solution.py:26
  3.2 3.1 %collective-permute-start = (bf16[256,768]{1,0:T(8,128)(2,1)S(1)}, bf16[256,768]{1,0:T(8,128)(2,1)S(1)}, u32[]{:S(2)}, u32[]{:S(2)}) collective-permute-start(bf16[256,768]{1,0:T(8,128)(2,1)S(1)} %get-tuple-element.17), channel_id=1, source_target_pairs={{0,1},{1,2},{2,3},{3,4},{4,5},{5,6},{6,7},{7,8},{8,9},{9,10},{10,1... | collective-permute-start | bytes 1179656 | tf_op jit(solution)/shard_map/ppermute | solution.py:25
  6.3 7.2 %collective-permute-start.2 = (bf16[256,768]{1,0:T(8,128)(2,1)S(1)}, bf16[256,768]{1,0:T(8,128)(2,1)}, u32[]{:S(2)}, u32[]{:S(2)}) collective-permute-start(bf16[256,768]{1,0:T(8,128)(2,1)S(1)} %get-tuple-element.16), channel_id=1, source_target_pairs={{0,8},{16,24}} | collective-permute-start | bytes 1179656 | tf_op jit(solution)/shard_map/ppermute | solution.py:53
  13.5 6.4 %slice_bitcast_fusion = (bf16[768,2304]{1,0:T(8,128)(2,1)}, bf16[768,2304]{1,0:T(8,128)(2,1)}) fusion(bf16[2,768,2304]{2,1,0:T(8,128)(2,1)} %param.20), kind=kLoop, calls=%fused_computation.10 | loop fusion | bytes 14155776 | tf_op jit(solution)/shard_map/squeeze | solution.py:182
  20.0 0.6 compare_reduce_fusion
  20.6 0.6 compare_reduce_fusion.1
  21.2 0.7 compare_reduce_fusion.2
  21.9 0.6 pad_add_fusion.pos_ref
  22.6 1.3 %collective-permute-start.3 = (bf16[256,768]{1,0:T(8,128)(2,1)S(1)}, bf16[256,768]{1,0:T(8,128)(2,1)S(1)}, u32[]{:S(2)}, u32[]{:S(2)}) collective-permute-start(bf16[256,768]{1,0:T(8,128)(2,1)S(1)} %broadcast_select_fusion.1), channel_id=1, source_target_pairs={{0,4},{8,12},{16,20},{24,28}} | collective-permute-start | bytes 1179656 | tf_op jit(solution)/shard_map/ppermute | solution.py:53
  24.0 0.3 convert_reduce_fusion.1
  24.2 0.6 fusion.7
  24.9 4.3 %collective-permute-done.3 = bf16[256,768]{1,0:T(8,128)(2,1)S(1)} collective-permute-done((bf16[256,768]{1,0:T(8,128)(2,1)S(1)}, bf16[256,768]{1,0:T(8,128)(2,1)S(1)}, u32[]{:S(2)}, u32[]{:S(2)}) %collective-permute-start.3) | collective-permute-done | bytes 393248 | tf_op jit(solution)/shard_map/ppermute | solution.py:53
  29.2 0.6 broadcast_select_fusion.5
  29.8 1.6 %collective-permute-start.4 = (bf16[256,768]{1,0:T(8,128)(2,1)S(1)}, bf16[256,768]{1,0:T(8,128)(2,1)S(1)}, u32[]{:S(2)}, u32[]{:S(2)}) collective-permute-start(bf16[256,768]{1,0:T(8,128)(2,1)S(1)} %broadcast_select_fusion.5), channel_id=1, source_target_pairs={{0,2},{4,6},{8,10},{12,14},{16,18},{20,22},{24,26},{28,30}} | collective-permute-start | bytes 1179656 | tf_op jit(solution)/shard_map/ppermute | solution.py:53
  31.4 1.9 %fusion.9 = bf16[1024,768]{1,0:T(8,128)(2,1)S(1)} fusion(f32[768]{0:T(1024)S(1)} %get-tuple-element.6, f32[1024]{0:T(1024)S(1)} %add_rsqrt_fusion.1, f32[1024]{0:T(1024)S(1)} %broadcast_multiply_fusion.1, bf16[256,768]{1,0:T(8,128)(2,1)S(1)} %collective-permute-done.1, bf16[512,768]{1,0:T(8,128)(2,1)S(1)} %copy-done.1, ...), kind=kLoop, calls=%fused_computation.17 | loop fusion | flops 7864320 | bytes 3156992 | tf_op jit(solution)/shard_map/convert_element_type | solution.py:65
  33.3 3.4 %collective-permute-done.4 = bf16[256,768]{1,0:T(8,128)(2,1)S(1)} collective-permute-done((bf16[256,768]{1,0:T(8,128)(2,1)S(1)}, bf16[256,768]{1,0:T(8,128)(2,1)S(1)}, u32[]{:S(2)}, u32[]{:S(2)}) %collective-permute-start.4) | collective-permute-done | bytes 393248 | tf_op jit(solution)/shard_map/ppermute | solution.py:53
  36.6 0.6 broadcast_select_fusion.7
  37.2 1.5 %collective-permute-start.5 = (bf16[256,768]{1,0:T(8,128)(2,1)S(1)}, bf16[256,768]{1,0:T(8,128)(2,1)S(1)}, u32[]{:S(2)}, u32[]{:S(2)}) collective-permute-start(bf16[256,768]{1,0:T(8,128)(2,1)S(1)} %broadcast_select_fusion.7), channel_id=1, source_target_pairs={{0,1},{2,3},{4,5},{6,7},{8,9},{10,11},{12,13},{14,15},{16,17},{18,... | collective-permute-start | bytes 1179656 | tf_op jit(solution)/shard_map/ppermute | solution.py:53
  38.7 4.1 %convolution_convert_fusion.1.refs_0_.refs_1_.refs_2_ = bf16[1024,1536]{1,0:T(8,128)(2,1)} fusion(bf16[1024,768]{1,0:T(8,128)(2,1)S(1)} %fusion.9, bf16[768,2304]{1,0:T(8,128)(2,1)S(1)} %copy-done.3), kind=kOutput, calls=%fused_computation.5 | convolution fusion | flops 2417491968 | bytes 7077888 | tf_op jit(solution)/shard_map/dot_general | solution.py:186
  42.8 1.7 %multiply_convert_fusion.1.q_ref = bf16[512,768]{1,0:T(8,128)(2,1)} fusion(bf16[768,2304]{1,0:T(8,128)(2,1)S(1)} %copy-done.3, bf16[1024,768]{1,0:T(8,128)(2,1)S(1)} %fusion.9), kind=kOutput, calls=%fused_computation.36 | convolution fusion | flops 604766208 | bytes 2752512 | tf_op jit(solution)/shard_map/dot_general | solution.py:191
  44.5 0.9 convert_reduce_fusion.4
  45.6 1.8 %convolution_convert_fusion.3.refs_3_ = bf16[256,1536]{1,0:T(8,128)(2,1)} fusion(bf16[768,2304]{1,0:T(8,128)(2,1)S(1)} %copy-done.3, bf16[256,768]{1,0:T(8,128)(2,1)S(1)} %get-tuple-element.10, f32[768]{0:T(1024)S(1)} %get-tuple-element.6, f32[256]{0:T(256)S(1)} %add_rsqrt_fusion.4, f32[256]{0:T(256)S(1)} %broadcast_multiply_fusion.4), kind=kOutput, calls=%fused_computation.19 | convolution fusion | flops 605356032 | bytes 3545088 | tf_op jit(solution)/shard_map/dot_general | solution.py:193
  47.4 15.6 %shard_map.185 = bf16[512,768]{1,0:T(8,128)(2,1)} custom-call(s32[2]{0:T(128)} %pad_add_fusion.pos_ref, bf16[512,768]{1,0:T(8,128)(2,1)} %multiply_convert_fusion.1.q_ref, bf16[1024,1536]{1,0:T(8,128)(2,1)} %convolution_convert_fusion.1.refs_0_.refs_1_.refs_2_, bf16[1024,1536]{1,0:T(8,128)(2,1)} %convolution_convert_fusion.1.refs_0_.refs_1_.refs_2_, ...), custom_call_target="tpu_custom_call" | custom-call | flops 6442450944 | bytes 7077888 | tf_op jit(solution)/shard_map/pallas_call | solution.py:141
  63.0 2.3 %add_convert_fusion.1 = bf16[512,768]{1,0:T(8,128)(2,1)S(1)} fusion(bf16[512,768]{1,0:T(8,128)(2,1)S(1)} %copy-done.1, bf16[512,768]{1,0:T(8,128)(2,1)} %shard_map.185, bf16[2,768,768]{2,1,0:T(8,128)(2,1)} %param.21), kind=kOutput, calls=%fused_computation.35 | convolution fusion | flops 605159424 | bytes 3538944 | tf_op jit(solution)/shard_map/dot_general | solution.py:199
  65.4 2.9 %collective-permute-start.8 = (bf16[256,768]{1,0:T(8,128)(2,1)S(1)}, bf16[256,768]{1,0:T(8,128)(2,1)S(1)}, u32[]{:S(2)}, u32[]{:S(2)}) collective-permute-start(bf16[256,768]{1,0:T(8,128)(2,1)S(1)} %get-tuple-element.13), channel_id=1, source_target_pairs={{0,8},{16,24}} | collective-permute-start | bytes 1179656 | tf_op jit(solution)/shard_map/ppermute | solution.py:53
  68.3 1.3 %collective-permute-start.7 = (bf16[256,768]{1,0:T(8,128)(2,1)S(1)}, bf16[256,768]{1,0:T(8,128)(2,1)S(1)}, u32[]{:S(2)}, u32[]{:S(2)}) collective-permute-start(bf16[256,768]{1,0:T(8,128)(2,1)S(1)} %get-tuple-element.14), channel_id=1, source_target_pairs={{1,0},{2,1},{3,2},{4,3},{5,4},{6,5},{7,6},{8,7},{9,8},{10,9},{11,1... | collective-permute-start | bytes 1179656 | tf_op jit(solution)/shard_map/ppermute | solution.py:26
  69.6 3.1 %collective-permute-start.6 = (bf16[256,768]{1,0:T(8,128)(2,1)S(1)}, bf16[256,768]{1,0:T(8,128)(2,1)S(1)}, u32[]{:S(2)}, u32[]{:S(2)}) collective-permute-start(bf16[256,768]{1,0:T(8,128)(2,1)S(1)} %get-tuple-element.15), channel_id=1, source_target_pairs={{0,1},{1,2},{2,3},{3,4},{4,5},{5,6},{6,7},{7,8},{8,9},{9,10},{10,1... | collective-permute-start | bytes 1179656 | tf_op jit(solution)/shard_map/ppermute | solution.py:25
  73.6 2.0 %collective-permute-start.9 = (bf16[256,768]{1,0:T(8,128)(2,1)S(1)}, bf16[256,768]{1,0:T(8,128)(2,1)S(1)}, u32[]{:S(2)}, u32[]{:S(2)}) collective-permute-start(bf16[256,768]{1,0:T(8,128)(2,1)S(1)} %broadcast_select_fusion), channel_id=1, source_target_pairs={{0,4},{8,12},{16,20},{24,28}} | collective-permute-start | bytes 1179656 | tf_op jit(solution)/shard_map/ppermute | solution.py:53
  75.6 0.3 convert_reduce_fusion
  75.9 0.6 fusion.4
  76.5 4.3 %collective-permute-done.9 = bf16[256,768]{1,0:T(8,128)(2,1)S(1)} collective-permute-done((bf16[256,768]{1,0:T(8,128)(2,1)S(1)}, bf16[256,768]{1,0:T(8,128)(2,1)S(1)}, u32[]{:S(2)}, u32[]{:S(2)}) %collective-permute-start.9) | collective-permute-done | bytes 393248 | tf_op jit(solution)/shard_map/ppermute | solution.py:53
  80.9 0.6 broadcast_select_fusion.4
  81.5 4.2 %collective-permute-start.10 = (bf16[256,768]{1,0:T(8,128)(2,1)S(1)}, bf16[256,768]{1,0:T(8,128)(2,1)S(1)}, u32[]{:S(2)}, u32[]{:S(2)}) collective-permute-start(bf16[256,768]{1,0:T(8,128)(2,1)S(1)} %broadcast_select_fusion.4), channel_id=1, source_target_pairs={{0,2},{4,6},{8,10},{12,14},{16,18},{20,22},{24,26},{28,30}} | collective-permute-start | bytes 1179656 | tf_op jit(solution)/shard_map/ppermute | solution.py:53
  85.7 1.9 %fusion.6 = bf16[1024,768]{1,0:T(8,128)(2,1)S(1)} fusion(f32[768]{0:T(1024)S(1)} %get-tuple-element.5, f32[1024]{0:T(1024)S(1)} %add_rsqrt_fusion, f32[1024]{0:T(1024)S(1)} %broadcast_multiply_fusion, bf16[256,768]{1,0:T(8,128)(2,1)S(1)} %collective-permute-done.7, bf16[512,768]{1,0:T(8,128)(2,1)S(1)} %add_convert_fusion.1, ...), kind=kLoop, calls=%fused_computation.14 | loop fusion | flops 7864320 | bytes 3156992 | tf_op jit(solution)/shard_map/convert_element_type | solution.py:65
  87.6 3.4 %collective-permute-done.10 = bf16[256,768]{1,0:T(8,128)(2,1)S(1)} collective-permute-done((bf16[256,768]{1,0:T(8,128)(2,1)S(1)}, bf16[256,768]{1,0:T(8,128)(2,1)S(1)}, u32[]{:S(2)}, u32[]{:S(2)}) %collective-permute-start.10) | collective-permute-done | bytes 393248 | tf_op jit(solution)/shard_map/ppermute | solution.py:53
  90.9 0.6 broadcast_select_fusion.6
  91.5 1.5 %collective-permute-start.11 = (bf16[256,768]{1,0:T(8,128)(2,1)S(1)}, bf16[256,768]{1,0:T(8,128)(2,1)S(1)}, u32[]{:S(2)}, u32[]{:S(2)}) collective-permute-start(bf16[256,768]{1,0:T(8,128)(2,1)S(1)} %broadcast_select_fusion.6), channel_id=1, source_target_pairs={{0,1},{2,3},{4,5},{6,7},{8,9},{10,11},{12,13},{14,15},{16,17},{18,... | collective-permute-start | bytes 1179656 | tf_op jit(solution)/shard_map/ppermute | solution.py:53
  93.1 4.0 %convolution_convert_fusion.refs_0_.refs_1_.refs_2_ = bf16[1024,1536]{1,0:T(8,128)(2,1)} fusion(bf16[1024,768]{1,0:T(8,128)(2,1)S(1)} %fusion.6, bf16[768,2304]{1,0:T(8,128)(2,1)S(1)} %copy-done.2), kind=kOutput, calls=%fused_computation.4 | convolution fusion | flops 2417491968 | bytes 7077888 | tf_op jit(solution)/shard_map/dot_general | solution.py:186
  97.1 1.7 %multiply_convert_fusion.q_ref = bf16[512,768]{1,0:T(8,128)(2,1)} fusion(bf16[768,2304]{1,0:T(8,128)(2,1)S(1)} %copy-done.2, bf16[1024,768]{1,0:T(8,128)(2,1)S(1)} %fusion.6), kind=kOutput, calls=%fused_computation.34 | convolution fusion | flops 604766208 | bytes 2752512 | tf_op jit(solution)/shard_map/dot_general | solution.py:191
  98.8 0.9 convert_reduce_fusion.3
  99.7 0.2 fusion.29
  99.9 1.8 %convolution_convert_fusion.2.refs_3_ = bf16[256,1536]{1,0:T(8,128)(2,1)} fusion(bf16[768,2304]{1,0:T(8,128)(2,1)S(1)} %copy-done.2, bf16[256,768]{1,0:T(8,128)(2,1)S(1)} %get-tuple-element.8, f32[768]{0:T(1024)S(1)} %get-tuple-element.5, f32[256]{0:T(256)S(1)} %add_rsqrt_fusion.3, f32[256]{0:T(256)S(1)} %broadcast_multiply_fusion.3), kind=kOutput, calls=%fused_computation.18 | convolution fusion | flops 605356032 | bytes 3545088 | tf_op jit(solution)/shard_map/dot_general | solution.py:193
  101.7 15.6 %shard_map.186 = bf16[512,768]{1,0:T(8,128)(2,1)} custom-call(s32[2]{0:T(128)} %pad_add_fusion.pos_ref, bf16[512,768]{1,0:T(8,128)(2,1)} %multiply_convert_fusion.q_ref, bf16[1024,1536]{1,0:T(8,128)(2,1)} %convolution_convert_fusion.refs_0_.refs_1_.refs_2_, bf16[1024,1536]{1,0:T(8,128)(2,1)} %convolution_convert_fusion.refs_0_.refs_1_.refs_2_, ...), custom_call_target="tpu_custom_call" | custom-call | flops 6442450944 | bytes 7077888 | tf_op jit(solution)/shard_map/pallas_call | solution.py:141
  117.3 2.4 %convert_reduce_fusion.2 = (f32[512]{0:T(512)S(1)}, bf16[512,768]{1,0:T(8,128)(2,1)S(1)}) fusion(bf16[512,768]{1,0:T(8,128)(2,1)} %shard_map.186, bf16[2,768,768]{2,1,0:T(8,128)(2,1)} %param.21, bf16[512,768]{1,0:T(8,128)(2,1)S(1)} %add_convert_fusion.1), kind=kOutput, calls=%fused_computation.25 | convolution fusion | flops 605945344 | bytes 3540992 | tf_op jit(solution)/shard_map/dot_general | solution.py:199
  119.7 0.4 fusion.16
  120.1 0.8 fusion.35
  121.4 0.6 multiply_add_fusion
  (52 shorter events, 1.3 us)
Async XLA Ops:
  0.6 119.5 %copy-start = (bf16[768,512]{1,0:T(8,128)(2,1)S(1)}, bf16[768,512]{1,0:T(8,128)(2,1)}, u32[]{:S(2)}) copy-start(bf16[768,512]{1,0:T(8,128)(2,1)} %param.23) | copy-start | bytes 2359300
  1.9 22.0 %collective-permute-start.1 = (bf16[256,768]{1,0:T(8,128)(2,1)S(1)}, bf16[256,768]{1,0:T(8,128)(2,1)S(1)}, u32[]{:S(2)}, u32[]{:S(2)}) collective-permute-start(bf16[256,768]{1,0:T(8,128)(2,1)S(1)} %get-tuple-element.18), channel_id=1, source_target_pairs={{1,0},{2,1},{3,2},{4,3},{5,4},{6,5},{7,6},{8,7},{9,8},{10,9},{11,1... | collective-permute-start | bytes 1179656 | tf_op jit(solution)/shard_map/ppermute | solution.py:26
  3.2 20.7 %collective-permute-start = (bf16[256,768]{1,0:T(8,128)(2,1)S(1)}, bf16[256,768]{1,0:T(8,128)(2,1)S(1)}, u32[]{:S(2)}, u32[]{:S(2)}) collective-permute-start(bf16[256,768]{1,0:T(8,128)(2,1)S(1)} %get-tuple-element.17), channel_id=1, source_target_pairs={{0,1},{1,2},{2,3},{3,4},{4,5},{5,6},{6,7},{7,8},{8,9},{9,10},{10,1... | collective-permute-start | bytes 1179656 | tf_op jit(solution)/shard_map/ppermute | solution.py:25
  6.3 13.7 %copy-start.12 = (s32[2]{0:T(128)S(1)}, s32[2]{0:T(128)}, u32[]{:S(2)}) copy-start(s32[2]{0:T(128)} %constant.53.clone) | copy-start | bytes 28
  6.3 14.3 %copy-start.11 = (s32[4]{0:T(128)S(1)}, s32[4]{0:T(128)}, u32[]{:S(2)}) copy-start(s32[4]{0:T(128)} %constant.54.clone) | copy-start | bytes 52
  6.3 14.9 %copy-start.10 = (s32[8]{0:T(128)S(1)}, s32[8]{0:T(128)}, u32[]{:S(2)}) copy-start(s32[8]{0:T(128)} %constant.55.clone) | copy-start | bytes 100
  6.3 16.2 %copy-start.5 = (f32[2,768]{1,0:T(2,128)S(1)}, f32[2,768]{1,0:T(2,128)}, u32[]{:S(2)}) copy-start(f32[2,768]{1,0:T(2,128)} %param.19) | copy-start | bytes 18436
  6.3 17.6 %copy-start.1 = (bf16[512,768]{1,0:T(8,128)(2,1)S(1)}, bf16[512,768]{1,0:T(8,128)(2,1)}, u32[]{:S(2)}) copy-start(bf16[512,768]{1,0:T(8,128)(2,1)} %param.18) | copy-start | bytes 2359300
  6.3 16.2 %collective-permute-start.2 = (bf16[256,768]{1,0:T(8,128)(2,1)S(1)}, bf16[256,768]{1,0:T(8,128)(2,1)}, u32[]{:S(2)}, u32[]{:S(2)}) collective-permute-start(bf16[256,768]{1,0:T(8,128)(2,1)S(1)} %get-tuple-element.16), channel_id=1, source_target_pairs={{0,8},{16,24}} | collective-permute-start | bytes 1179656 | tf_op jit(solution)/shard_map/ppermute | solution.py:53
  22.6 6.6 %collective-permute-start.3 = (bf16[256,768]{1,0:T(8,128)(2,1)S(1)}, bf16[256,768]{1,0:T(8,128)(2,1)S(1)}, u32[]{:S(2)}, u32[]{:S(2)}) collective-permute-start(bf16[256,768]{1,0:T(8,128)(2,1)S(1)} %broadcast_select_fusion.1), channel_id=1, source_target_pairs={{0,4},{8,12},{16,20},{24,28}} | collective-permute-start | bytes 1179656 | tf_op jit(solution)/shard_map/ppermute | solution.py:53
  29.8 8.9 %copy-start.3 = (bf16[768,2304]{1,0:T(8,128)(2,1)S(1)}, bf16[768,2304]{1,0:T(8,128)(2,1)}, u32[]{:S(2)}) copy-start(bf16[768,2304]{1,0:T(8,128)(2,1)} %get-tuple-element.12) | copy-start | bytes 10616836
  29.8 6.8 %collective-permute-start.4 = (bf16[256,768]{1,0:T(8,128)(2,1)S(1)}, bf16[256,768]{1,0:T(8,128)(2,1)S(1)}, u32[]{:S(2)}, u32[]{:S(2)}) collective-permute-start(bf16[256,768]{1,0:T(8,128)(2,1)S(1)} %broadcast_select_fusion.5), channel_id=1, source_target_pairs={{0,2},{4,6},{8,10},{12,14},{16,18},{20,22},{24,26},{28,30}} | collective-permute-start | bytes 1179656 | tf_op jit(solution)/shard_map/ppermute | solution.py:53
  37.2 7.3 %collective-permute-start.5 = (bf16[256,768]{1,0:T(8,128)(2,1)S(1)}, bf16[256,768]{1,0:T(8,128)(2,1)S(1)}, u32[]{:S(2)}, u32[]{:S(2)}) collective-permute-start(bf16[256,768]{1,0:T(8,128)(2,1)S(1)} %broadcast_select_fusion.7), channel_id=1, source_target_pairs={{0,1},{2,3},{4,5},{6,7},{8,9},{10,11},{12,13},{14,15},{16,17},{18,... | collective-permute-start | bytes 1179656 | tf_op jit(solution)/shard_map/ppermute | solution.py:53
  65.4 8.1 %collective-permute-start.8 = (bf16[256,768]{1,0:T(8,128)(2,1)S(1)}, bf16[256,768]{1,0:T(8,128)(2,1)S(1)}, u32[]{:S(2)}, u32[]{:S(2)}) collective-permute-start(bf16[256,768]{1,0:T(8,128)(2,1)S(1)} %get-tuple-element.13), channel_id=1, source_target_pairs={{0,8},{16,24}} | collective-permute-start | bytes 1179656 | tf_op jit(solution)/shard_map/ppermute | solution.py:53
  68.3 7.3 %collective-permute-start.7 = (bf16[256,768]{1,0:T(8,128)(2,1)S(1)}, bf16[256,768]{1,0:T(8,128)(2,1)S(1)}, u32[]{:S(2)}, u32[]{:S(2)}) collective-permute-start(bf16[256,768]{1,0:T(8,128)(2,1)S(1)} %get-tuple-element.14), channel_id=1, source_target_pairs={{1,0},{2,1},{3,2},{4,3},{5,4},{6,5},{7,6},{8,7},{9,8},{10,9},{11,1... | collective-permute-start | bytes 1179656 | tf_op jit(solution)/shard_map/ppermute | solution.py:26
  69.6 6.0 %collective-permute-start.6 = (bf16[256,768]{1,0:T(8,128)(2,1)S(1)}, bf16[256,768]{1,0:T(8,128)(2,1)S(1)}, u32[]{:S(2)}, u32[]{:S(2)}) collective-permute-start(bf16[256,768]{1,0:T(8,128)(2,1)S(1)} %get-tuple-element.15), channel_id=1, source_target_pairs={{0,1},{1,2},{2,3},{3,4},{4,5},{5,6},{6,7},{7,8},{8,9},{9,10},{10,1... | collective-permute-start | bytes 1179656 | tf_op jit(solution)/shard_map/ppermute | solution.py:25
  73.6 7.2 %collective-permute-start.9 = (bf16[256,768]{1,0:T(8,128)(2,1)S(1)}, bf16[256,768]{1,0:T(8,128)(2,1)S(1)}, u32[]{:S(2)}, u32[]{:S(2)}) collective-permute-start(bf16[256,768]{1,0:T(8,128)(2,1)S(1)} %broadcast_select_fusion), channel_id=1, source_target_pairs={{0,4},{8,12},{16,20},{24,28}} | collective-permute-start | bytes 1179656 | tf_op jit(solution)/shard_map/ppermute | solution.py:53
  81.5 11.6 %copy-start.2 = (bf16[768,2304]{1,0:T(8,128)(2,1)S(1)}, bf16[768,2304]{1,0:T(8,128)(2,1)}, u32[]{:S(2)}) copy-start(bf16[768,2304]{1,0:T(8,128)(2,1)} %get-tuple-element.11) | copy-start | bytes 10616836
  81.5 9.5 %collective-permute-start.10 = (bf16[256,768]{1,0:T(8,128)(2,1)S(1)}, bf16[256,768]{1,0:T(8,128)(2,1)S(1)}, u32[]{:S(2)}, u32[]{:S(2)}) collective-permute-start(bf16[256,768]{1,0:T(8,128)(2,1)S(1)} %broadcast_select_fusion.4), channel_id=1, source_target_pairs={{0,2},{4,6},{8,10},{12,14},{16,18},{20,22},{24,26},{28,30}} | collective-permute-start | bytes 1179656 | tf_op jit(solution)/shard_map/ppermute | solution.py:53
  91.5 7.2 %collective-permute-start.11 = (bf16[256,768]{1,0:T(8,128)(2,1)S(1)}, bf16[256,768]{1,0:T(8,128)(2,1)S(1)}, u32[]{:S(2)}, u32[]{:S(2)}) collective-permute-start(bf16[256,768]{1,0:T(8,128)(2,1)S(1)} %broadcast_select_fusion.6), channel_id=1, source_target_pairs={{0,1},{2,3},{4,5},{6,7},{8,9},{10,11},{12,13},{14,15},{16,17},{18,... | collective-permute-start | bytes 1179656 | tf_op jit(solution)/shard_map/ppermute | solution.py:53
  117.3 2.8 %copy-start.9 = (f32[768]{0:T(1024)S(1)}, f32[768]{0:T(1024)}, u32[]{:S(2)}) copy-start(f32[768]{0:T(1024)} %param.22) | copy-start | bytes 9220
  119.7 1.4 %copy-start.6 = (s32[512]{0:T(512)S(1)}, s32[512]{0:T(512)}, u32[]{:S(2)}) copy-start(s32[512]{0:T(512)} %param.24) | copy-start | bytes 6148
  120.1 1.2 %copy-start.7 = (f32[512]{0:T(512)S(1)}, f32[512]{0:T(512)}, u32[]{:S(2)}) copy-start(f32[512]{0:T(512)} %param.26) | copy-start | bytes 6148
  120.1 1.2 copy-start.8
  121.3 0.6 copy-start.4

commit v11 on v10

--- a/solution.py
+++ b/solution.py
@@ -195,10 +195,21 @@
             weights[:, feat_width:],
             preferred_element_type=jnp.float32,
         ).astype(jnp.bfloat16)
+        if layer_idx + 1 < LAYERS and PROMPT + HALF <= tok_rows:
+            early = attention(
+                queries, band_kv, band_kv[HALF : HALF + PROMPT], first_pos, total_len, 0, PROMPT
+            )
+            early_proj = jnp.dot(early, w_out[layer_idx], preferred_element_type=jnp.float32)
+            early_rows = (hidden_state[:PROMPT].astype(jnp.float32) + early_proj).astype(
+                jnp.bfloat16
+            )
         attended = attention(queries, band_kv, prompt_kv, first_pos, total_len, 0, tok_rows)
         projection = jnp.dot(attended, w_out[layer_idx], preferred_element_type=jnp.float32)
         hidden_state = (hidden_state.astype(jnp.float32) + projection).astype(jnp.bfloat16)
-        prompt_source = hidden_state[:PROMPT]
+        if layer_idx + 1 < LAYERS and PROMPT + HALF <= tok_rows:
+            prompt_source = early_rows
+        else:
+            prompt_source = hidden_state[:PROMPT]
     final = layer_norm(hidden_state, final_gain)
     head_out = jnp.dot(final, w_heads, preferred_element_type=jnp.float32)
     logits = head_out[:, :ACTIONS]

time: 122 us -> 128 us (1.049)
  the two profiles are of different devices: /device:TPU:0 before, /device:TPU:21 now
where the time goes in v11:
time: 128 us
  Pallas kernels  40.6 us (32%)
  starting transfers between devices  25.1 us (20%)
  matrix products  21.4 us (17%)
  other arithmetic  16.6 us (13%)
  waiting for transfers between devices  14.5 us (11%)
  local copies, waits for them, and re-layouts  7.57 us (6%)
  between operations  1.78 us (1%)
    pallas_call x3, Pallas kernels, attention(): pl.pallas_call(functools.partial(attention_kernel, row0), out_shape=jax.S...  40.6 us
    ppermute x2, starting transfers between devices, with_halo(): before = lax.ppermute(last, axis, up)  14.1 us
    ppermute x8, waiting for transfers between devices, spread(): got = lax.ppermute(block, axis, op)  9.09 us
    ppermute x8, starting transfers between devices, spread(): got = lax.ppermute(block, axis, op)  7.14 us
    dot_general x2, matrix products, per_device(): jnp.dot(extended_normed, weights[:, feat_width:], preferred_element_type=...  6.86 us
    squeeze x1, local copies, waits for them, and re-layouts, per_device(): weights = w_qkv[layer_idx]  6.45 us
    ppermute x2, waiting for transfers between devices, with_halo(): after = lax.ppermute(leading, axis, down)  5.3 us
    dot_general x2, matrix products, per_device(): jnp.dot(attended, w_out[layer_idx], preferred_element_type=jnp.float32)  4.68 us
  transfers between devices with their start and end apart: 12, of which 3 were waited for; matrix products, arithmetic and copies ran while one was open for 28% of the time, Pallas kernels for 20%

profile of v11, /device:TPU:21, one launch (start us, length us, event | category | flops | bytes accessed | tf_op | source)
XLA Modules:
  0.0 127.6 jit_solution(9895177791527699240)
XLA Ops:
  0.7 2.0 %broadcast_select_fusion.2 = (bf16[256,768]{1,0:T(8,128)(2,1)S(1)}, bf16[256,768]{1,0:T(8,128)(2,1)}, bf16[256,768]{1,0:T(8,128)(2,1)S(1)}) fusion(pred[]{:T(512)S(6)} %eq.68, bf16[512,768]{1,0:T(8,128)(2,1)} %param.18), kind=kLoop, calls=%fused_computation.84 | loop fusion | flops 196608 | bytes 1966081 | tf_op jit(solution)/shard_map/jit(_where)/select_n | solution.py:49
  2.7 3.7 %collective-permute-start = (bf16[256,768]{1,0:T(8,128)(2,1)}, bf16[256,768]{1,0:T(8,128)(2,1)S(1)}, u32[]{:S(2)}, u32[]{:S(2)}) collective-permute-start(bf16[256,768]{1,0:T(8,128)(2,1)} %get-tuple-element.16), channel_id=1, source_target_pairs={{0,1},{1,2},{2,3},{3,4},{4,5},{5,6},{6,7},{7,8},{8,9},{9,10},{10,1... | collective-permute-start | bytes 1179656 | tf_op jit(solution)/shard_map/ppermute | solution.py:25
  6.4 1.9 %collective-permute-start.1 = (bf16[256,768]{1,0:T(8,128)(2,1)S(1)}, bf16[256,768]{1,0:T(8,128)(2,1)S(1)}, u32[]{:S(2)}, u32[]{:S(2)}) collective-permute-start(bf16[256,768]{1,0:T(8,128)(2,1)S(1)} %get-tuple-element.17), channel_id=1, source_target_pairs={{1,0},{2,1},{3,2},{4,3},{5,4},{6,5},{7,6},{8,7},{9,8},{10,9},{11,1... | collective-permute-start | bytes 1179656 | tf_op jit(solution)/shard_map/ppermute | solution.py:26
  8.3 0.8 collective-permute-start.2
  9.2 6.5 %slice_bitcast_fusion = (bf16[768,2304]{1,0:T(8,128)(2,1)}, bf16[768,2304]{1,0:T(8,128)(2,1)}) fusion(bf16[2,768,2304]{2,1,0:T(8,128)(2,1)} %param.20), kind=kLoop, calls=%fused_computation.10 | loop fusion | bytes 14155776 | tf_op jit(solution)/shard_map/squeeze | solution.py:182
  15.6 0.6 pad_add_fusion.pos_ref
  16.2 0.6 compare_reduce_fusion
  16.9 0.3 convert_reduce_fusion.1
  17.2 0.6 fusion.7
  17.8 1.9 %fusion.9 = bf16[1024,768]{1,0:T(8,128)(2,1)S(1)} fusion(f32[768]{0:T(1024)S(1)} %get-tuple-element.6, f32[1024]{0:T(1024)S(1)} %add_rsqrt_fusion.1, f32[1024]{0:T(1024)S(1)} %broadcast_multiply_fusion.1, bf16[256,768]{1,0:T(8,128)(2,1)S(1)} %collective-permute-done.1, bf16[512,768]{1,0:T(8,128)(2,1)S(1)} %copy-done.1, ...), kind=kLoop, calls=%fused_computation.17 | loop fusion | flops 7864320 | bytes 3156992 | tf_op jit(solution)/shard_map/convert_element_type | solution.py:65
  19.7 2.8 %convolution_convert_fusion.1.refs_0_.refs_1_.refs_2_ = bf16[1024,1536]{1,0:T(8,128)(2,1)S(1)} fusion(bf16[1024,768]{1,0:T(8,128)(2,1)S(1)} %fusion.9, bf16[768,2304]{1,0:T(8,128)(2,1)S(1)} %copy-done.3), kind=kOutput, calls=%fused_computation.5 | convolution fusion | flops 2417491968 | bytes 7077888 | tf_op jit(solution)/shard_map/dot_general | solution.py:186
  22.6 2.0 %multiply_convert_fusion.1.q_ref = bf16[512,768]{1,0:T(8,128)(2,1)} fusion(bf16[768,2304]{1,0:T(8,128)(2,1)S(1)} %copy-done.3, bf16[1024,768]{1,0:T(8,128)(2,1)S(1)} %fusion.9), kind=kOutput, calls=%fused_computation.36 | convolution fusion | flops 604766208 | bytes 2752512 | tf_op jit(solution)/shard_map/dot_general | solution.py:191
  24.6 0.7 collective-permute-start.3
  25.3 1.0 slice.89.refs_3_
  26.3 9.3 %shard_map.186 = bf16[256,768]{1,0:T(8,128)(2,1)} custom-call(s32[2]{0:T(128)} %pad_add_fusion.pos_ref, bf16[512,768]{1,0:T(8,128)(2,1)} %multiply_convert_fusion.1.q_ref, bf16[1024,1536]{1,0:T(8,128)(2,1)} %copy-done.5, bf16[1024,1536]{1,0:T(8,128)(2,1)} %copy-done.5, bf16[1024,1536]{1,0:T(8,128)(2,1)} %copy-done.5, bf16[256,1536]{1,0:T(8,128)(2,1)} %slice.89.refs_3_), custom_call_target="tpu_custom_call" | custom-call | flops 3221225472 | bytes 3932160 | tf_op jit(solution)/shard_map/pallas_call | solution.py:141
  35.6 1.9 %fusion.20 = bf16[256,768]{1,0:T(8,128)(2,1)S(1)} fusion(bf16[256,768]{1,0:T(8,128)(2,1)} %shard_map.186, bf16[2,768,768]{2,1,0:T(8,128)(2,1)} %param.21, pred[]{:T(512)S(6)} %eq.68, bf16[512,768]{1,0:T(8,128)(2,1)S(1)} %copy-done.1), kind=kOutput, calls=%fused_computation.39 | convolution fusion | flops 302776320 | bytes 2359297 | tf_op jit(solution)/shard_map/dot_general | solution.py:202
  37.5 0.7 collective-permute-start.8
  38.2 0.7 broadcast_select_fusion.4
  38.9 0.7 collective-permute-start.4
  39.6 0.6 compare_reduce_fusion.1
  40.3 0.8 collective-permute-start.9
  41.2 0.8 broadcast_select_fusion.6
  42.0 1.5 %collective-permute-start.5 = (bf16[256,768]{1,0:T(8,128)(2,1)S(1)}, bf16[256,768]{1,0:T(8,128)(2,1)S(1)}, u32[]{:S(2)}, u32[]{:S(2)}) collective-permute-start(bf16[256,768]{1,0:T(8,128)(2,1)S(1)} %broadcast_select_fusion.6), channel_id=1, source_target_pairs={{0,1},{2,3},{4,5},{6,7},{8,9},{10,11},{12,13},{14,15},{16,17},{18,... | collective-permute-start | bytes 1179656 | tf_op jit(solution)/shard_map/ppermute | solution.py:53
  43.5 0.6 compare_reduce_fusion.2
  44.1 0.7 broadcast_select_fusion.3
  44.8 0.7 collective-permute-start.10
  45.5 9.1 %collective-permute-done.5 = bf16[256,768]{1,0:T(8,128)(2,1)S(1)} collective-permute-done((bf16[256,768]{1,0:T(8,128)(2,1)S(1)}, bf16[256,768]{1,0:T(8,128)(2,1)S(1)}, u32[]{:S(2)}, u32[]{:S(2)}) %collective-permute-start.5) | collective-permute-done | bytes 393248 | tf_op jit(solution)/shard_map/ppermute | solution.py:53
  54.6 0.7 convert_reduce_fusion.4
  55.6 1.7 %convolution_convert_fusion.3.refs_3_ = bf16[256,1536]{1,0:T(8,128)(2,1)} fusion(bf16[768,2304]{1,0:T(8,128)(2,1)S(1)} %copy-done.4, bf16[256,768]{1,0:T(8,128)(2,1)S(1)} %get-tuple-element.10, f32[768]{0:T(1024)S(1)} %get-tuple-element.6, f32[256]{0:T(256)S(1)} %add_rsqrt_fusion.4, f32[256]{0:T(256)S(1)} %broadcast_multiply_fusion.4), kind=kOutput, calls=%fused_computation.19 | convolution fusion | flops 605356032 | bytes 3545088 | tf_op jit(solution)/shard_map/dot_general | solution.py:193
  57.3 15.6 %shard_map.185 = bf16[512,768]{1,0:T(8,128)(2,1)} custom-call(s32[2]{0:T(128)} %pad_add_fusion.pos_ref, bf16[512,768]{1,0:T(8,128)(2,1)} %multiply_convert_fusion.1.q_ref, bf16[1024,1536]{1,0:T(8,128)(2,1)} %copy-done.5, bf16[1024,1536]{1,0:T(8,128)(2,1)} %copy-done.5, bf16[1024,1536]{1,0:T(8,128)(2,1)} %copy-done.5, ...), custom_call_target="tpu_custom_call" | custom-call | flops 6442450944 | bytes 7077888 | tf_op jit(solution)/shard_map/pallas_call | solution.py:141
  73.0 2.3 %add_convert_fusion.1 = bf16[512,768]{1,0:T(8,128)(2,1)S(1)} fusion(bf16[512,768]{1,0:T(8,128)(2,1)S(1)} %copy-done.1, bf16[512,768]{1,0:T(8,128)(2,1)} %shard_map.185, bf16[2,768,768]{2,1,0:T(8,128)(2,1)} %param.21), kind=kOutput, calls=%fused_computation.35 | convolution fusion | flops 605159424 | bytes 3538944 | tf_op jit(solution)/shard_map/dot_general | solution.py:207
  75.3 10.5 %collective-permute-start.6 = (bf16[256,768]{1,0:T(8,128)(2,1)S(1)}, bf16[256,768]{1,0:T(8,128)(2,1)S(1)}, u32[]{:S(2)}, u32[]{:S(2)}) collective-permute-start(bf16[256,768]{1,0:T(8,128)(2,1)S(1)} %get-tuple-element.13), channel_id=1, source_target_pairs={{0,1},{1,2},{2,3},{3,4},{4,5},{5,6},{6,7},{7,8},{8,9},{9,10},{10,1... | collective-permute-start | bytes 1179656 | tf_op jit(solution)/shard_map/ppermute | solution.py:25
  85.8 1.9 %collective-permute-start.7 = (bf16[256,768]{1,0:T(8,128)(2,1)S(1)}, bf16[256,768]{1,0:T(8,128)(2,1)S(1)}, u32[]{:S(2)}, u32[]{:S(2)}) collective-permute-start(bf16[256,768]{1,0:T(8,128)(2,1)S(1)} %get-tuple-element.14), channel_id=1, source_target_pairs={{1,0},{2,1},{3,2},{4,3},{5,4},{6,5},{7,6},{8,7},{9,8},{10,9},{11,1... | collective-permute-start | bytes 1179656 | tf_op jit(solution)/shard_map/ppermute | solution.py:26
  88.4 0.7 broadcast_select_fusion.5
  89.0 1.3 %collective-permute-start.11 = (bf16[256,768]{1,0:T(8,128)(2,1)S(1)}, bf16[256,768]{1,0:T(8,128)(2,1)S(1)}, u32[]{:S(2)}, u32[]{:S(2)}) collective-permute-start(bf16[256,768]{1,0:T(8,128)(2,1)S(1)} %broadcast_select_fusion.5), channel_id=1, source_target_pairs={{0,1},{2,3},{4,5},{6,7},{8,9},{10,11},{12,13},{14,15},{16,17},{18,... | collective-permute-start | bytes 1179656 | tf_op jit(solution)/shard_map/ppermute | solution.py:53
  90.5 5.3 %collective-permute-done.7 = bf16[256,768]{1,0:T(8,128)(2,1)S(1)} collective-permute-done((bf16[256,768]{1,0:T(8,128)(2,1)S(1)}, bf16[256,768]{1,0:T(8,128)(2,1)S(1)}, u32[]{:S(2)}, u32[]{:S(2)}) %collective-permute-start.7) | collective-permute-done | bytes 393248 | tf_op jit(solution)/shard_map/ppermute | solution.py:26
  95.8 0.3 convert_reduce_fusion
  96.1 0.6 fusion.4
  96.7 2.1 %fusion.6 = bf16[1024,768]{1,0:T(8,128)(2,1)S(1)} fusion(f32[768]{0:T(1024)S(1)} %get-tuple-element.5, f32[1024]{0:T(1024)S(1)} %add_rsqrt_fusion, f32[1024]{0:T(1024)S(1)} %broadcast_multiply_fusion, bf16[256,768]{1,0:T(8,128)(2,1)S(1)} %collective-permute-done.7, bf16[512,768]{1,0:T(8,128)(2,1)S(1)} %add_convert_fusion.1, ...), kind=kLoop, calls=%fused_computation.14 | loop fusion | flops 7864320 | bytes 3156992 | tf_op jit(solution)/shard_map/convert_element_type | solution.py:65
  98.8 4.0 %convolution_convert_fusion.refs_0_.refs_1_.refs_2_ = bf16[1024,1536]{1,0:T(8,128)(2,1)} fusion(bf16[1024,768]{1,0:T(8,128)(2,1)S(1)} %fusion.6, bf16[768,2304]{1,0:T(8,128)(2,1)S(1)} %copy-done.2), kind=kOutput, calls=%fused_computation.4 | convolution fusion | flops 2417491968 | bytes 7077888 | tf_op jit(solution)/shard_map/dot_general | solution.py:186
  102.9 1.7 %multiply_convert_fusion.q_ref = bf16[512,768]{1,0:T(8,128)(2,1)} fusion(bf16[768,2304]{1,0:T(8,128)(2,1)S(1)} %copy-done.2, bf16[1024,768]{1,0:T(8,128)(2,1)S(1)} %fusion.6), kind=kOutput, calls=%fused_computation.34 | convolution fusion | flops 604766208 | bytes 2752512 | tf_op jit(solution)/shard_map/dot_general | solution.py:191
  104.5 0.7 convert_reduce_fusion.3
  105.5 1.8 %convolution_convert_fusion.2.refs_3_ = bf16[256,1536]{1,0:T(8,128)(2,1)} fusion(bf16[768,2304]{1,0:T(8,128)(2,1)S(1)} %copy-done.2, bf16[256,768]{1,0:T(8,128)(2,1)S(1)} %get-tuple-element.8, f32[768]{0:T(1024)S(1)} %get-tuple-element.5, f32[256]{0:T(256)S(1)} %add_rsqrt_fusion.3, f32[256]{0:T(256)S(1)} %broadcast_multiply_fusion.3), kind=kOutput, calls=%fused_computation.18 | convolution fusion | flops 605356032 | bytes 3545088 | tf_op jit(solution)/shard_map/dot_general | solution.py:193
  107.3 15.6 %shard_map.187 = bf16[512,768]{1,0:T(8,128)(2,1)} custom-call(s32[2]{0:T(128)} %pad_add_fusion.pos_ref, bf16[512,768]{1,0:T(8,128)(2,1)} %multiply_convert_fusion.q_ref, bf16[1024,1536]{1,0:T(8,128)(2,1)} %convolution_convert_fusion.refs_0_.refs_1_.refs_2_, bf16[1024,1536]{1,0:T(8,128)(2,1)} %convolution_convert_fusion.refs_0_.refs_1_.refs_2_, ...), custom_call_target="tpu_custom_call" | custom-call | flops 6442450944 | bytes 7077888 | tf_op jit(solution)/shard_map/pallas_call | solution.py:141
  122.9 2.4 %convert_reduce_fusion.2 = (f32[512]{0:T(512)S(1)}, bf16[512,768]{1,0:T(8,128)(2,1)S(1)}) fusion(bf16[512,768]{1,0:T(8,128)(2,1)} %shard_map.187, bf16[2,768,768]{2,1,0:T(8,128)(2,1)} %param.21, bf16[512,768]{1,0:T(8,128)(2,1)S(1)} %add_convert_fusion.1), kind=kOutput, calls=%fused_computation.25 | convolution fusion | flops 605945344 | bytes 3540992 | tf_op jit(solution)/shard_map/dot_general | solution.py:207
  125.3 0.4 fusion.16
  125.7 0.8 fusion.39
  127.0 0.6 multiply_add_fusion
  (59 shorter events, 1.3 us)
Async XLA Ops:
  0.6 125.1 %copy-start = (bf16[768,512]{1,0:T(8,128)(2,1)S(1)}, bf16[768,512]{1,0:T(8,128)(2,1)}, u32[]{:S(2)}) copy-start(bf16[768,512]{1,0:T(8,128)(2,1)} %param.23) | copy-start | bytes 2359300
  2.7 14.2 %collective-permute-start = (bf16[256,768]{1,0:T(8,128)(2,1)}, bf16[256,768]{1,0:T(8,128)(2,1)S(1)}, u32[]{:S(2)}, u32[]{:S(2)}) collective-permute-start(bf16[256,768]{1,0:T(8,128)(2,1)} %get-tuple-element.16), channel_id=1, source_target_pairs={{0,1},{1,2},{2,3},{3,4},{4,5},{5,6},{6,7},{7,8},{8,9},{9,10},{10,1... | collective-permute-start | bytes 1179656 | tf_op jit(solution)/shard_map/ppermute | solution.py:25
  6.4 10.5 %collective-permute-start.1 = (bf16[256,768]{1,0:T(8,128)(2,1)S(1)}, bf16[256,768]{1,0:T(8,128)(2,1)S(1)}, u32[]{:S(2)}, u32[]{:S(2)}) collective-permute-start(bf16[256,768]{1,0:T(8,128)(2,1)S(1)} %get-tuple-element.17), channel_id=1, source_target_pairs={{1,0},{2,1},{3,2},{4,3},{5,4},{6,5},{7,6},{8,7},{9,8},{10,9},{11,1... | collective-permute-start | bytes 1179656 | tf_op jit(solution)/shard_map/ppermute | solution.py:26
  8.3 7.9 %copy-start.14 = (s32[2]{0:T(128)S(1)}, s32[2]{0:T(128)}, u32[]{:S(2)}) copy-start(s32[2]{0:T(128)} %constant.53.clone) | copy-start | bytes 28
  8.3 8.5 %copy-start.7 = (f32[2,768]{1,0:T(2,128)S(1)}, f32[2,768]{1,0:T(2,128)}, u32[]{:S(2)}) copy-start(f32[2,768]{1,0:T(2,128)} %param.19) | copy-start | bytes 18436
  8.3 8.6 %copy-start.1 = (bf16[512,768]{1,0:T(8,128)(2,1)S(1)}, bf16[512,768]{1,0:T(8,128)(2,1)}, u32[]{:S(2)}) copy-start(bf16[512,768]{1,0:T(8,128)(2,1)} %param.18) | copy-start | bytes 2359300
  8.3 16.2 %collective-permute-start.2 = (bf16[256,768]{1,0:T(8,128)(2,1)S(1)}, bf16[256,768]{1,0:T(8,128)(2,1)S(1)}, u32[]{:S(2)}, u32[]{:S(2)}) collective-permute-start(bf16[256,768]{1,0:T(8,128)(2,1)S(1)} %get-tuple-element.15), channel_id=1, source_target_pairs={{0,8},{16,24}} | collective-permute-start | bytes 1179656 | tf_op jit(solution)/shard_map/ppermute | solution.py:53
  17.2 2.5 %copy-start.3 = (bf16[768,2304]{1,0:T(8,128)(2,1)S(1)}, bf16[768,2304]{1,0:T(8,128)(2,1)}, u32[]{:S(2)}) copy-start(bf16[768,2304]{1,0:T(8,128)(2,1)} %get-tuple-element.12) | copy-start | bytes 10616836
  22.6 2.7 %copy-start.5 = (bf16[1024,1536]{1,0:T(8,128)(2,1)}, bf16[1024,1536]{1,0:T(8,128)(2,1)S(1)}, u32[]{:S(2)}) copy-start(bf16[1024,1536]{1,0:T(8,128)(2,1)S(1)} %convolution_convert_fusion.1.refs_0_.refs_1_.refs_2_) | copy-start | bytes 9437188
  24.6 13.6 %collective-permute-start.3 = (bf16[256,768]{1,0:T(8,128)(2,1)S(1)}, bf16[256,768]{1,0:T(8,128)(2,1)S(1)}, u32[]{:S(2)}, u32[]{:S(2)}) collective-permute-start(bf16[256,768]{1,0:T(8,128)(2,1)S(1)} %broadcast_select_fusion.1), channel_id=1, source_target_pairs={{0,4},{8,12},{16,20},{24,28}} | collective-permute-start | bytes 1179656 | tf_op jit(solution)/shard_map/ppermute | solution.py:53
  35.6 4.0 %copy-start.13 = (s32[4]{0:T(128)S(1)}, s32[4]{0:T(128)}, u32[]{:S(2)}) copy-start(s32[4]{0:T(128)} %constant.54.clone) | copy-start | bytes 52
  37.5 6.0 %copy-start.12 = (s32[8]{0:T(128)S(1)}, s32[8]{0:T(128)}, u32[]{:S(2)}) copy-start(s32[8]{0:T(128)} %constant.55.clone) | copy-start | bytes 100
  37.5 2.8 %collective-permute-start.8 = (bf16[256,768]{1,0:T(8,128)(2,1)S(1)}, bf16[256,768]{1,0:T(8,128)(2,1)S(1)}, u32[]{:S(2)}, u32[]{:S(2)}) collective-permute-start(bf16[256,768]{1,0:T(8,128)(2,1)S(1)} %fusion.20), channel_id=1, source_target_pairs={{0,8},{16,24}} | collective-permute-start | bytes 1179656 | tf_op jit(solution)/shard_map/ppermute | solution.py:53
  38.9 2.2 %collective-permute-start.4 = (bf16[256,768]{1,0:T(8,128)(2,1)S(1)}, bf16[256,768]{1,0:T(8,128)(2,1)S(1)}, u32[]{:S(2)}, u32[]{:S(2)}) collective-permute-start(bf16[256,768]{1,0:T(8,128)(2,1)S(1)} %broadcast_select_fusion.4), channel_id=1, source_target_pairs={{0,2},{4,6},{8,10},{12,14},{16,18},{20,22},{24,26},{28,30}} | collective-permute-start | bytes 1179656 | tf_op jit(solution)/shard_map/ppermute | solution.py:53
  40.3 15.3 %copy-start.4 = (bf16[768,2304]{1,0:T(8,128)(2,1)S(1)}, bf16[768,2304]{1,0:T(8,128)(2,1)}, u32[]{:S(2)}) copy-start(bf16[768,2304]{1,0:T(8,128)(2,1)} %get-tuple-element.12) | copy-start | bytes 10616836
  40.3 3.8 %collective-permute-start.9 = (bf16[256,768]{1,0:T(8,128)(2,1)S(1)}, bf16[256,768]{1,0:T(8,128)(2,1)S(1)}, u32[]{:S(2)}, u32[]{:S(2)}) collective-permute-start(bf16[256,768]{1,0:T(8,128)(2,1)S(1)} %broadcast_select_fusion), channel_id=1, source_target_pairs={{0,4},{8,12},{16,20},{24,28}} | collective-permute-start | bytes 1179656 | tf_op jit(solution)/shard_map/ppermute | solution.py:53
  42.0 12.6 %collective-permute-start.5 = (bf16[256,768]{1,0:T(8,128)(2,1)S(1)}, bf16[256,768]{1,0:T(8,128)(2,1)S(1)}, u32[]{:S(2)}, u32[]{:S(2)}) collective-permute-start(bf16[256,768]{1,0:T(8,128)(2,1)S(1)} %broadcast_select_fusion.6), channel_id=1, source_target_pairs={{0,1},{2,3},{4,5},{6,7},{8,9},{10,11},{12,13},{14,15},{16,17},{18,... | collective-permute-start | bytes 1179656 | tf_op jit(solution)/shard_map/ppermute | solution.py:53
  44.8 43.6 %collective-permute-start.10 = (bf16[256,768]{1,0:T(8,128)(2,1)S(1)}, bf16[256,768]{1,0:T(8,128)(2,1)S(1)}, u32[]{:S(2)}, u32[]{:S(2)}) collective-permute-start(bf16[256,768]{1,0:T(8,128)(2,1)S(1)} %broadcast_select_fusion.3), channel_id=1, source_target_pairs={{0,2},{4,6},{8,10},{12,14},{16,18},{20,22},{24,26},{28,30}} | collective-permute-start | bytes 1179656 | tf_op jit(solution)/shard_map/ppermute | solution.py:53
  75.3 15.2 %collective-permute-start.6 = (bf16[256,768]{1,0:T(8,128)(2,1)S(1)}, bf16[256,768]{1,0:T(8,128)(2,1)S(1)}, u32[]{:S(2)}, u32[]{:S(2)}) collective-permute-start(bf16[256,768]{1,0:T(8,128)(2,1)S(1)} %get-tuple-element.13), channel_id=1, source_target_pairs={{0,1},{1,2},{2,3},{3,4},{4,5},{5,6},{6,7},{7,8},{8,9},{9,10},{10,1... | collective-permute-start | bytes 1179656 | tf_op jit(solution)/shard_map/ppermute | solution.py:25
  85.8 10.0 %collective-permute-start.7 = (bf16[256,768]{1,0:T(8,128)(2,1)S(1)}, bf16[256,768]{1,0:T(8,128)(2,1)S(1)}, u32[]{:S(2)}, u32[]{:S(2)}) collective-permute-start(bf16[256,768]{1,0:T(8,128)(2,1)S(1)} %get-tuple-element.14), channel_id=1, source_target_pairs={{1,0},{2,1},{3,2},{4,3},{5,4},{6,5},{7,6},{8,7},{9,8},{10,9},{11,1... | collective-permute-start | bytes 1179656 | tf_op jit(solution)/shard_map/ppermute | solution.py:26
  89.0 15.5 %collective-permute-start.11 = (bf16[256,768]{1,0:T(8,128)(2,1)S(1)}, bf16[256,768]{1,0:T(8,128)(2,1)S(1)}, u32[]{:S(2)}, u32[]{:S(2)}) collective-permute-start(bf16[256,768]{1,0:T(8,128)(2,1)S(1)} %broadcast_select_fusion.5), channel_id=1, source_target_pairs={{0,1},{2,3},{4,5},{6,7},{8,9},{10,11},{12,13},{14,15},{16,17},{18,... | collective-permute-start | bytes 1179656 | tf_op jit(solution)/shard_map/ppermute | solution.py:53
  96.1 2.8 %copy-start.2 = (bf16[768,2304]{1,0:T(8,128)(2,1)S(1)}, bf16[768,2304]{1,0:T(8,128)(2,1)}, u32[]{:S(2)}) copy-start(bf16[768,2304]{1,0:T(8,128)(2,1)} %get-tuple-element.11) | copy-start | bytes 10616836
  122.9 2.8 %copy-start.11 = (f32[768]{0:T(1024)S(1)}, f32[768]{0:T(1024)}, u32[]{:S(2)}) copy-start(f32[768]{0:T(1024)} %param.22) | copy-start | bytes 9220
  125.3 1.4 %copy-start.8 = (s32[512]{0:T(512)S(1)}, s32[512]{0:T(512)}, u32[]{:S(2)}) copy-start(s32[512]{0:T(512)} %param.24) | copy-start | bytes 6148
  125.7 1.2 copy-start.9
  125.7 1.2 copy-start.10
  126.9 0.6 copy-start.6

commit v12 on v10

--- a/solution.py
+++ b/solution.py
@@ -46,7 +46,6 @@
 
 def spread(block, axis):
     place = lax.axis_index(axis)
-    block = jnp.where(place == 0, block, jnp.zeros_like(block))
     for ops in tree_rounds(lax.axis_size(axis)):
         received = block
         for op in ops:

time: 122 us -> 122 us (level)
  the two profiles are of different devices: /device:TPU:0 before, /device:TPU:20 now
where the time goes in v12:
time: 122 us
  Pallas kernels  31.3 us (26%)
  waiting for transfers between devices  29.2 us (24%)
  matrix products  20.4 us (17%)
  starting transfers between devices  17.1 us (14%)
  other arithmetic  14.3 us (12%)
  local copies, waits for them, and re-layouts  7.68 us (6%)
  between operations  1.72 us (1%)
    pallas_call x2, Pallas kernels, attention(): pl.pallas_call(functools.partial(attention_kernel, row0), out_shape=jax.S...  31.3 us
    ppermute x8, waiting for transfers between devices, spread(): got = lax.ppermute(block, axis, op)  18 us
    ppermute x2, waiting for transfers between devices, with_halo(): before = lax.ppermute(last, axis, up)  9.74 us
    ppermute x8, starting transfers between devices, spread(): got = lax.ppermute(block, axis, op)  8.36 us
    dot_general x2, matrix products, per_device(): jnp.dot(extended_normed, weights[:, feat_width:], preferred_element_type=...  8.09 us
    squeeze x1, local copies, waits for them, and re-layouts, per_device(): weights = w_qkv[layer_idx]  6.45 us
    ppermute x2, starting transfers between devices, with_halo(): before = lax.ppermute(last, axis, up)  4.81 us
    dot_general x2, matrix products, per_device(): jnp.dot(attended, w_out[layer_idx], preferred_element_type=jnp.float32)  4.68 us
  transfers between devices with their start and end apart: 12, of which 5 were waited for; matrix products, arithmetic and copies ran while one was open for 21% of the time, Pallas kernels for 0%

profile of v12, /device:TPU:20, one launch (start us, length us, event | category | flops | bytes accessed | tf_op | source)
XLA Modules:
  0.0 121.7 jit_solution(4693231157325583157)
XLA Ops:
  0.6 1.1 slice.59
  1.8 2.1 %collective-permute-start.1 = (bf16[256,768]{1,0:T(8,128)(2,1)S(1)}, bf16[256,768]{1,0:T(8,128)(2,1)S(1)}, u32[]{:S(2)}, u32[]{:S(2)}) collective-permute-start(bf16[256,768]{1,0:T(8,128)(2,1)S(1)} %slice.59), channel_id=1, source_target_pairs={{1,0},{2,1},{3,2},{4,3},{5,4},{6,5},{7,6},{8,7},{9,8},{10,9},{11,1... | collective-permute-start | bytes 1179656 | tf_op jit(solution)/shard_map/ppermute | solution.py:26
  3.9 0.7 collective-permute-start.2
  4.6 6.5 %slice_bitcast_fusion = (bf16[768,2304]{1,0:T(8,128)(2,1)}, bf16[768,2304]{1,0:T(8,128)(2,1)}) fusion(bf16[2,768,2304]{2,1,0:T(8,128)(2,1)} %param.20), kind=kLoop, calls=%fused_computation.10 | loop fusion | bytes 14155776 | tf_op jit(solution)/shard_map/squeeze | solution.py:181
  11.0 0.6 compare_reduce_fusion
  11.7 2.4 %collective-permute-start = (bf16[256,768]{1,0:T(8,128)(2,1)S(1)}, bf16[256,768]{1,0:T(8,128)(2,1)S(1)}, u32[]{:S(2)}, u32[]{:S(2)}) collective-permute-start(bf16[256,768]{1,0:T(8,128)(2,1)S(1)} %get-tuple-element.16), channel_id=1, source_target_pairs={{0,1},{1,2},{2,3},{3,4},{4,5},{5,6},{6,7},{7,8},{8,9},{9,10},{10,1... | collective-permute-start | bytes 1179656 | tf_op jit(solution)/shard_map/ppermute | solution.py:25
  14.1 0.6 compare_reduce_fusion.1
  14.8 0.7 compare_reduce_fusion.2
  15.5 0.7 collective-permute-start.3
  16.2 0.6 pad_add_fusion.pos_ref
  16.8 4.0 %collective-permute-done = bf16[256,768]{1,0:T(8,128)(2,1)S(1)} collective-permute-done((bf16[256,768]{1,0:T(8,128)(2,1)S(1)}, bf16[256,768]{1,0:T(8,128)(2,1)S(1)}, u32[]{:S(2)}, u32[]{:S(2)}) %collective-permute-start) | collective-permute-done | bytes 393248 | tf_op jit(solution)/shard_map/ppermute | solution.py:25
  20.8 0.3 convert_reduce_fusion.1
  21.1 0.6 broadcast_select_fusion.3
  21.7 1.3 %collective-permute-start.4 = (bf16[256,768]{1,0:T(8,128)(2,1)S(1)}, bf16[256,768]{1,0:T(8,128)(2,1)S(1)}, u32[]{:S(2)}, u32[]{:S(2)}) collective-permute-start(bf16[256,768]{1,0:T(8,128)(2,1)S(1)} %broadcast_select_fusion.3), channel_id=1, source_target_pairs={{0,2},{4,6},{8,10},{12,14},{16,18},{20,22},{24,26},{28,30}} | collective-permute-start | bytes 1179656 | tf_op jit(solution)/shard_map/ppermute | solution.py:52
  23.0 0.6 fusion.7
  23.7 1.9 %fusion.9 = bf16[1024,768]{1,0:T(8,128)(2,1)S(1)} fusion(f32[768]{0:T(1024)S(1)} %get-tuple-element.6, f32[1024]{0:T(1024)S(1)} %add_rsqrt_fusion.1, f32[1024]{0:T(1024)S(1)} %broadcast_multiply_fusion.1, bf16[256,768]{1,0:T(8,128)(2,1)S(1)} %collective-permute-done.1, bf16[512,768]{1,0:T(8,128)(2,1)S(1)} %copy-done.1, ...), kind=kLoop, calls=%fused_computation.17 | loop fusion | flops 7864320 | bytes 3156992 | tf_op jit(solution)/shard_map/convert_element_type | solution.py:64
  25.6 8.2 %collective-permute-done.4 = bf16[256,768]{1,0:T(8,128)(2,1)S(1)} collective-permute-done((bf16[256,768]{1,0:T(8,128)(2,1)S(1)}, bf16[256,768]{1,0:T(8,128)(2,1)S(1)}, u32[]{:S(2)}, u32[]{:S(2)}) %collective-permute-start.4) | collective-permute-done | bytes 393248 | tf_op jit(solution)/shard_map/ppermute | solution.py:52
  33.8 0.6 broadcast_select_fusion.5
  34.4 1.5 %collective-permute-start.5 = (bf16[256,768]{1,0:T(8,128)(2,1)S(1)}, bf16[256,768]{1,0:T(8,128)(2,1)S(1)}, u32[]{:S(2)}, u32[]{:S(2)}) collective-permute-start(bf16[256,768]{1,0:T(8,128)(2,1)S(1)} %broadcast_select_fusion.5), channel_id=1, source_target_pairs={{0,1},{2,3},{4,5},{6,7},{8,9},{10,11},{12,13},{14,15},{16,17},{18,... | collective-permute-start | bytes 1179656 | tf_op jit(solution)/shard_map/ppermute | solution.py:52
  35.9 4.1 %convolution_convert_fusion.1.refs_0_.refs_1_.refs_2_ = bf16[1024,1536]{1,0:T(8,128)(2,1)} fusion(bf16[1024,768]{1,0:T(8,128)(2,1)S(1)} %fusion.9, bf16[768,2304]{1,0:T(8,128)(2,1)S(1)} %copy-done.3), kind=kOutput, calls=%fused_computation.5 | convolution fusion | flops 2417491968 | bytes 7077888 | tf_op jit(solution)/shard_map/dot_general | solution.py:185
  40.0 1.7 %multiply_convert_fusion.1.q_ref = bf16[512,768]{1,0:T(8,128)(2,1)} fusion(bf16[768,2304]{1,0:T(8,128)(2,1)S(1)} %copy-done.3, bf16[1024,768]{1,0:T(8,128)(2,1)S(1)} %fusion.9), kind=kOutput, calls=%fused_computation.36 | convolution fusion | flops 604766208 | bytes 2752512 | tf_op jit(solution)/shard_map/dot_general | solution.py:190
  41.6 0.9 convert_reduce_fusion.4
  42.8 1.8 %convolution_convert_fusion.3.refs_3_ = bf16[256,1536]{1,0:T(8,128)(2,1)} fusion(bf16[768,2304]{1,0:T(8,128)(2,1)S(1)} %copy-done.3, bf16[256,768]{1,0:T(8,128)(2,1)S(1)} %get-tuple-element.10, f32[768]{0:T(1024)S(1)} %get-tuple-element.6, f32[256]{0:T(256)S(1)} %add_rsqrt_fusion.4, f32[256]{0:T(256)S(1)} %broadcast_multiply_fusion.4), kind=kOutput, calls=%fused_computation.19 | convolution fusion | flops 605356032 | bytes 3545088 | tf_op jit(solution)/shard_map/dot_general | solution.py:192
  44.5 15.6 %shard_map.185 = bf16[512,768]{1,0:T(8,128)(2,1)} custom-call(s32[2]{0:T(128)} %pad_add_fusion.pos_ref, bf16[512,768]{1,0:T(8,128)(2,1)} %multiply_convert_fusion.1.q_ref, bf16[1024,1536]{1,0:T(8,128)(2,1)} %convolution_convert_fusion.1.refs_0_.refs_1_.refs_2_, bf16[1024,1536]{1,0:T(8,128)(2,1)} %convolution_convert_fusion.1.refs_0_.refs_1_.refs_2_, ...), custom_call_target="tpu_custom_call" | custom-call | flops 6442450944 | bytes 7077888 | tf_op jit(solution)/shard_map/pallas_call | solution.py:140
  60.2 2.3 %add_convert_fusion.1 = bf16[512,768]{1,0:T(8,128)(2,1)S(1)} fusion(bf16[512,768]{1,0:T(8,128)(2,1)S(1)} %copy-done.1, bf16[512,768]{1,0:T(8,128)(2,1)} %shard_map.185, bf16[2,768,768]{2,1,0:T(8,128)(2,1)} %param.21), kind=kOutput, calls=%fused_computation.35 | convolution fusion | flops 605159424 | bytes 3538944 | tf_op jit(solution)/shard_map/dot_general | solution.py:198
  62.5 0.7 collective-permute-start.8
  63.2 1.9 %collective-permute-start.7 = (bf16[256,768]{1,0:T(8,128)(2,1)S(1)}, bf16[256,768]{1,0:T(8,128)(2,1)S(1)}, u32[]{:S(2)}, u32[]{:S(2)}) collective-permute-start(bf16[256,768]{1,0:T(8,128)(2,1)S(1)} %slice.80), channel_id=1, source_target_pairs={{1,0},{2,1},{3,2},{4,3},{5,4},{6,5},{7,6},{8,7},{9,8},{10,9},{11,1... | collective-permute-start | bytes 1179656 | tf_op jit(solution)/shard_map/ppermute | solution.py:26
  65.2 2.4 %collective-permute-start.6 = (bf16[256,768]{1,0:T(8,128)(2,1)S(1)}, bf16[256,768]{1,0:T(8,128)(2,1)S(1)}, u32[]{:S(2)}, u32[]{:S(2)}) collective-permute-start(bf16[256,768]{1,0:T(8,128)(2,1)S(1)} %get-tuple-element.14), channel_id=1, source_target_pairs={{0,1},{1,2},{2,3},{3,4},{4,5},{5,6},{6,7},{7,8},{8,9},{9,10},{10,1... | collective-permute-start | bytes 1179656 | tf_op jit(solution)/shard_map/ppermute | solution.py:25
  67.6 0.7 collective-permute-start.9
  69.0 1.4 %collective-permute-done.7 = bf16[256,768]{1,0:T(8,128)(2,1)S(1)} collective-permute-done((bf16[256,768]{1,0:T(8,128)(2,1)S(1)}, bf16[256,768]{1,0:T(8,128)(2,1)S(1)}, u32[]{:S(2)}, u32[]{:S(2)}) %collective-permute-start.7) | collective-permute-done | bytes 393248 | tf_op jit(solution)/shard_map/ppermute | solution.py:26
  70.4 5.7 %collective-permute-done.6 = bf16[256,768]{1,0:T(8,128)(2,1)S(1)} collective-permute-done((bf16[256,768]{1,0:T(8,128)(2,1)S(1)}, bf16[256,768]{1,0:T(8,128)(2,1)S(1)}, u32[]{:S(2)}, u32[]{:S(2)}) %collective-permute-start.6) | collective-permute-done | bytes 393248 | tf_op jit(solution)/shard_map/ppermute | solution.py:25
  76.1 0.3 convert_reduce_fusion
  76.4 0.6 broadcast_select_fusion.2
  77.0 1.3 %collective-permute-start.10 = (bf16[256,768]{1,0:T(8,128)(2,1)S(1)}, bf16[256,768]{1,0:T(8,128)(2,1)S(1)}, u32[]{:S(2)}, u32[]{:S(2)}) collective-permute-start(bf16[256,768]{1,0:T(8,128)(2,1)S(1)} %broadcast_select_fusion.2), channel_id=1, source_target_pairs={{0,2},{4,6},{8,10},{12,14},{16,18},{20,22},{24,26},{28,30}} | collective-permute-start | bytes 1179656 | tf_op jit(solution)/shard_map/ppermute | solution.py:52
  78.3 0.6 fusion.4
  79.0 1.9 %fusion.6 = bf16[1024,768]{1,0:T(8,128)(2,1)S(1)} fusion(f32[768]{0:T(1024)S(1)} %get-tuple-element.5, f32[1024]{0:T(1024)S(1)} %add_rsqrt_fusion, f32[1024]{0:T(1024)S(1)} %broadcast_multiply_fusion, bf16[256,768]{1,0:T(8,128)(2,1)S(1)} %collective-permute-done.7, bf16[512,768]{1,0:T(8,128)(2,1)S(1)} %add_convert_fusion.1, ...), kind=kLoop, calls=%fused_computation.14 | loop fusion | flops 7864320 | bytes 3156992 | tf_op jit(solution)/shard_map/convert_element_type | solution.py:64
  80.8 9.8 %collective-permute-done.10 = bf16[256,768]{1,0:T(8,128)(2,1)S(1)} collective-permute-done((bf16[256,768]{1,0:T(8,128)(2,1)S(1)}, bf16[256,768]{1,0:T(8,128)(2,1)S(1)}, u32[]{:S(2)}, u32[]{:S(2)}) %collective-permute-start.10) | collective-permute-done | bytes 393248 | tf_op jit(solution)/shard_map/ppermute | solution.py:52
  90.6 0.6 broadcast_select_fusion.4
  91.2 1.5 %collective-permute-start.11 = (bf16[256,768]{1,0:T(8,128)(2,1)S(1)}, bf16[256,768]{1,0:T(8,128)(2,1)S(1)}, u32[]{:S(2)}, u32[]{:S(2)}) collective-permute-start(bf16[256,768]{1,0:T(8,128)(2,1)S(1)} %broadcast_select_fusion.4), channel_id=1, source_target_pairs={{0,1},{2,3},{4,5},{6,7},{8,9},{10,11},{12,13},{14,15},{16,17},{18,... | collective-permute-start | bytes 1179656 | tf_op jit(solution)/shard_map/ppermute | solution.py:52
  92.8 4.0 %convolution_convert_fusion.refs_0_.refs_1_.refs_2_ = bf16[1024,1536]{1,0:T(8,128)(2,1)} fusion(bf16[1024,768]{1,0:T(8,128)(2,1)S(1)} %fusion.6, bf16[768,2304]{1,0:T(8,128)(2,1)S(1)} %copy-done.2), kind=kOutput, calls=%fused_computation.4 | convolution fusion | flops 2417491968 | bytes 7077888 | tf_op jit(solution)/shard_map/dot_general | solution.py:185
  96.8 1.7 %multiply_convert_fusion.q_ref = bf16[512,768]{1,0:T(8,128)(2,1)} fusion(bf16[768,2304]{1,0:T(8,128)(2,1)S(1)} %copy-done.2, bf16[1024,768]{1,0:T(8,128)(2,1)S(1)} %fusion.6), kind=kOutput, calls=%fused_computation.34 | convolution fusion | flops 604766208 | bytes 2752512 | tf_op jit(solution)/shard_map/dot_general | solution.py:190
  98.5 0.9 convert_reduce_fusion.3
  99.6 1.8 %convolution_convert_fusion.2.refs_3_ = bf16[256,1536]{1,0:T(8,128)(2,1)} fusion(bf16[768,2304]{1,0:T(8,128)(2,1)S(1)} %copy-done.2, bf16[256,768]{1,0:T(8,128)(2,1)S(1)} %get-tuple-element.8, f32[768]{0:T(1024)S(1)} %get-tuple-element.5, f32[256]{0:T(256)S(1)} %add_rsqrt_fusion.3, f32[256]{0:T(256)S(1)} %broadcast_multiply_fusion.3), kind=kOutput, calls=%fused_computation.18 | convolution fusion | flops 605356032 | bytes 3545088 | tf_op jit(solution)/shard_map/dot_general | solution.py:192
  101.4 15.6 %shard_map.186 = bf16[512,768]{1,0:T(8,128)(2,1)} custom-call(s32[2]{0:T(128)} %pad_add_fusion.pos_ref, bf16[512,768]{1,0:T(8,128)(2,1)} %multiply_convert_fusion.q_ref, bf16[1024,1536]{1,0:T(8,128)(2,1)} %convolution_convert_fusion.refs_0_.refs_1_.refs_2_, bf16[1024,1536]{1,0:T(8,128)(2,1)} %convolution_convert_fusion.refs_0_.refs_1_.refs_2_, ...), custom_call_target="tpu_custom_call" | custom-call | flops 6442450944 | bytes 7077888 | tf_op jit(solution)/shard_map/pallas_call | solution.py:140
  117.0 2.4 %convert_reduce_fusion.2 = (f32[512]{0:T(512)S(1)}, bf16[512,768]{1,0:T(8,128)(2,1)S(1)}) fusion(bf16[512,768]{1,0:T(8,128)(2,1)} %shard_map.186, bf16[2,768,768]{2,1,0:T(8,128)(2,1)} %param.21, bf16[512,768]{1,0:T(8,128)(2,1)S(1)} %add_convert_fusion.1), kind=kOutput, calls=%fused_computation.25 | convolution fusion | flops 605945344 | bytes 3540992 | tf_op jit(solution)/shard_map/dot_general | solution.py:198
  119.4 0.4 fusion.16
  119.8 0.8 fusion.35
  121.1 0.6 multiply_add_fusion
  (52 shorter events, 1.2 us)
Async XLA Ops:
  0.6 119.2 %copy-start = (bf16[768,512]{1,0:T(8,128)(2,1)S(1)}, bf16[768,512]{1,0:T(8,128)(2,1)}, u32[]{:S(2)}) copy-start(bf16[768,512]{1,0:T(8,128)(2,1)} %param.23) | copy-start | bytes 2359300
  1.7 9.3 %copy-start.12 = (s32[2]{0:T(128)S(1)}, s32[2]{0:T(128)}, u32[]{:S(2)}) copy-start(s32[2]{0:T(128)} %constant.49.clone) | copy-start | bytes 28
  1.8 9.9 %copy-start.1 = (bf16[512,768]{1,0:T(8,128)(2,1)S(1)}, bf16[512,768]{1,0:T(8,128)(2,1)}, u32[]{:S(2)}) copy-start(bf16[512,768]{1,0:T(8,128)(2,1)} %param.18) | copy-start | bytes 2359300
  1.8 12.4 %copy-start.11 = (s32[4]{0:T(128)S(1)}, s32[4]{0:T(128)}, u32[]{:S(2)}) copy-start(s32[4]{0:T(128)} %constant.50.clone) | copy-start | bytes 52
  1.8 13.0 %copy-start.10 = (s32[8]{0:T(128)S(1)}, s32[8]{0:T(128)}, u32[]{:S(2)}) copy-start(s32[8]{0:T(128)} %constant.51.clone) | copy-start | bytes 100
  1.8 13.7 %copy-start.5 = (f32[2,768]{1,0:T(2,128)S(1)}, f32[2,768]{1,0:T(2,128)}, u32[]{:S(2)}) copy-start(f32[2,768]{1,0:T(2,128)} %param.19) | copy-start | bytes 18436
  1.8 15.0 %collective-permute-start.1 = (bf16[256,768]{1,0:T(8,128)(2,1)S(1)}, bf16[256,768]{1,0:T(8,128)(2,1)S(1)}, u32[]{:S(2)}, u32[]{:S(2)}) collective-permute-start(bf16[256,768]{1,0:T(8,128)(2,1)S(1)} %slice.59), channel_id=1, source_target_pairs={{1,0},{2,1},{3,2},{4,3},{5,4},{6,5},{7,6},{8,7},{9,8},{10,9},{11,1... | collective-permute-start | bytes 1179656 | tf_op jit(solution)/shard_map/ppermute | solution.py:26
  3.9 7.8 %collective-permute-start.2 = (bf16[256,768]{1,0:T(8,128)(2,1)S(1)}, bf16[256,768]{1,0:T(8,128)(2,1)S(1)}, u32[]{:S(2)}, u32[]{:S(2)}) collective-permute-start(bf16[256,768]{1,0:T(8,128)(2,1)S(1)} %slice.59), channel_id=1, source_target_pairs={{0,8},{16,24}} | collective-permute-start | bytes 1179656 | tf_op jit(solution)/shard_map/ppermute | solution.py:52
  11.7 9.1 %collective-permute-start = (bf16[256,768]{1,0:T(8,128)(2,1)S(1)}, bf16[256,768]{1,0:T(8,128)(2,1)S(1)}, u32[]{:S(2)}, u32[]{:S(2)}) collective-permute-start(bf16[256,768]{1,0:T(8,128)(2,1)S(1)} %get-tuple-element.16), channel_id=1, source_target_pairs={{0,1},{1,2},{2,3},{3,4},{4,5},{5,6},{6,7},{7,8},{8,9},{9,10},{10,1... | collective-permute-start | bytes 1179656 | tf_op jit(solution)/shard_map/ppermute | solution.py:25
  15.5 5.6 %collective-permute-start.3 = (bf16[256,768]{1,0:T(8,128)(2,1)S(1)}, bf16[256,768]{1,0:T(8,128)(2,1)S(1)}, u32[]{:S(2)}, u32[]{:S(2)}) collective-permute-start(bf16[256,768]{1,0:T(8,128)(2,1)S(1)} %get-tuple-element.15), channel_id=1, source_target_pairs={{0,4},{8,12},{16,20},{24,28}} | collective-permute-start | bytes 1179656 | tf_op jit(solution)/shard_map/ppermute | solution.py:52
  21.7 12.1 %collective-permute-start.4 = (bf16[256,768]{1,0:T(8,128)(2,1)S(1)}, bf16[256,768]{1,0:T(8,128)(2,1)S(1)}, u32[]{:S(2)}, u32[]{:S(2)}) collective-permute-start(bf16[256,768]{1,0:T(8,128)(2,1)S(1)} %broadcast_select_fusion.3), channel_id=1, source_target_pairs={{0,2},{4,6},{8,10},{12,14},{16,18},{20,22},{24,26},{28,30}} | collective-permute-start | bytes 1179656 | tf_op jit(solution)/shard_map/ppermute | solution.py:52
  23.7 12.2 %copy-start.3 = (bf16[768,2304]{1,0:T(8,128)(2,1)S(1)}, bf16[768,2304]{1,0:T(8,128)(2,1)}, u32[]{:S(2)}) copy-start(bf16[768,2304]{1,0:T(8,128)(2,1)} %get-tuple-element.12) | copy-start | bytes 10616836
  34.4 7.3 %collective-permute-start.5 = (bf16[256,768]{1,0:T(8,128)(2,1)S(1)}, bf16[256,768]{1,0:T(8,128)(2,1)S(1)}, u32[]{:S(2)}, u32[]{:S(2)}) collective-permute-start(bf16[256,768]{1,0:T(8,128)(2,1)S(1)} %broadcast_select_fusion.5), channel_id=1, source_target_pairs={{0,1},{2,3},{4,5},{6,7},{8,9},{10,11},{12,13},{14,15},{16,17},{18,... | collective-permute-start | bytes 1179656 | tf_op jit(solution)/shard_map/ppermute | solution.py:52
  62.5 2.6 %collective-permute-start.8 = (bf16[256,768]{1,0:T(8,128)(2,1)S(1)}, bf16[256,768]{1,0:T(8,128)(2,1)S(1)}, u32[]{:S(2)}, u32[]{:S(2)}) collective-permute-start(bf16[256,768]{1,0:T(8,128)(2,1)S(1)} %slice.80), channel_id=1, source_target_pairs={{0,8},{16,24}} | collective-permute-start | bytes 1179656 | tf_op jit(solution)/shard_map/ppermute | solution.py:52
  63.2 7.2 %collective-permute-start.7 = (bf16[256,768]{1,0:T(8,128)(2,1)S(1)}, bf16[256,768]{1,0:T(8,128)(2,1)S(1)}, u32[]{:S(2)}, u32[]{:S(2)}) collective-permute-start(bf16[256,768]{1,0:T(8,128)(2,1)S(1)} %slice.80), channel_id=1, source_target_pairs={{1,0},{2,1},{3,2},{4,3},{5,4},{6,5},{7,6},{8,7},{9,8},{10,9},{11,1... | collective-permute-start | bytes 1179656 | tf_op jit(solution)/shard_map/ppermute | solution.py:26
  65.2 10.9 %collective-permute-start.6 = (bf16[256,768]{1,0:T(8,128)(2,1)S(1)}, bf16[256,768]{1,0:T(8,128)(2,1)S(1)}, u32[]{:S(2)}, u32[]{:S(2)}) collective-permute-start(bf16[256,768]{1,0:T(8,128)(2,1)S(1)} %get-tuple-element.14), channel_id=1, source_target_pairs={{0,1},{1,2},{2,3},{3,4},{4,5},{5,6},{6,7},{7,8},{8,9},{9,10},{10,1... | collective-permute-start | bytes 1179656 | tf_op jit(solution)/shard_map/ppermute | solution.py:25
  67.6 8.8 %collective-permute-start.9 = (bf16[256,768]{1,0:T(8,128)(2,1)S(1)}, bf16[256,768]{1,0:T(8,128)(2,1)S(1)}, u32[]{:S(2)}, u32[]{:S(2)}) collective-permute-start(bf16[256,768]{1,0:T(8,128)(2,1)S(1)} %get-tuple-element.13), channel_id=1, source_target_pairs={{0,4},{8,12},{16,20},{24,28}} | collective-permute-start | bytes 1179656 | tf_op jit(solution)/shard_map/ppermute | solution.py:52
  77.0 13.6 %collective-permute-start.10 = (bf16[256,768]{1,0:T(8,128)(2,1)S(1)}, bf16[256,768]{1,0:T(8,128)(2,1)S(1)}, u32[]{:S(2)}, u32[]{:S(2)}) collective-permute-start(bf16[256,768]{1,0:T(8,128)(2,1)S(1)} %broadcast_select_fusion.2), channel_id=1, source_target_pairs={{0,2},{4,6},{8,10},{12,14},{16,18},{20,22},{24,26},{28,30}} | collective-permute-start | bytes 1179656 | tf_op jit(solution)/shard_map/ppermute | solution.py:52
  78.9 13.8 %copy-start.2 = (bf16[768,2304]{1,0:T(8,128)(2,1)S(1)}, bf16[768,2304]{1,0:T(8,128)(2,1)}, u32[]{:S(2)}) copy-start(bf16[768,2304]{1,0:T(8,128)(2,1)} %get-tuple-element.11) | copy-start | bytes 10616836
  91.2 7.2 %collective-permute-start.11 = (bf16[256,768]{1,0:T(8,128)(2,1)S(1)}, bf16[256,768]{1,0:T(8,128)(2,1)S(1)}, u32[]{:S(2)}, u32[]{:S(2)}) collective-permute-start(bf16[256,768]{1,0:T(8,128)(2,1)S(1)} %broadcast_select_fusion.4), channel_id=1, source_target_pairs={{0,1},{2,3},{4,5},{6,7},{8,9},{10,11},{12,13},{14,15},{16,17},{18,... | collective-permute-start | bytes 1179656 | tf_op jit(solution)/shard_map/ppermute | solution.py:52
  117.0 2.8 %copy-start.9 = (f32[768]{0:T(1024)S(1)}, f32[768]{0:T(1024)}, u32[]{:S(2)}) copy-start(f32[768]{0:T(1024)} %param.22) | copy-start | bytes 9220
  119.4 1.4 %copy-start.6 = (s32[512]{0:T(512)S(1)}, s32[512]{0:T(512)}, u32[]{:S(2)}) copy-start(s32[512]{0:T(512)} %param.24) | copy-start | bytes 6148
  119.8 1.2 %copy-start.7 = (f32[512]{0:T(512)S(1)}, f32[512]{0:T(512)}, u32[]{:S(2)}) copy-start(f32[512]{0:T(512)} %param.26) | copy-start | bytes 6148
  119.8 1.2 %copy-start.8 = (s32[512]{0:T(512)S(1)}, s32[512]{0:T(512)}, u32[]{:S(2)}) copy-start(s32[512]{0:T(512)} %param.25) | copy-start | bytes 6148
  121.0 0.6 copy-start.4

commit v13 on v12

--- a/solution.py
+++ b/solution.py
@@ -178,7 +178,11 @@
     prompt_source = hidden_in[:PROMPT]
     for layer_idx in range(LAYERS):
         gain = ln_gain[layer_idx]
-        weights = w_qkv[layer_idx]
+        if layer_idx == 0:
+            weights = w_qkv[0]
+        else:
+            later_weights, hidden_state = lax.optimization_barrier((w_qkv, hidden_state))
+            weights = later_weights[layer_idx]
         extended = with_halo(hidden_state, (("seq", 0),), HALF)
         prompt_rows = spread(prompt_source, "seq")
         extended_normed = layer_norm(extended, gain)

time: 122 us -> 124 us (1.016)
    ppermute x2, waiting for transfers between devices: 9.74 us -> 4.87 us  [with_halo(): before = lax.ppermute(last, axis, up)]
    ppermute x8, waiting for transfers between devices: 18 us -> 21.5 us  [spread(): got = lax.ppermute(block, axis, op)]
    ppermute x2, waiting for transfers between devices: 1.43 us -> 3.39 us  [with_halo(): after = lax.ppermute(leading, axis, down)]
    squeeze x1 -> x2, local copies, waits for them, and re-layouts: 6.45 us -> 6.22 us  [the longest x1 3.99 us: per_device(): weights = w_qkv[0]]
where the time goes in v13:
time: 124 us; the launch traced here: 123 us
  Pallas kernels  31.3 us (25%)
  waiting for transfers between devices  29.7 us (24%)
  matrix products  20.4 us (16%)
  starting transfers between devices  17.4 us (14%)
  other arithmetic  14.6 us (12%)
  local copies, waits for them, and re-layouts  7.49 us (6%)
  between operations  1.72 us (1%)
    pallas_call x2, Pallas kernels, attention(): pl.pallas_call(functools.partial(attention_kernel, row0), out_shape=jax.S...  31.3 us
    ppermute x8, waiting for transfers between devices, spread(): got = lax.ppermute(block, axis, op)  21.5 us
    ppermute x8, starting transfers between devices, spread(): got = lax.ppermute(block, axis, op)  8.62 us
    dot_general x2, matrix products, per_device(): jnp.dot(extended_normed, weights[:, feat_width:], preferred_element_type=...  8.04 us
    ppermute x2, waiting for transfers between devices, with_halo(): before = lax.ppermute(last, axis, up)  4.87 us
    ppermute x2, starting transfers between devices, with_halo(): before = lax.ppermute(last, axis, up)  4.81 us
    dot_general x2, matrix products, per_device(): jnp.dot(attended, w_out[layer_idx], preferred_element_type=jnp.float32)  4.68 us
    squeeze x1, local copies, waits for them, and re-layouts, per_device(): weights = w_qkv[0]  3.99 us
  transfers between devices with their start and end apart: 12, of which 5 were waited for; matrix products, arithmetic and copies ran while one was open for 21% of the time, Pallas kernels for 0%

profile of v13, /device:TPU:20, one launch (start us, length us, event | category | flops | bytes accessed | tf_op | source)
XLA Modules:
  0.0 122.6 jit_solution(1153176541094487622)
XLA Ops:
  0.6 1.1 slice.61
  1.8 2.1 %collective-permute-start.1 = (bf16[256,768]{1,0:T(8,128)(2,1)S(1)}, bf16[256,768]{1,0:T(8,128)(2,1)S(1)}, u32[]{:S(2)}, u32[]{:S(2)}) collective-permute-start(bf16[256,768]{1,0:T(8,128)(2,1)S(1)} %slice.61), channel_id=1, source_target_pairs={{1,0},{2,1},{3,2},{4,3},{5,4},{6,5},{7,6},{8,7},{9,8},{10,9},{11,1... | collective-permute-start | bytes 1179656 | tf_op jit(solution)/shard_map/ppermute | solution.py:26
  3.9 0.7 collective-permute-start.2
  4.6 4.0 %slice_bitcast_fusion.1 = bf16[768,2304]{1,0:T(8,128)(2,1)} fusion(bf16[2,768,2304]{2,1,0:T(8,128)(2,1)} %param.20), kind=kLoop, calls=%fused_computation.11 | loop fusion | bytes 7077888 | tf_op jit(solution)/shard_map/squeeze | solution.py:182
  8.5 0.6 compare_reduce_fusion
  9.3 2.4 %collective-permute-start = (bf16[256,768]{1,0:T(8,128)(2,1)S(1)}, bf16[256,768]{1,0:T(8,128)(2,1)S(1)}, u32[]{:S(2)}, u32[]{:S(2)}) collective-permute-start(bf16[256,768]{1,0:T(8,128)(2,1)S(1)} %get-tuple-element.18), channel_id=1, source_target_pairs={{0,1},{1,2},{2,3},{3,4},{4,5},{5,6},{6,7},{7,8},{8,9},{9,10},{10,1... | collective-permute-start | bytes 1179656 | tf_op jit(solution)/shard_map/ppermute | solution.py:25
  11.7 0.7 compare_reduce_fusion.1
  12.4 0.7 compare_reduce_fusion.2
  13.1 0.7 collective-permute-start.3
  13.8 0.6 pad_add_fusion.pos_ref
  15.1 3.3 %collective-permute-done = bf16[256,768]{1,0:T(8,128)(2,1)S(1)} collective-permute-done((bf16[256,768]{1,0:T(8,128)(2,1)S(1)}, bf16[256,768]{1,0:T(8,128)(2,1)S(1)}, u32[]{:S(2)}, u32[]{:S(2)}) %collective-permute-start) | collective-permute-done | bytes 393248 | tf_op jit(solution)/shard_map/ppermute | solution.py:25
  18.4 0.3 convert_reduce_fusion.1
  18.7 0.7 broadcast_select_fusion.3
  19.3 1.6 %collective-permute-start.4 = (bf16[256,768]{1,0:T(8,128)(2,1)S(1)}, bf16[256,768]{1,0:T(8,128)(2,1)S(1)}, u32[]{:S(2)}, u32[]{:S(2)}) collective-permute-start(bf16[256,768]{1,0:T(8,128)(2,1)S(1)} %broadcast_select_fusion.3), channel_id=1, source_target_pairs={{0,2},{4,6},{8,10},{12,14},{16,18},{20,22},{24,26},{28,30}} | collective-permute-start | bytes 1179656 | tf_op jit(solution)/shard_map/ppermute | solution.py:52
  20.9 0.6 fusion.7
  21.6 1.9 %fusion.9 = bf16[1024,768]{1,0:T(8,128)(2,1)S(1)} fusion(f32[768]{0:T(1024)S(1)} %get-tuple-element.10, f32[1024]{0:T(1024)S(1)} %add_rsqrt_fusion.1, f32[1024]{0:T(1024)S(1)} %broadcast_multiply_fusion.1, bf16[256,768]{1,0:T(8,128)(2,1)S(1)} %collective-permute-done.1, bf16[512,768]{1,0:T(8,128)(2,1)S(1)} %copy-done.1, ...), kind=kLoop, calls=%fused_computation.17 | loop fusion | flops 7864320 | bytes 3156992 | tf_op jit(solution)/shard_map/convert_element_type | solution.py:64
  23.4 10.7 %collective-permute-done.4 = bf16[256,768]{1,0:T(8,128)(2,1)S(1)} collective-permute-done((bf16[256,768]{1,0:T(8,128)(2,1)S(1)}, bf16[256,768]{1,0:T(8,128)(2,1)S(1)}, u32[]{:S(2)}, u32[]{:S(2)}) %collective-permute-start.4) | collective-permute-done | bytes 393248 | tf_op jit(solution)/shard_map/ppermute | solution.py:52
  34.1 0.7 broadcast_select_fusion.5
  34.8 1.5 %collective-permute-start.5 = (bf16[256,768]{1,0:T(8,128)(2,1)S(1)}, bf16[256,768]{1,0:T(8,128)(2,1)S(1)}, u32[]{:S(2)}, u32[]{:S(2)}) collective-permute-start(bf16[256,768]{1,0:T(8,128)(2,1)S(1)} %broadcast_select_fusion.5), channel_id=1, source_target_pairs={{0,1},{2,3},{4,5},{6,7},{8,9},{10,11},{12,13},{14,15},{16,17},{18,... | collective-permute-start | bytes 1179656 | tf_op jit(solution)/shard_map/ppermute | solution.py:52
  36.3 4.0 %convolution_convert_fusion.1.refs_0_.refs_1_.refs_2_ = bf16[1024,1536]{1,0:T(8,128)(2,1)} fusion(bf16[1024,768]{1,0:T(8,128)(2,1)S(1)} %fusion.9, bf16[768,2304]{1,0:T(8,128)(2,1)S(1)} %copy-done.2), kind=kOutput, calls=%fused_computation.5 | convolution fusion | flops 2417491968 | bytes 7077888 | tf_op jit(solution)/shard_map/dot_general | solution.py:189
  40.3 1.7 %multiply_convert_fusion.1.q_ref = bf16[512,768]{1,0:T(8,128)(2,1)} fusion(bf16[768,2304]{1,0:T(8,128)(2,1)S(1)} %copy-done.2, bf16[1024,768]{1,0:T(8,128)(2,1)S(1)} %fusion.9), kind=kOutput, calls=%fused_computation.36 | convolution fusion | flops 604766208 | bytes 2752512 | tf_op jit(solution)/shard_map/dot_general | solution.py:194
  42.0 0.9 convert_reduce_fusion.4
  43.1 1.8 %convolution_convert_fusion.3.refs_3_ = bf16[256,1536]{1,0:T(8,128)(2,1)} fusion(bf16[768,2304]{1,0:T(8,128)(2,1)S(1)} %copy-done.2, bf16[256,768]{1,0:T(8,128)(2,1)S(1)} %get-tuple-element.14, f32[768]{0:T(1024)S(1)} %get-tuple-element.10, f32[256]{0:T(256)S(1)} %add_rsqrt_fusion.4, f32[256]{0:T(256)S(1)} %broadcast_multiply_fusion.4), kind=kOutput, calls=%fused_computation.19 | convolution fusion | flops 605356032 | bytes 3545088 | tf_op jit(solution)/shard_map/dot_general | solution.py:196
  44.9 15.6 %shard_map.185 = bf16[512,768]{1,0:T(8,128)(2,1)} custom-call(s32[2]{0:T(128)} %pad_add_fusion.pos_ref, bf16[512,768]{1,0:T(8,128)(2,1)} %multiply_convert_fusion.1.q_ref, bf16[1024,1536]{1,0:T(8,128)(2,1)} %convolution_convert_fusion.1.refs_0_.refs_1_.refs_2_, bf16[1024,1536]{1,0:T(8,128)(2,1)} %convolution_convert_fusion.1.refs_0_.refs_1_.refs_2_, ...), custom_call_target="tpu_custom_call" | custom-call | flops 6442450944 | bytes 7077888 | tf_op jit(solution)/shard_map/pallas_call | solution.py:140
  60.5 2.3 %add_convert_fusion.1 = bf16[512,768]{1,0:T(8,128)(2,1)S(1)} fusion(bf16[512,768]{1,0:T(8,128)(2,1)S(1)} %copy-done.1, bf16[512,768]{1,0:T(8,128)(2,1)} %shard_map.185, bf16[2,768,768]{2,1,0:T(8,128)(2,1)} %param.21), kind=kOutput, calls=%fused_computation.35 | convolution fusion | flops 605159424 | bytes 3538944 | tf_op jit(solution)/shard_map/dot_general | solution.py:202
  62.9 1.9 %collective-permute-start.7 = (bf16[256,768]{1,0:T(8,128)(2,1)S(1)}, bf16[256,768]{1,0:T(8,128)(2,1)S(1)}, u32[]{:S(2)}, u32[]{:S(2)}) collective-permute-start(bf16[256,768]{1,0:T(8,128)(2,1)S(1)} %get-tuple-element.16), channel_id=1, source_target_pairs={{1,0},{2,1},{3,2},{4,3},{5,4},{6,5},{7,6},{8,7},{9,8},{10,9},{11,1... | collective-permute-start | bytes 1179656 | tf_op jit(solution)/shard_map/ppermute | solution.py:26
  64.8 2.4 %collective-permute-start.6 = (bf16[256,768]{1,0:T(8,128)(2,1)S(1)}, bf16[256,768]{1,0:T(8,128)(2,1)S(1)}, u32[]{:S(2)}, u32[]{:S(2)}) collective-permute-start(bf16[256,768]{1,0:T(8,128)(2,1)S(1)} %get-tuple-element.15), channel_id=1, source_target_pairs={{0,1},{1,2},{2,3},{3,4},{4,5},{5,6},{6,7},{7,8},{8,9},{9,10},{10,1... | collective-permute-start | bytes 1179656 | tf_op jit(solution)/shard_map/ppermute | solution.py:25
  67.3 0.7 collective-permute-start.8
  67.9 2.2 %slice_bitcast_fusion = bf16[768,2304]{1,0:T(8,128)(2,1)S(1)} fusion(bf16[2,768,2304]{2,1,0:T(8,128)(2,1)} %param.20), kind=kLoop, calls=%fused_computation.10 | loop fusion | bytes 7077888 | tf_op jit(solution)/shard_map/squeeze | solution.py:185
  70.2 0.7 collective-permute-start.9
  70.9 3.4 %collective-permute-done.7 = bf16[256,768]{1,0:T(8,128)(2,1)S(1)} collective-permute-done((bf16[256,768]{1,0:T(8,128)(2,1)S(1)}, bf16[256,768]{1,0:T(8,128)(2,1)S(1)}, u32[]{:S(2)}, u32[]{:S(2)}) %collective-permute-start.7) | collective-permute-done | bytes 393248 | tf_op jit(solution)/shard_map/ppermute | solution.py:26
  74.3 1.6 %collective-permute-done.6 = bf16[256,768]{1,0:T(8,128)(2,1)S(1)} collective-permute-done((bf16[256,768]{1,0:T(8,128)(2,1)S(1)}, bf16[256,768]{1,0:T(8,128)(2,1)S(1)}, u32[]{:S(2)}, u32[]{:S(2)}) %collective-permute-start.6) | collective-permute-done | bytes 393248 | tf_op jit(solution)/shard_map/ppermute | solution.py:25
  76.2 0.6 fusion.4
  76.8 0.7 broadcast_select_fusion.2
  77.5 1.5 %collective-permute-start.10 = (bf16[256,768]{1,0:T(8,128)(2,1)S(1)}, bf16[256,768]{1,0:T(8,128)(2,1)S(1)}, u32[]{:S(2)}, u32[]{:S(2)}) collective-permute-start(bf16[256,768]{1,0:T(8,128)(2,1)S(1)} %broadcast_select_fusion.2), channel_id=1, source_target_pairs={{0,2},{4,6},{8,10},{12,14},{16,18},{20,22},{24,26},{28,30}} | collective-permute-start | bytes 1179656 | tf_op jit(solution)/shard_map/ppermute | solution.py:52
  79.0 1.9 %fusion.6 = bf16[1024,768]{1,0:T(8,128)(2,1)S(1)} fusion(f32[768]{0:T(1024)S(1)} %get-tuple-element.9, f32[1024]{0:T(1024)S(1)} %add_rsqrt_fusion, f32[1024]{0:T(1024)S(1)} %broadcast_multiply_fusion, bf16[256,768]{1,0:T(8,128)(2,1)S(1)} %collective-permute-done.7, bf16[512,768]{1,0:T(8,128)(2,1)S(1)} %add_convert_fusion.1, ...), kind=kLoop, calls=%fused_computation.14 | loop fusion | flops 7864320 | bytes 3156992 | tf_op jit(solution)/shard_map/convert_element_type | solution.py:64
  80.9 10.8 %collective-permute-done.10 = bf16[256,768]{1,0:T(8,128)(2,1)S(1)} collective-permute-done((bf16[256,768]{1,0:T(8,128)(2,1)S(1)}, bf16[256,768]{1,0:T(8,128)(2,1)S(1)}, u32[]{:S(2)}, u32[]{:S(2)}) %collective-permute-start.10) | collective-permute-done | bytes 393248 | tf_op jit(solution)/shard_map/ppermute | solution.py:52
  91.7 0.7 broadcast_select_fusion.4
  92.4 1.3 %collective-permute-start.11 = (bf16[256,768]{1,0:T(8,128)(2,1)S(1)}, bf16[256,768]{1,0:T(8,128)(2,1)S(1)}, u32[]{:S(2)}, u32[]{:S(2)}) collective-permute-start(bf16[256,768]{1,0:T(8,128)(2,1)S(1)} %broadcast_select_fusion.4), channel_id=1, source_target_pairs={{0,1},{2,3},{4,5},{6,7},{8,9},{10,11},{12,13},{14,15},{16,17},{18,... | collective-permute-start | bytes 1179656 | tf_op jit(solution)/shard_map/ppermute | solution.py:52
  93.7 4.0 %convolution_convert_fusion.refs_0_.refs_1_.refs_2_ = bf16[1024,1536]{1,0:T(8,128)(2,1)} fusion(bf16[1024,768]{1,0:T(8,128)(2,1)S(1)} %fusion.6, bf16[768,2304]{1,0:T(8,128)(2,1)S(1)} %slice_bitcast_fusion), kind=kOutput, calls=%fused_computation.4 | convolution fusion | flops 2417491968 | bytes 7077888 | tf_op jit(solution)/shard_map/dot_general | solution.py:189
  97.7 1.7 %multiply_convert_fusion.q_ref = bf16[512,768]{1,0:T(8,128)(2,1)} fusion(bf16[768,2304]{1,0:T(8,128)(2,1)S(1)} %slice_bitcast_fusion, bf16[1024,768]{1,0:T(8,128)(2,1)S(1)} %fusion.6), kind=kOutput, calls=%fused_computation.34 | convolution fusion | flops 604766208 | bytes 2752512 | tf_op jit(solution)/shard_map/dot_general | solution.py:194
  99.4 0.9 convert_reduce_fusion.3
  100.5 1.8 %convolution_convert_fusion.2.refs_3_ = bf16[256,1536]{1,0:T(8,128)(2,1)} fusion(bf16[768,2304]{1,0:T(8,128)(2,1)S(1)} %slice_bitcast_fusion, bf16[256,768]{1,0:T(8,128)(2,1)S(1)} %get-tuple-element.12, f32[768]{0:T(1024)S(1)} %get-tuple-element.9, f32[256]{0:T(256)S(1)} %add_rsqrt_fusion.3, f32[256]{0:T(256)S(1)} %broadcast_multiply_fusion.3), kind=kOutput, calls=%fused_computation.18 | convolution fusion | flops 605356032 | bytes 3545088 | tf_op jit(solution)/shard_map/dot_general | solution.py:196
  102.3 15.6 %shard_map.186 = bf16[512,768]{1,0:T(8,128)(2,1)} custom-call(s32[2]{0:T(128)} %pad_add_fusion.pos_ref, bf16[512,768]{1,0:T(8,128)(2,1)} %multiply_convert_fusion.q_ref, bf16[1024,1536]{1,0:T(8,128)(2,1)} %convolution_convert_fusion.refs_0_.refs_1_.refs_2_, bf16[1024,1536]{1,0:T(8,128)(2,1)} %convolution_convert_fusion.refs_0_.refs_1_.refs_2_, ...), custom_call_target="tpu_custom_call" | custom-call | flops 6442450944 | bytes 7077888 | tf_op jit(solution)/shard_map/pallas_call | solution.py:140
  117.9 2.4 %convert_reduce_fusion.2 = (f32[512]{0:T(512)S(1)}, bf16[512,768]{1,0:T(8,128)(2,1)S(1)}) fusion(bf16[512,768]{1,0:T(8,128)(2,1)} %shard_map.186, bf16[2,768,768]{2,1,0:T(8,128)(2,1)} %param.21, bf16[512,768]{1,0:T(8,128)(2,1)S(1)} %add_convert_fusion.1), kind=kOutput, calls=%fused_computation.25 | convolution fusion | flops 605945344 | bytes 3540992 | tf_op jit(solution)/shard_map/dot_general | solution.py:202
  120.4 0.4 fusion.16
  120.7 0.8 fusion.35
  122.0 0.6 multiply_add_fusion
  (52 shorter events, 1.5 us)
Async XLA Ops:
  0.6 120.1 %copy-start = (bf16[768,512]{1,0:T(8,128)(2,1)S(1)}, bf16[768,512]{1,0:T(8,128)(2,1)}, u32[]{:S(2)}) copy-start(bf16[768,512]{1,0:T(8,128)(2,1)} %param.23) | copy-start | bytes 2359300
  1.7 6.8 %copy-start.11 = (s32[2]{0:T(128)S(1)}, s32[2]{0:T(128)}, u32[]{:S(2)}) copy-start(s32[2]{0:T(128)} %constant.49.clone) | copy-start | bytes 28
  1.8 7.4 %copy-start.1 = (bf16[512,768]{1,0:T(8,128)(2,1)S(1)}, bf16[512,768]{1,0:T(8,128)(2,1)}, u32[]{:S(2)}) copy-start(bf16[512,768]{1,0:T(8,128)(2,1)} %param.18) | copy-start | bytes 2359300
  1.8 9.9 %copy-start.10 = (s32[4]{0:T(128)S(1)}, s32[4]{0:T(128)}, u32[]{:S(2)}) copy-start(s32[4]{0:T(128)} %constant.50.clone) | copy-start | bytes 52
  1.8 10.6 %copy-start.9 = (s32[8]{0:T(128)S(1)}, s32[8]{0:T(128)}, u32[]{:S(2)}) copy-start(s32[8]{0:T(128)} %constant.51.clone) | copy-start | bytes 100
  1.8 11.3 %copy-start.4 = (f32[2,768]{1,0:T(2,128)S(1)}, f32[2,768]{1,0:T(2,128)}, u32[]{:S(2)}) copy-start(f32[2,768]{1,0:T(2,128)} %param.19) | copy-start | bytes 18436
  1.8 13.3 %collective-permute-start.1 = (bf16[256,768]{1,0:T(8,128)(2,1)S(1)}, bf16[256,768]{1,0:T(8,128)(2,1)S(1)}, u32[]{:S(2)}, u32[]{:S(2)}) collective-permute-start(bf16[256,768]{1,0:T(8,128)(2,1)S(1)} %slice.61), channel_id=1, source_target_pairs={{1,0},{2,1},{3,2},{4,3},{5,4},{6,5},{7,6},{8,7},{9,8},{10,9},{11,1... | collective-permute-start | bytes 1179656 | tf_op jit(solution)/shard_map/ppermute | solution.py:26
  3.9 5.3 %collective-permute-start.2 = (bf16[256,768]{1,0:T(8,128)(2,1)S(1)}, bf16[256,768]{1,0:T(8,128)(2,1)S(1)}, u32[]{:S(2)}, u32[]{:S(2)}) collective-permute-start(bf16[256,768]{1,0:T(8,128)(2,1)S(1)} %slice.61), channel_id=1, source_target_pairs={{0,8},{16,24}} | collective-permute-start | bytes 1179656 | tf_op jit(solution)/shard_map/ppermute | solution.py:52
  9.3 9.1 %collective-permute-start = (bf16[256,768]{1,0:T(8,128)(2,1)S(1)}, bf16[256,768]{1,0:T(8,128)(2,1)S(1)}, u32[]{:S(2)}, u32[]{:S(2)}) collective-permute-start(bf16[256,768]{1,0:T(8,128)(2,1)S(1)} %get-tuple-element.18), channel_id=1, source_target_pairs={{0,1},{1,2},{2,3},{3,4},{4,5},{5,6},{6,7},{7,8},{8,9},{9,10},{10,1... | collective-permute-start | bytes 1179656 | tf_op jit(solution)/shard_map/ppermute | solution.py:25
  13.1 5.5 %collective-permute-start.3 = (bf16[256,768]{1,0:T(8,128)(2,1)S(1)}, bf16[256,768]{1,0:T(8,128)(2,1)S(1)}, u32[]{:S(2)}, u32[]{:S(2)}) collective-permute-start(bf16[256,768]{1,0:T(8,128)(2,1)S(1)} %get-tuple-element.17), channel_id=1, source_target_pairs={{0,4},{8,12},{16,20},{24,28}} | collective-permute-start | bytes 1179656 | tf_op jit(solution)/shard_map/ppermute | solution.py:52
  19.3 17.0 %copy-start.2 = (bf16[768,2304]{1,0:T(8,128)(2,1)S(1)}, bf16[768,2304]{1,0:T(8,128)(2,1)}, u32[]{:S(2)}) copy-start(bf16[768,2304]{1,0:T(8,128)(2,1)} %slice_bitcast_fusion.1) | copy-start | bytes 10616836
  19.3 14.8 %collective-permute-start.4 = (bf16[256,768]{1,0:T(8,128)(2,1)S(1)}, bf16[256,768]{1,0:T(8,128)(2,1)S(1)}, u32[]{:S(2)}, u32[]{:S(2)}) collective-permute-start(bf16[256,768]{1,0:T(8,128)(2,1)S(1)} %broadcast_select_fusion.3), channel_id=1, source_target_pairs={{0,2},{4,6},{8,10},{12,14},{16,18},{20,22},{24,26},{28,30}} | collective-permute-start | bytes 1179656 | tf_op jit(solution)/shard_map/ppermute | solution.py:52
  34.8 7.2 %collective-permute-start.5 = (bf16[256,768]{1,0:T(8,128)(2,1)S(1)}, bf16[256,768]{1,0:T(8,128)(2,1)S(1)}, u32[]{:S(2)}, u32[]{:S(2)}) collective-permute-start(bf16[256,768]{1,0:T(8,128)(2,1)S(1)} %broadcast_select_fusion.5), channel_id=1, source_target_pairs={{0,1},{2,3},{4,5},{6,7},{8,9},{10,11},{12,13},{14,15},{16,17},{18,... | collective-permute-start | bytes 1179656 | tf_op jit(solution)/shard_map/ppermute | solution.py:52
  62.9 11.4 %collective-permute-start.7 = (bf16[256,768]{1,0:T(8,128)(2,1)S(1)}, bf16[256,768]{1,0:T(8,128)(2,1)S(1)}, u32[]{:S(2)}, u32[]{:S(2)}) collective-permute-start(bf16[256,768]{1,0:T(8,128)(2,1)S(1)} %get-tuple-element.16), channel_id=1, source_target_pairs={{1,0},{2,1},{3,2},{4,3},{5,4},{6,5},{7,6},{8,7},{9,8},{10,9},{11,1... | collective-permute-start | bytes 1179656 | tf_op jit(solution)/shard_map/ppermute | solution.py:26
  64.8 11.0 %collective-permute-start.6 = (bf16[256,768]{1,0:T(8,128)(2,1)S(1)}, bf16[256,768]{1,0:T(8,128)(2,1)S(1)}, u32[]{:S(2)}, u32[]{:S(2)}) collective-permute-start(bf16[256,768]{1,0:T(8,128)(2,1)S(1)} %get-tuple-element.15), channel_id=1, source_target_pairs={{0,1},{1,2},{2,3},{3,4},{4,5},{5,6},{6,7},{7,8},{8,9},{9,10},{10,1... | collective-permute-start | bytes 1179656 | tf_op jit(solution)/shard_map/ppermute | solution.py:25
  67.3 2.9 %collective-permute-start.8 = (bf16[256,768]{1,0:T(8,128)(2,1)S(1)}, bf16[256,768]{1,0:T(8,128)(2,1)S(1)}, u32[]{:S(2)}, u32[]{:S(2)}) collective-permute-start(bf16[256,768]{1,0:T(8,128)(2,1)S(1)} %slice.85), channel_id=1, source_target_pairs={{0,8},{16,24}} | collective-permute-start | bytes 1179656 | tf_op jit(solution)/shard_map/ppermute | solution.py:52
  70.2 6.6 %collective-permute-start.9 = (bf16[256,768]{1,0:T(8,128)(2,1)S(1)}, bf16[256,768]{1,0:T(8,128)(2,1)S(1)}, u32[]{:S(2)}, u32[]{:S(2)}) collective-permute-start(bf16[256,768]{1,0:T(8,128)(2,1)S(1)} %broadcast_select_fusion), channel_id=1, source_target_pairs={{0,4},{8,12},{16,20},{24,28}} | collective-permute-start | bytes 1179656 | tf_op jit(solution)/shard_map/ppermute | solution.py:52
  77.5 14.2 %collective-permute-start.10 = (bf16[256,768]{1,0:T(8,128)(2,1)S(1)}, bf16[256,768]{1,0:T(8,128)(2,1)S(1)}, u32[]{:S(2)}, u32[]{:S(2)}) collective-permute-start(bf16[256,768]{1,0:T(8,128)(2,1)S(1)} %broadcast_select_fusion.2), channel_id=1, source_target_pairs={{0,2},{4,6},{8,10},{12,14},{16,18},{20,22},{24,26},{28,30}} | collective-permute-start | bytes 1179656 | tf_op jit(solution)/shard_map/ppermute | solution.py:52
  92.4 7.0 %collective-permute-start.11 = (bf16[256,768]{1,0:T(8,128)(2,1)S(1)}, bf16[256,768]{1,0:T(8,128)(2,1)S(1)}, u32[]{:S(2)}, u32[]{:S(2)}) collective-permute-start(bf16[256,768]{1,0:T(8,128)(2,1)S(1)} %broadcast_select_fusion.4), channel_id=1, source_target_pairs={{0,1},{2,3},{4,5},{6,7},{8,9},{10,11},{12,13},{14,15},{16,17},{18,... | collective-permute-start | bytes 1179656 | tf_op jit(solution)/shard_map/ppermute | solution.py:52
  117.9 2.8 %copy-start.8 = (f32[768]{0:T(1024)S(1)}, f32[768]{0:T(1024)}, u32[]{:S(2)}) copy-start(f32[768]{0:T(1024)} %param.22) | copy-start | bytes 9220
  120.3 1.4 %copy-start.5 = (s32[512]{0:T(512)S(1)}, s32[512]{0:T(512)}, u32[]{:S(2)}) copy-start(s32[512]{0:T(512)} %param.24) | copy-start | bytes 6148
  120.3 1.6 %copy-start.6 = (f32[512]{0:T(512)S(1)}, f32[512]{0:T(512)}, u32[]{:S(2)}) copy-start(f32[512]{0:T(512)} %param.26) | copy-start | bytes 6148
  120.3 1.6 %copy-start.7 = (s32[512]{0:T(512)S(1)}, s32[512]{0:T(512)}, u32[]{:S(2)}) copy-start(s32[512]{0:T(512)} %param.25) | copy-start | bytes 6148
  121.9 0.6 copy-start.3

commit v14 on v12

--- a/solution.py
+++ b/solution.py
@@ -44,9 +44,11 @@
     return rounds
 
 
-def spread(block, axis):
+def spread(block, axis, hold=None):
     place = lax.axis_index(axis)
-    for ops in tree_rounds(lax.axis_size(axis)):
+    for round_idx, ops in enumerate(tree_rounds(lax.axis_size(axis))):
+        if round_idx == 1 and hold is not None:
+            block, hold = lax.optimization_barrier((block, hold))
         received = block
         for op in ops:
             got = lax.ppermute(block, axis, op)
@@ -180,7 +182,6 @@
         gain = ln_gain[layer_idx]
         weights = w_qkv[layer_idx]
         extended = with_halo(hidden_state, (("seq", 0),), HALF)
-        prompt_rows = spread(prompt_source, "seq")
         extended_normed = layer_norm(extended, gain)
         band_kv = jnp.dot(
             extended_normed, weights[:, feat_width:], preferred_element_type=jnp.float32
@@ -189,6 +190,7 @@
         queries = (
             jnp.dot(normed, weights[:, :feat_width], preferred_element_type=jnp.float32) * 0.125
         ).astype(jnp.bfloat16)
+        prompt_rows = spread(prompt_source, "seq", hold=(band_kv, queries))
         prompt_kv = jnp.dot(
             layer_norm(prompt_rows, gain),
             weights[:, feat_width:],

time: 122 us -> 145 us (1.19); the launches traced: 122 us -> 143 us
  waiting for transfers between devices: 29.2 us -> 48.2 us
  matrix products: 20.4 us -> 22.1 us
    ppermute x8, waiting for transfers between devices: 18 us -> 34.8 us  [spread(): got = lax.ppermute(block, axis, op)]
    dot_general x2, matrix products: 3.51 us -> 5.18 us  [per_device(): jnp.dot(layer_norm(prompt_rows, gain), weights[:, feat_width:], preferred...]
  transfers between devices with their start and end apart: 12 -> 12, of which waited for: 5 -> 6; matrix products, arithmetic and copies ran while one was open for 21% -> 6% of each run, Pallas kernels for 0% -> 0%
where the time goes in v14:
time: 145 us; the launch traced here: 143 us
  waiting for transfers between devices  48.2 us (33%)
  Pallas kernels  31.3 us (22%)
  matrix products  22.1 us (15%)
  starting transfers between devices  17.1 us (12%)
  other arithmetic  15.6 us (11%)
  local copies, waits for them, and re-layouts  6.51 us (4%)
  between operations  1.7 us (1%)
    ppermute x8, waiting for transfers between devices, spread(): got = lax.ppermute(block, axis, op)  34.8 us
    pallas_call x2, Pallas kernels, attention(): pl.pallas_call(functools.partial(attention_kernel, row0), out_shape=jax.S...  31.3 us
    ppermute x2, waiting for transfers between devices, with_halo(): before = lax.ppermute(last, axis, up)  10.6 us
    ppermute x8, starting transfers between devices, spread(): got = lax.ppermute(block, axis, op)  8.33 us
    dot_general x2, matrix products, per_device(): jnp.dot(extended_normed, weights[:, feat_width:], preferred_element_type=...  8.09 us
    squeeze x1, local copies, waits for them, and re-layouts, per_device(): weights = w_qkv[layer_idx]  5.3 us
    dot_general x2, matrix products, per_device(): jnp.dot(layer_norm(prompt_rows, gain), weights[:, feat_width:], preferred...  5.18 us
    ppermute x2, starting transfers between devices, with_halo(): before = lax.ppermute(last, axis, up)  4.94 us
  transfers between devices with their start and end apart: 12, of which 6 were waited for; matrix products, arithmetic and copies ran while one was open for 6% of the time, Pallas kernels for 0%

profile of v14, /device:TPU:20, one launch (start us, length us, event | category | flops | bytes accessed | tf_op | source)
XLA Modules:
  0.0 142.6 jit_solution(11949826046715420607)
XLA Ops:
  0.6 1.1 slice.59
  1.7 0.7 collective-permute-start.2
  2.4 1.9 %collective-permute-start.1 = (bf16[256,768]{1,0:T(8,128)(2,1)S(1)}, bf16[256,768]{1,0:T(8,128)(2,1)S(1)}, u32[]{:S(2)}, u32[]{:S(2)}) collective-permute-start(bf16[256,768]{1,0:T(8,128)(2,1)S(1)} %slice.59), channel_id=1, source_target_pairs={{1,0},{2,1},{3,2},{4,3},{5,4},{6,5},{7,6},{8,7},{9,8},{10,9},{11,1... | collective-permute-start | bytes 1179656 | tf_op jit(solution)/shard_map/ppermute | solution.py:26
  4.4 1.2 broadcast_select_fusion.1
  5.6 2.5 %collective-permute-start = (bf16[256,768]{1,0:T(8,128)(2,1)S(1)}, bf16[256,768]{1,0:T(8,128)(2,1)S(1)}, u32[]{:S(2)}, u32[]{:S(2)}) collective-permute-start(bf16[256,768]{1,0:T(8,128)(2,1)S(1)} %get-tuple-element.20), channel_id=1, source_target_pairs={{0,1},{1,2},{2,3},{3,4},{4,5},{5,6},{6,7},{7,8},{8,9},{9,10},{10,1... | collective-permute-start | bytes 1179656 | tf_op jit(solution)/shard_map/ppermute | solution.py:25
  8.1 5.3 %slice_bitcast_fusion = (bf16[768,2304]{1,0:T(8,128)(2,1)}, bf16[768,2304]{1,0:T(8,128)(2,1)S(1)}) fusion(bf16[2,768,2304]{2,1,0:T(8,128)(2,1)} %param.20), kind=kLoop, calls=%fused_computation.10 | loop fusion | bytes 14155776 | tf_op jit(solution)/shard_map/squeeze | solution.py:183
  13.5 3.2 %collective-permute-done = bf16[256,768]{1,0:T(8,128)(2,1)S(1)} collective-permute-done((bf16[256,768]{1,0:T(8,128)(2,1)S(1)}, bf16[256,768]{1,0:T(8,128)(2,1)S(1)}, u32[]{:S(2)}, u32[]{:S(2)}) %collective-permute-start) | collective-permute-done | bytes 393248 | tf_op jit(solution)/shard_map/ppermute | solution.py:25
  16.9 0.6 fusion.7
  17.6 1.9 %fusion.9 = bf16[1024,768]{1,0:T(8,128)(2,1)S(1)} fusion(f32[768]{0:T(1024)S(1)} %get-tuple-element.10, f32[1024]{0:T(1024)S(1)} %add_rsqrt_fusion.1, f32[1024]{0:T(1024)S(1)} %broadcast_multiply_fusion.1, bf16[256,768]{1,0:T(8,128)(2,1)S(1)} %collective-permute-done.1, bf16[512,768]{1,0:T(8,128)(2,1)S(1)} %copy-done.1, ...), kind=kLoop, calls=%fused_computation.17 | loop fusion | flops 7864320 | bytes 3156992 | tf_op jit(solution)/shard_map/convert_element_type | solution.py:66
  19.5 4.1 %convolution_convert_fusion.1.refs_0_.refs_1_.refs_2_ = bf16[1024,1536]{1,0:T(8,128)(2,1)} fusion(bf16[1024,768]{1,0:T(8,128)(2,1)S(1)} %fusion.9, bf16[768,2304]{1,0:T(8,128)(2,1)S(1)} %get-tuple-element.16), kind=kOutput, calls=%fused_computation.5 | convolution fusion | flops 2417491968 | bytes 7077888 | tf_op jit(solution)/shard_map/dot_general | solution.py:186
  23.6 1.7 %multiply_convert_fusion.1.q_ref = bf16[512,768]{1,0:T(8,128)(2,1)} fusion(bf16[768,2304]{1,0:T(8,128)(2,1)S(1)} %get-tuple-element.16, bf16[1024,768]{1,0:T(8,128)(2,1)S(1)} %fusion.9), kind=kOutput, calls=%fused_computation.36 | convolution fusion | flops 604766208 | bytes 2752512 | tf_op jit(solution)/shard_map/dot_general | solution.py:191
  25.3 0.7 collective-permute-start.3
  26.0 0.7 compare_reduce_fusion
  26.7 0.7 broadcast_select_fusion.3
  27.3 1.3 collective-permute-start.4
  28.7 0.7 compare_reduce_fusion.1
  29.3 17.7 %collective-permute-done.4 = bf16[256,768]{1,0:T(8,128)(2,1)S(1)} collective-permute-done((bf16[256,768]{1,0:T(8,128)(2,1)S(1)}, bf16[256,768]{1,0:T(8,128)(2,1)S(1)}, u32[]{:S(2)}, u32[]{:S(2)}) %collective-permute-start.4) | collective-permute-done | bytes 393248 | tf_op jit(solution)/shard_map/ppermute | solution.py:54
  47.0 0.7 broadcast_select_fusion.5
  47.7 1.5 %collective-permute-start.5 = (bf16[256,768]{1,0:T(8,128)(2,1)S(1)}, bf16[256,768]{1,0:T(8,128)(2,1)S(1)}, u32[]{:S(2)}, u32[]{:S(2)}) collective-permute-start(bf16[256,768]{1,0:T(8,128)(2,1)S(1)} %broadcast_select_fusion.5), channel_id=1, source_target_pairs={{0,1},{2,3},{4,5},{6,7},{8,9},{10,11},{12,13},{14,15},{16,17},{18,... | collective-permute-start | bytes 1179656 | tf_op jit(solution)/shard_map/ppermute | solution.py:54
  49.2 0.6 pad_add_fusion.pos_ref
  49.8 0.6 compare_reduce_fusion.2
  50.5 0.8 convert_reduce_fusion.4
  51.6 3.4 %convolution_convert_fusion.3.refs_3_ = bf16[256,1536]{1,0:T(8,128)(2,1)} fusion(bf16[768,2304]{1,0:T(8,128)(2,1)} %copy-done.3, bf16[256,768]{1,0:T(8,128)(2,1)S(1)} %get-tuple-element.14, f32[768]{0:T(1024)S(1)} %get-tuple-element.10, f32[256]{0:T(256)S(1)} %add_rsqrt_fusion.4, f32[256]{0:T(256)S(1)} %broadcast_multiply_fusion.4), kind=kOutput, calls=%fused_computation.19 | convolution fusion | flops 605356032 | bytes 3544064 | tf_op jit(solution)/shard_map/dot_general | solution.py:194
  55.0 15.6 %shard_map.185 = bf16[512,768]{1,0:T(8,128)(2,1)} custom-call(s32[2]{0:T(128)} %pad_add_fusion.pos_ref, bf16[512,768]{1,0:T(8,128)(2,1)} %multiply_convert_fusion.1.q_ref, bf16[1024,1536]{1,0:T(8,128)(2,1)} %convolution_convert_fusion.1.refs_0_.refs_1_.refs_2_, bf16[1024,1536]{1,0:T(8,128)(2,1)} %convolution_convert_fusion.1.refs_0_.refs_1_.refs_2_, ...), custom_call_target="tpu_custom_call" | custom-call | flops 6442450944 | bytes 7077888 | tf_op jit(solution)/shard_map/pallas_call | solution.py:142
  70.6 2.3 %add_convert_fusion.1 = bf16[512,768]{1,0:T(8,128)(2,1)S(1)} fusion(bf16[512,768]{1,0:T(8,128)(2,1)S(1)} %copy-done.1, bf16[512,768]{1,0:T(8,128)(2,1)} %shard_map.185, bf16[2,768,768]{2,1,0:T(8,128)(2,1)} %param.21), kind=kOutput, calls=%fused_computation.35 | convolution fusion | flops 605159424 | bytes 3538944 | tf_op jit(solution)/shard_map/dot_general | solution.py:200
  73.0 0.7 collective-permute-start.8
  73.7 1.9 %collective-permute-start.7 = (bf16[256,768]{1,0:T(8,128)(2,1)S(1)}, bf16[256,768]{1,0:T(8,128)(2,1)S(1)}, u32[]{:S(2)}, u32[]{:S(2)}) collective-permute-start(bf16[256,768]{1,0:T(8,128)(2,1)S(1)} %slice.80), channel_id=1, source_target_pairs={{1,0},{2,1},{3,2},{4,3},{5,4},{6,5},{7,6},{8,7},{9,8},{10,9},{11,1... | collective-permute-start | bytes 1179656 | tf_op jit(solution)/shard_map/ppermute | solution.py:26
  75.7 2.4 %collective-permute-start.6 = (bf16[256,768]{1,0:T(8,128)(2,1)S(1)}, bf16[256,768]{1,0:T(8,128)(2,1)S(1)}, u32[]{:S(2)}, u32[]{:S(2)}) collective-permute-start(bf16[256,768]{1,0:T(8,128)(2,1)S(1)} %get-tuple-element.18), channel_id=1, source_target_pairs={{0,1},{1,2},{2,3},{3,4},{4,5},{5,6},{6,7},{7,8},{8,9},{9,10},{10,1... | collective-permute-start | bytes 1179656 | tf_op jit(solution)/shard_map/ppermute | solution.py:25
  78.1 2.8 %collective-permute-done.7 = bf16[256,768]{1,0:T(8,128)(2,1)S(1)} collective-permute-done((bf16[256,768]{1,0:T(8,128)(2,1)S(1)}, bf16[256,768]{1,0:T(8,128)(2,1)S(1)}, u32[]{:S(2)}, u32[]{:S(2)}) %collective-permute-start.7) | collective-permute-done | bytes 393248 | tf_op jit(solution)/shard_map/ppermute | solution.py:26
  80.9 7.5 %collective-permute-done.6 = bf16[256,768]{1,0:T(8,128)(2,1)S(1)} collective-permute-done((bf16[256,768]{1,0:T(8,128)(2,1)S(1)}, bf16[256,768]{1,0:T(8,128)(2,1)S(1)}, u32[]{:S(2)}, u32[]{:S(2)}) %collective-permute-start.6) | collective-permute-done | bytes 393248 | tf_op jit(solution)/shard_map/ppermute | solution.py:25
  88.6 0.6 fusion.4
  89.3 1.9 %fusion.6 = bf16[1024,768]{1,0:T(8,128)(2,1)S(1)} fusion(f32[768]{0:T(1024)S(1)} %get-tuple-element.9, f32[1024]{0:T(1024)S(1)} %add_rsqrt_fusion, f32[1024]{0:T(1024)S(1)} %broadcast_multiply_fusion, bf16[256,768]{1,0:T(8,128)(2,1)S(1)} %collective-permute-done.7, bf16[512,768]{1,0:T(8,128)(2,1)S(1)} %add_convert_fusion.1, ...), kind=kLoop, calls=%fused_computation.14 | loop fusion | flops 7864320 | bytes 3156992 | tf_op jit(solution)/shard_map/convert_element_type | solution.py:66
  91.1 4.0 %convolution_convert_fusion.refs_0_.refs_1_.refs_2_ = bf16[1024,1536]{1,0:T(8,128)(2,1)} fusion(bf16[1024,768]{1,0:T(8,128)(2,1)S(1)} %fusion.6, bf16[768,2304]{1,0:T(8,128)(2,1)S(1)} %copy-done.2), kind=kOutput, calls=%fused_computation.4 | convolution fusion | flops 2417491968 | bytes 7077888 | tf_op jit(solution)/shard_map/dot_general | solution.py:186
  95.2 1.7 %multiply_convert_fusion.q_ref = bf16[512,768]{1,0:T(8,128)(2,1)} fusion(bf16[768,2304]{1,0:T(8,128)(2,1)S(1)} %copy-done.2, bf16[1024,768]{1,0:T(8,128)(2,1)S(1)} %fusion.6), kind=kOutput, calls=%fused_computation.34 | convolution fusion | flops 604766208 | bytes 2752512 | tf_op jit(solution)/shard_map/dot_general | solution.py:191
  96.8 0.7 collective-permute-start.9
  97.5 0.7 broadcast_select_fusion.2
  98.2 1.3 collective-permute-start.10
  99.5 16.4 %collective-permute-done.10 = bf16[256,768]{1,0:T(8,128)(2,1)S(1)} collective-permute-done((bf16[256,768]{1,0:T(8,128)(2,1)S(1)}, bf16[256,768]{1,0:T(8,128)(2,1)S(1)}, u32[]{:S(2)}, u32[]{:S(2)}) %collective-permute-start.10) | collective-permute-done | bytes 393248 | tf_op jit(solution)/shard_map/ppermute | solution.py:54
  115.9 0.7 broadcast_select_fusion.4
  116.6 1.5 %collective-permute-start.11 = (bf16[256,768]{1,0:T(8,128)(2,1)S(1)}, bf16[256,768]{1,0:T(8,128)(2,1)S(1)}, u32[]{:S(2)}, u32[]{:S(2)}) collective-permute-start(bf16[256,768]{1,0:T(8,128)(2,1)S(1)} %broadcast_select_fusion.4), channel_id=1, source_target_pairs={{0,1},{2,3},{4,5},{6,7},{8,9},{10,11},{12,13},{14,15},{16,17},{18,... | collective-permute-start | bytes 1179656 | tf_op jit(solution)/shard_map/ppermute | solution.py:54
  118.8 0.7 collective-permute-done.11
  119.5 0.8 convert_reduce_fusion.3
  120.6 1.8 %convolution_convert_fusion.2.refs_3_ = bf16[256,1536]{1,0:T(8,128)(2,1)} fusion(bf16[768,2304]{1,0:T(8,128)(2,1)S(1)} %copy-done.2, bf16[256,768]{1,0:T(8,128)(2,1)S(1)} %get-tuple-element.12, f32[768]{0:T(1024)S(1)} %get-tuple-element.9, f32[256]{0:T(256)S(1)} %add_rsqrt_fusion.3, f32[256]{0:T(256)S(1)} %broadcast_multiply_fusion.3), kind=kOutput, calls=%fused_computation.18 | convolution fusion | flops 605356032 | bytes 3545088 | tf_op jit(solution)/shard_map/dot_general | solution.py:194
  122.3 15.6 %shard_map.186 = bf16[512,768]{1,0:T(8,128)(2,1)} custom-call(s32[2]{0:T(128)} %pad_add_fusion.pos_ref, bf16[512,768]{1,0:T(8,128)(2,1)} %multiply_convert_fusion.q_ref, bf16[1024,1536]{1,0:T(8,128)(2,1)} %convolution_convert_fusion.refs_0_.refs_1_.refs_2_, bf16[1024,1536]{1,0:T(8,128)(2,1)} %convolution_convert_fusion.refs_0_.refs_1_.refs_2_, ...), custom_call_target="tpu_custom_call" | custom-call | flops 6442450944 | bytes 7077888 | tf_op jit(solution)/shard_map/pallas_call | solution.py:142
  138.0 2.4 %convert_reduce_fusion.2 = (f32[512]{0:T(512)S(1)}, bf16[512,768]{1,0:T(8,128)(2,1)S(1)}) fusion(bf16[512,768]{1,0:T(8,128)(2,1)} %shard_map.186, bf16[2,768,768]{2,1,0:T(8,128)(2,1)} %param.21, bf16[512,768]{1,0:T(8,128)(2,1)S(1)} %add_convert_fusion.1), kind=kOutput, calls=%fused_computation.25 | convolution fusion | flops 605945344 | bytes 3540992 | tf_op jit(solution)/shard_map/dot_general | solution.py:200
  140.4 0.4 fusion.16
  140.8 0.8 fusion.35
  142.0 0.6 multiply_add_fusion
  (52 shorter events, 1.7 us)
Async XLA Ops:
  0.6 140.1 %copy-start = (bf16[768,512]{1,0:T(8,128)(2,1)S(1)}, bf16[768,512]{1,0:T(8,128)(2,1)}, u32[]{:S(2)}) copy-start(bf16[768,512]{1,0:T(8,128)(2,1)} %param.23) | copy-start | bytes 2359300
  1.7 2.6 %collective-permute-start.2 = (bf16[256,768]{1,0:T(8,128)(2,1)S(1)}, bf16[256,768]{1,0:T(8,128)(2,1)S(1)}, u32[]{:S(2)}, u32[]{:S(2)}) collective-permute-start(bf16[256,768]{1,0:T(8,128)(2,1)S(1)} %slice.59), channel_id=1, source_target_pairs={{0,8},{16,24}} | collective-permute-start | bytes 1179656 | tf_op jit(solution)/shard_map/ppermute | solution.py:54
  2.4 11.0 %collective-permute-start.1 = (bf16[256,768]{1,0:T(8,128)(2,1)S(1)}, bf16[256,768]{1,0:T(8,128)(2,1)S(1)}, u32[]{:S(2)}, u32[]{:S(2)}) collective-permute-start(bf16[256,768]{1,0:T(8,128)(2,1)S(1)} %slice.59), channel_id=1, source_target_pairs={{1,0},{2,1},{3,2},{4,3},{5,4},{6,5},{7,6},{8,7},{9,8},{10,9},{11,1... | collective-permute-start | bytes 1179656 | tf_op jit(solution)/shard_map/ppermute | solution.py:26
  5.6 7.9 %copy-start.5 = (f32[2,768]{1,0:T(2,128)S(1)}, f32[2,768]{1,0:T(2,128)}, u32[]{:S(2)}) copy-start(f32[2,768]{1,0:T(2,128)} %param.19) | copy-start | bytes 18436
  5.6 11.1 %copy-start.1 = (bf16[512,768]{1,0:T(8,128)(2,1)S(1)}, bf16[512,768]{1,0:T(8,128)(2,1)}, u32[]{:S(2)}) copy-start(bf16[512,768]{1,0:T(8,128)(2,1)} %param.18) | copy-start | bytes 2359300
  5.6 11.1 %collective-permute-start = (bf16[256,768]{1,0:T(8,128)(2,1)S(1)}, bf16[256,768]{1,0:T(8,128)(2,1)S(1)}, u32[]{:S(2)}, u32[]{:S(2)}) collective-permute-start(bf16[256,768]{1,0:T(8,128)(2,1)S(1)} %get-tuple-element.20), channel_id=1, source_target_pairs={{0,1},{1,2},{2,3},{3,4},{4,5},{5,6},{6,7},{7,8},{8,9},{9,10},{10,1... | collective-permute-start | bytes 1179656 | tf_op jit(solution)/shard_map/ppermute | solution.py:25
  13.4 10.1 %copy-start.3 = (bf16[768,2304]{1,0:T(8,128)(2,1)}, bf16[768,2304]{1,0:T(8,128)(2,1)S(1)}, u32[]{:S(2)}) copy-start(bf16[768,2304]{1,0:T(8,128)(2,1)S(1)} %get-tuple-element.16) | copy-start | bytes 10616836
  23.6 2.4 %copy-start.12 = (s32[2]{0:T(128)S(1)}, s32[2]{0:T(128)}, u32[]{:S(2)}) copy-start(s32[2]{0:T(128)} %constant.49.clone) | copy-start | bytes 28
  23.6 5.1 %copy-start.11 = (s32[4]{0:T(128)S(1)}, s32[4]{0:T(128)}, u32[]{:S(2)}) copy-start(s32[4]{0:T(128)} %constant.50.clone) | copy-start | bytes 52
  23.6 26.3 %copy-start.10 = (s32[8]{0:T(128)S(1)}, s32[8]{0:T(128)}, u32[]{:S(2)}) copy-start(s32[8]{0:T(128)} %constant.51.clone) | copy-start | bytes 100
  25.3 1.4 collective-permute-start.3
  27.3 19.7 %collective-permute-start.4 = (bf16[256,768]{1,0:T(8,128)(2,1)S(1)}, bf16[256,768]{1,0:T(8,128)(2,1)S(1)}, u32[]{:S(2)}, u32[]{:S(2)}) collective-permute-start(bf16[256,768]{1,0:T(8,128)(2,1)S(1)} %broadcast_select_fusion.3), channel_id=1, source_target_pairs={{0,2},{4,6},{8,10},{12,14},{16,18},{20,22},{24,26},{28,30}} | collective-permute-start | bytes 1179656 | tf_op jit(solution)/shard_map/ppermute | solution.py:54
  47.7 2.7 %collective-permute-start.5 = (bf16[256,768]{1,0:T(8,128)(2,1)S(1)}, bf16[256,768]{1,0:T(8,128)(2,1)S(1)}, u32[]{:S(2)}, u32[]{:S(2)}) collective-permute-start(bf16[256,768]{1,0:T(8,128)(2,1)S(1)} %broadcast_select_fusion.5), channel_id=1, source_target_pairs={{0,1},{2,3},{4,5},{6,7},{8,9},{10,11},{12,13},{14,15},{16,17},{18,... | collective-permute-start | bytes 1179656 | tf_op jit(solution)/shard_map/ppermute | solution.py:54
  73.0 2.6 %collective-permute-start.8 = (bf16[256,768]{1,0:T(8,128)(2,1)S(1)}, bf16[256,768]{1,0:T(8,128)(2,1)S(1)}, u32[]{:S(2)}, u32[]{:S(2)}) collective-permute-start(bf16[256,768]{1,0:T(8,128)(2,1)S(1)} %slice.80), channel_id=1, source_target_pairs={{0,8},{16,24}} | collective-permute-start | bytes 1179656 | tf_op jit(solution)/shard_map/ppermute | solution.py:54
  73.7 7.2 %collective-permute-start.7 = (bf16[256,768]{1,0:T(8,128)(2,1)S(1)}, bf16[256,768]{1,0:T(8,128)(2,1)S(1)}, u32[]{:S(2)}, u32[]{:S(2)}) collective-permute-start(bf16[256,768]{1,0:T(8,128)(2,1)S(1)} %slice.80), channel_id=1, source_target_pairs={{1,0},{2,1},{3,2},{4,3},{5,4},{6,5},{7,6},{8,7},{9,8},{10,9},{11,1... | collective-permute-start | bytes 1179656 | tf_op jit(solution)/shard_map/ppermute | solution.py:26
  75.7 12.6 %collective-permute-start.6 = (bf16[256,768]{1,0:T(8,128)(2,1)S(1)}, bf16[256,768]{1,0:T(8,128)(2,1)S(1)}, u32[]{:S(2)}, u32[]{:S(2)}) collective-permute-start(bf16[256,768]{1,0:T(8,128)(2,1)S(1)} %get-tuple-element.18), channel_id=1, source_target_pairs={{0,1},{1,2},{2,3},{3,4},{4,5},{5,6},{6,7},{7,8},{8,9},{9,10},{10,1... | collective-permute-start | bytes 1179656 | tf_op jit(solution)/shard_map/ppermute | solution.py:25
  88.6 2.5 %copy-start.2 = (bf16[768,2304]{1,0:T(8,128)(2,1)S(1)}, bf16[768,2304]{1,0:T(8,128)(2,1)}, u32[]{:S(2)}) copy-start(bf16[768,2304]{1,0:T(8,128)(2,1)} %get-tuple-element.15) | copy-start | bytes 10616836
  96.8 0.7 collective-permute-start.9
  98.2 17.7 %collective-permute-start.10 = (bf16[256,768]{1,0:T(8,128)(2,1)S(1)}, bf16[256,768]{1,0:T(8,128)(2,1)S(1)}, u32[]{:S(2)}, u32[]{:S(2)}) collective-permute-start(bf16[256,768]{1,0:T(8,128)(2,1)S(1)} %broadcast_select_fusion.2), channel_id=1, source_target_pairs={{0,2},{4,6},{8,10},{12,14},{16,18},{20,22},{24,26},{28,30}} | collective-permute-start | bytes 1179656 | tf_op jit(solution)/shard_map/ppermute | solution.py:54
  116.6 2.8 %collective-permute-start.11 = (bf16[256,768]{1,0:T(8,128)(2,1)S(1)}, bf16[256,768]{1,0:T(8,128)(2,1)S(1)}, u32[]{:S(2)}, u32[]{:S(2)}) collective-permute-start(bf16[256,768]{1,0:T(8,128)(2,1)S(1)} %broadcast_select_fusion.4), channel_id=1, source_target_pairs={{0,1},{2,3},{4,5},{6,7},{8,9},{10,11},{12,13},{14,15},{16,17},{18,... | collective-permute-start | bytes 1179656 | tf_op jit(solution)/shard_map/ppermute | solution.py:54
  138.0 2.8 %copy-start.9 = (f32[768]{0:T(1024)S(1)}, f32[768]{0:T(1024)}, u32[]{:S(2)}) copy-start(f32[768]{0:T(1024)} %param.22) | copy-start | bytes 9220
  140.3 1.4 copy-start.6
  140.8 1.2 copy-start.7
  140.8 1.2 copy-start.8
  142.0 0.6 copy-start.4

commit v15 on v12

--- a/solution.py
+++ b/solution.py
@@ -69,12 +69,12 @@
 
 
 def attention_kernel(row0, pos_ref, q_ref, *refs):
-    band_refs = refs[:-2]
-    prompt_ref, out_ref = refs[-2:]
+    key_refs = refs[: (len(refs) - 3) // 2]
+    value_refs = refs[(len(refs) - 3) // 2 : -3]
+    prompt_key_ref, prompt_value_ref, out_ref = refs[-3:]
     tile = q_ref.shape[0]
-    width = tile * len(band_refs)
-    feat = q_ref.shape[1]
-    lanes = GROUP * HEAD
+    width = tile * len(key_refs)
+    lanes = q_ref.shape[1]
     block = pl.program_id(0)
     first = pos_ref[0]
     total = pos_ref[1]
@@ -86,55 +86,54 @@
     prompt_ok = jnp.abs(prompt_pos - query_pos) > HALF
     contract = (((1,), (1,)), ((), ()))
     lane_head = lax.broadcasted_iota(jnp.int32, (1, lanes), 1) // HEAD
-    for group in range(feat // lanes):
-        cols = slice(group * lanes, (group + 1) * lanes)
-        vcols = slice(feat + group * lanes, feat + (group + 1) * lanes)
-        band_keys = jnp.concatenate([ref[:, cols] for ref in band_refs], axis=0)
-        band_values = jnp.concatenate([ref[:, vcols] for ref in band_refs], axis=0)
-        query = q_ref[:, cols]
-        stacked = jnp.concatenate(
-            [jnp.where(lane_head == j, query, jnp.zeros_like(query)) for j in range(GROUP)],
-            axis=0,
-        )
-        band_scores = lax.dot_general(
-            stacked, band_keys, contract, preferred_element_type=jnp.float32
-        ).reshape(GROUP, tile, width)
-        prompt_scores = lax.dot_general(
-            stacked, prompt_ref[:, cols], contract, preferred_element_type=jnp.float32
-        ).reshape(GROUP, tile, PROMPT)
-        band_scores = jnp.where(band_ok[None], band_scores, -1e30)
-        prompt_scores = jnp.where(prompt_ok[None], prompt_scores, -1e30)
-        row_max = jnp.maximum(
-            jnp.max(band_scores, axis=2, keepdims=True),
-            jnp.max(prompt_scores, axis=2, keepdims=True),
-        )
-        band_exp = jnp.exp(band_scores - row_max)
-        prompt_exp = jnp.exp(prompt_scores - row_max)
-        denom = jnp.sum(band_exp, axis=2, keepdims=True) + jnp.sum(
-            prompt_exp, axis=2, keepdims=True
-        )
-        band_probs = band_exp.astype(jnp.bfloat16).reshape(GROUP * tile, width)
-        prompt_probs = prompt_exp.astype(jnp.bfloat16).reshape(GROUP * tile, PROMPT)
-        mixed = jnp.dot(band_probs, band_values, preferred_element_type=jnp.float32) + jnp.dot(
-            prompt_probs, prompt_ref[:, vcols], preferred_element_type=jnp.float32
-        )
-        mixed = mixed * (1.0 / denom.reshape(GROUP * tile, 1))
-        attn = mixed[:tile]
-        for j in range(1, GROUP):
-            attn = jnp.where(lane_head == j, mixed[j * tile : (j + 1) * tile], attn)
-        out_ref[:, cols] = attn.astype(out_ref.dtype)
+    band_keys = jnp.concatenate([ref[...] for ref in key_refs], axis=0)
+    band_values = jnp.concatenate([ref[...] for ref in value_refs], axis=0)
+    query = q_ref[...]
+    stacked = jnp.concatenate(
+        [jnp.where(lane_head == j, query, jnp.zeros_like(query)) for j in range(GROUP)],
+        axis=0,
+    )
+    band_scores = lax.dot_general(
+        stacked, band_keys, contract, preferred_element_type=jnp.float32
+    ).reshape(GROUP, tile, width)
+    prompt_scores = lax.dot_general(
+        stacked, prompt_key_ref[...], contract, preferred_element_type=jnp.float32
+    ).reshape(GROUP, tile, PROMPT)
+    band_scores = jnp.where(band_ok[None], band_scores, -1e30)
+    prompt_scores = jnp.where(prompt_ok[None], prompt_scores, -1e30)
+    row_max = jnp.maximum(
+        jnp.max(band_scores, axis=2, keepdims=True),
+        jnp.max(prompt_scores, axis=2, keepdims=True),
+    )
+    band_exp = jnp.exp(band_scores - row_max)
+    prompt_exp = jnp.exp(prompt_scores - row_max)
+    denom = jnp.sum(band_exp, axis=2, keepdims=True) + jnp.sum(prompt_exp, axis=2, keepdims=True)
+    band_probs = band_exp.astype(jnp.bfloat16).reshape(GROUP * tile, width)
+    prompt_probs = prompt_exp.astype(jnp.bfloat16).reshape(GROUP * tile, PROMPT)
+    mixed = jnp.dot(band_probs, band_values, preferred_element_type=jnp.float32) + jnp.dot(
+        prompt_probs, prompt_value_ref[...], preferred_element_type=jnp.float32
+    )
+    mixed = mixed * (1.0 / denom.reshape(GROUP * tile, 1))
+    attn = mixed[:tile]
+    for j in range(1, GROUP):
+        attn = jnp.where(lane_head == j, mixed[j * tile : (j + 1) * tile], attn)
+    out_ref[...] = attn.astype(out_ref.dtype)
 
 
 def attention(queries, band_kv, prompt_kv, first_pos, total_len, row0, count):
     feat = queries.shape[1]
     tile = min(QUERY_TILE, count)
+    lanes = GROUP * HEAD
+    groups = feat // lanes
     pos = jnp.stack([first_pos, total_len]).astype(jnp.int32)
     pieces = 1 + 2 * HALF // tile
     width = tile * pieces
-    flops = 4 * count * (width + PROMPT) * feat * GROUP
     skip = row0 // tile
-    band_specs = [
-        pl.BlockSpec((tile, band_kv.shape[1]), lambda b, p, k=k: (b + skip + k, 0))
+    key_specs = [
+        pl.BlockSpec((tile, lanes), lambda b, g, p, k=k: (b + skip + k, g)) for k in range(pieces)
+    ]
+    value_specs = [
+        pl.BlockSpec((tile, lanes), lambda b, g, p, k=k: (b + skip + k, g + groups))
         for k in range(pieces)
     ]
     return pl.pallas_call(
@@ -142,18 +141,22 @@
         out_shape=jax.ShapeDtypeStruct((count, feat), jnp.bfloat16),
         grid_spec=pltpu.PrefetchScalarGridSpec(
             num_scalar_prefetch=1,
-            grid=(count // tile,),
-            in_specs=[pl.BlockSpec((tile, feat), lambda b, p: (b + skip, 0))]
-            + band_specs
-            + [pl.BlockSpec(prompt_kv.shape, lambda b, p: (0, 0))],
-            out_specs=pl.BlockSpec((tile, feat), lambda b, p: (b, 0)),
+            grid=(count // tile, groups),
+            in_specs=[pl.BlockSpec((tile, lanes), lambda b, g, p: (b + skip, g))]
+            + key_specs
+            + value_specs
+            + [
+                pl.BlockSpec((PROMPT, lanes), lambda b, g, p: (0, g)),
+                pl.BlockSpec((PROMPT, lanes), lambda b, g, p: (0, g + groups)),
+            ],
+            out_specs=pl.BlockSpec((tile, lanes), lambda b, g, p: (b, g)),
         ),
         cost_estimate=pl.CostEstimate(
-            flops=flops,
+            flops=4 * count * (width + PROMPT) * feat * GROUP,
             transcendentals=count * (width + PROMPT) * HEADS,
             bytes_accessed=2 * (2 * count * feat + pieces * count * band_kv.shape[1] + prompt_kv.size),
         ),
-    )(pos, queries, *([band_kv] * pieces), prompt_kv)
+    )(pos, queries, *([band_kv] * (2 * pieces)), prompt_kv, prompt_kv)
 
 
 def per_device(

time: 122 us -> 131 us (1.074)
  Pallas kernels: 31.3 us -> 40.3 us
    pallas_call x2, Pallas kernels: 31.3 us -> 40.3 us  [attention(): pl.pallas_call(functools.partial(attention_kernel, row0), out_shape=jax.S...]
  transfers between devices with their start and end apart: 12 -> 12, of which waited for: 5 -> 5; matrix products, arithmetic and copies ran while one was open for 21% -> 20% of each run, Pallas kernels for 0% -> 0%
where the time goes in v15:
time: 131 us; the launch traced here: 130 us
  Pallas kernels  40.3 us (31%)
  waiting for transfers between devices  29 us (22%)
  matrix products  20.4 us (16%)
  starting transfers between devices  16.9 us (13%)
  other arithmetic  14.3 us (11%)
  local copies, waits for them, and re-layouts  7.68 us (6%)
  between operations  1.72 us (1%)
    pallas_call x2, Pallas kernels, attention(): pl.pallas_call(functools.partial(attention_kernel, row0), out_shape=jax.S...  40.3 us
    ppermute x8, waiting for transfers between devices, spread(): got = lax.ppermute(block, axis, op)  17.8 us
    ppermute x2, waiting for transfers between devices, with_halo(): before = lax.ppermute(last, axis, up)  9.74 us
    ppermute x8, starting transfers between devices, spread(): got = lax.ppermute(block, axis, op)  8.14 us
    dot_general x2, matrix products, per_device(): jnp.dot(extended_normed, weights[:, feat_width:], preferred_element_type=...  8.09 us
    squeeze x1, local copies, waits for them, and re-layouts, per_device(): weights = w_qkv[layer_idx]  6.45 us
    ppermute x2, starting transfers between devices, with_halo(): before = lax.ppermute(last, axis, up)  4.81 us
    dot_general x2, matrix products, per_device(): jnp.dot(attended, w_out[layer_idx], preferred_element_type=jnp.float32)  4.68 us
  transfers between devices with their start and end apart: 12, of which 5 were waited for; matrix products, arithmetic and copies ran while one was open for 20% of the time, Pallas kernels for 0%

profile of v15, /device:TPU:20, one launch (start us, length us, event | category | flops | bytes accessed | tf_op | source)
XLA Modules:
  0.0 130.3 jit_solution(9704951815703724485)
XLA Ops:
  0.6 1.1 slice.59
  1.8 2.1 %collective-permute-start.1 = (bf16[256,768]{1,0:T(8,128)(2,1)S(1)}, bf16[256,768]{1,0:T(8,128)(2,1)S(1)}, u32[]{:S(2)}, u32[]{:S(2)}) collective-permute-start(bf16[256,768]{1,0:T(8,128)(2,1)S(1)} %slice.59), channel_id=1, source_target_pairs={{1,0},{2,1},{3,2},{4,3},{5,4},{6,5},{7,6},{8,7},{9,8},{10,9},{11,1... | collective-permute-start | bytes 1179656 | tf_op jit(solution)/shard_map/ppermute | solution.py:26
  3.9 0.7 collective-permute-start.2
  4.6 6.5 %slice_bitcast_fusion = (bf16[768,2304]{1,0:T(8,128)(2,1)}, bf16[768,2304]{1,0:T(8,128)(2,1)}) fusion(bf16[2,768,2304]{2,1,0:T(8,128)(2,1)} %param.20), kind=kLoop, calls=%fused_computation.10 | loop fusion | bytes 14155776 | tf_op jit(solution)/shard_map/squeeze | solution.py:184
  11.0 0.6 compare_reduce_fusion
  11.7 2.4 %collective-permute-start = (bf16[256,768]{1,0:T(8,128)(2,1)S(1)}, bf16[256,768]{1,0:T(8,128)(2,1)S(1)}, u32[]{:S(2)}, u32[]{:S(2)}) collective-permute-start(bf16[256,768]{1,0:T(8,128)(2,1)S(1)} %get-tuple-element.16), channel_id=1, source_target_pairs={{0,1},{1,2},{2,3},{3,4},{4,5},{5,6},{6,7},{7,8},{8,9},{9,10},{10,1... | collective-permute-start | bytes 1179656 | tf_op jit(solution)/shard_map/ppermute | solution.py:25
  14.1 0.6 compare_reduce_fusion.1
  14.8 0.7 compare_reduce_fusion.2
  15.5 0.7 collective-permute-start.3
  16.2 0.6 pad_add_fusion.pos_ref
  16.8 4.0 %collective-permute-done = bf16[256,768]{1,0:T(8,128)(2,1)S(1)} collective-permute-done((bf16[256,768]{1,0:T(8,128)(2,1)S(1)}, bf16[256,768]{1,0:T(8,128)(2,1)S(1)}, u32[]{:S(2)}, u32[]{:S(2)}) %collective-permute-start) | collective-permute-done | bytes 393248 | tf_op jit(solution)/shard_map/ppermute | solution.py:25
  20.8 0.3 convert_reduce_fusion.1
  21.1 0.6 broadcast_select_fusion.3
  21.7 1.3 collective-permute-start.4
  23.0 0.6 fusion.7
  23.7 1.9 %fusion.9 = bf16[1024,768]{1,0:T(8,128)(2,1)S(1)} fusion(f32[768]{0:T(1024)S(1)} %get-tuple-element.6, f32[1024]{0:T(1024)S(1)} %add_rsqrt_fusion.1, f32[1024]{0:T(1024)S(1)} %broadcast_multiply_fusion.1, bf16[256,768]{1,0:T(8,128)(2,1)S(1)} %collective-permute-done.1, bf16[512,768]{1,0:T(8,128)(2,1)S(1)} %copy-done.1, ...), kind=kLoop, calls=%fused_computation.17 | loop fusion | flops 7864320 | bytes 3156992 | tf_op jit(solution)/shard_map/convert_element_type | solution.py:64
  25.6 8.2 %collective-permute-done.4 = bf16[256,768]{1,0:T(8,128)(2,1)S(1)} collective-permute-done((bf16[256,768]{1,0:T(8,128)(2,1)S(1)}, bf16[256,768]{1,0:T(8,128)(2,1)S(1)}, u32[]{:S(2)}, u32[]{:S(2)}) %collective-permute-start.4) | collective-permute-done | bytes 393248 | tf_op jit(solution)/shard_map/ppermute | solution.py:52
  33.8 0.6 broadcast_select_fusion.5
  34.4 1.3 %collective-permute-start.5 = (bf16[256,768]{1,0:T(8,128)(2,1)S(1)}, bf16[256,768]{1,0:T(8,128)(2,1)S(1)}, u32[]{:S(2)}, u32[]{:S(2)}) collective-permute-start(bf16[256,768]{1,0:T(8,128)(2,1)S(1)} %broadcast_select_fusion.5), channel_id=1, source_target_pairs={{0,1},{2,3},{4,5},{6,7},{8,9},{10,11},{12,13},{14,15},{16,17},{18,... | collective-permute-start | bytes 1179656 | tf_op jit(solution)/shard_map/ppermute | solution.py:52
  35.7 4.1 %convolution_convert_fusion.1.refs_0_.refs_1_.refs_2_.refs_3_.refs_4_.refs_5_ = bf16[1024,1536]{1,0:T(8,128)(2,1)} fusion(bf16[1024,768]{1,0:T(8,128)(2,1)S(1)} %fusion.9, bf16[768,2304]{1,0:T(8,128)(2,1)S(1)} %copy-done.3), kind=kOutput, calls=%fused_computation.5 | convolution fusion | flops 2417491968 | bytes 7077888 | tf_op jit(solution)/shard_map/dot_general | solution.py:188
  39.8 1.7 %multiply_convert_fusion.1.q_ref = bf16[512,768]{1,0:T(8,128)(2,1)} fusion(bf16[768,2304]{1,0:T(8,128)(2,1)S(1)} %copy-done.3, bf16[1024,768]{1,0:T(8,128)(2,1)S(1)} %fusion.9), kind=kOutput, calls=%fused_computation.36 | convolution fusion | flops 604766208 | bytes 2752512 | tf_op jit(solution)/shard_map/dot_general | solution.py:193
  41.4 0.9 convert_reduce_fusion.4
  42.6 1.8 %convolution_convert_fusion.3.refs_6_.refs_7_ = bf16[256,1536]{1,0:T(8,128)(2,1)} fusion(bf16[768,2304]{1,0:T(8,128)(2,1)S(1)} %copy-done.3, bf16[256,768]{1,0:T(8,128)(2,1)S(1)} %get-tuple-element.10, f32[768]{0:T(1024)S(1)} %get-tuple-element.6, f32[256]{0:T(256)S(1)} %add_rsqrt_fusion.4, f32[256]{0:T(256)S(1)} %broadcast_multiply_fusion.4), kind=kOutput, calls=%fused_computation.19 | convolution fusion | flops 605356032 | bytes 3545088 | tf_op jit(solution)/shard_map/dot_general | solution.py:195
  44.4 20.2 %shard_map.185 = bf16[512,768]{1,0:T(8,128)(2,1)} custom-call(s32[2]{0:T(128)} %pad_add_fusion.pos_ref, bf16[512,768]{1,0:T(8,128)(2,1)} %multiply_convert_fusion.1.q_ref, bf16[1024,1536]{1,0:T(8,128)(2,1)} %convolution_convert_fusion.1.refs_0_.refs_1_.refs_2_.refs_3_.refs_4_.refs_5_, ...), custom_call_target="tpu_custom_call" | custom-call | flops 6442450944 | bytes 7077888 | tf_op jit(solution)/shard_map/pallas_call | solution.py:139
  64.5 2.3 %add_convert_fusion.1 = bf16[512,768]{1,0:T(8,128)(2,1)S(1)} fusion(bf16[512,768]{1,0:T(8,128)(2,1)S(1)} %copy-done.1, bf16[512,768]{1,0:T(8,128)(2,1)} %shard_map.185, bf16[2,768,768]{2,1,0:T(8,128)(2,1)} %param.21), kind=kOutput, calls=%fused_computation.35 | convolution fusion | flops 605159424 | bytes 3538944 | tf_op jit(solution)/shard_map/dot_general | solution.py:201
  66.8 0.7 collective-permute-start.8
  67.5 1.9 %collective-permute-start.7 = (bf16[256,768]{1,0:T(8,128)(2,1)S(1)}, bf16[256,768]{1,0:T(8,128)(2,1)S(1)}, u32[]{:S(2)}, u32[]{:S(2)}) collective-permute-start(bf16[256,768]{1,0:T(8,128)(2,1)S(1)} %slice.80), channel_id=1, source_target_pairs={{1,0},{2,1},{3,2},{4,3},{5,4},{6,5},{7,6},{8,7},{9,8},{10,9},{11,1... | collective-permute-start | bytes 1179656 | tf_op jit(solution)/shard_map/ppermute | solution.py:26
  69.6 2.4 %collective-permute-start.6 = (bf16[256,768]{1,0:T(8,128)(2,1)S(1)}, bf16[256,768]{1,0:T(8,128)(2,1)S(1)}, u32[]{:S(2)}, u32[]{:S(2)}) collective-permute-start(bf16[256,768]{1,0:T(8,128)(2,1)S(1)} %get-tuple-element.14), channel_id=1, source_target_pairs={{0,1},{1,2},{2,3},{3,4},{4,5},{5,6},{6,7},{7,8},{8,9},{9,10},{10,1... | collective-permute-start | bytes 1179656 | tf_op jit(solution)/shard_map/ppermute | solution.py:25
  72.0 0.7 collective-permute-start.9
  73.3 1.4 %collective-permute-done.7 = bf16[256,768]{1,0:T(8,128)(2,1)S(1)} collective-permute-done((bf16[256,768]{1,0:T(8,128)(2,1)S(1)}, bf16[256,768]{1,0:T(8,128)(2,1)S(1)}, u32[]{:S(2)}, u32[]{:S(2)}) %collective-permute-start.7) | collective-permute-done | bytes 393248 | tf_op jit(solution)/shard_map/ppermute | solution.py:26
  74.7 5.7 %collective-permute-done.6 = bf16[256,768]{1,0:T(8,128)(2,1)S(1)} collective-permute-done((bf16[256,768]{1,0:T(8,128)(2,1)S(1)}, bf16[256,768]{1,0:T(8,128)(2,1)S(1)}, u32[]{:S(2)}, u32[]{:S(2)}) %collective-permute-start.6) | collective-permute-done | bytes 393248 | tf_op jit(solution)/shard_map/ppermute | solution.py:25
  80.4 0.3 convert_reduce_fusion
  80.7 0.6 broadcast_select_fusion.2
  81.3 1.5 %collective-permute-start.10 = (bf16[256,768]{1,0:T(8,128)(2,1)S(1)}, bf16[256,768]{1,0:T(8,128)(2,1)S(1)}, u32[]{:S(2)}, u32[]{:S(2)}) collective-permute-start(bf16[256,768]{1,0:T(8,128)(2,1)S(1)} %broadcast_select_fusion.2), channel_id=1, source_target_pairs={{0,2},{4,6},{8,10},{12,14},{16,18},{20,22},{24,26},{28,30}} | collective-permute-start | bytes 1179656 | tf_op jit(solution)/shard_map/ppermute | solution.py:52
  82.8 0.6 fusion.4
  83.5 1.9 %fusion.6 = bf16[1024,768]{1,0:T(8,128)(2,1)S(1)} fusion(f32[768]{0:T(1024)S(1)} %get-tuple-element.5, f32[1024]{0:T(1024)S(1)} %add_rsqrt_fusion, f32[1024]{0:T(1024)S(1)} %broadcast_multiply_fusion, bf16[256,768]{1,0:T(8,128)(2,1)S(1)} %collective-permute-done.7, bf16[512,768]{1,0:T(8,128)(2,1)S(1)} %add_convert_fusion.1, ...), kind=kLoop, calls=%fused_computation.14 | loop fusion | flops 7864320 | bytes 3156992 | tf_op jit(solution)/shard_map/convert_element_type | solution.py:64
  85.4 9.6 %collective-permute-done.10 = bf16[256,768]{1,0:T(8,128)(2,1)S(1)} collective-permute-done((bf16[256,768]{1,0:T(8,128)(2,1)S(1)}, bf16[256,768]{1,0:T(8,128)(2,1)S(1)}, u32[]{:S(2)}, u32[]{:S(2)}) %collective-permute-start.10) | collective-permute-done | bytes 393248 | tf_op jit(solution)/shard_map/ppermute | solution.py:52
  95.0 0.6 broadcast_select_fusion.4
  95.6 1.3 %collective-permute-start.11 = (bf16[256,768]{1,0:T(8,128)(2,1)S(1)}, bf16[256,768]{1,0:T(8,128)(2,1)S(1)}, u32[]{:S(2)}, u32[]{:S(2)}) collective-permute-start(bf16[256,768]{1,0:T(8,128)(2,1)S(1)} %broadcast_select_fusion.4), channel_id=1, source_target_pairs={{0,1},{2,3},{4,5},{6,7},{8,9},{10,11},{12,13},{14,15},{16,17},{18,... | collective-permute-start | bytes 1179656 | tf_op jit(solution)/shard_map/ppermute | solution.py:52
  96.9 4.0 %convolution_convert_fusion.refs_0_.refs_1_.refs_2_.refs_3_.refs_4_.refs_5_ = bf16[1024,1536]{1,0:T(8,128)(2,1)} fusion(bf16[1024,768]{1,0:T(8,128)(2,1)S(1)} %fusion.6, bf16[768,2304]{1,0:T(8,128)(2,1)S(1)} %copy-done.2), kind=kOutput, calls=%fused_computation.4 | convolution fusion | flops 2417491968 | bytes 7077888 | tf_op jit(solution)/shard_map/dot_general | solution.py:188
  100.9 1.7 %multiply_convert_fusion.q_ref = bf16[512,768]{1,0:T(8,128)(2,1)} fusion(bf16[768,2304]{1,0:T(8,128)(2,1)S(1)} %copy-done.2, bf16[1024,768]{1,0:T(8,128)(2,1)S(1)} %fusion.6), kind=kOutput, calls=%fused_computation.34 | convolution fusion | flops 604766208 | bytes 2752512 | tf_op jit(solution)/shard_map/dot_general | solution.py:193
  102.6 0.9 convert_reduce_fusion.3
  103.7 1.8 %convolution_convert_fusion.2.refs_6_.refs_7_ = bf16[256,1536]{1,0:T(8,128)(2,1)} fusion(bf16[768,2304]{1,0:T(8,128)(2,1)S(1)} %copy-done.2, bf16[256,768]{1,0:T(8,128)(2,1)S(1)} %get-tuple-element.8, f32[768]{0:T(1024)S(1)} %get-tuple-element.5, f32[256]{0:T(256)S(1)} %add_rsqrt_fusion.3, f32[256]{0:T(256)S(1)} %broadcast_multiply_fusion.3), kind=kOutput, calls=%fused_computation.18 | convolution fusion | flops 605356032 | bytes 3545088 | tf_op jit(solution)/shard_map/dot_general | solution.py:195
  105.5 20.2 %shard_map.186 = bf16[512,768]{1,0:T(8,128)(2,1)} custom-call(s32[2]{0:T(128)} %pad_add_fusion.pos_ref, bf16[512,768]{1,0:T(8,128)(2,1)} %multiply_convert_fusion.q_ref, bf16[1024,1536]{1,0:T(8,128)(2,1)} %convolution_convert_fusion.refs_0_.refs_1_.refs_2_.refs_3_.refs_4_.refs_5_, ...), custom_call_target="tpu_custom_call" | custom-call | flops 6442450944 | bytes 7077888 | tf_op jit(solution)/shard_map/pallas_call | solution.py:139
  125.7 2.4 %convert_reduce_fusion.2 = (f32[512]{0:T(512)S(1)}, bf16[512,768]{1,0:T(8,128)(2,1)S(1)}) fusion(bf16[512,768]{1,0:T(8,128)(2,1)} %shard_map.186, bf16[2,768,768]{2,1,0:T(8,128)(2,1)} %param.21, bf16[512,768]{1,0:T(8,128)(2,1)S(1)} %add_convert_fusion.1), kind=kOutput, calls=%fused_computation.25 | convolution fusion | flops 605945344 | bytes 3540992 | tf_op jit(solution)/shard_map/dot_general | solution.py:201
  128.1 0.4 fusion.16
  128.5 0.8 fusion.35
  129.7 0.6 multiply_add_fusion
  (52 shorter events, 1.2 us)
Async XLA Ops:
  0.6 127.8 %copy-start = (bf16[768,512]{1,0:T(8,128)(2,1)S(1)}, bf16[768,512]{1,0:T(8,128)(2,1)}, u32[]{:S(2)}) copy-start(bf16[768,512]{1,0:T(8,128)(2,1)} %param.23) | copy-start | bytes 2359300
  1.7 9.3 %copy-start.12 = (s32[2]{0:T(128)S(1)}, s32[2]{0:T(128)}, u32[]{:S(2)}) copy-start(s32[2]{0:T(128)} %constant.49.clone) | copy-start | bytes 28
  1.8 9.9 %copy-start.1 = (bf16[512,768]{1,0:T(8,128)(2,1)S(1)}, bf16[512,768]{1,0:T(8,128)(2,1)}, u32[]{:S(2)}) copy-start(bf16[512,768]{1,0:T(8,128)(2,1)} %param.18) | copy-start | bytes 2359300
  1.8 12.4 %copy-start.11 = (s32[4]{0:T(128)S(1)}, s32[4]{0:T(128)}, u32[]{:S(2)}) copy-start(s32[4]{0:T(128)} %constant.50.clone) | copy-start | bytes 52
  1.8 13.0 %copy-start.10 = (s32[8]{0:T(128)S(1)}, s32[8]{0:T(128)}, u32[]{:S(2)}) copy-start(s32[8]{0:T(128)} %constant.51.clone) | copy-start | bytes 100
  1.8 13.7 %copy-start.5 = (f32[2,768]{1,0:T(2,128)S(1)}, f32[2,768]{1,0:T(2,128)}, u32[]{:S(2)}) copy-start(f32[2,768]{1,0:T(2,128)} %param.19) | copy-start | bytes 18436
  1.8 15.0 %collective-permute-start.1 = (bf16[256,768]{1,0:T(8,128)(2,1)S(1)}, bf16[256,768]{1,0:T(8,128)(2,1)S(1)}, u32[]{:S(2)}, u32[]{:S(2)}) collective-permute-start(bf16[256,768]{1,0:T(8,128)(2,1)S(1)} %slice.59), channel_id=1, source_target_pairs={{1,0},{2,1},{3,2},{4,3},{5,4},{6,5},{7,6},{8,7},{9,8},{10,9},{11,1... | collective-permute-start | bytes 1179656 | tf_op jit(solution)/shard_map/ppermute | solution.py:26
  3.9 7.8 %collective-permute-start.2 = (bf16[256,768]{1,0:T(8,128)(2,1)S(1)}, bf16[256,768]{1,0:T(8,128)(2,1)S(1)}, u32[]{:S(2)}, u32[]{:S(2)}) collective-permute-start(bf16[256,768]{1,0:T(8,128)(2,1)S(1)} %slice.59), channel_id=1, source_target_pairs={{0,8},{16,24}} | collective-permute-start | bytes 1179656 | tf_op jit(solution)/shard_map/ppermute | solution.py:52
  11.7 9.1 %collective-permute-start = (bf16[256,768]{1,0:T(8,128)(2,1)S(1)}, bf16[256,768]{1,0:T(8,128)(2,1)S(1)}, u32[]{:S(2)}, u32[]{:S(2)}) collective-permute-start(bf16[256,768]{1,0:T(8,128)(2,1)S(1)} %get-tuple-element.16), channel_id=1, source_target_pairs={{0,1},{1,2},{2,3},{3,4},{4,5},{5,6},{6,7},{7,8},{8,9},{9,10},{10,1... | collective-permute-start | bytes 1179656 | tf_op jit(solution)/shard_map/ppermute | solution.py:25
  15.5 5.6 %collective-permute-start.3 = (bf16[256,768]{1,0:T(8,128)(2,1)S(1)}, bf16[256,768]{1,0:T(8,128)(2,1)S(1)}, u32[]{:S(2)}, u32[]{:S(2)}) collective-permute-start(bf16[256,768]{1,0:T(8,128)(2,1)S(1)} %get-tuple-element.15), channel_id=1, source_target_pairs={{0,4},{8,12},{16,20},{24,28}} | collective-permute-start | bytes 1179656 | tf_op jit(solution)/shard_map/ppermute | solution.py:52
  21.7 12.1 %collective-permute-start.4 = (bf16[256,768]{1,0:T(8,128)(2,1)S(1)}, bf16[256,768]{1,0:T(8,128)(2,1)S(1)}, u32[]{:S(2)}, u32[]{:S(2)}) collective-permute-start(bf16[256,768]{1,0:T(8,128)(2,1)S(1)} %broadcast_select_fusion.3), channel_id=1, source_target_pairs={{0,2},{4,6},{8,10},{12,14},{16,18},{20,22},{24,26},{28,30}} | collective-permute-start | bytes 1179656 | tf_op jit(solution)/shard_map/ppermute | solution.py:52
  23.7 12.0 %copy-start.3 = (bf16[768,2304]{1,0:T(8,128)(2,1)S(1)}, bf16[768,2304]{1,0:T(8,128)(2,1)}, u32[]{:S(2)}) copy-start(bf16[768,2304]{1,0:T(8,128)(2,1)} %get-tuple-element.12) | copy-start | bytes 10616836
  34.4 7.1 %collective-permute-start.5 = (bf16[256,768]{1,0:T(8,128)(2,1)S(1)}, bf16[256,768]{1,0:T(8,128)(2,1)S(1)}, u32[]{:S(2)}, u32[]{:S(2)}) collective-permute-start(bf16[256,768]{1,0:T(8,128)(2,1)S(1)} %broadcast_select_fusion.5), channel_id=1, source_target_pairs={{0,1},{2,3},{4,5},{6,7},{8,9},{10,11},{12,13},{14,15},{16,17},{18,... | collective-permute-start | bytes 1179656 | tf_op jit(solution)/shard_map/ppermute | solution.py:52
  66.8 2.6 %collective-permute-start.8 = (bf16[256,768]{1,0:T(8,128)(2,1)S(1)}, bf16[256,768]{1,0:T(8,128)(2,1)S(1)}, u32[]{:S(2)}, u32[]{:S(2)}) collective-permute-start(bf16[256,768]{1,0:T(8,128)(2,1)S(1)} %slice.80), channel_id=1, source_target_pairs={{0,8},{16,24}} | collective-permute-start | bytes 1179656 | tf_op jit(solution)/shard_map/ppermute | solution.py:52
  67.5 7.2 %collective-permute-start.7 = (bf16[256,768]{1,0:T(8,128)(2,1)S(1)}, bf16[256,768]{1,0:T(8,128)(2,1)S(1)}, u32[]{:S(2)}, u32[]{:S(2)}) collective-permute-start(bf16[256,768]{1,0:T(8,128)(2,1)S(1)} %slice.80), channel_id=1, source_target_pairs={{1,0},{2,1},{3,2},{4,3},{5,4},{6,5},{7,6},{8,7},{9,8},{10,9},{11,1... | collective-permute-start | bytes 1179656 | tf_op jit(solution)/shard_map/ppermute | solution.py:26
  69.6 10.9 %collective-permute-start.6 = (bf16[256,768]{1,0:T(8,128)(2,1)S(1)}, bf16[256,768]{1,0:T(8,128)(2,1)S(1)}, u32[]{:S(2)}, u32[]{:S(2)}) collective-permute-start(bf16[256,768]{1,0:T(8,128)(2,1)S(1)} %get-tuple-element.14), channel_id=1, source_target_pairs={{0,1},{1,2},{2,3},{3,4},{4,5},{5,6},{6,7},{7,8},{8,9},{9,10},{10,1... | collective-permute-start | bytes 1179656 | tf_op jit(solution)/shard_map/ppermute | solution.py:25
  72.0 8.8 %collective-permute-start.9 = (bf16[256,768]{1,0:T(8,128)(2,1)S(1)}, bf16[256,768]{1,0:T(8,128)(2,1)S(1)}, u32[]{:S(2)}, u32[]{:S(2)}) collective-permute-start(bf16[256,768]{1,0:T(8,128)(2,1)S(1)} %get-tuple-element.13), channel_id=1, source_target_pairs={{0,4},{8,12},{16,20},{24,28}} | collective-permute-start | bytes 1179656 | tf_op jit(solution)/shard_map/ppermute | solution.py:52
  81.3 13.6 %collective-permute-start.10 = (bf16[256,768]{1,0:T(8,128)(2,1)S(1)}, bf16[256,768]{1,0:T(8,128)(2,1)S(1)}, u32[]{:S(2)}, u32[]{:S(2)}) collective-permute-start(bf16[256,768]{1,0:T(8,128)(2,1)S(1)} %broadcast_select_fusion.2), channel_id=1, source_target_pairs={{0,2},{4,6},{8,10},{12,14},{16,18},{20,22},{24,26},{28,30}} | collective-permute-start | bytes 1179656 | tf_op jit(solution)/shard_map/ppermute | solution.py:52
  83.5 13.4 %copy-start.2 = (bf16[768,2304]{1,0:T(8,128)(2,1)S(1)}, bf16[768,2304]{1,0:T(8,128)(2,1)}, u32[]{:S(2)}) copy-start(bf16[768,2304]{1,0:T(8,128)(2,1)} %get-tuple-element.11) | copy-start | bytes 10616836
  95.6 7.0 %collective-permute-start.11 = (bf16[256,768]{1,0:T(8,128)(2,1)S(1)}, bf16[256,768]{1,0:T(8,128)(2,1)S(1)}, u32[]{:S(2)}, u32[]{:S(2)}) collective-permute-start(bf16[256,768]{1,0:T(8,128)(2,1)S(1)} %broadcast_select_fusion.4), channel_id=1, source_target_pairs={{0,1},{2,3},{4,5},{6,7},{8,9},{10,11},{12,13},{14,15},{16,17},{18,... | collective-permute-start | bytes 1179656 | tf_op jit(solution)/shard_map/ppermute | solution.py:52
  125.7 2.8 %copy-start.9 = (f32[768]{0:T(1024)S(1)}, f32[768]{0:T(1024)}, u32[]{:S(2)}) copy-start(f32[768]{0:T(1024)} %param.22) | copy-start | bytes 9220
  128.1 1.4 %copy-start.6 = (s32[512]{0:T(512)S(1)}, s32[512]{0:T(512)}, u32[]{:S(2)}) copy-start(s32[512]{0:T(512)} %param.24) | copy-start | bytes 6148
  128.5 1.2 copy-start.7
  128.5 1.2 copy-start.8
  129.7 0.6 copy-start.4

commit v16 on v12

--- a/solution.py
+++ b/solution.py
@@ -179,8 +179,8 @@
     for layer_idx in range(LAYERS):
         gain = ln_gain[layer_idx]
         weights = w_qkv[layer_idx]
+        prompt_rows = spread(prompt_source, "seq")
         extended = with_halo(hidden_state, (("seq", 0),), HALF)
-        prompt_rows = spread(prompt_source, "seq")
         extended_normed = layer_norm(extended, gain)
         band_kv = jnp.dot(
             extended_normed, weights[:, feat_width:], preferred_element_type=jnp.float32

time: 122 us -> 122 us (level)
  no operation moved by 1% of the time
where the time goes in v16:
time: 122 us
  Pallas kernels  31.3 us (26%)
  waiting for transfers between devices  29.2 us (24%)
  matrix products  20.4 us (17%)
  starting transfers between devices  17.1 us (14%)
  other arithmetic  14.3 us (12%)
  local copies, waits for them, and re-layouts  7.68 us (6%)
  between operations  1.72 us (1%)
    pallas_call x2, Pallas kernels, attention(): pl.pallas_call(functools.partial(attention_kernel, row0), out_shape=jax.S...  31.3 us
    ppermute x8, waiting for transfers between devices, spread(): got = lax.ppermute(block, axis, op)  18 us
    ppermute x2, waiting for transfers between devices, with_halo(): before = lax.ppermute(last, axis, up)  9.74 us
    ppermute x8, starting transfers between devices, spread(): got = lax.ppermute(block, axis, op)  8.36 us
    dot_general x2, matrix products, per_device(): jnp.dot(extended_normed, weights[:, feat_width:], preferred_element_type=...  8.09 us
    squeeze x1, local copies, waits for them, and re-layouts, per_device(): weights = w_qkv[layer_idx]  6.45 us
    ppermute x2, starting transfers between devices, with_halo(): before = lax.ppermute(last, axis, up)  4.81 us
    dot_general x2, matrix products, per_device(): jnp.dot(attended, w_out[layer_idx], preferred_element_type=jnp.float32)  4.68 us
  transfers between devices with their start and end apart: 12, of which 5 were waited for; matrix products, arithmetic and copies ran while one was open for 21% of the time, Pallas kernels for 0%

profile of v16, /device:TPU:20, one launch (start us, length us, event | category | flops | bytes accessed | tf_op | source)
XLA Modules:
  0.0 121.7 jit_solution(4693231157325583157)
XLA Ops:
  0.6 1.1 slice.59
  1.8 2.1 %collective-permute-start.1 = (bf16[256,768]{1,0:T(8,128)(2,1)S(1)}, bf16[256,768]{1,0:T(8,128)(2,1)S(1)}, u32[]{:S(2)}, u32[]{:S(2)}) collective-permute-start(bf16[256,768]{1,0:T(8,128)(2,1)S(1)} %slice.59), channel_id=1, source_target_pairs={{1,0},{2,1},{3,2},{4,3},{5,4},{6,5},{7,6},{8,7},{9,8},{10,9},{11,1... | collective-permute-start | bytes 1179656 | tf_op jit(solution)/shard_map/ppermute | solution.py:26
  3.9 0.7 collective-permute-start.2
  4.6 6.5 %slice_bitcast_fusion = (bf16[768,2304]{1,0:T(8,128)(2,1)}, bf16[768,2304]{1,0:T(8,128)(2,1)}) fusion(bf16[2,768,2304]{2,1,0:T(8,128)(2,1)} %param.20), kind=kLoop, calls=%fused_computation.10 | loop fusion | bytes 14155776 | tf_op jit(solution)/shard_map/squeeze | solution.py:181
  11.0 0.6 compare_reduce_fusion
  11.7 2.4 %collective-permute-start = (bf16[256,768]{1,0:T(8,128)(2,1)S(1)}, bf16[256,768]{1,0:T(8,128)(2,1)S(1)}, u32[]{:S(2)}, u32[]{:S(2)}) collective-permute-start(bf16[256,768]{1,0:T(8,128)(2,1)S(1)} %get-tuple-element.16), channel_id=1, source_target_pairs={{0,1},{1,2},{2,3},{3,4},{4,5},{5,6},{6,7},{7,8},{8,9},{9,10},{10,1... | collective-permute-start | bytes 1179656 | tf_op jit(solution)/shard_map/ppermute | solution.py:25
  14.1 0.6 compare_reduce_fusion.1
  14.8 0.7 compare_reduce_fusion.2
  15.5 0.7 collective-permute-start.3
  16.2 0.6 pad_add_fusion.pos_ref
  16.8 4.0 %collective-permute-done = bf16[256,768]{1,0:T(8,128)(2,1)S(1)} collective-permute-done((bf16[256,768]{1,0:T(8,128)(2,1)S(1)}, bf16[256,768]{1,0:T(8,128)(2,1)S(1)}, u32[]{:S(2)}, u32[]{:S(2)}) %collective-permute-start) | collective-permute-done | bytes 393248 | tf_op jit(solution)/shard_map/ppermute | solution.py:25
  20.8 0.3 convert_reduce_fusion.1
  21.1 0.6 broadcast_select_fusion.3
  21.7 1.3 %collective-permute-start.4 = (bf16[256,768]{1,0:T(8,128)(2,1)S(1)}, bf16[256,768]{1,0:T(8,128)(2,1)S(1)}, u32[]{:S(2)}, u32[]{:S(2)}) collective-permute-start(bf16[256,768]{1,0:T(8,128)(2,1)S(1)} %broadcast_select_fusion.3), channel_id=1, source_target_pairs={{0,2},{4,6},{8,10},{12,14},{16,18},{20,22},{24,26},{28,30}} | collective-permute-start | bytes 1179656 | tf_op jit(solution)/shard_map/ppermute | solution.py:52
  23.0 0.6 fusion.7
  23.7 1.9 %fusion.9 = bf16[1024,768]{1,0:T(8,128)(2,1)S(1)} fusion(f32[768]{0:T(1024)S(1)} %get-tuple-element.6, f32[1024]{0:T(1024)S(1)} %add_rsqrt_fusion.1, f32[1024]{0:T(1024)S(1)} %broadcast_multiply_fusion.1, bf16[256,768]{1,0:T(8,128)(2,1)S(1)} %collective-permute-done.1, bf16[512,768]{1,0:T(8,128)(2,1)S(1)} %copy-done.1, ...), kind=kLoop, calls=%fused_computation.17 | loop fusion | flops 7864320 | bytes 3156992 | tf_op jit(solution)/shard_map/convert_element_type | solution.py:64
  25.6 8.2 %collective-permute-done.4 = bf16[256,768]{1,0:T(8,128)(2,1)S(1)} collective-permute-done((bf16[256,768]{1,0:T(8,128)(2,1)S(1)}, bf16[256,768]{1,0:T(8,128)(2,1)S(1)}, u32[]{:S(2)}, u32[]{:S(2)}) %collective-permute-start.4) | collective-permute-done | bytes 393248 | tf_op jit(solution)/shard_map/ppermute | solution.py:52
  33.8 0.6 broadcast_select_fusion.5
  34.4 1.5 %collective-permute-start.5 = (bf16[256,768]{1,0:T(8,128)(2,1)S(1)}, bf16[256,768]{1,0:T(8,128)(2,1)S(1)}, u32[]{:S(2)}, u32[]{:S(2)}) collective-permute-start(bf16[256,768]{1,0:T(8,128)(2,1)S(1)} %broadcast_select_fusion.5), channel_id=1, source_target_pairs={{0,1},{2,3},{4,5},{6,7},{8,9},{10,11},{12,13},{14,15},{16,17},{18,... | collective-permute-start | bytes 1179656 | tf_op jit(solution)/shard_map/ppermute | solution.py:52
  35.9 4.1 %convolution_convert_fusion.1.refs_0_.refs_1_.refs_2_ = bf16[1024,1536]{1,0:T(8,128)(2,1)} fusion(bf16[1024,768]{1,0:T(8,128)(2,1)S(1)} %fusion.9, bf16[768,2304]{1,0:T(8,128)(2,1)S(1)} %copy-done.3), kind=kOutput, calls=%fused_computation.5 | convolution fusion | flops 2417491968 | bytes 7077888 | tf_op jit(solution)/shard_map/dot_general | solution.py:185
  40.0 1.7 %multiply_convert_fusion.1.q_ref = bf16[512,768]{1,0:T(8,128)(2,1)} fusion(bf16[768,2304]{1,0:T(8,128)(2,1)S(1)} %copy-done.3, bf16[1024,768]{1,0:T(8,128)(2,1)S(1)} %fusion.9), kind=kOutput, calls=%fused_computation.36 | convolution fusion | flops 604766208 | bytes 2752512 | tf_op jit(solution)/shard_map/dot_general | solution.py:190
  41.6 0.9 convert_reduce_fusion.4
  42.8 1.8 %convolution_convert_fusion.3.refs_3_ = bf16[256,1536]{1,0:T(8,128)(2,1)} fusion(bf16[768,2304]{1,0:T(8,128)(2,1)S(1)} %copy-done.3, bf16[256,768]{1,0:T(8,128)(2,1)S(1)} %get-tuple-element.10, f32[768]{0:T(1024)S(1)} %get-tuple-element.6, f32[256]{0:T(256)S(1)} %add_rsqrt_fusion.4, f32[256]{0:T(256)S(1)} %broadcast_multiply_fusion.4), kind=kOutput, calls=%fused_computation.19 | convolution fusion | flops 605356032 | bytes 3545088 | tf_op jit(solution)/shard_map/dot_general | solution.py:192
  44.5 15.6 %shard_map.185 = bf16[512,768]{1,0:T(8,128)(2,1)} custom-call(s32[2]{0:T(128)} %pad_add_fusion.pos_ref, bf16[512,768]{1,0:T(8,128)(2,1)} %multiply_convert_fusion.1.q_ref, bf16[1024,1536]{1,0:T(8,128)(2,1)} %convolution_convert_fusion.1.refs_0_.refs_1_.refs_2_, bf16[1024,1536]{1,0:T(8,128)(2,1)} %convolution_convert_fusion.1.refs_0_.refs_1_.refs_2_, ...), custom_call_target="tpu_custom_call" | custom-call | flops 6442450944 | bytes 7077888 | tf_op jit(solution)/shard_map/pallas_call | solution.py:140
  60.2 2.3 %add_convert_fusion.1 = bf16[512,768]{1,0:T(8,128)(2,1)S(1)} fusion(bf16[512,768]{1,0:T(8,128)(2,1)S(1)} %copy-done.1, bf16[512,768]{1,0:T(8,128)(2,1)} %shard_map.185, bf16[2,768,768]{2,1,0:T(8,128)(2,1)} %param.21), kind=kOutput, calls=%fused_computation.35 | convolution fusion | flops 605159424 | bytes 3538944 | tf_op jit(solution)/shard_map/dot_general | solution.py:198
  62.5 0.7 collective-permute-start.8
  63.2 1.9 %collective-permute-start.7 = (bf16[256,768]{1,0:T(8,128)(2,1)S(1)}, bf16[256,768]{1,0:T(8,128)(2,1)S(1)}, u32[]{:S(2)}, u32[]{:S(2)}) collective-permute-start(bf16[256,768]{1,0:T(8,128)(2,1)S(1)} %slice.80), channel_id=1, source_target_pairs={{1,0},{2,1},{3,2},{4,3},{5,4},{6,5},{7,6},{8,7},{9,8},{10,9},{11,1... | collective-permute-start | bytes 1179656 | tf_op jit(solution)/shard_map/ppermute | solution.py:26
  65.2 2.4 %collective-permute-start.6 = (bf16[256,768]{1,0:T(8,128)(2,1)S(1)}, bf16[256,768]{1,0:T(8,128)(2,1)S(1)}, u32[]{:S(2)}, u32[]{:S(2)}) collective-permute-start(bf16[256,768]{1,0:T(8,128)(2,1)S(1)} %get-tuple-element.14), channel_id=1, source_target_pairs={{0,1},{1,2},{2,3},{3,4},{4,5},{5,6},{6,7},{7,8},{8,9},{9,10},{10,1... | collective-permute-start | bytes 1179656 | tf_op jit(solution)/shard_map/ppermute | solution.py:25
  67.6 0.7 collective-permute-start.9
  69.0 1.4 %collective-permute-done.7 = bf16[256,768]{1,0:T(8,128)(2,1)S(1)} collective-permute-done((bf16[256,768]{1,0:T(8,128)(2,1)S(1)}, bf16[256,768]{1,0:T(8,128)(2,1)S(1)}, u32[]{:S(2)}, u32[]{:S(2)}) %collective-permute-start.7) | collective-permute-done | bytes 393248 | tf_op jit(solution)/shard_map/ppermute | solution.py:26
  70.4 5.7 %collective-permute-done.6 = bf16[256,768]{1,0:T(8,128)(2,1)S(1)} collective-permute-done((bf16[256,768]{1,0:T(8,128)(2,1)S(1)}, bf16[256,768]{1,0:T(8,128)(2,1)S(1)}, u32[]{:S(2)}, u32[]{:S(2)}) %collective-permute-start.6) | collective-permute-done | bytes 393248 | tf_op jit(solution)/shard_map/ppermute | solution.py:25
  76.1 0.3 convert_reduce_fusion
  76.4 0.6 broadcast_select_fusion.2
  77.0 1.3 %collective-permute-start.10 = (bf16[256,768]{1,0:T(8,128)(2,1)S(1)}, bf16[256,768]{1,0:T(8,128)(2,1)S(1)}, u32[]{:S(2)}, u32[]{:S(2)}) collective-permute-start(bf16[256,768]{1,0:T(8,128)(2,1)S(1)} %broadcast_select_fusion.2), channel_id=1, source_target_pairs={{0,2},{4,6},{8,10},{12,14},{16,18},{20,22},{24,26},{28,30}} | collective-permute-start | bytes 1179656 | tf_op jit(solution)/shard_map/ppermute | solution.py:52
  78.3 0.6 fusion.4
  79.0 1.9 %fusion.6 = bf16[1024,768]{1,0:T(8,128)(2,1)S(1)} fusion(f32[768]{0:T(1024)S(1)} %get-tuple-element.5, f32[1024]{0:T(1024)S(1)} %add_rsqrt_fusion, f32[1024]{0:T(1024)S(1)} %broadcast_multiply_fusion, bf16[256,768]{1,0:T(8,128)(2,1)S(1)} %collective-permute-done.7, bf16[512,768]{1,0:T(8,128)(2,1)S(1)} %add_convert_fusion.1, ...), kind=kLoop, calls=%fused_computation.14 | loop fusion | flops 7864320 | bytes 3156992 | tf_op jit(solution)/shard_map/convert_element_type | solution.py:64
  80.8 9.8 %collective-permute-done.10 = bf16[256,768]{1,0:T(8,128)(2,1)S(1)} collective-permute-done((bf16[256,768]{1,0:T(8,128)(2,1)S(1)}, bf16[256,768]{1,0:T(8,128)(2,1)S(1)}, u32[]{:S(2)}, u32[]{:S(2)}) %collective-permute-start.10) | collective-permute-done | bytes 393248 | tf_op jit(solution)/shard_map/ppermute | solution.py:52
  90.6 0.6 broadcast_select_fusion.4
  91.2 1.5 %collective-permute-start.11 = (bf16[256,768]{1,0:T(8,128)(2,1)S(1)}, bf16[256,768]{1,0:T(8,128)(2,1)S(1)}, u32[]{:S(2)}, u32[]{:S(2)}) collective-permute-start(bf16[256,768]{1,0:T(8,128)(2,1)S(1)} %broadcast_select_fusion.4), channel_id=1, source_target_pairs={{0,1},{2,3},{4,5},{6,7},{8,9},{10,11},{12,13},{14,15},{16,17},{18,... | collective-permute-start | bytes 1179656 | tf_op jit(solution)/shard_map/ppermute | solution.py:52
  92.8 4.0 %convolution_convert_fusion.refs_0_.refs_1_.refs_2_ = bf16[1024,1536]{1,0:T(8,128)(2,1)} fusion(bf16[1024,768]{1,0:T(8,128)(2,1)S(1)} %fusion.6, bf16[768,2304]{1,0:T(8,128)(2,1)S(1)} %copy-done.2), kind=kOutput, calls=%fused_computation.4 | convolution fusion | flops 2417491968 | bytes 7077888 | tf_op jit(solution)/shard_map/dot_general | solution.py:185
  96.8 1.7 %multiply_convert_fusion.q_ref = bf16[512,768]{1,0:T(8,128)(2,1)} fusion(bf16[768,2304]{1,0:T(8,128)(2,1)S(1)} %copy-done.2, bf16[1024,768]{1,0:T(8,128)(2,1)S(1)} %fusion.6), kind=kOutput, calls=%fused_computation.34 | convolution fusion | flops 604766208 | bytes 2752512 | tf_op jit(solution)/shard_map/dot_general | solution.py:190
  98.5 0.9 convert_reduce_fusion.3
  99.6 1.8 %convolution_convert_fusion.2.refs_3_ = bf16[256,1536]{1,0:T(8,128)(2,1)} fusion(bf16[768,2304]{1,0:T(8,128)(2,1)S(1)} %copy-done.2, bf16[256,768]{1,0:T(8,128)(2,1)S(1)} %get-tuple-element.8, f32[768]{0:T(1024)S(1)} %get-tuple-element.5, f32[256]{0:T(256)S(1)} %add_rsqrt_fusion.3, f32[256]{0:T(256)S(1)} %broadcast_multiply_fusion.3), kind=kOutput, calls=%fused_computation.18 | convolution fusion | flops 605356032 | bytes 3545088 | tf_op jit(solution)/shard_map/dot_general | solution.py:192
  101.4 15.6 %shard_map.186 = bf16[512,768]{1,0:T(8,128)(2,1)} custom-call(s32[2]{0:T(128)} %pad_add_fusion.pos_ref, bf16[512,768]{1,0:T(8,128)(2,1)} %multiply_convert_fusion.q_ref, bf16[1024,1536]{1,0:T(8,128)(2,1)} %convolution_convert_fusion.refs_0_.refs_1_.refs_2_, bf16[1024,1536]{1,0:T(8,128)(2,1)} %convolution_convert_fusion.refs_0_.refs_1_.refs_2_, ...), custom_call_target="tpu_custom_call" | custom-call | flops 6442450944 | bytes 7077888 | tf_op jit(solution)/shard_map/pallas_call | solution.py:140
  117.0 2.4 %convert_reduce_fusion.2 = (f32[512]{0:T(512)S(1)}, bf16[512,768]{1,0:T(8,128)(2,1)S(1)}) fusion(bf16[512,768]{1,0:T(8,128)(2,1)} %shard_map.186, bf16[2,768,768]{2,1,0:T(8,128)(2,1)} %param.21, bf16[512,768]{1,0:T(8,128)(2,1)S(1)} %add_convert_fusion.1), kind=kOutput, calls=%fused_computation.25 | convolution fusion | flops 605945344 | bytes 3540992 | tf_op jit(solution)/shard_map/dot_general | solution.py:198
  119.4 0.4 fusion.16
  119.8 0.8 fusion.35
  121.1 0.6 multiply_add_fusion
  (52 shorter events, 1.2 us)
Async XLA Ops:
  0.6 119.2 %copy-start = (bf16[768,512]{1,0:T(8,128)(2,1)S(1)}, bf16[768,512]{1,0:T(8,128)(2,1)}, u32[]{:S(2)}) copy-start(bf16[768,512]{1,0:T(8,128)(2,1)} %param.23) | copy-start | bytes 2359300
  1.7 9.3 %copy-start.12 = (s32[2]{0:T(128)S(1)}, s32[2]{0:T(128)}, u32[]{:S(2)}) copy-start(s32[2]{0:T(128)} %constant.49.clone) | copy-start | bytes 28
  1.8 9.9 %copy-start.1 = (bf16[512,768]{1,0:T(8,128)(2,1)S(1)}, bf16[512,768]{1,0:T(8,128)(2,1)}, u32[]{:S(2)}) copy-start(bf16[512,768]{1,0:T(8,128)(2,1)} %param.18) | copy-start | bytes 2359300
  1.8 12.4 %copy-start.11 = (s32[4]{0:T(128)S(1)}, s32[4]{0:T(128)}, u32[]{:S(2)}) copy-start(s32[4]{0:T(128)} %constant.50.clone) | copy-start | bytes 52
  1.8 13.0 %copy-start.10 = (s32[8]{0:T(128)S(1)}, s32[8]{0:T(128)}, u32[]{:S(2)}) copy-start(s32[8]{0:T(128)} %constant.51.clone) | copy-start | bytes 100
  1.8 13.7 %copy-start.5 = (f32[2,768]{1,0:T(2,128)S(1)}, f32[2,768]{1,0:T(2,128)}, u32[]{:S(2)}) copy-start(f32[2,768]{1,0:T(2,128)} %param.19) | copy-start | bytes 18436
  1.8 15.0 %collective-permute-start.1 = (bf16[256,768]{1,0:T(8,128)(2,1)S(1)}, bf16[256,768]{1,0:T(8,128)(2,1)S(1)}, u32[]{:S(2)}, u32[]{:S(2)}) collective-permute-start(bf16[256,768]{1,0:T(8,128)(2,1)S(1)} %slice.59), channel_id=1, source_target_pairs={{1,0},{2,1},{3,2},{4,3},{5,4},{6,5},{7,6},{8,7},{9,8},{10,9},{11,1... | collective-permute-start | bytes 1179656 | tf_op jit(solution)/shard_map/ppermute | solution.py:26
  3.9 7.8 %collective-permute-start.2 = (bf16[256,768]{1,0:T(8,128)(2,1)S(1)}, bf16[256,768]{1,0:T(8,128)(2,1)S(1)}, u32[]{:S(2)}, u32[]{:S(2)}) collective-permute-start(bf16[256,768]{1,0:T(8,128)(2,1)S(1)} %slice.59), channel_id=1, source_target_pairs={{0,8},{16,24}} | collective-permute-start | bytes 1179656 | tf_op jit(solution)/shard_map/ppermute | solution.py:52
  11.7 9.1 %collective-permute-start = (bf16[256,768]{1,0:T(8,128)(2,1)S(1)}, bf16[256,768]{1,0:T(8,128)(2,1)S(1)}, u32[]{:S(2)}, u32[]{:S(2)}) collective-permute-start(bf16[256,768]{1,0:T(8,128)(2,1)S(1)} %get-tuple-element.16), channel_id=1, source_target_pairs={{0,1},{1,2},{2,3},{3,4},{4,5},{5,6},{6,7},{7,8},{8,9},{9,10},{10,1... | collective-permute-start | bytes 1179656 | tf_op jit(solution)/shard_map/ppermute | solution.py:25
  15.5 5.6 %collective-permute-start.3 = (bf16[256,768]{1,0:T(8,128)(2,1)S(1)}, bf16[256,768]{1,0:T(8,128)(2,1)S(1)}, u32[]{:S(2)}, u32[]{:S(2)}) collective-permute-start(bf16[256,768]{1,0:T(8,128)(2,1)S(1)} %get-tuple-element.15), channel_id=1, source_target_pairs={{0,4},{8,12},{16,20},{24,28}} | collective-permute-start | bytes 1179656 | tf_op jit(solution)/shard_map/ppermute | solution.py:52
  21.7 12.1 %collective-permute-start.4 = (bf16[256,768]{1,0:T(8,128)(2,1)S(1)}, bf16[256,768]{1,0:T(8,128)(2,1)S(1)}, u32[]{:S(2)}, u32[]{:S(2)}) collective-permute-start(bf16[256,768]{1,0:T(8,128)(2,1)S(1)} %broadcast_select_fusion.3), channel_id=1, source_target_pairs={{0,2},{4,6},{8,10},{12,14},{16,18},{20,22},{24,26},{28,30}} | collective-permute-start | bytes 1179656 | tf_op jit(solution)/shard_map/ppermute | solution.py:52
  23.7 12.2 %copy-start.3 = (bf16[768,2304]{1,0:T(8,128)(2,1)S(1)}, bf16[768,2304]{1,0:T(8,128)(2,1)}, u32[]{:S(2)}) copy-start(bf16[768,2304]{1,0:T(8,128)(2,1)} %get-tuple-element.12) | copy-start | bytes 10616836
  34.4 7.3 %collective-permute-start.5 = (bf16[256,768]{1,0:T(8,128)(2,1)S(1)}, bf16[256,768]{1,0:T(8,128)(2,1)S(1)}, u32[]{:S(2)}, u32[]{:S(2)}) collective-permute-start(bf16[256,768]{1,0:T(8,128)(2,1)S(1)} %broadcast_select_fusion.5), channel_id=1, source_target_pairs={{0,1},{2,3},{4,5},{6,7},{8,9},{10,11},{12,13},{14,15},{16,17},{18,... | collective-permute-start | bytes 1179656 | tf_op jit(solution)/shard_map/ppermute | solution.py:52
  62.5 2.6 %collective-permute-start.8 = (bf16[256,768]{1,0:T(8,128)(2,1)S(1)}, bf16[256,768]{1,0:T(8,128)(2,1)S(1)}, u32[]{:S(2)}, u32[]{:S(2)}) collective-permute-start(bf16[256,768]{1,0:T(8,128)(2,1)S(1)} %slice.80), channel_id=1, source_target_pairs={{0,8},{16,24}} | collective-permute-start | bytes 1179656 | tf_op jit(solution)/shard_map/ppermute | solution.py:52
  63.2 7.2 %collective-permute-start.7 = (bf16[256,768]{1,0:T(8,128)(2,1)S(1)}, bf16[256,768]{1,0:T(8,128)(2,1)S(1)}, u32[]{:S(2)}, u32[]{:S(2)}) collective-permute-start(bf16[256,768]{1,0:T(8,128)(2,1)S(1)} %slice.80), channel_id=1, source_target_pairs={{1,0},{2,1},{3,2},{4,3},{5,4},{6,5},{7,6},{8,7},{9,8},{10,9},{11,1... | collective-permute-start | bytes 1179656 | tf_op jit(solution)/shard_map/ppermute | solution.py:26
  65.2 10.9 %collective-permute-start.6 = (bf16[256,768]{1,0:T(8,128)(2,1)S(1)}, bf16[256,768]{1,0:T(8,128)(2,1)S(1)}, u32[]{:S(2)}, u32[]{:S(2)}) collective-permute-start(bf16[256,768]{1,0:T(8,128)(2,1)S(1)} %get-tuple-element.14), channel_id=1, source_target_pairs={{0,1},{1,2},{2,3},{3,4},{4,5},{5,6},{6,7},{7,8},{8,9},{9,10},{10,1... | collective-permute-start | bytes 1179656 | tf_op jit(solution)/shard_map/ppermute | solution.py:25
  67.6 8.8 %collective-permute-start.9 = (bf16[256,768]{1,0:T(8,128)(2,1)S(1)}, bf16[256,768]{1,0:T(8,128)(2,1)S(1)}, u32[]{:S(2)}, u32[]{:S(2)}) collective-permute-start(bf16[256,768]{1,0:T(8,128)(2,1)S(1)} %get-tuple-element.13), channel_id=1, source_target_pairs={{0,4},{8,12},{16,20},{24,28}} | collective-permute-start | bytes 1179656 | tf_op jit(solution)/shard_map/ppermute | solution.py:52
  77.0 13.6 %collective-permute-start.10 = (bf16[256,768]{1,0:T(8,128)(2,1)S(1)}, bf16[256,768]{1,0:T(8,128)(2,1)S(1)}, u32[]{:S(2)}, u32[]{:S(2)}) collective-permute-start(bf16[256,768]{1,0:T(8,128)(2,1)S(1)} %broadcast_select_fusion.2), channel_id=1, source_target_pairs={{0,2},{4,6},{8,10},{12,14},{16,18},{20,22},{24,26},{28,30}} | collective-permute-start | bytes 1179656 | tf_op jit(solution)/shard_map/ppermute | solution.py:52
  78.9 13.8 %copy-start.2 = (bf16[768,2304]{1,0:T(8,128)(2,1)S(1)}, bf16[768,2304]{1,0:T(8,128)(2,1)}, u32[]{:S(2)}) copy-start(bf16[768,2304]{1,0:T(8,128)(2,1)} %get-tuple-element.11) | copy-start | bytes 10616836
  91.2 7.2 %collective-permute-start.11 = (bf16[256,768]{1,0:T(8,128)(2,1)S(1)}, bf16[256,768]{1,0:T(8,128)(2,1)S(1)}, u32[]{:S(2)}, u32[]{:S(2)}) collective-permute-start(bf16[256,768]{1,0:T(8,128)(2,1)S(1)} %broadcast_select_fusion.4), channel_id=1, source_target_pairs={{0,1},{2,3},{4,5},{6,7},{8,9},{10,11},{12,13},{14,15},{16,17},{18,... | collective-permute-start | bytes 1179656 | tf_op jit(solution)/shard_map/ppermute | solution.py:52
  117.0 2.8 %copy-start.9 = (f32[768]{0:T(1024)S(1)}, f32[768]{0:T(1024)}, u32[]{:S(2)}) copy-start(f32[768]{0:T(1024)} %param.22) | copy-start | bytes 9220
  119.4 1.4 %copy-start.6 = (s32[512]{0:T(512)S(1)}, s32[512]{0:T(512)}, u32[]{:S(2)}) copy-start(s32[512]{0:T(512)} %param.24) | copy-start | bytes 6148
  119.8 1.2 %copy-start.7 = (f32[512]{0:T(512)S(1)}, f32[512]{0:T(512)}, u32[]{:S(2)}) copy-start(f32[512]{0:T(512)} %param.26) | copy-start | bytes 6148
  119.8 1.2 %copy-start.8 = (s32[512]{0:T(512)S(1)}, s32[512]{0:T(512)}, u32[]{:S(2)}) copy-start(s32[512]{0:T(512)} %param.25) | copy-start | bytes 6148
  121.0 0.6 copy-start.4

commit v17 on v12

--- a/solution.py
+++ b/solution.py
@@ -69,8 +69,8 @@
 
 
 def attention_kernel(row0, pos_ref, q_ref, *refs):
-    band_refs = refs[:-2]
-    prompt_ref, out_ref = refs[-2:]
+    band_refs = refs[:-5]
+    prompt_ref, hidden_ref, w_out_ref, out_ref, attn_ref = refs[-5:]
     tile = q_ref.shape[0]
     width = tile * len(band_refs)
     feat = q_ref.shape[1]
@@ -122,16 +122,18 @@
         attn = mixed[:tile]
         for j in range(1, GROUP):
             attn = jnp.where(lane_head == j, mixed[j * tile : (j + 1) * tile], attn)
-        out_ref[:, cols] = attn.astype(out_ref.dtype)
-
-
-def attention(queries, band_kv, prompt_kv, first_pos, total_len, row0, count):
+        attn_ref[:, cols] = attn.astype(attn_ref.dtype)
+    projection = jnp.dot(attn_ref[...], w_out_ref[...], preferred_element_type=jnp.float32)
+    out_ref[...] = (hidden_ref[...].astype(jnp.float32) + projection).astype(out_ref.dtype)
+
+
+def attention(queries, band_kv, prompt_kv, first_pos, total_len, row0, count, hidden, w_out, layer):
     feat = queries.shape[1]
     tile = min(QUERY_TILE, count)
     pos = jnp.stack([first_pos, total_len]).astype(jnp.int32)
     pieces = 1 + 2 * HALF // tile
     width = tile * pieces
-    flops = 4 * count * (width + PROMPT) * feat * GROUP
+    flops = 4 * count * (width + PROMPT) * feat * GROUP + 2 * count * feat * feat
     skip = row0 // tile
     band_specs = [
         pl.BlockSpec((tile, band_kv.shape[1]), lambda b, p, k=k: (b + skip + k, 0))
@@ -145,15 +147,20 @@
             grid=(count // tile,),
             in_specs=[pl.BlockSpec((tile, feat), lambda b, p: (b + skip, 0))]
             + band_specs
-            + [pl.BlockSpec(prompt_kv.shape, lambda b, p: (0, 0))],
+            + [
+                pl.BlockSpec(prompt_kv.shape, lambda b, p: (0, 0)),
+                pl.BlockSpec((tile, feat), lambda b, p: (b + skip, 0)),
+                pl.BlockSpec((None, feat, feat), lambda b, p: (layer, 0, 0)),
+            ],
             out_specs=pl.BlockSpec((tile, feat), lambda b, p: (b, 0)),
+            scratch_shapes=[pltpu.VMEM((tile, feat), jnp.bfloat16)],
         ),
         cost_estimate=pl.CostEstimate(
             flops=flops,
             transcendentals=count * (width + PROMPT) * HEADS,
-            bytes_accessed=2 * (2 * count * feat + pieces * count * band_kv.shape[1] + prompt_kv.size),
+            bytes_accessed=2 * (3 * count * feat + pieces * count * band_kv.shape[1] + prompt_kv.size + feat * feat),
         ),
-    )(pos, queries, *([band_kv] * pieces), prompt_kv)
+    )(pos, queries, *([band_kv] * pieces), prompt_kv, hidden, w_out)
 
 
 def per_device(
@@ -194,9 +201,10 @@
             weights[:, feat_width:],
             preferred_element_type=jnp.float32,
         ).astype(jnp.bfloat16)
-        attended = attention(queries, band_kv, prompt_kv, first_pos, total_len, 0, tok_rows)
-        projection = jnp.dot(attended, w_out[layer_idx], preferred_element_type=jnp.float32)
-        hidden_state = (hidden_state.astype(jnp.float32) + projection).astype(jnp.bfloat16)
+        hidden_state = attention(
+            queries, band_kv, prompt_kv, first_pos, total_len, 0, tok_rows,
+            hidden_state, w_out, layer_idx,
+        )
         prompt_source = hidden_state[:PROMPT]
     final = layer_norm(hidden_state, final_gain)
     head_out = jnp.dot(final, w_heads, preferred_element_type=jnp.float32)

time: 122 us -> 126 us (1.033)
  matrix products: 20.4 us -> 16.9 us
  other arithmetic: 14.3 us -> 17.8 us
  Pallas kernels: 31.3 us -> 33.7 us
    dot_general x2 -> x0, matrix products: 4.68 us -> none  [per_device(): jnp.dot(attended, w_out[layer_idx], preferred_element_type=jnp.float32)]
    pallas_call x2, Pallas kernels: 31.3 us -> 33.7 us  [attention(): pl.pallas_call(functools.partial(attention_kernel, row0), out_shape=jax.S...]
    reduce_sum x4 -> x5, other arithmetic: 2.31 us -> 3.63 us  [layer_norm(): row_mean = jnp.mean(values_f, axis=-1, keepdims=True)]
    ppermute x8, waiting for transfers between devices: 18 us -> 19.3 us  [spread(): got = lax.ppermute(block, axis, op)]
  transfers between devices with their start and end apart: 12 -> 12, of which waited for: 5 -> 5; matrix products, arithmetic and copies ran while one was open for 21% -> 22% of each run, Pallas kernels for 0% -> 0%
where the time goes in v17:
time: 126 us
  Pallas kernels  33.7 us (27%)
  waiting for transfers between devices  29.4 us (23%)
  other arithmetic  17.8 us (14%)
  starting transfers between devices  17.7 us (14%)
  matrix products  16.9 us (13%)
  local copies, waits for them, and re-layouts  8.64 us (7%)
  between operations  1.69 us (1%)
    pallas_call x2, Pallas kernels, attention(): pl.pallas_call(functools.partial(attention_kernel, row0), out_shape=jax.S...  33.7 us
    ppermute x8, waiting for transfers between devices, spread(): got = lax.ppermute(block, axis, op)  19.3 us
    ppermute x2, waiting for transfers between devices, with_halo(): before = lax.ppermute(last, axis, up)  9.74 us
    ppermute x8, starting transfers between devices, spread(): got = lax.ppermute(block, axis, op)  8.88 us
    dot_general x2, matrix products, per_device(): jnp.dot(extended_normed, weights[:, feat_width:], preferred_element_type=...  8.08 us
    squeeze x1, local copies, waits for them, and re-layouts, per_device(): weights = w_qkv[layer_idx]  6.35 us
    ppermute x2, starting transfers between devices, with_halo(): before = lax.ppermute(last, axis, up)  4.81 us
    ppermute x2, starting transfers between devices, with_halo(): after = lax.ppermute(leading, axis, down)  3.97 us
  transfers between devices with their start and end apart: 12, of which 5 were waited for; matrix products, arithmetic and copies ran while one was open for 22% of the time, Pallas kernels for 0%

profile of v17, /device:TPU:20, one launch (start us, length us, event | category | flops | bytes accessed | tf_op | source)
XLA Modules:
  0.0 125.7 jit_solution(4687196044043112476)
XLA Ops:
  0.6 1.1 slice.53
  1.8 2.1 %collective-permute-start.1 = (bf16[256,768]{1,0:T(8,128)(2,1)S(1)}, bf16[256,768]{1,0:T(8,128)(2,1)S(1)}, u32[]{:S(2)}, u32[]{:S(2)}) collective-permute-start(bf16[256,768]{1,0:T(8,128)(2,1)S(1)} %slice.53), channel_id=1, source_target_pairs={{1,0},{2,1},{3,2},{4,3},{5,4},{6,5},{7,6},{8,7},{9,8},{10,9},{11,1... | collective-permute-start | bytes 1179656 | tf_op jit(solution)/shard_map/ppermute | solution.py:26
  3.9 0.7 collective-permute-start.2
  4.6 6.4 %slice_bitcast_fusion.1 = (bf16[768,2304]{1,0:T(8,128)(2,1)}, bf16[768,2304]{1,0:T(8,128)(2,1)}) fusion(bf16[2,768,2304]{2,1,0:T(8,128)(2,1)} %param.20), kind=kLoop, calls=%fused_computation.11 | loop fusion | bytes 14155776 | tf_op jit(solution)/shard_map/squeeze | solution.py:188
  10.9 0.6 compare_reduce_fusion
  11.6 2.4 %collective-permute-start = (bf16[256,768]{1,0:T(8,128)(2,1)S(1)}, bf16[256,768]{1,0:T(8,128)(2,1)S(1)}, u32[]{:S(2)}, u32[]{:S(2)}) collective-permute-start(bf16[256,768]{1,0:T(8,128)(2,1)S(1)} %get-tuple-element.16), channel_id=1, source_target_pairs={{0,1},{1,2},{2,3},{3,4},{4,5},{5,6},{6,7},{7,8},{8,9},{9,10},{10,1... | collective-permute-start | bytes 1179656 | tf_op jit(solution)/shard_map/ppermute | solution.py:25
  14.0 0.6 compare_reduce_fusion.1
  14.6 0.7 compare_reduce_fusion.2
  15.4 0.7 collective-permute-start.3
  16.1 0.6 pad_add_fusion.pos_ref
  16.7 4.0 %collective-permute-done = bf16[256,768]{1,0:T(8,128)(2,1)S(1)} collective-permute-done((bf16[256,768]{1,0:T(8,128)(2,1)S(1)}, bf16[256,768]{1,0:T(8,128)(2,1)S(1)}, u32[]{:S(2)}, u32[]{:S(2)}) %collective-permute-start) | collective-permute-done | bytes 393248 | tf_op jit(solution)/shard_map/ppermute | solution.py:25
  20.7 0.3 convert_reduce_fusion.1
  21.0 0.6 broadcast_select_fusion.3
  21.6 1.6 %collective-permute-start.4 = (bf16[256,768]{1,0:T(8,128)(2,1)S(1)}, bf16[256,768]{1,0:T(8,128)(2,1)S(1)}, u32[]{:S(2)}, u32[]{:S(2)}) collective-permute-start(bf16[256,768]{1,0:T(8,128)(2,1)S(1)} %broadcast_select_fusion.3), channel_id=1, source_target_pairs={{0,2},{4,6},{8,10},{12,14},{16,18},{20,22},{24,26},{28,30}} | collective-permute-start | bytes 1179656 | tf_op jit(solution)/shard_map/ppermute | solution.py:52
  23.2 0.6 fusion.7
  23.8 1.9 %fusion.9 = bf16[1024,768]{1,0:T(8,128)(2,1)S(1)} fusion(f32[768]{0:T(1024)S(1)} %get-tuple-element.5, f32[1024]{0:T(1024)S(1)} %add_rsqrt_fusion.1, f32[1024]{0:T(1024)S(1)} %broadcast_multiply_fusion.1, bf16[256,768]{1,0:T(8,128)(2,1)S(1)} %collective-permute-done.1, bf16[512,768]{1,0:T(8,128)(2,1)S(1)} %copy-done.1, ...), kind=kLoop, calls=%fused_computation.17 | loop fusion | flops 7864320 | bytes 3156992 | tf_op jit(solution)/shard_map/convert_element_type | solution.py:64
  25.7 8.4 %collective-permute-done.4 = bf16[256,768]{1,0:T(8,128)(2,1)S(1)} collective-permute-done((bf16[256,768]{1,0:T(8,128)(2,1)S(1)}, bf16[256,768]{1,0:T(8,128)(2,1)S(1)}, u32[]{:S(2)}, u32[]{:S(2)}) %collective-permute-start.4) | collective-permute-done | bytes 393248 | tf_op jit(solution)/shard_map/ppermute | solution.py:52
  34.1 0.6 broadcast_select_fusion.5
  34.6 1.5 %collective-permute-start.5 = (bf16[256,768]{1,0:T(8,128)(2,1)S(1)}, bf16[256,768]{1,0:T(8,128)(2,1)S(1)}, u32[]{:S(2)}, u32[]{:S(2)}) collective-permute-start(bf16[256,768]{1,0:T(8,128)(2,1)S(1)} %broadcast_select_fusion.5), channel_id=1, source_target_pairs={{0,1},{2,3},{4,5},{6,7},{8,9},{10,11},{12,13},{14,15},{16,17},{18,... | collective-permute-start | bytes 1179656 | tf_op jit(solution)/shard_map/ppermute | solution.py:52
  36.2 4.1 %convolution_convert_fusion.1.refs_0_.refs_1_.refs_2_ = bf16[1024,1536]{1,0:T(8,128)(2,1)} fusion(bf16[1024,768]{1,0:T(8,128)(2,1)S(1)} %fusion.9, bf16[768,2304]{1,0:T(8,128)(2,1)S(1)} %copy-done.4), kind=kOutput, calls=%fused_computation.5 | convolution fusion | flops 2417491968 | bytes 7077888 | tf_op jit(solution)/shard_map/dot_general | solution.py:192
  40.2 1.7 %multiply_convert_fusion.1.q_ref = bf16[512,768]{1,0:T(8,128)(2,1)} fusion(bf16[768,2304]{1,0:T(8,128)(2,1)S(1)} %copy-done.4, bf16[1024,768]{1,0:T(8,128)(2,1)S(1)} %fusion.9), kind=kOutput, calls=%fused_computation.34 | convolution fusion | flops 604766208 | bytes 2752512 | tf_op jit(solution)/shard_map/dot_general | solution.py:197
  41.9 0.9 convert_reduce_fusion.4
  43.0 1.8 %convolution_convert_fusion.3.refs_3_ = bf16[256,1536]{1,0:T(8,128)(2,1)} fusion(bf16[768,2304]{1,0:T(8,128)(2,1)S(1)} %copy-done.4, bf16[256,768]{1,0:T(8,128)(2,1)S(1)} %get-tuple-element.10, f32[768]{0:T(1024)S(1)} %get-tuple-element.5, f32[256]{0:T(256)S(1)} %add_rsqrt_fusion.4, f32[256]{0:T(256)S(1)} %broadcast_multiply_fusion.4), kind=kOutput, calls=%fused_computation.19 | convolution fusion | flops 605356032 | bytes 3545088 | tf_op jit(solution)/shard_map/dot_general | solution.py:199
  44.9 16.8 %shard_map.185.refs_4_ = bf16[512,768]{1,0:T(8,128)(2,1)} custom-call(s32[2]{0:T(128)} %pad_add_fusion.pos_ref, bf16[512,768]{1,0:T(8,128)(2,1)} %multiply_convert_fusion.1.q_ref, bf16[1024,1536]{1,0:T(8,128)(2,1)} %convolution_convert_fusion.1.refs_0_.refs_1_.refs_2_, bf16[1024,1536]{1,0:T(8,128)(2,1)} %convolution_convert_fusion.1.refs_0_.refs_1_.refs_2_, ...), custom_call_target="tpu_custom_call" | custom-call | flops 7046430720 | bytes 9043968 | tf_op jit(solution)/shard_map/pallas_call | solution.py:142
  61.6 1.1 slice.72
  62.7 0.7 collective-permute-start.8
  63.4 1.9 %collective-permute-start.7 = (bf16[256,768]{1,0:T(8,128)(2,1)S(1)}, bf16[256,768]{1,0:T(8,128)(2,1)S(1)}, u32[]{:S(2)}, u32[]{:S(2)}) collective-permute-start(bf16[256,768]{1,0:T(8,128)(2,1)S(1)} %slice.72), channel_id=1, source_target_pairs={{1,0},{2,1},{3,2},{4,3},{5,4},{6,5},{7,6},{8,7},{9,8},{10,9},{11,1... | collective-permute-start | bytes 1179656 | tf_op jit(solution)/shard_map/ppermute | solution.py:26
  65.4 1.2 broadcast_select_fusion
  66.6 2.4 %collective-permute-start.6 = (bf16[256,768]{1,0:T(8,128)(2,1)S(1)}, bf16[256,768]{1,0:T(8,128)(2,1)S(1)}, u32[]{:S(2)}, u32[]{:S(2)}) collective-permute-start(bf16[256,768]{1,0:T(8,128)(2,1)S(1)} %get-tuple-element.14), channel_id=1, source_target_pairs={{0,1},{1,2},{2,3},{3,4},{4,5},{5,6},{6,7},{7,8},{8,9},{9,10},{10,1... | collective-permute-start | bytes 1179656 | tf_op jit(solution)/shard_map/ppermute | solution.py:25
  69.0 0.7 collective-permute-start.9
  70.3 0.3 collective-permute-done.7
  70.6 5.7 %collective-permute-done.6 = bf16[256,768]{1,0:T(8,128)(2,1)S(1)} collective-permute-done((bf16[256,768]{1,0:T(8,128)(2,1)S(1)}, bf16[256,768]{1,0:T(8,128)(2,1)S(1)}, u32[]{:S(2)}, u32[]{:S(2)}) %collective-permute-start.6) | collective-permute-done | bytes 393248 | tf_op jit(solution)/shard_map/ppermute | solution.py:25
  76.6 0.6 broadcast_select_fusion.2
  77.3 1.6 %collective-permute-start.10 = (bf16[256,768]{1,0:T(8,128)(2,1)S(1)}, bf16[256,768]{1,0:T(8,128)(2,1)S(1)}, u32[]{:S(2)}, u32[]{:S(2)}) collective-permute-start(bf16[256,768]{1,0:T(8,128)(2,1)S(1)} %broadcast_select_fusion.2), channel_id=1, source_target_pairs={{0,2},{4,6},{8,10},{12,14},{16,18},{20,22},{24,26},{28,30}} | collective-permute-start | bytes 1179656 | tf_op jit(solution)/shard_map/ppermute | solution.py:52
  78.8 0.6 fusion.4
  79.4 1.9 %fusion.6 = bf16[1024,768]{1,0:T(8,128)(2,1)S(1)} fusion(f32[768]{0:T(1024)S(1)} %get-tuple-element.6, f32[1024]{0:T(1024)S(1)} %add_rsqrt_fusion, f32[1024]{0:T(1024)S(1)} %broadcast_multiply_fusion, bf16[256,768]{1,0:T(8,128)(2,1)S(1)} %collective-permute-done.7, bf16[512,768]{1,0:T(8,128)(2,1)S(1)} %copy-done.2, ...), kind=kLoop, calls=%fused_computation.14 | loop fusion | flops 7864320 | bytes 3156992 | tf_op jit(solution)/shard_map/convert_element_type | solution.py:64
  81.3 10.9 %collective-permute-done.10 = bf16[256,768]{1,0:T(8,128)(2,1)S(1)} collective-permute-done((bf16[256,768]{1,0:T(8,128)(2,1)S(1)}, bf16[256,768]{1,0:T(8,128)(2,1)S(1)}, u32[]{:S(2)}, u32[]{:S(2)}) %collective-permute-start.10) | collective-permute-done | bytes 393248 | tf_op jit(solution)/shard_map/ppermute | solution.py:52
  92.2 0.6 broadcast_select_fusion.4
  92.8 1.5 %collective-permute-start.11 = (bf16[256,768]{1,0:T(8,128)(2,1)S(1)}, bf16[256,768]{1,0:T(8,128)(2,1)S(1)}, u32[]{:S(2)}, u32[]{:S(2)}) collective-permute-start(bf16[256,768]{1,0:T(8,128)(2,1)S(1)} %broadcast_select_fusion.4), channel_id=1, source_target_pairs={{0,1},{2,3},{4,5},{6,7},{8,9},{10,11},{12,13},{14,15},{16,17},{18,... | collective-permute-start | bytes 1179656 | tf_op jit(solution)/shard_map/ppermute | solution.py:52
  94.4 4.0 %convolution_convert_fusion.refs_0_.refs_1_.refs_2_ = bf16[1024,1536]{1,0:T(8,128)(2,1)} fusion(bf16[1024,768]{1,0:T(8,128)(2,1)S(1)} %fusion.6, bf16[768,2304]{1,0:T(8,128)(2,1)S(1)} %copy-done.3), kind=kOutput, calls=%fused_computation.4 | convolution fusion | flops 2417491968 | bytes 7077888 | tf_op jit(solution)/shard_map/dot_general | solution.py:192
  98.4 1.7 %multiply_convert_fusion.q_ref = bf16[512,768]{1,0:T(8,128)(2,1)} fusion(bf16[768,2304]{1,0:T(8,128)(2,1)S(1)} %copy-done.3, bf16[1024,768]{1,0:T(8,128)(2,1)S(1)} %fusion.6), kind=kOutput, calls=%fused_computation.33 | convolution fusion | flops 604766208 | bytes 2752512 | tf_op jit(solution)/shard_map/dot_general | solution.py:197
  100.1 0.9 convert_reduce_fusion.3
  101.2 1.7 %convolution_convert_fusion.2.refs_3_ = bf16[256,1536]{1,0:T(8,128)(2,1)} fusion(bf16[768,2304]{1,0:T(8,128)(2,1)S(1)} %copy-done.3, bf16[256,768]{1,0:T(8,128)(2,1)S(1)} %get-tuple-element.8, f32[768]{0:T(1024)S(1)} %get-tuple-element.6, f32[256]{0:T(256)S(1)} %add_rsqrt_fusion.3, f32[256]{0:T(256)S(1)} %broadcast_multiply_fusion.3), kind=kOutput, calls=%fused_computation.18 | convolution fusion | flops 605356032 | bytes 3545088 | tf_op jit(solution)/shard_map/dot_general | solution.py:199
  103.0 16.9 %shard_map.186 = bf16[512,768]{1,0:T(8,128)(2,1)} custom-call(s32[2]{0:T(128)} %pad_add_fusion.pos_ref, bf16[512,768]{1,0:T(8,128)(2,1)} %multiply_convert_fusion.q_ref, bf16[1024,1536]{1,0:T(8,128)(2,1)} %convolution_convert_fusion.refs_0_.refs_1_.refs_2_, bf16[1024,1536]{1,0:T(8,128)(2,1)} %convolution_convert_fusion.refs_0_.refs_1_.refs_2_, ...), custom_call_target="tpu_custom_call" | custom-call | flops 7046430720 | bytes 9043968 | tf_op jit(solution)/shard_map/pallas_call | solution.py:142
  119.9 1.3 %convert_reduce_fusion.2 = f32[512]{0:T(512)S(1)} fusion(bf16[512,768]{1,0:T(8,128)(2,1)} %shard_map.186), kind=kLoop, calls=%fused_computation.25 | loop fusion | flops 785920 | bytes 788480 | tf_op jit(solution)/shard_map/reduce_sum | solution.py:61
  121.2 1.5 %fusion.16 = f32[512]{0:T(512)S(1)} fusion(bf16[512,768]{1,0:T(8,128)(2,1)} %shard_map.186, f32[512]{0:T(512)S(1)} %broadcast_multiply_fusion.2), kind=kLoop, calls=%fused_computation.28 | loop fusion | flops 1572352 | bytes 790528 | tf_op jit(solution)/shard_map/reduce_sum | solution.py:63
  122.7 1.9 %fusion.31 = f32[512,512]{0,1:T(8,128)S(1)} fusion(bf16[768,512]{1,0:T(8,128)(2,1)S(1)} %copy-done, bf16[512,768]{1,0:T(8,128)(2,1)} %shard_map.186, f32[768]{0:T(1024)S(1)} %copy-done.10, f32[512]{0:T(512)S(1)} %add_rsqrt_fusion.2, f32[512]{0:T(512)S(1)} %broadcast_multiply_fusion.2), kind=kOutput, calls=%fused_computation.51 | convolution fusion | flops 404619264 | bytes 2628608 | tf_op jit(solution)/shard_map/dot_general | solution.py:210
  125.1 0.6 multiply_add_fusion
  (53 shorter events, 1.4 us)
Async XLA Ops:
  0.6 122.1 %copy-start = (bf16[768,512]{1,0:T(8,128)(2,1)S(1)}, bf16[768,512]{1,0:T(8,128)(2,1)}, u32[]{:S(2)}) copy-start(bf16[768,512]{1,0:T(8,128)(2,1)} %param.23) | copy-start | bytes 2359300
  1.7 9.2 %copy-start.13 = (s32[2]{0:T(128)S(1)}, s32[2]{0:T(128)}, u32[]{:S(2)}) copy-start(s32[2]{0:T(128)} %constant.49.clone) | copy-start | bytes 28
  1.8 9.8 %copy-start.1 = (bf16[512,768]{1,0:T(8,128)(2,1)S(1)}, bf16[512,768]{1,0:T(8,128)(2,1)}, u32[]{:S(2)}) copy-start(bf16[512,768]{1,0:T(8,128)(2,1)} %refs_4_.1) | copy-start | bytes 2359300
  1.8 12.3 %copy-start.12 = (s32[4]{0:T(128)S(1)}, s32[4]{0:T(128)}, u32[]{:S(2)}) copy-start(s32[4]{0:T(128)} %constant.50.clone) | copy-start | bytes 52
  1.8 12.9 %copy-start.11 = (s32[8]{0:T(128)S(1)}, s32[8]{0:T(128)}, u32[]{:S(2)}) copy-start(s32[8]{0:T(128)} %constant.51.clone) | copy-start | bytes 100
  1.8 13.6 %copy-start.6 = (f32[2,768]{1,0:T(2,128)S(1)}, f32[2,768]{1,0:T(2,128)}, u32[]{:S(2)}) copy-start(f32[2,768]{1,0:T(2,128)} %param.19) | copy-start | bytes 18436
  1.8 14.9 %collective-permute-start.1 = (bf16[256,768]{1,0:T(8,128)(2,1)S(1)}, bf16[256,768]{1,0:T(8,128)(2,1)S(1)}, u32[]{:S(2)}, u32[]{:S(2)}) collective-permute-start(bf16[256,768]{1,0:T(8,128)(2,1)S(1)} %slice.53), channel_id=1, source_target_pairs={{1,0},{2,1},{3,2},{4,3},{5,4},{6,5},{7,6},{8,7},{9,8},{10,9},{11,1... | collective-permute-start | bytes 1179656 | tf_op jit(solution)/shard_map/ppermute | solution.py:26
  3.9 7.7 %collective-permute-start.2 = (bf16[256,768]{1,0:T(8,128)(2,1)S(1)}, bf16[256,768]{1,0:T(8,128)(2,1)S(1)}, u32[]{:S(2)}, u32[]{:S(2)}) collective-permute-start(bf16[256,768]{1,0:T(8,128)(2,1)S(1)} %slice.53), channel_id=1, source_target_pairs={{0,8},{16,24}} | collective-permute-start | bytes 1179656 | tf_op jit(solution)/shard_map/ppermute | solution.py:52
  11.6 9.1 %collective-permute-start = (bf16[256,768]{1,0:T(8,128)(2,1)S(1)}, bf16[256,768]{1,0:T(8,128)(2,1)S(1)}, u32[]{:S(2)}, u32[]{:S(2)}) collective-permute-start(bf16[256,768]{1,0:T(8,128)(2,1)S(1)} %get-tuple-element.16), channel_id=1, source_target_pairs={{0,1},{1,2},{2,3},{3,4},{4,5},{5,6},{6,7},{7,8},{8,9},{9,10},{10,1... | collective-permute-start | bytes 1179656 | tf_op jit(solution)/shard_map/ppermute | solution.py:25
  15.4 5.6 %collective-permute-start.3 = (bf16[256,768]{1,0:T(8,128)(2,1)S(1)}, bf16[256,768]{1,0:T(8,128)(2,1)S(1)}, u32[]{:S(2)}, u32[]{:S(2)}) collective-permute-start(bf16[256,768]{1,0:T(8,128)(2,1)S(1)} %get-tuple-element.15), channel_id=1, source_target_pairs={{0,4},{8,12},{16,20},{24,28}} | collective-permute-start | bytes 1179656 | tf_op jit(solution)/shard_map/ppermute | solution.py:52
  21.6 14.5 %copy-start.4 = (bf16[768,2304]{1,0:T(8,128)(2,1)S(1)}, bf16[768,2304]{1,0:T(8,128)(2,1)}, u32[]{:S(2)}) copy-start(bf16[768,2304]{1,0:T(8,128)(2,1)} %get-tuple-element.11) | copy-start | bytes 10616836
  21.6 12.4 %collective-permute-start.4 = (bf16[256,768]{1,0:T(8,128)(2,1)S(1)}, bf16[256,768]{1,0:T(8,128)(2,1)S(1)}, u32[]{:S(2)}, u32[]{:S(2)}) collective-permute-start(bf16[256,768]{1,0:T(8,128)(2,1)S(1)} %broadcast_select_fusion.3), channel_id=1, source_target_pairs={{0,2},{4,6},{8,10},{12,14},{16,18},{20,22},{24,26},{28,30}} | collective-permute-start | bytes 1179656 | tf_op jit(solution)/shard_map/ppermute | solution.py:52
  34.6 7.2 %collective-permute-start.5 = (bf16[256,768]{1,0:T(8,128)(2,1)S(1)}, bf16[256,768]{1,0:T(8,128)(2,1)S(1)}, u32[]{:S(2)}, u32[]{:S(2)}) collective-permute-start(bf16[256,768]{1,0:T(8,128)(2,1)S(1)} %broadcast_select_fusion.5), channel_id=1, source_target_pairs={{0,1},{2,3},{4,5},{6,7},{8,9},{10,11},{12,13},{14,15},{16,17},{18,... | collective-permute-start | bytes 1179656 | tf_op jit(solution)/shard_map/ppermute | solution.py:52
  61.6 14.7 %copy-start.2 = (bf16[512,768]{1,0:T(8,128)(2,1)S(1)}, bf16[512,768]{1,0:T(8,128)(2,1)}, u32[]{:S(2)}) copy-start(bf16[512,768]{1,0:T(8,128)(2,1)} %shard_map.185.refs_4_) | copy-start | bytes 2359300
  62.7 2.6 %collective-permute-start.8 = (bf16[256,768]{1,0:T(8,128)(2,1)S(1)}, bf16[256,768]{1,0:T(8,128)(2,1)S(1)}, u32[]{:S(2)}, u32[]{:S(2)}) collective-permute-start(bf16[256,768]{1,0:T(8,128)(2,1)S(1)} %slice.72), channel_id=1, source_target_pairs={{0,8},{16,24}} | collective-permute-start | bytes 1179656 | tf_op jit(solution)/shard_map/ppermute | solution.py:52
  63.4 7.2 %collective-permute-start.7 = (bf16[256,768]{1,0:T(8,128)(2,1)S(1)}, bf16[256,768]{1,0:T(8,128)(2,1)S(1)}, u32[]{:S(2)}, u32[]{:S(2)}) collective-permute-start(bf16[256,768]{1,0:T(8,128)(2,1)S(1)} %slice.72), channel_id=1, source_target_pairs={{1,0},{2,1},{3,2},{4,3},{5,4},{6,5},{7,6},{8,7},{9,8},{10,9},{11,1... | collective-permute-start | bytes 1179656 | tf_op jit(solution)/shard_map/ppermute | solution.py:26
  66.6 9.8 %collective-permute-start.6 = (bf16[256,768]{1,0:T(8,128)(2,1)S(1)}, bf16[256,768]{1,0:T(8,128)(2,1)S(1)}, u32[]{:S(2)}, u32[]{:S(2)}) collective-permute-start(bf16[256,768]{1,0:T(8,128)(2,1)S(1)} %get-tuple-element.14), channel_id=1, source_target_pairs={{0,1},{1,2},{2,3},{3,4},{4,5},{5,6},{6,7},{7,8},{8,9},{9,10},{10,1... | collective-permute-start | bytes 1179656 | tf_op jit(solution)/shard_map/ppermute | solution.py:25
  69.0 7.6 %collective-permute-start.9 = (bf16[256,768]{1,0:T(8,128)(2,1)S(1)}, bf16[256,768]{1,0:T(8,128)(2,1)S(1)}, u32[]{:S(2)}, u32[]{:S(2)}) collective-permute-start(bf16[256,768]{1,0:T(8,128)(2,1)S(1)} %get-tuple-element.13), channel_id=1, source_target_pairs={{0,4},{8,12},{16,20},{24,28}} | collective-permute-start | bytes 1179656 | tf_op jit(solution)/shard_map/ppermute | solution.py:52
  77.2 17.1 %copy-start.3 = (bf16[768,2304]{1,0:T(8,128)(2,1)S(1)}, bf16[768,2304]{1,0:T(8,128)(2,1)}, u32[]{:S(2)}) copy-start(bf16[768,2304]{1,0:T(8,128)(2,1)} %get-tuple-element.12) | copy-start | bytes 10616836
  77.3 15.0 %collective-permute-start.10 = (bf16[256,768]{1,0:T(8,128)(2,1)S(1)}, bf16[256,768]{1,0:T(8,128)(2,1)S(1)}, u32[]{:S(2)}, u32[]{:S(2)}) collective-permute-start(bf16[256,768]{1,0:T(8,128)(2,1)S(1)} %broadcast_select_fusion.2), channel_id=1, source_target_pairs={{0,2},{4,6},{8,10},{12,14},{16,18},{20,22},{24,26},{28,30}} | collective-permute-start | bytes 1179656 | tf_op jit(solution)/shard_map/ppermute | solution.py:52
  92.8 7.2 %collective-permute-start.11 = (bf16[256,768]{1,0:T(8,128)(2,1)S(1)}, bf16[256,768]{1,0:T(8,128)(2,1)S(1)}, u32[]{:S(2)}, u32[]{:S(2)}) collective-permute-start(bf16[256,768]{1,0:T(8,128)(2,1)S(1)} %broadcast_select_fusion.4), channel_id=1, source_target_pairs={{0,1},{2,3},{4,5},{6,7},{8,9},{10,11},{12,13},{14,15},{16,17},{18,... | collective-permute-start | bytes 1179656 | tf_op jit(solution)/shard_map/ppermute | solution.py:52
  103.0 19.8 %copy-start.10 = (f32[768]{0:T(1024)S(1)}, f32[768]{0:T(1024)}, u32[]{:S(2)}) copy-start(f32[768]{0:T(1024)} %param.22) | copy-start | bytes 9220
  119.9 5.0 %copy-start.7 = (s32[512]{0:T(512)S(1)}, s32[512]{0:T(512)}, u32[]{:S(2)}) copy-start(s32[512]{0:T(512)} %param.24) | copy-start | bytes 6148
  121.2 3.9 %copy-start.8 = (f32[512]{0:T(512)S(1)}, f32[512]{0:T(512)}, u32[]{:S(2)}) copy-start(f32[512]{0:T(512)} %param.26) | copy-start | bytes 6148
  121.2 3.9 %copy-start.9 = (s32[512]{0:T(512)S(1)}, s32[512]{0:T(512)}, u32[]{:S(2)}) copy-start(s32[512]{0:T(512)} %param.25) | copy-start | bytes 6148
  125.1 0.6 copy-start.5

commit v18 on v17

--- a/solution.py
+++ b/solution.py
@@ -69,8 +69,8 @@
 
 
 def attention_kernel(row0, pos_ref, q_ref, *refs):
-    band_refs = refs[:-5]
-    prompt_ref, hidden_ref, w_out_ref, out_ref, attn_ref = refs[-5:]
+    band_refs = refs[:-6]
+    prompt_ref, hidden_ref, w_out_ref, out_ref, head_ref, attn_ref = refs[-6:]
     tile = q_ref.shape[0]
     width = tile * len(band_refs)
     feat = q_ref.shape[1]
@@ -124,10 +124,17 @@
             attn = jnp.where(lane_head == j, mixed[j * tile : (j + 1) * tile], attn)
         attn_ref[:, cols] = attn.astype(attn_ref.dtype)
     projection = jnp.dot(attn_ref[...], w_out_ref[...], preferred_element_type=jnp.float32)
-    out_ref[...] = (hidden_ref[...].astype(jnp.float32) + projection).astype(out_ref.dtype)
-
-
-def attention(queries, band_kv, prompt_kv, first_pos, total_len, row0, count, hidden, w_out, layer):
+    new_rows = (hidden_ref[...].astype(jnp.float32) + projection).astype(out_ref.dtype)
+    out_ref[...] = new_rows
+
+    @pl.when(block == 0)
+    def _():
+        head_ref[...] = new_rows[: head_ref.shape[0]]
+
+
+def attention(
+    queries, band_kv, prompt_kv, first_pos, total_len, row0, count, hidden, w_out, layer, head_rows
+):
     feat = queries.shape[1]
     tile = min(QUERY_TILE, count)
     pos = jnp.stack([first_pos, total_len]).astype(jnp.int32)
@@ -141,7 +148,10 @@
     ]
     return pl.pallas_call(
         functools.partial(attention_kernel, row0),
-        out_shape=jax.ShapeDtypeStruct((count, feat), jnp.bfloat16),
+        out_shape=(
+            jax.ShapeDtypeStruct((count, feat), jnp.bfloat16),
+            jax.ShapeDtypeStruct((head_rows, feat), jnp.bfloat16),
+        ),
         grid_spec=pltpu.PrefetchScalarGridSpec(
             num_scalar_prefetch=1,
             grid=(count // tile,),
@@ -152,7 +162,10 @@
                 pl.BlockSpec((tile, feat), lambda b, p: (b + skip, 0)),
                 pl.BlockSpec((None, feat, feat), lambda b, p: (layer, 0, 0)),
             ],
-            out_specs=pl.BlockSpec((tile, feat), lambda b, p: (b, 0)),
+            out_specs=(
+                pl.BlockSpec((tile, feat), lambda b, p: (b, 0)),
+                pl.BlockSpec((head_rows, feat), lambda b, p: (0, 0)),
+            ),
             scratch_shapes=[pltpu.VMEM((tile, feat), jnp.bfloat16)],
         ),
         cost_estimate=pl.CostEstimate(
@@ -201,11 +214,13 @@
             weights[:, feat_width:],
             preferred_element_type=jnp.float32,
         ).astype(jnp.bfloat16)
-        hidden_state = attention(
+        tile_rows = min(QUERY_TILE, tok_rows)
+        head_rows = PROMPT if PROMPT <= tile_rows else tile_rows
+        hidden_state, head_part = attention(
             queries, band_kv, prompt_kv, first_pos, total_len, 0, tok_rows,
-            hidden_state, w_out, layer_idx,
-        )
-        prompt_source = hidden_state[:PROMPT]
+            hidden_state, w_out, layer_idx, head_rows,
+        )
+        prompt_source = head_part if head_rows == PROMPT else hidden_state[:PROMPT]
     final = layer_norm(hidden_state, final_gain)
     head_out = jnp.dot(final, w_heads, preferred_element_type=jnp.float32)
     logits = head_out[:, :ACTIONS]

time: 126 us -> 124 us (0.984); the launches traced: 126 us -> 122 us
  waiting for transfers between devices: 29.4 us -> 25 us
    ppermute x8, waiting for transfers between devices: 19.3 us -> 14.8 us  [spread(): got = lax.ppermute(block, axis, op)]
    ppermute x2, waiting for transfers between devices: 0.32 us -> 4.67 us  [with_halo(): after = lax.ppermute(leading, axis, down)]
    ppermute x2, waiting for transfers between devices: 9.74 us -> 5.53 us  [with_halo(): before = lax.ppermute(last, axis, up)]
  transfers between devices with their start and end apart: 12 -> 12, of which waited for: 5 -> 5; matrix products, arithmetic and copies ran while one was open for 22% -> 23% of each run, Pallas kernels for 0% -> 0%
where the time goes in v18:
time: 124 us; the launch traced here: 122 us
  Pallas kernels  34 us (27%)
  waiting for transfers between devices  25 us (20%)
  other arithmetic  18.2 us (15%)
  starting transfers between devices  17.7 us (14%)
  matrix products  16.9 us (14%)
  local copies, waits for them, and re-layouts  8.72 us (7%)
  between operations  1.7 us (1%)
    pallas_call x2, Pallas kernels, attention(): pl.pallas_call(functools.partial(attention_kernel, row0), out_shape=(jax....  34 us
    ppermute x8, waiting for transfers between devices, spread(): got = lax.ppermute(block, axis, op)  14.8 us
    ppermute x8, starting transfers between devices, spread(): got = lax.ppermute(block, axis, op)  8.88 us
    dot_general x2, matrix products, per_device(): jnp.dot(extended_normed, weights[:, feat_width:], preferred_element_type=...  8.08 us
    squeeze x1, local copies, waits for them, and re-layouts, per_device(): weights = w_qkv[layer_idx]  6.35 us
    ppermute x2, waiting for transfers between devices, with_halo(): before = lax.ppermute(last, axis, up)  5.53 us
    ppermute x2, starting transfers between devices, with_halo(): before = lax.ppermute(last, axis, up)  4.81 us
    ppermute x2, waiting for transfers between devices, with_halo(): after = lax.ppermute(leading, axis, down)  4.67 us
  transfers between devices with their start and end apart: 12, of which 5 were waited for; matrix products, arithmetic and copies ran while one was open for 23% of the time, Pallas kernels for 0%

profile of v18, /device:TPU:20, one launch (start us, length us, event | category | flops | bytes accessed | tf_op | source)
XLA Modules:
  0.0 122.2 jit_solution(16673727021376436119)
XLA Ops:
  0.6 1.1 slice.52
  1.8 2.1 %collective-permute-start.1 = (bf16[256,768]{1,0:T(8,128)(2,1)S(1)}, bf16[256,768]{1,0:T(8,128)(2,1)S(1)}, u32[]{:S(2)}, u32[]{:S(2)}) collective-permute-start(bf16[256,768]{1,0:T(8,128)(2,1)S(1)} %slice.52), channel_id=1, source_target_pairs={{1,0},{2,1},{3,2},{4,3},{5,4},{6,5},{7,6},{8,7},{9,8},{10,9},{11,1... | collective-permute-start | bytes 1179656 | tf_op jit(solution)/shard_map/ppermute | solution.py:26
  3.9 0.7 collective-permute-start.2
  4.6 6.4 %slice_bitcast_fusion.1 = (bf16[768,2304]{1,0:T(8,128)(2,1)}, bf16[768,2304]{1,0:T(8,128)(2,1)}) fusion(bf16[2,768,2304]{2,1,0:T(8,128)(2,1)} %param.20), kind=kLoop, calls=%fused_computation.11 | loop fusion | bytes 14155776 | tf_op jit(solution)/shard_map/squeeze | solution.py:201
  10.9 0.7 compare_reduce_fusion
  11.7 2.4 %collective-permute-start = (bf16[256,768]{1,0:T(8,128)(2,1)S(1)}, bf16[256,768]{1,0:T(8,128)(2,1)S(1)}, u32[]{:S(2)}, u32[]{:S(2)}) collective-permute-start(bf16[256,768]{1,0:T(8,128)(2,1)S(1)} %get-tuple-element.22), channel_id=1, source_target_pairs={{0,1},{1,2},{2,3},{3,4},{4,5},{5,6},{6,7},{7,8},{8,9},{9,10},{10,1... | collective-permute-start | bytes 1179656 | tf_op jit(solution)/shard_map/ppermute | solution.py:25
  14.1 0.7 compare_reduce_fusion.1
  14.8 0.7 compare_reduce_fusion.2
  15.5 0.7 collective-permute-start.3
  16.2 0.6 pad_add_fusion.pos_ref
  16.8 4.0 %collective-permute-done = bf16[256,768]{1,0:T(8,128)(2,1)S(1)} collective-permute-done((bf16[256,768]{1,0:T(8,128)(2,1)S(1)}, bf16[256,768]{1,0:T(8,128)(2,1)S(1)}, u32[]{:S(2)}, u32[]{:S(2)}) %collective-permute-start) | collective-permute-done | bytes 393248 | tf_op jit(solution)/shard_map/ppermute | solution.py:25
  21.1 0.7 broadcast_select_fusion.3
  21.8 1.6 %collective-permute-start.4 = (bf16[256,768]{1,0:T(8,128)(2,1)S(1)}, bf16[256,768]{1,0:T(8,128)(2,1)S(1)}, u32[]{:S(2)}, u32[]{:S(2)}) collective-permute-start(bf16[256,768]{1,0:T(8,128)(2,1)S(1)} %broadcast_select_fusion.3), channel_id=1, source_target_pairs={{0,2},{4,6},{8,10},{12,14},{16,18},{20,22},{24,26},{28,30}} | collective-permute-start | bytes 1179656 | tf_op jit(solution)/shard_map/ppermute | solution.py:52
  23.4 0.6 fusion.7
  24.0 1.9 %fusion.9 = bf16[1024,768]{1,0:T(8,128)(2,1)S(1)} fusion(f32[768]{0:T(1024)S(1)} %get-tuple-element.11, f32[1024]{0:T(1024)S(1)} %add_rsqrt_fusion.1, f32[1024]{0:T(1024)S(1)} %broadcast_multiply_fusion.1, bf16[256,768]{1,0:T(8,128)(2,1)S(1)} %collective-permute-done.1, bf16[512,768]{1,0:T(8,128)(2,1)S(1)} %copy-done.1, ...), kind=kLoop, calls=%fused_computation.17 | loop fusion | flops 7864320 | bytes 3156992 | tf_op jit(solution)/shard_map/convert_element_type | solution.py:64
  25.9 8.3 %collective-permute-done.4 = bf16[256,768]{1,0:T(8,128)(2,1)S(1)} collective-permute-done((bf16[256,768]{1,0:T(8,128)(2,1)S(1)}, bf16[256,768]{1,0:T(8,128)(2,1)S(1)}, u32[]{:S(2)}, u32[]{:S(2)}) %collective-permute-start.4) | collective-permute-done | bytes 393248 | tf_op jit(solution)/shard_map/ppermute | solution.py:52
  34.2 0.7 broadcast_select_fusion.5
  34.9 1.5 %collective-permute-start.5 = (bf16[256,768]{1,0:T(8,128)(2,1)S(1)}, bf16[256,768]{1,0:T(8,128)(2,1)S(1)}, u32[]{:S(2)}, u32[]{:S(2)}) collective-permute-start(bf16[256,768]{1,0:T(8,128)(2,1)S(1)} %broadcast_select_fusion.5), channel_id=1, source_target_pairs={{0,1},{2,3},{4,5},{6,7},{8,9},{10,11},{12,13},{14,15},{16,17},{18,... | collective-permute-start | bytes 1179656 | tf_op jit(solution)/shard_map/ppermute | solution.py:52
  36.4 4.1 %convolution_convert_fusion.1.refs_0_.refs_1_.refs_2_ = bf16[1024,1536]{1,0:T(8,128)(2,1)} fusion(bf16[1024,768]{1,0:T(8,128)(2,1)S(1)} %fusion.9, bf16[768,2304]{1,0:T(8,128)(2,1)S(1)} %copy-done.4), kind=kOutput, calls=%fused_computation.5 | convolution fusion | flops 2417491968 | bytes 7077888 | tf_op jit(solution)/shard_map/dot_general | solution.py:205
  40.4 1.7 %multiply_convert_fusion.1.q_ref = bf16[512,768]{1,0:T(8,128)(2,1)} fusion(bf16[768,2304]{1,0:T(8,128)(2,1)S(1)} %copy-done.4, bf16[1024,768]{1,0:T(8,128)(2,1)S(1)} %fusion.9), kind=kOutput, calls=%fused_computation.34 | convolution fusion | flops 604766208 | bytes 2752512 | tf_op jit(solution)/shard_map/dot_general | solution.py:210
  42.1 0.8 convert_reduce_fusion.4
  43.2 1.8 %convolution_convert_fusion.3.refs_3_ = bf16[256,1536]{1,0:T(8,128)(2,1)} fusion(bf16[768,2304]{1,0:T(8,128)(2,1)S(1)} %copy-done.4, bf16[256,768]{1,0:T(8,128)(2,1)S(1)} %get-tuple-element.16, f32[768]{0:T(1024)S(1)} %get-tuple-element.11, f32[256]{0:T(256)S(1)} %add_rsqrt_fusion.4, f32[256]{0:T(256)S(1)} %broadcast_multiply_fusion.4), kind=kOutput, calls=%fused_computation.19 | convolution fusion | flops 605356032 | bytes 3545088 | tf_op jit(solution)/shard_map/dot_general | solution.py:212
  45.0 17.0 %shard_map.185 = (bf16[512,768]{1,0:T(8,128)(2,1)}, bf16[256,768]{1,0:T(8,128)(2,1)}) custom-call(s32[2]{0:T(128)} %pad_add_fusion.pos_ref, bf16[512,768]{1,0:T(8,128)(2,1)} %multiply_convert_fusion.1.q_ref, bf16[1024,1536]{1,0:T(8,128)(2,1)} %convolution_convert_fusion.1.refs_0_.refs_1_.refs_2_, ...), custom_call_target="tpu_custom_call" | custom-call | flops 7046430720 | bytes 9043968 | tf_op jit(solution)/shard_map/pallas_call | solution.py:149
  62.0 0.8 collective-permute-start.8
  62.8 1.2 fusion.48
  64.0 1.9 %collective-permute-start.7 = (bf16[256,768]{1,0:T(8,128)(2,1)S(1)}, bf16[256,768]{1,0:T(8,128)(2,1)S(1)}, u32[]{:S(2)}, u32[]{:S(2)}) collective-permute-start(bf16[256,768]{1,0:T(8,128)(2,1)S(1)} %get-tuple-element.20), channel_id=1, source_target_pairs={{1,0},{2,1},{3,2},{4,3},{5,4},{6,5},{7,6},{8,7},{9,8},{10,9},{11,1... | collective-permute-start | bytes 1179656 | tf_op jit(solution)/shard_map/ppermute | solution.py:26
  65.9 2.4 %collective-permute-start.6 = (bf16[256,768]{1,0:T(8,128)(2,1)S(1)}, bf16[256,768]{1,0:T(8,128)(2,1)S(1)}, u32[]{:S(2)}, u32[]{:S(2)}) collective-permute-start(bf16[256,768]{1,0:T(8,128)(2,1)S(1)} %get-tuple-element.19), channel_id=1, source_target_pairs={{0,1},{1,2},{2,3},{3,4},{4,5},{5,6},{6,7},{7,8},{8,9},{9,10},{10,1... | collective-permute-start | bytes 1179656 | tf_op jit(solution)/shard_map/ppermute | solution.py:25
  69.0 1.0 broadcast_select_fusion
  70.0 0.7 collective-permute-start.9
  70.7 4.7 %collective-permute-done.7 = bf16[256,768]{1,0:T(8,128)(2,1)S(1)} collective-permute-done((bf16[256,768]{1,0:T(8,128)(2,1)S(1)}, bf16[256,768]{1,0:T(8,128)(2,1)S(1)}, u32[]{:S(2)}, u32[]{:S(2)}) %collective-permute-start.7) | collective-permute-done | bytes 393248 | tf_op jit(solution)/shard_map/ppermute | solution.py:26
  75.4 1.6 %collective-permute-done.6 = bf16[256,768]{1,0:T(8,128)(2,1)S(1)} collective-permute-done((bf16[256,768]{1,0:T(8,128)(2,1)S(1)}, bf16[256,768]{1,0:T(8,128)(2,1)S(1)}, u32[]{:S(2)}, u32[]{:S(2)}) %collective-permute-start.6) | collective-permute-done | bytes 393248 | tf_op jit(solution)/shard_map/ppermute | solution.py:25
  77.0 0.3 convert_reduce_fusion
  77.3 0.6 fusion.4
  77.9 0.9 broadcast_select_fusion.2
  78.8 1.4 %collective-permute-start.10 = (bf16[256,768]{1,0:T(8,128)(2,1)S(1)}, bf16[256,768]{1,0:T(8,128)(2,1)S(1)}, u32[]{:S(2)}, u32[]{:S(2)}) collective-permute-start(bf16[256,768]{1,0:T(8,128)(2,1)S(1)} %broadcast_select_fusion.2), channel_id=1, source_target_pairs={{0,2},{4,6},{8,10},{12,14},{16,18},{20,22},{24,26},{28,30}} | collective-permute-start | bytes 1179656 | tf_op jit(solution)/shard_map/ppermute | solution.py:52
  80.2 1.9 %fusion.6 = bf16[1024,768]{1,0:T(8,128)(2,1)S(1)} fusion(f32[768]{0:T(1024)S(1)} %get-tuple-element.12, f32[1024]{0:T(1024)S(1)} %add_rsqrt_fusion, f32[1024]{0:T(1024)S(1)} %broadcast_multiply_fusion, bf16[256,768]{1,0:T(8,128)(2,1)S(1)} %collective-permute-done.7, bf16[512,768]{1,0:T(8,128)(2,1)S(1)} %copy-done.2, ...), kind=kLoop, calls=%fused_computation.14 | loop fusion | flops 7864320 | bytes 3156992 | tf_op jit(solution)/shard_map/convert_element_type | solution.py:64
  82.1 6.5 %collective-permute-done.10 = bf16[256,768]{1,0:T(8,128)(2,1)S(1)} collective-permute-done((bf16[256,768]{1,0:T(8,128)(2,1)S(1)}, bf16[256,768]{1,0:T(8,128)(2,1)S(1)}, u32[]{:S(2)}, u32[]{:S(2)}) %collective-permute-start.10) | collective-permute-done | bytes 393248 | tf_op jit(solution)/shard_map/ppermute | solution.py:52
  88.6 0.7 broadcast_select_fusion.4
  89.3 1.5 %collective-permute-start.11 = (bf16[256,768]{1,0:T(8,128)(2,1)S(1)}, bf16[256,768]{1,0:T(8,128)(2,1)S(1)}, u32[]{:S(2)}, u32[]{:S(2)}) collective-permute-start(bf16[256,768]{1,0:T(8,128)(2,1)S(1)} %broadcast_select_fusion.4), channel_id=1, source_target_pairs={{0,1},{2,3},{4,5},{6,7},{8,9},{10,11},{12,13},{14,15},{16,17},{18,... | collective-permute-start | bytes 1179656 | tf_op jit(solution)/shard_map/ppermute | solution.py:52
  90.8 4.0 %convolution_convert_fusion.refs_0_.refs_1_.refs_2_ = bf16[1024,1536]{1,0:T(8,128)(2,1)} fusion(bf16[1024,768]{1,0:T(8,128)(2,1)S(1)} %fusion.6, bf16[768,2304]{1,0:T(8,128)(2,1)S(1)} %copy-done.3), kind=kOutput, calls=%fused_computation.4 | convolution fusion | flops 2417491968 | bytes 7077888 | tf_op jit(solution)/shard_map/dot_general | solution.py:205
  94.8 1.7 %multiply_convert_fusion.q_ref = bf16[512,768]{1,0:T(8,128)(2,1)} fusion(bf16[768,2304]{1,0:T(8,128)(2,1)S(1)} %copy-done.3, bf16[1024,768]{1,0:T(8,128)(2,1)S(1)} %fusion.6), kind=kOutput, calls=%fused_computation.33 | convolution fusion | flops 604766208 | bytes 2752512 | tf_op jit(solution)/shard_map/dot_general | solution.py:210
  96.5 0.8 convert_reduce_fusion.3
  97.6 1.7 %convolution_convert_fusion.2.refs_3_ = bf16[256,1536]{1,0:T(8,128)(2,1)} fusion(bf16[768,2304]{1,0:T(8,128)(2,1)S(1)} %copy-done.3, bf16[256,768]{1,0:T(8,128)(2,1)S(1)} %get-tuple-element.14, f32[768]{0:T(1024)S(1)} %get-tuple-element.12, f32[256]{0:T(256)S(1)} %add_rsqrt_fusion.3, f32[256]{0:T(256)S(1)} %broadcast_multiply_fusion.3), kind=kOutput, calls=%fused_computation.18 | convolution fusion | flops 605356032 | bytes 3545088 | tf_op jit(solution)/shard_map/dot_general | solution.py:212
  99.3 17.1 %shard_map.186 = (bf16[512,768]{1,0:T(8,128)(2,1)}, bf16[256,768]{1,0:T(8,128)(2,1)}) custom-call(s32[2]{0:T(128)} %pad_add_fusion.pos_ref, bf16[512,768]{1,0:T(8,128)(2,1)} %multiply_convert_fusion.q_ref, bf16[1024,1536]{1,0:T(8,128)(2,1)} %convolution_convert_fusion.refs_0_.refs_1_.refs_2_, ...), custom_call_target="tpu_custom_call" | custom-call | flops 7046430720 | bytes 9043968 | tf_op jit(solution)/shard_map/pallas_call | solution.py:149
  116.4 1.3 %convert_reduce_fusion.2 = f32[512]{0:T(512)S(1)} fusion(bf16[512,768]{1,0:T(8,128)(2,1)} %get-tuple-element.7), kind=kLoop, calls=%fused_computation.25 | loop fusion | flops 785920 | bytes 788480 | tf_op jit(solution)/shard_map/reduce_sum | solution.py:61
  117.7 1.5 %fusion.16 = f32[512]{0:T(512)S(1)} fusion(bf16[512,768]{1,0:T(8,128)(2,1)} %get-tuple-element.7, f32[512]{0:T(512)S(1)} %broadcast_multiply_fusion.2), kind=kLoop, calls=%fused_computation.28 | loop fusion | flops 1572352 | bytes 790528 | tf_op jit(solution)/shard_map/reduce_sum | solution.py:63
  119.3 1.9 %fusion.31 = f32[512,512]{0,1:T(8,128)S(1)} fusion(bf16[768,512]{1,0:T(8,128)(2,1)S(1)} %copy-done, bf16[512,768]{1,0:T(8,128)(2,1)} %get-tuple-element.7, f32[768]{0:T(1024)S(1)} %copy-done.10, f32[512]{0:T(512)S(1)} %add_rsqrt_fusion.2, f32[512]{0:T(512)S(1)} %broadcast_multiply_fusion.2), kind=kOutput, calls=%fused_computation.51 | convolution fusion | flops 404619264 | bytes 2628608 | tf_op jit(solution)/shard_map/dot_general | solution.py:225
  121.6 0.6 multiply_add_fusion
  (53 shorter events, 1.4 us)
Async XLA Ops:
  0.6 118.6 %copy-start = (bf16[768,512]{1,0:T(8,128)(2,1)S(1)}, bf16[768,512]{1,0:T(8,128)(2,1)}, u32[]{:S(2)}) copy-start(bf16[768,512]{1,0:T(8,128)(2,1)} %param.23) | copy-start | bytes 2359300
  1.7 9.2 %copy-start.13 = (s32[2]{0:T(128)S(1)}, s32[2]{0:T(128)}, u32[]{:S(2)}) copy-start(s32[2]{0:T(128)} %constant.49.clone) | copy-start | bytes 28
  1.8 9.9 %copy-start.1 = (bf16[512,768]{1,0:T(8,128)(2,1)S(1)}, bf16[512,768]{1,0:T(8,128)(2,1)}, u32[]{:S(2)}) copy-start(bf16[512,768]{1,0:T(8,128)(2,1)} %refs_4_.1) | copy-start | bytes 2359300
  1.8 12.3 %copy-start.12 = (s32[4]{0:T(128)S(1)}, s32[4]{0:T(128)}, u32[]{:S(2)}) copy-start(s32[4]{0:T(128)} %constant.50.clone) | copy-start | bytes 52
  1.8 13.0 %copy-start.11 = (s32[8]{0:T(128)S(1)}, s32[8]{0:T(128)}, u32[]{:S(2)}) copy-start(s32[8]{0:T(128)} %constant.51.clone) | copy-start | bytes 100
  1.8 13.7 %copy-start.6 = (f32[2,768]{1,0:T(2,128)S(1)}, f32[2,768]{1,0:T(2,128)}, u32[]{:S(2)}) copy-start(f32[2,768]{1,0:T(2,128)} %param.19) | copy-start | bytes 18436
  1.8 15.0 %collective-permute-start.1 = (bf16[256,768]{1,0:T(8,128)(2,1)S(1)}, bf16[256,768]{1,0:T(8,128)(2,1)S(1)}, u32[]{:S(2)}, u32[]{:S(2)}) collective-permute-start(bf16[256,768]{1,0:T(8,128)(2,1)S(1)} %slice.52), channel_id=1, source_target_pairs={{1,0},{2,1},{3,2},{4,3},{5,4},{6,5},{7,6},{8,7},{9,8},{10,9},{11,1... | collective-permute-start | bytes 1179656 | tf_op jit(solution)/shard_map/ppermute | solution.py:26
  3.9 7.8 %collective-permute-start.2 = (bf16[256,768]{1,0:T(8,128)(2,1)S(1)}, bf16[256,768]{1,0:T(8,128)(2,1)S(1)}, u32[]{:S(2)}, u32[]{:S(2)}) collective-permute-start(bf16[256,768]{1,0:T(8,128)(2,1)S(1)} %slice.52), channel_id=1, source_target_pairs={{0,8},{16,24}} | collective-permute-start | bytes 1179656 | tf_op jit(solution)/shard_map/ppermute | solution.py:52
  11.7 9.1 %collective-permute-start = (bf16[256,768]{1,0:T(8,128)(2,1)S(1)}, bf16[256,768]{1,0:T(8,128)(2,1)S(1)}, u32[]{:S(2)}, u32[]{:S(2)}) collective-permute-start(bf16[256,768]{1,0:T(8,128)(2,1)S(1)} %get-tuple-element.22), channel_id=1, source_target_pairs={{0,1},{1,2},{2,3},{3,4},{4,5},{5,6},{6,7},{7,8},{8,9},{9,10},{10,1... | collective-permute-start | bytes 1179656 | tf_op jit(solution)/shard_map/ppermute | solution.py:25
  15.5 5.5 %collective-permute-start.3 = (bf16[256,768]{1,0:T(8,128)(2,1)S(1)}, bf16[256,768]{1,0:T(8,128)(2,1)S(1)}, u32[]{:S(2)}, u32[]{:S(2)}) collective-permute-start(bf16[256,768]{1,0:T(8,128)(2,1)S(1)} %get-tuple-element.21), channel_id=1, source_target_pairs={{0,4},{8,12},{16,20},{24,28}} | collective-permute-start | bytes 1179656 | tf_op jit(solution)/shard_map/ppermute | solution.py:52
  21.8 14.5 %copy-start.4 = (bf16[768,2304]{1,0:T(8,128)(2,1)S(1)}, bf16[768,2304]{1,0:T(8,128)(2,1)}, u32[]{:S(2)}) copy-start(bf16[768,2304]{1,0:T(8,128)(2,1)} %get-tuple-element.17) | copy-start | bytes 10616836
  21.8 12.3 %collective-permute-start.4 = (bf16[256,768]{1,0:T(8,128)(2,1)S(1)}, bf16[256,768]{1,0:T(8,128)(2,1)S(1)}, u32[]{:S(2)}, u32[]{:S(2)}) collective-permute-start(bf16[256,768]{1,0:T(8,128)(2,1)S(1)} %broadcast_select_fusion.3), channel_id=1, source_target_pairs={{0,2},{4,6},{8,10},{12,14},{16,18},{20,22},{24,26},{28,30}} | collective-permute-start | bytes 1179656 | tf_op jit(solution)/shard_map/ppermute | solution.py:52
  34.9 7.2 %collective-permute-start.5 = (bf16[256,768]{1,0:T(8,128)(2,1)S(1)}, bf16[256,768]{1,0:T(8,128)(2,1)S(1)}, u32[]{:S(2)}, u32[]{:S(2)}) collective-permute-start(bf16[256,768]{1,0:T(8,128)(2,1)S(1)} %broadcast_select_fusion.5), channel_id=1, source_target_pairs={{0,1},{2,3},{4,5},{6,7},{8,9},{10,11},{12,13},{14,15},{16,17},{18,... | collective-permute-start | bytes 1179656 | tf_op jit(solution)/shard_map/ppermute | solution.py:52
  62.0 15.0 %copy-start.2 = (bf16[512,768]{1,0:T(8,128)(2,1)S(1)}, bf16[512,768]{1,0:T(8,128)(2,1)}, u32[]{:S(2)}) copy-start(bf16[512,768]{1,0:T(8,128)(2,1)} %get-tuple-element.5.refs_4_) | copy-start | bytes 2359300
  62.0 7.0 %collective-permute-start.8 = (bf16[256,768]{1,0:T(8,128)(2,1)}, bf16[256,768]{1,0:T(8,128)(2,1)S(1)}, u32[]{:S(2)}, u32[]{:S(2)}) collective-permute-start(bf16[256,768]{1,0:T(8,128)(2,1)} %get-tuple-element.6), channel_id=1, source_target_pairs={{0,8},{16,24}} | collective-permute-start | bytes 1179656 | tf_op jit(solution)/shard_map/ppermute | solution.py:52
  64.0 11.4 %collective-permute-start.7 = (bf16[256,768]{1,0:T(8,128)(2,1)S(1)}, bf16[256,768]{1,0:T(8,128)(2,1)S(1)}, u32[]{:S(2)}, u32[]{:S(2)}) collective-permute-start(bf16[256,768]{1,0:T(8,128)(2,1)S(1)} %get-tuple-element.20), channel_id=1, source_target_pairs={{1,0},{2,1},{3,2},{4,3},{5,4},{6,5},{7,6},{8,7},{9,8},{10,9},{11,1... | collective-permute-start | bytes 1179656 | tf_op jit(solution)/shard_map/ppermute | solution.py:26
  65.9 11.0 %collective-permute-start.6 = (bf16[256,768]{1,0:T(8,128)(2,1)S(1)}, bf16[256,768]{1,0:T(8,128)(2,1)S(1)}, u32[]{:S(2)}, u32[]{:S(2)}) collective-permute-start(bf16[256,768]{1,0:T(8,128)(2,1)S(1)} %get-tuple-element.19), channel_id=1, source_target_pairs={{0,1},{1,2},{2,3},{3,4},{4,5},{5,6},{6,7},{7,8},{8,9},{9,10},{10,1... | collective-permute-start | bytes 1179656 | tf_op jit(solution)/shard_map/ppermute | solution.py:25
  70.0 7.8 %collective-permute-start.9 = (bf16[256,768]{1,0:T(8,128)(2,1)S(1)}, bf16[256,768]{1,0:T(8,128)(2,1)S(1)}, u32[]{:S(2)}, u32[]{:S(2)}) collective-permute-start(bf16[256,768]{1,0:T(8,128)(2,1)S(1)} %broadcast_select_fusion), channel_id=1, source_target_pairs={{0,4},{8,12},{16,20},{24,28}} | collective-permute-start | bytes 1179656 | tf_op jit(solution)/shard_map/ppermute | solution.py:52
  77.9 12.9 %copy-start.3 = (bf16[768,2304]{1,0:T(8,128)(2,1)S(1)}, bf16[768,2304]{1,0:T(8,128)(2,1)}, u32[]{:S(2)}) copy-start(bf16[768,2304]{1,0:T(8,128)(2,1)} %get-tuple-element.18) | copy-start | bytes 10616836
  78.8 9.8 %collective-permute-start.10 = (bf16[256,768]{1,0:T(8,128)(2,1)S(1)}, bf16[256,768]{1,0:T(8,128)(2,1)S(1)}, u32[]{:S(2)}, u32[]{:S(2)}) collective-permute-start(bf16[256,768]{1,0:T(8,128)(2,1)S(1)} %broadcast_select_fusion.2), channel_id=1, source_target_pairs={{0,2},{4,6},{8,10},{12,14},{16,18},{20,22},{24,26},{28,30}} | collective-permute-start | bytes 1179656 | tf_op jit(solution)/shard_map/ppermute | solution.py:52
  89.3 7.2 %collective-permute-start.11 = (bf16[256,768]{1,0:T(8,128)(2,1)S(1)}, bf16[256,768]{1,0:T(8,128)(2,1)S(1)}, u32[]{:S(2)}, u32[]{:S(2)}) collective-permute-start(bf16[256,768]{1,0:T(8,128)(2,1)S(1)} %broadcast_select_fusion.4), channel_id=1, source_target_pairs={{0,1},{2,3},{4,5},{6,7},{8,9},{10,11},{12,13},{14,15},{16,17},{18,... | collective-permute-start | bytes 1179656 | tf_op jit(solution)/shard_map/ppermute | solution.py:52
  99.3 19.9 %copy-start.10 = (f32[768]{0:T(1024)S(1)}, f32[768]{0:T(1024)}, u32[]{:S(2)}) copy-start(f32[768]{0:T(1024)} %param.22) | copy-start | bytes 9220
  116.4 5.0 %copy-start.7 = (s32[512]{0:T(512)S(1)}, s32[512]{0:T(512)}, u32[]{:S(2)}) copy-start(s32[512]{0:T(512)} %param.24) | copy-start | bytes 6148
  117.7 3.9 %copy-start.8 = (f32[512]{0:T(512)S(1)}, f32[512]{0:T(512)}, u32[]{:S(2)}) copy-start(f32[512]{0:T(512)} %param.26) | copy-start | bytes 6148
  117.7 3.9 %copy-start.9 = (s32[512]{0:T(512)S(1)}, s32[512]{0:T(512)}, u32[]{:S(2)}) copy-start(s32[512]{0:T(512)} %param.25) | copy-start | bytes 6148
  121.6 0.6 copy-start.5

commit v19 on v12

--- a/solution.py
+++ b/solution.py
@@ -35,7 +35,14 @@
         while step:
             bits.append(step)
             step //= 2
-        return [[[(i, i + bit) for i in range(0, count, 2 * bit)]] for bit in bits]
+        if len(bits) >= 3:
+            bits = [bits[-2]] + bits[:-2] + [bits[-1]]
+        rounds = []
+        held = [0]
+        for bit in bits:
+            rounds.append([[(i, i + bit) for i in held]])
+            held = sorted(held + [i + bit for i in held])
+        return rounds
     rounds = []
     held = 1
     while held < count:

time: 122 us -> 125 us (1.025)
  starting transfers between devices: 17.1 us -> 18.4 us
    ppermute x2, waiting for transfers between devices: 9.74 us -> 5.84 us  [with_halo(): before = lax.ppermute(last, axis, up)]
    ppermute x2, waiting for transfers between devices: 1.43 us -> 5.04 us  [with_halo(): after = lax.ppermute(leading, axis, down)]
    ppermute x8, starting transfers between devices: 8.36 us -> 9.61 us  [spread(): got = lax.ppermute(block, axis, op)]
  transfers between devices with their start and end apart: 12 -> 12, of which waited for: 5 -> 7; matrix products, arithmetic and copies ran while one was open for 21% -> 21% of each run, Pallas kernels for 0% -> 0%
where the time goes in v19:
time: 125 us; the launch traced here: 123 us
  Pallas kernels  31.3 us (25%)
  waiting for transfers between devices  29.8 us (24%)
  matrix products  20.4 us (16%)
  starting transfers between devices  18.4 us (15%)
  other arithmetic  14.2 us (11%)
  local copies, waits for them, and re-layouts  7.68 us (6%)
  between operations  1.7 us (1%)
    pallas_call x2, Pallas kernels, attention(): pl.pallas_call(functools.partial(attention_kernel, row0), out_shape=jax.S...  31.3 us
    ppermute x8, waiting for transfers between devices, spread(): got = lax.ppermute(block, axis, op)  18.9 us
    ppermute x8, starting transfers between devices, spread(): got = lax.ppermute(block, axis, op)  9.61 us
    dot_general x2, matrix products, per_device(): jnp.dot(extended_normed, weights[:, feat_width:], preferred_element_type=...  8.09 us
    squeeze x1, local copies, waits for them, and re-layouts, per_device(): weights = w_qkv[layer_idx]  6.45 us
    ppermute x2, waiting for transfers between devices, with_halo(): before = lax.ppermute(last, axis, up)  5.84 us
    ppermute x2, waiting for transfers between devices, with_halo(): after = lax.ppermute(leading, axis, down)  5.04 us
    ppermute x2, starting transfers between devices, with_halo(): before = lax.ppermute(last, axis, up)  4.81 us
  transfers between devices with their start and end apart: 12, of which 7 were waited for; matrix products, arithmetic and copies ran while one was open for 21% of the time, Pallas kernels for 0%

profile of v19, /device:TPU:20, one launch (start us, length us, event | category | flops | bytes accessed | tf_op | source)
XLA Modules:
  0.0 123.5 jit_solution(10355762942361023798)
XLA Ops:
  0.6 1.1 slice.59
  1.8 2.1 %collective-permute-start.1 = (bf16[256,768]{1,0:T(8,128)(2,1)S(1)}, bf16[256,768]{1,0:T(8,128)(2,1)S(1)}, u32[]{:S(2)}, u32[]{:S(2)}) collective-permute-start(bf16[256,768]{1,0:T(8,128)(2,1)S(1)} %slice.59), channel_id=1, source_target_pairs={{1,0},{2,1},{3,2},{4,3},{5,4},{6,5},{7,6},{8,7},{9,8},{10,9},{11,1... | collective-permute-start | bytes 1179656 | tf_op jit(solution)/shard_map/ppermute | solution.py:26
  3.9 0.7 collective-permute-start.2
  4.6 6.5 %slice_bitcast_fusion = (bf16[768,2304]{1,0:T(8,128)(2,1)}, bf16[768,2304]{1,0:T(8,128)(2,1)}) fusion(bf16[2,768,2304]{2,1,0:T(8,128)(2,1)} %param.20), kind=kLoop, calls=%fused_computation.10 | loop fusion | bytes 14155776 | tf_op jit(solution)/shard_map/squeeze | solution.py:188
  11.0 0.6 compare_reduce_fusion
  11.7 2.4 %collective-permute-start = (bf16[256,768]{1,0:T(8,128)(2,1)S(1)}, bf16[256,768]{1,0:T(8,128)(2,1)S(1)}, u32[]{:S(2)}, u32[]{:S(2)}) collective-permute-start(bf16[256,768]{1,0:T(8,128)(2,1)S(1)} %get-tuple-element.16), channel_id=1, source_target_pairs={{0,1},{1,2},{2,3},{3,4},{4,5},{5,6},{6,7},{7,8},{8,9},{9,10},{10,1... | collective-permute-start | bytes 1179656 | tf_op jit(solution)/shard_map/ppermute | solution.py:25
  14.1 0.6 compare_reduce_fusion.1
  14.8 0.7 compare_reduce_fusion.2
  15.5 1.3 %collective-permute-start.3 = (bf16[256,768]{1,0:T(8,128)(2,1)S(1)}, bf16[256,768]{1,0:T(8,128)(2,1)S(1)}, u32[]{:S(2)}, u32[]{:S(2)}) collective-permute-start(bf16[256,768]{1,0:T(8,128)(2,1)S(1)} %get-tuple-element.15), channel_id=1, source_target_pairs={{0,8},{2,10},{16,24},{18,26}} | collective-permute-start | bytes 1179656 | tf_op jit(solution)/shard_map/ppermute | solution.py:59
  16.8 0.6 pad_add_fusion.pos_ref
  17.4 3.4 %collective-permute-done = bf16[256,768]{1,0:T(8,128)(2,1)S(1)} collective-permute-done((bf16[256,768]{1,0:T(8,128)(2,1)S(1)}, bf16[256,768]{1,0:T(8,128)(2,1)S(1)}, u32[]{:S(2)}, u32[]{:S(2)}) %collective-permute-start) | collective-permute-done | bytes 393248 | tf_op jit(solution)/shard_map/ppermute | solution.py:25
  21.1 5.8 %collective-permute-done.3 = bf16[256,768]{1,0:T(8,128)(2,1)S(1)} collective-permute-done((bf16[256,768]{1,0:T(8,128)(2,1)S(1)}, bf16[256,768]{1,0:T(8,128)(2,1)S(1)}, u32[]{:S(2)}, u32[]{:S(2)}) %collective-permute-start.3) | collective-permute-done | bytes 393248 | tf_op jit(solution)/shard_map/ppermute | solution.py:59
  26.9 0.6 broadcast_select_fusion.3
  27.5 1.3 %collective-permute-start.4 = (bf16[256,768]{1,0:T(8,128)(2,1)S(1)}, bf16[256,768]{1,0:T(8,128)(2,1)S(1)}, u32[]{:S(2)}, u32[]{:S(2)}) collective-permute-start(bf16[256,768]{1,0:T(8,128)(2,1)S(1)} %broadcast_select_fusion.3), channel_id=1, source_target_pairs={{0,4},{2,6},{8,12},{10,14},{16,20},{18,22},{24,28},{26,30}} | collective-permute-start | bytes 1179656 | tf_op jit(solution)/shard_map/ppermute | solution.py:59
  28.8 0.6 fusion.7
  29.5 1.9 %fusion.9 = bf16[1024,768]{1,0:T(8,128)(2,1)S(1)} fusion(f32[768]{0:T(1024)S(1)} %get-tuple-element.6, f32[1024]{0:T(1024)S(1)} %add_rsqrt_fusion.1, f32[1024]{0:T(1024)S(1)} %broadcast_multiply_fusion.1, bf16[256,768]{1,0:T(8,128)(2,1)S(1)} %collective-permute-done.1, bf16[512,768]{1,0:T(8,128)(2,1)S(1)} %copy-done.1, ...), kind=kLoop, calls=%fused_computation.17 | loop fusion | flops 7864320 | bytes 3156992 | tf_op jit(solution)/shard_map/convert_element_type | solution.py:71
  31.4 2.7 %collective-permute-done.4 = bf16[256,768]{1,0:T(8,128)(2,1)S(1)} collective-permute-done((bf16[256,768]{1,0:T(8,128)(2,1)S(1)}, bf16[256,768]{1,0:T(8,128)(2,1)S(1)}, u32[]{:S(2)}, u32[]{:S(2)}) %collective-permute-start.4) | collective-permute-done | bytes 393248 | tf_op jit(solution)/shard_map/ppermute | solution.py:59
  34.1 0.6 broadcast_select_fusion.5
  34.7 1.5 %collective-permute-start.5 = (bf16[256,768]{1,0:T(8,128)(2,1)S(1)}, bf16[256,768]{1,0:T(8,128)(2,1)S(1)}, u32[]{:S(2)}, u32[]{:S(2)}) collective-permute-start(bf16[256,768]{1,0:T(8,128)(2,1)S(1)} %broadcast_select_fusion.5), channel_id=1, source_target_pairs={{0,1},{2,3},{4,5},{6,7},{8,9},{10,11},{12,13},{14,15},{16,17},{18,... | collective-permute-start | bytes 1179656 | tf_op jit(solution)/shard_map/ppermute | solution.py:59
  36.2 4.1 %convolution_convert_fusion.1.refs_0_.refs_1_.refs_2_ = bf16[1024,1536]{1,0:T(8,128)(2,1)} fusion(bf16[1024,768]{1,0:T(8,128)(2,1)S(1)} %fusion.9, bf16[768,2304]{1,0:T(8,128)(2,1)S(1)} %copy-done.3), kind=kOutput, calls=%fused_computation.5 | convolution fusion | flops 2417491968 | bytes 7077888 | tf_op jit(solution)/shard_map/dot_general | solution.py:192
  40.2 1.7 %multiply_convert_fusion.1.q_ref = bf16[512,768]{1,0:T(8,128)(2,1)} fusion(bf16[768,2304]{1,0:T(8,128)(2,1)S(1)} %copy-done.3, bf16[1024,768]{1,0:T(8,128)(2,1)S(1)} %fusion.9), kind=kOutput, calls=%fused_computation.36 | convolution fusion | flops 604766208 | bytes 2752512 | tf_op jit(solution)/shard_map/dot_general | solution.py:197
  41.9 0.9 convert_reduce_fusion.4
  43.1 1.8 %convolution_convert_fusion.3.refs_3_ = bf16[256,1536]{1,0:T(8,128)(2,1)} fusion(bf16[768,2304]{1,0:T(8,128)(2,1)S(1)} %copy-done.3, bf16[256,768]{1,0:T(8,128)(2,1)S(1)} %get-tuple-element.10, f32[768]{0:T(1024)S(1)} %get-tuple-element.6, f32[256]{0:T(256)S(1)} %add_rsqrt_fusion.4, f32[256]{0:T(256)S(1)} %broadcast_multiply_fusion.4), kind=kOutput, calls=%fused_computation.19 | convolution fusion | flops 605356032 | bytes 3545088 | tf_op jit(solution)/shard_map/dot_general | solution.py:199
  44.8 15.6 %shard_map.185 = bf16[512,768]{1,0:T(8,128)(2,1)} custom-call(s32[2]{0:T(128)} %pad_add_fusion.pos_ref, bf16[512,768]{1,0:T(8,128)(2,1)} %multiply_convert_fusion.1.q_ref, bf16[1024,1536]{1,0:T(8,128)(2,1)} %convolution_convert_fusion.1.refs_0_.refs_1_.refs_2_, bf16[1024,1536]{1,0:T(8,128)(2,1)} %convolution_convert_fusion.1.refs_0_.refs_1_.refs_2_, ...), custom_call_target="tpu_custom_call" | custom-call | flops 6442450944 | bytes 7077888 | tf_op jit(solution)/shard_map/pallas_call | solution.py:147
  60.5 2.3 %add_convert_fusion.1 = bf16[512,768]{1,0:T(8,128)(2,1)S(1)} fusion(bf16[512,768]{1,0:T(8,128)(2,1)S(1)} %copy-done.1, bf16[512,768]{1,0:T(8,128)(2,1)} %shard_map.185, bf16[2,768,768]{2,1,0:T(8,128)(2,1)} %param.21), kind=kOutput, calls=%fused_computation.35 | convolution fusion | flops 605159424 | bytes 3538944 | tf_op jit(solution)/shard_map/dot_general | solution.py:205
  62.8 0.7 collective-permute-start.8
  63.5 1.9 %collective-permute-start.7 = (bf16[256,768]{1,0:T(8,128)(2,1)S(1)}, bf16[256,768]{1,0:T(8,128)(2,1)S(1)}, u32[]{:S(2)}, u32[]{:S(2)}) collective-permute-start(bf16[256,768]{1,0:T(8,128)(2,1)S(1)} %slice.80), channel_id=1, source_target_pairs={{1,0},{2,1},{3,2},{4,3},{5,4},{6,5},{7,6},{8,7},{9,8},{10,9},{11,1... | collective-permute-start | bytes 1179656 | tf_op jit(solution)/shard_map/ppermute | solution.py:26
  65.5 2.4 %collective-permute-start.6 = (bf16[256,768]{1,0:T(8,128)(2,1)S(1)}, bf16[256,768]{1,0:T(8,128)(2,1)S(1)}, u32[]{:S(2)}, u32[]{:S(2)}) collective-permute-start(bf16[256,768]{1,0:T(8,128)(2,1)S(1)} %get-tuple-element.14), channel_id=1, source_target_pairs={{0,1},{1,2},{2,3},{3,4},{4,5},{5,6},{6,7},{7,8},{8,9},{9,10},{10,1... | collective-permute-start | bytes 1179656 | tf_op jit(solution)/shard_map/ppermute | solution.py:25
  67.9 1.3 %collective-permute-start.9 = (bf16[256,768]{1,0:T(8,128)(2,1)S(1)}, bf16[256,768]{1,0:T(8,128)(2,1)S(1)}, u32[]{:S(2)}, u32[]{:S(2)}) collective-permute-start(bf16[256,768]{1,0:T(8,128)(2,1)S(1)} %get-tuple-element.13), channel_id=1, source_target_pairs={{0,8},{2,10},{16,24},{18,26}} | collective-permute-start | bytes 1179656 | tf_op jit(solution)/shard_map/ppermute | solution.py:59
  69.9 5.0 %collective-permute-done.7 = bf16[256,768]{1,0:T(8,128)(2,1)S(1)} collective-permute-done((bf16[256,768]{1,0:T(8,128)(2,1)S(1)}, bf16[256,768]{1,0:T(8,128)(2,1)S(1)}, u32[]{:S(2)}, u32[]{:S(2)}) %collective-permute-start.7) | collective-permute-done | bytes 393248 | tf_op jit(solution)/shard_map/ppermute | solution.py:26
  74.9 2.4 %collective-permute-done.6 = bf16[256,768]{1,0:T(8,128)(2,1)S(1)} collective-permute-done((bf16[256,768]{1,0:T(8,128)(2,1)S(1)}, bf16[256,768]{1,0:T(8,128)(2,1)S(1)}, u32[]{:S(2)}, u32[]{:S(2)}) %collective-permute-start.6) | collective-permute-done | bytes 393248 | tf_op jit(solution)/shard_map/ppermute | solution.py:25
  77.6 7.7 %collective-permute-done.9 = bf16[256,768]{1,0:T(8,128)(2,1)S(1)} collective-permute-done((bf16[256,768]{1,0:T(8,128)(2,1)S(1)}, bf16[256,768]{1,0:T(8,128)(2,1)S(1)}, u32[]{:S(2)}, u32[]{:S(2)}) %collective-permute-start.9) | collective-permute-done | bytes 393248 | tf_op jit(solution)/shard_map/ppermute | solution.py:59
  85.3 0.6 broadcast_select_fusion.2
  85.9 1.3 %collective-permute-start.10 = (bf16[256,768]{1,0:T(8,128)(2,1)S(1)}, bf16[256,768]{1,0:T(8,128)(2,1)S(1)}, u32[]{:S(2)}, u32[]{:S(2)}) collective-permute-start(bf16[256,768]{1,0:T(8,128)(2,1)S(1)} %broadcast_select_fusion.2), channel_id=1, source_target_pairs={{0,4},{2,6},{8,12},{10,14},{16,20},{18,22},{24,28},{26,30}} | collective-permute-start | bytes 1179656 | tf_op jit(solution)/shard_map/ppermute | solution.py:59
  87.2 0.6 fusion.4
  87.8 1.9 %fusion.6 = bf16[1024,768]{1,0:T(8,128)(2,1)S(1)} fusion(f32[768]{0:T(1024)S(1)} %get-tuple-element.5, f32[1024]{0:T(1024)S(1)} %add_rsqrt_fusion, f32[1024]{0:T(1024)S(1)} %broadcast_multiply_fusion, bf16[256,768]{1,0:T(8,128)(2,1)S(1)} %collective-permute-done.7, bf16[512,768]{1,0:T(8,128)(2,1)S(1)} %add_convert_fusion.1, ...), kind=kLoop, calls=%fused_computation.14 | loop fusion | flops 7864320 | bytes 3156992 | tf_op jit(solution)/shard_map/convert_element_type | solution.py:71
  89.7 2.7 %collective-permute-done.10 = bf16[256,768]{1,0:T(8,128)(2,1)S(1)} collective-permute-done((bf16[256,768]{1,0:T(8,128)(2,1)S(1)}, bf16[256,768]{1,0:T(8,128)(2,1)S(1)}, u32[]{:S(2)}, u32[]{:S(2)}) %collective-permute-start.10) | collective-permute-done | bytes 393248 | tf_op jit(solution)/shard_map/ppermute | solution.py:59
  92.4 0.6 broadcast_select_fusion.4
  93.0 1.5 %collective-permute-start.11 = (bf16[256,768]{1,0:T(8,128)(2,1)S(1)}, bf16[256,768]{1,0:T(8,128)(2,1)S(1)}, u32[]{:S(2)}, u32[]{:S(2)}) collective-permute-start(bf16[256,768]{1,0:T(8,128)(2,1)S(1)} %broadcast_select_fusion.4), channel_id=1, source_target_pairs={{0,1},{2,3},{4,5},{6,7},{8,9},{10,11},{12,13},{14,15},{16,17},{18,... | collective-permute-start | bytes 1179656 | tf_op jit(solution)/shard_map/ppermute | solution.py:59
  94.6 4.0 %convolution_convert_fusion.refs_0_.refs_1_.refs_2_ = bf16[1024,1536]{1,0:T(8,128)(2,1)} fusion(bf16[1024,768]{1,0:T(8,128)(2,1)S(1)} %fusion.6, bf16[768,2304]{1,0:T(8,128)(2,1)S(1)} %copy-done.2), kind=kOutput, calls=%fused_computation.4 | convolution fusion | flops 2417491968 | bytes 7077888 | tf_op jit(solution)/shard_map/dot_general | solution.py:192
  98.6 1.7 %multiply_convert_fusion.q_ref = bf16[512,768]{1,0:T(8,128)(2,1)} fusion(bf16[768,2304]{1,0:T(8,128)(2,1)S(1)} %copy-done.2, bf16[1024,768]{1,0:T(8,128)(2,1)S(1)} %fusion.6), kind=kOutput, calls=%fused_computation.34 | convolution fusion | flops 604766208 | bytes 2752512 | tf_op jit(solution)/shard_map/dot_general | solution.py:197
  100.3 0.9 convert_reduce_fusion.3
  101.4 1.8 %convolution_convert_fusion.2.refs_3_ = bf16[256,1536]{1,0:T(8,128)(2,1)} fusion(bf16[768,2304]{1,0:T(8,128)(2,1)S(1)} %copy-done.2, bf16[256,768]{1,0:T(8,128)(2,1)S(1)} %get-tuple-element.8, f32[768]{0:T(1024)S(1)} %get-tuple-element.5, f32[256]{0:T(256)S(1)} %add_rsqrt_fusion.3, f32[256]{0:T(256)S(1)} %broadcast_multiply_fusion.3), kind=kOutput, calls=%fused_computation.18 | convolution fusion | flops 605356032 | bytes 3545088 | tf_op jit(solution)/shard_map/dot_general | solution.py:199
  103.2 15.6 %shard_map.186 = bf16[512,768]{1,0:T(8,128)(2,1)} custom-call(s32[2]{0:T(128)} %pad_add_fusion.pos_ref, bf16[512,768]{1,0:T(8,128)(2,1)} %multiply_convert_fusion.q_ref, bf16[1024,1536]{1,0:T(8,128)(2,1)} %convolution_convert_fusion.refs_0_.refs_1_.refs_2_, bf16[1024,1536]{1,0:T(8,128)(2,1)} %convolution_convert_fusion.refs_0_.refs_1_.refs_2_, ...), custom_call_target="tpu_custom_call" | custom-call | flops 6442450944 | bytes 7077888 | tf_op jit(solution)/shard_map/pallas_call | solution.py:147
  118.8 2.4 %convert_reduce_fusion.2 = (f32[512]{0:T(512)S(1)}, bf16[512,768]{1,0:T(8,128)(2,1)S(1)}) fusion(bf16[512,768]{1,0:T(8,128)(2,1)} %shard_map.186, bf16[2,768,768]{2,1,0:T(8,128)(2,1)} %param.21, bf16[512,768]{1,0:T(8,128)(2,1)S(1)} %add_convert_fusion.1), kind=kOutput, calls=%fused_computation.25 | convolution fusion | flops 605945344 | bytes 3540992 | tf_op jit(solution)/shard_map/dot_general | solution.py:205
  121.2 0.4 fusion.16
  121.6 0.8 fusion.35
  122.9 0.6 multiply_add_fusion
  (52 shorter events, 1.8 us)
Async XLA Ops:
  0.6 121.0 %copy-start = (bf16[768,512]{1,0:T(8,128)(2,1)S(1)}, bf16[768,512]{1,0:T(8,128)(2,1)}, u32[]{:S(2)}) copy-start(bf16[768,512]{1,0:T(8,128)(2,1)} %param.23) | copy-start | bytes 2359300
  1.7 9.3 %copy-start.12 = (s32[2]{0:T(128)S(1)}, s32[2]{0:T(128)}, u32[]{:S(2)}) copy-start(s32[2]{0:T(128)} %constant.49.clone) | copy-start | bytes 28
  1.8 9.9 %copy-start.1 = (bf16[512,768]{1,0:T(8,128)(2,1)S(1)}, bf16[512,768]{1,0:T(8,128)(2,1)}, u32[]{:S(2)}) copy-start(bf16[512,768]{1,0:T(8,128)(2,1)} %param.18) | copy-start | bytes 2359300
  1.8 12.4 %copy-start.11 = (s32[4]{0:T(128)S(1)}, s32[4]{0:T(128)}, u32[]{:S(2)}) copy-start(s32[4]{0:T(128)} %constant.50.clone) | copy-start | bytes 52
  1.8 13.0 %copy-start.10 = (s32[8]{0:T(128)S(1)}, s32[8]{0:T(128)}, u32[]{:S(2)}) copy-start(s32[8]{0:T(128)} %constant.51.clone) | copy-start | bytes 100
  1.8 13.7 %copy-start.5 = (f32[2,768]{1,0:T(2,128)S(1)}, f32[2,768]{1,0:T(2,128)}, u32[]{:S(2)}) copy-start(f32[2,768]{1,0:T(2,128)} %param.19) | copy-start | bytes 18436
  1.8 15.6 %collective-permute-start.1 = (bf16[256,768]{1,0:T(8,128)(2,1)S(1)}, bf16[256,768]{1,0:T(8,128)(2,1)S(1)}, u32[]{:S(2)}, u32[]{:S(2)}) collective-permute-start(bf16[256,768]{1,0:T(8,128)(2,1)S(1)} %slice.59), channel_id=1, source_target_pairs={{1,0},{2,1},{3,2},{4,3},{5,4},{6,5},{7,6},{8,7},{9,8},{10,9},{11,1... | collective-permute-start | bytes 1179656 | tf_op jit(solution)/shard_map/ppermute | solution.py:26
  3.9 7.8 %collective-permute-start.2 = (bf16[256,768]{1,0:T(8,128)(2,1)S(1)}, bf16[256,768]{1,0:T(8,128)(2,1)S(1)}, u32[]{:S(2)}, u32[]{:S(2)}) collective-permute-start(bf16[256,768]{1,0:T(8,128)(2,1)S(1)} %slice.59), channel_id=1, source_target_pairs={{0,2},{16,18}} | collective-permute-start | bytes 1179656 | tf_op jit(solution)/shard_map/ppermute | solution.py:59
  11.7 9.1 %collective-permute-start = (bf16[256,768]{1,0:T(8,128)(2,1)S(1)}, bf16[256,768]{1,0:T(8,128)(2,1)S(1)}, u32[]{:S(2)}, u32[]{:S(2)}) collective-permute-start(bf16[256,768]{1,0:T(8,128)(2,1)S(1)} %get-tuple-element.16), channel_id=1, source_target_pairs={{0,1},{1,2},{2,3},{3,4},{4,5},{5,6},{6,7},{7,8},{8,9},{9,10},{10,1... | collective-permute-start | bytes 1179656 | tf_op jit(solution)/shard_map/ppermute | solution.py:25
  15.5 11.4 %collective-permute-start.3 = (bf16[256,768]{1,0:T(8,128)(2,1)S(1)}, bf16[256,768]{1,0:T(8,128)(2,1)S(1)}, u32[]{:S(2)}, u32[]{:S(2)}) collective-permute-start(bf16[256,768]{1,0:T(8,128)(2,1)S(1)} %get-tuple-element.15), channel_id=1, source_target_pairs={{0,8},{2,10},{16,24},{18,26}} | collective-permute-start | bytes 1179656 | tf_op jit(solution)/shard_map/ppermute | solution.py:59
  27.5 6.6 %collective-permute-start.4 = (bf16[256,768]{1,0:T(8,128)(2,1)S(1)}, bf16[256,768]{1,0:T(8,128)(2,1)S(1)}, u32[]{:S(2)}, u32[]{:S(2)}) collective-permute-start(bf16[256,768]{1,0:T(8,128)(2,1)S(1)} %broadcast_select_fusion.3), channel_id=1, source_target_pairs={{0,4},{2,6},{8,12},{10,14},{16,20},{18,22},{24,28},{26,30}} | collective-permute-start | bytes 1179656 | tf_op jit(solution)/shard_map/ppermute | solution.py:59
  29.4 6.7 %copy-start.3 = (bf16[768,2304]{1,0:T(8,128)(2,1)S(1)}, bf16[768,2304]{1,0:T(8,128)(2,1)}, u32[]{:S(2)}) copy-start(bf16[768,2304]{1,0:T(8,128)(2,1)} %get-tuple-element.12) | copy-start | bytes 10616836
  34.7 7.3 %collective-permute-start.5 = (bf16[256,768]{1,0:T(8,128)(2,1)S(1)}, bf16[256,768]{1,0:T(8,128)(2,1)S(1)}, u32[]{:S(2)}, u32[]{:S(2)}) collective-permute-start(bf16[256,768]{1,0:T(8,128)(2,1)S(1)} %broadcast_select_fusion.5), channel_id=1, source_target_pairs={{0,1},{2,3},{4,5},{6,7},{8,9},{10,11},{12,13},{14,15},{16,17},{18,... | collective-permute-start | bytes 1179656 | tf_op jit(solution)/shard_map/ppermute | solution.py:59
  62.8 2.6 %collective-permute-start.8 = (bf16[256,768]{1,0:T(8,128)(2,1)S(1)}, bf16[256,768]{1,0:T(8,128)(2,1)S(1)}, u32[]{:S(2)}, u32[]{:S(2)}) collective-permute-start(bf16[256,768]{1,0:T(8,128)(2,1)S(1)} %slice.80), channel_id=1, source_target_pairs={{0,2},{16,18}} | collective-permute-start | bytes 1179656 | tf_op jit(solution)/shard_map/ppermute | solution.py:59
  63.5 11.4 %collective-permute-start.7 = (bf16[256,768]{1,0:T(8,128)(2,1)S(1)}, bf16[256,768]{1,0:T(8,128)(2,1)S(1)}, u32[]{:S(2)}, u32[]{:S(2)}) collective-permute-start(bf16[256,768]{1,0:T(8,128)(2,1)S(1)} %slice.80), channel_id=1, source_target_pairs={{1,0},{2,1},{3,2},{4,3},{5,4},{6,5},{7,6},{8,7},{9,8},{10,9},{11,1... | collective-permute-start | bytes 1179656 | tf_op jit(solution)/shard_map/ppermute | solution.py:26
  65.5 11.8 %collective-permute-start.6 = (bf16[256,768]{1,0:T(8,128)(2,1)S(1)}, bf16[256,768]{1,0:T(8,128)(2,1)S(1)}, u32[]{:S(2)}, u32[]{:S(2)}) collective-permute-start(bf16[256,768]{1,0:T(8,128)(2,1)S(1)} %get-tuple-element.14), channel_id=1, source_target_pairs={{0,1},{1,2},{2,3},{3,4},{4,5},{5,6},{6,7},{7,8},{8,9},{9,10},{10,1... | collective-permute-start | bytes 1179656 | tf_op jit(solution)/shard_map/ppermute | solution.py:25
  67.9 17.3 %collective-permute-start.9 = (bf16[256,768]{1,0:T(8,128)(2,1)S(1)}, bf16[256,768]{1,0:T(8,128)(2,1)S(1)}, u32[]{:S(2)}, u32[]{:S(2)}) collective-permute-start(bf16[256,768]{1,0:T(8,128)(2,1)S(1)} %get-tuple-element.13), channel_id=1, source_target_pairs={{0,8},{2,10},{16,24},{18,26}} | collective-permute-start | bytes 1179656 | tf_op jit(solution)/shard_map/ppermute | solution.py:59
  85.9 6.6 %collective-permute-start.10 = (bf16[256,768]{1,0:T(8,128)(2,1)S(1)}, bf16[256,768]{1,0:T(8,128)(2,1)S(1)}, u32[]{:S(2)}, u32[]{:S(2)}) collective-permute-start(bf16[256,768]{1,0:T(8,128)(2,1)S(1)} %broadcast_select_fusion.2), channel_id=1, source_target_pairs={{0,4},{2,6},{8,12},{10,14},{16,20},{18,22},{24,28},{26,30}} | collective-permute-start | bytes 1179656 | tf_op jit(solution)/shard_map/ppermute | solution.py:59
  87.8 6.8 %copy-start.2 = (bf16[768,2304]{1,0:T(8,128)(2,1)S(1)}, bf16[768,2304]{1,0:T(8,128)(2,1)}, u32[]{:S(2)}) copy-start(bf16[768,2304]{1,0:T(8,128)(2,1)} %get-tuple-element.11) | copy-start | bytes 10616836
  93.0 7.2 %collective-permute-start.11 = (bf16[256,768]{1,0:T(8,128)(2,1)S(1)}, bf16[256,768]{1,0:T(8,128)(2,1)S(1)}, u32[]{:S(2)}, u32[]{:S(2)}) collective-permute-start(bf16[256,768]{1,0:T(8,128)(2,1)S(1)} %broadcast_select_fusion.4), channel_id=1, source_target_pairs={{0,1},{2,3},{4,5},{6,7},{8,9},{10,11},{12,13},{14,15},{16,17},{18,... | collective-permute-start | bytes 1179656 | tf_op jit(solution)/shard_map/ppermute | solution.py:59
  118.8 2.8 %copy-start.9 = (f32[768]{0:T(1024)S(1)}, f32[768]{0:T(1024)}, u32[]{:S(2)}) copy-start(f32[768]{0:T(1024)} %param.22) | copy-start | bytes 9220
  121.2 1.4 %copy-start.6 = (s32[512]{0:T(512)S(1)}, s32[512]{0:T(512)}, u32[]{:S(2)}) copy-start(s32[512]{0:T(512)} %param.24) | copy-start | bytes 6148
  121.6 1.2 copy-start.7
  121.6 1.2 copy-start.8
  122.8 0.6 copy-start.4

commit v20 on v12

--- a/solution.py
+++ b/solution.py
@@ -35,23 +35,27 @@
         while step:
             bits.append(step)
             step //= 2
-        return [[[(i, i + bit) for i in range(0, count, 2 * bit)]] for bit in bits]
+        return [([[(i, i + bit) for i in range(0, count, 2 * bit)]], bit) for bit in bits]
     rounds = []
     held = 1
     while held < count:
-        rounds.append([[(i, i + held) for i in range(min(held, count - held))]])
+        rounds.append(([[(i, i + held) for i in range(min(held, count - held))]], None))
         held *= 2
     return rounds
 
 
 def spread(block, axis):
     place = lax.axis_index(axis)
-    for ops in tree_rounds(lax.axis_size(axis)):
+    for ops, bit in tree_rounds(lax.axis_size(axis)):
         received = block
         for op in ops:
             got = lax.ppermute(block, axis, op)
-            targets = jnp.array([t for _, t in op], dtype=jnp.int32)
-            received = jnp.where(jnp.any(place == targets), got, received)
+            if bit is not None:
+                is_target = place % (2 * bit) == bit
+            else:
+                targets = jnp.array([t for _, t in op], dtype=jnp.int32)
+                is_target = jnp.any(place == targets)
+            received = jnp.where(is_target, got, received)
         block = received
     return block
 

time: 122 us -> 122 us (level)
  other arithmetic: 14.3 us -> 9.94 us
  waiting for transfers between devices: 29.2 us -> 32.3 us
    ppermute x8, waiting for transfers between devices: 18 us -> 23.7 us  [spread(): got = lax.ppermute(block, axis, op)]
    ppermute x2, waiting for transfers between devices: 9.74 us -> 7.23 us  [with_halo(): before = lax.ppermute(last, axis, up)]
    reduce_or x3 -> x0, other arithmetic: 1.94 us -> none  [spread(): received = jnp.where(jnp.any(place == targets), got, received)]
    reduce_sum x4, other arithmetic: 2.31 us -> 0.93 us  [layer_norm(): row_mean = jnp.mean(values_f, axis=-1, keepdims=True)]
  transfers between devices with their start and end apart: 12 -> 12, of which waited for: 5 -> 4; matrix products, arithmetic and copies ran while one was open for 21% -> 21% of each run, Pallas kernels for 0% -> 0%
where the time goes in v20:
time: 122 us; the launch traced here: 121 us
  waiting for transfers between devices  32.3 us (26%)
  Pallas kernels  31.3 us (26%)
  matrix products  20.4 us (17%)
  starting transfers between devices  17.9 us (15%)
  other arithmetic  9.94 us (8%)
  local copies, waits for them, and re-layouts  7.66 us (6%)
  between operations  1.67 us (1%)
    pallas_call x2, Pallas kernels, attention(): pl.pallas_call(functools.partial(attention_kernel, row0), out_shape=jax.S...  31.3 us
    ppermute x8, waiting for transfers between devices, spread(): got = lax.ppermute(block, axis, op)  23.7 us
    ppermute x8, starting transfers between devices, spread(): got = lax.ppermute(block, axis, op)  9.09 us
    dot_general x2, matrix products, per_device(): jnp.dot(extended_normed, weights[:, feat_width:], preferred_element_type=...  8.1 us
    ppermute x2, waiting for transfers between devices, with_halo(): before = lax.ppermute(last, axis, up)  7.23 us
    squeeze x1, local copies, waits for them, and re-layouts, per_device(): weights = w_qkv[layer_idx]  6.45 us
    ppermute x2, starting transfers between devices, with_halo(): before = lax.ppermute(last, axis, up)  4.94 us
    dot_general x2, matrix products, per_device(): jnp.dot(attended, w_out[layer_idx], preferred_element_type=jnp.float32)  4.68 us
  transfers between devices with their start and end apart: 12, of which 4 were waited for; matrix products, arithmetic and copies ran while one was open for 21% of the time, Pallas kernels for 0%

profile of v20, /device:TPU:20, one launch (start us, length us, event | category | flops | bytes accessed | tf_op | source)
XLA Modules:
  0.0 121.1 jit_solution(17766532666513675422)
XLA Ops:
  0.6 1.1 slice.59
  1.7 0.7 collective-permute-start.2
  2.4 1.9 %collective-permute-start.1 = (bf16[256,768]{1,0:T(8,128)(2,1)S(1)}, bf16[256,768]{1,0:T(8,128)(2,1)S(1)}, u32[]{:S(2)}, u32[]{:S(2)}) collective-permute-start(bf16[256,768]{1,0:T(8,128)(2,1)S(1)} %slice.59), channel_id=1, source_target_pairs={{1,0},{2,1},{3,2},{4,3},{5,4},{6,5},{7,6},{8,7},{9,8},{10,9},{11,1... | collective-permute-start | bytes 1179656 | tf_op jit(solution)/shard_map/ppermute | solution.py:26
  4.4 1.2 %broadcast_select_fusion.1 = (bf16[256,768]{1,0:T(8,128)(2,1)S(1)}, bf16[256,768]{1,0:T(8,128)(2,1)S(1)}) fusion(bf16[256,768]{1,0:T(8,128)(2,1)S(1)} %collective-permute-done.2, pred[]{:T(512)S(6)} %eq.44, bf16[512,768]{1,0:T(8,128)(2,1)} %param.10), kind=kLoop, calls=%fused_computation.78 | loop fusion | flops 196608 | bytes 1966081 | tf_op jit(solution)/shard_map/jit(_where)/select_n | solution.py:58
  5.6 2.5 %collective-permute-start = (bf16[256,768]{1,0:T(8,128)(2,1)S(1)}, bf16[256,768]{1,0:T(8,128)(2,1)S(1)}, u32[]{:S(2)}, u32[]{:S(2)}) collective-permute-start(bf16[256,768]{1,0:T(8,128)(2,1)S(1)} %get-tuple-element.16), channel_id=1, source_target_pairs={{0,1},{1,2},{2,3},{3,4},{4,5},{5,6},{6,7},{7,8},{8,9},{9,10},{10,1... | collective-permute-start | bytes 1179656 | tf_op jit(solution)/shard_map/ppermute | solution.py:25
  8.2 6.5 %slice_bitcast_fusion = (bf16[768,2304]{1,0:T(8,128)(2,1)}, bf16[768,2304]{1,0:T(8,128)(2,1)}) fusion(bf16[2,768,2304]{2,1,0:T(8,128)(2,1)} %param.12), kind=kLoop, calls=%fused_computation.10 | loop fusion | bytes 14155776 | tf_op jit(solution)/shard_map/squeeze | solution.py:185
  14.7 1.4 %collective-permute-start.3 = (bf16[256,768]{1,0:T(8,128)(2,1)S(1)}, bf16[256,768]{1,0:T(8,128)(2,1)}, u32[]{:S(2)}, u32[]{:S(2)}) collective-permute-start(bf16[256,768]{1,0:T(8,128)(2,1)S(1)} %get-tuple-element.15), channel_id=1, source_target_pairs={{0,4},{8,12},{16,20},{24,28}} | collective-permute-start | bytes 1179656 | tf_op jit(solution)/shard_map/ppermute | solution.py:52
  16.1 0.6 pad_add_fusion.pos_ref
  16.7 0.3 convert_reduce_fusion.1
  17.0 0.1 broadcast_select_fusion.3
  17.1 1.3 %collective-permute-start.4 = (bf16[256,768]{1,0:T(8,128)(2,1)S(1)}, bf16[256,768]{1,0:T(8,128)(2,1)S(1)}, u32[]{:S(2)}, u32[]{:S(2)}) collective-permute-start(bf16[256,768]{1,0:T(8,128)(2,1)S(1)} %broadcast_select_fusion.3), channel_id=1, source_target_pairs={{0,2},{4,6},{8,10},{12,14},{16,18},{20,22},{24,26},{28,30}} | collective-permute-start | bytes 1179656 | tf_op jit(solution)/shard_map/ppermute | solution.py:52
  18.4 0.6 fusion.7
  19.0 1.9 %fusion.9 = bf16[1024,768]{1,0:T(8,128)(2,1)S(1)} fusion(f32[768]{0:T(1024)S(1)} %get-tuple-element.6, f32[1024]{0:T(1024)S(1)} %add_rsqrt_fusion.1, f32[1024]{0:T(1024)S(1)} %broadcast_multiply_fusion.1, bf16[256,768]{1,0:T(8,128)(2,1)S(1)} %collective-permute-done.1, bf16[512,768]{1,0:T(8,128)(2,1)S(1)} %copy-done.1, ...), kind=kLoop, calls=%fused_computation.17 | loop fusion | flops 7864320 | bytes 3156992 | tf_op jit(solution)/shard_map/convert_element_type | solution.py:68
  20.9 15.4 %collective-permute-done.4 = bf16[256,768]{1,0:T(8,128)(2,1)S(1)} collective-permute-done((bf16[256,768]{1,0:T(8,128)(2,1)S(1)}, bf16[256,768]{1,0:T(8,128)(2,1)S(1)}, u32[]{:S(2)}, u32[]{:S(2)}) %collective-permute-start.4) | collective-permute-done | bytes 393248 | tf_op jit(solution)/shard_map/ppermute | solution.py:52
  36.3 1.5 %collective-permute-start.5 = (bf16[256,768]{1,0:T(8,128)(2,1)S(1)}, bf16[256,768]{1,0:T(8,128)(2,1)S(1)}, u32[]{:S(2)}, u32[]{:S(2)}) collective-permute-start(bf16[256,768]{1,0:T(8,128)(2,1)S(1)} %broadcast_select_fusion.5), channel_id=1, source_target_pairs={{0,1},{2,3},{4,5},{6,7},{8,9},{10,11},{12,13},{14,15},{16,17},{18,... | collective-permute-start | bytes 1179656 | tf_op jit(solution)/shard_map/ppermute | solution.py:52
  37.9 4.1 %convolution_convert_fusion.1.refs_0_.refs_1_.refs_2_ = bf16[1024,1536]{1,0:T(8,128)(2,1)} fusion(bf16[1024,768]{1,0:T(8,128)(2,1)S(1)} %fusion.9, bf16[768,2304]{1,0:T(8,128)(2,1)S(1)} %copy-done.3), kind=kOutput, calls=%fused_computation.5 | convolution fusion | flops 2417491968 | bytes 7077888 | tf_op jit(solution)/shard_map/dot_general | solution.py:189
  41.9 1.7 %multiply_convert_fusion.1.q_ref = bf16[512,768]{1,0:T(8,128)(2,1)} fusion(bf16[768,2304]{1,0:T(8,128)(2,1)S(1)} %copy-done.3, bf16[1024,768]{1,0:T(8,128)(2,1)S(1)} %fusion.9), kind=kOutput, calls=%fused_computation.36 | convolution fusion | flops 604766208 | bytes 2752512 | tf_op jit(solution)/shard_map/dot_general | solution.py:194
  43.6 0.2 convert_reduce_fusion.4
  43.8 0.2 fusion.32
  44.1 1.8 %convolution_convert_fusion.3.refs_3_ = bf16[256,1536]{1,0:T(8,128)(2,1)} fusion(bf16[768,2304]{1,0:T(8,128)(2,1)S(1)} %copy-done.3, bf16[256,768]{1,0:T(8,128)(2,1)S(1)} %get-tuple-element.10, f32[768]{0:T(1024)S(1)} %get-tuple-element.6, f32[256]{0:T(256)S(1)} %add_rsqrt_fusion.4, f32[256]{0:T(256)S(1)} %broadcast_multiply_fusion.4), kind=kOutput, calls=%fused_computation.19 | convolution fusion | flops 605356032 | bytes 3545088 | tf_op jit(solution)/shard_map/dot_general | solution.py:196
  45.8 15.6 %shard_map.113 = bf16[512,768]{1,0:T(8,128)(2,1)} custom-call(s32[2]{0:T(128)} %pad_add_fusion.pos_ref, bf16[512,768]{1,0:T(8,128)(2,1)} %multiply_convert_fusion.1.q_ref, bf16[1024,1536]{1,0:T(8,128)(2,1)} %convolution_convert_fusion.1.refs_0_.refs_1_.refs_2_, bf16[1024,1536]{1,0:T(8,128)(2,1)} %convolution_convert_fusion.1.refs_0_.refs_1_.refs_2_, ...), custom_call_target="tpu_custom_call" | custom-call | flops 6442450944 | bytes 7077888 | tf_op jit(solution)/shard_map/pallas_call | solution.py:144
  61.5 2.3 %add_convert_fusion.1 = bf16[512,768]{1,0:T(8,128)(2,1)S(1)} fusion(bf16[512,768]{1,0:T(8,128)(2,1)S(1)} %copy-done.1, bf16[512,768]{1,0:T(8,128)(2,1)} %shard_map.113, bf16[2,768,768]{2,1,0:T(8,128)(2,1)} %param.13), kind=kOutput, calls=%fused_computation.35 | convolution fusion | flops 605159424 | bytes 3538944 | tf_op jit(solution)/shard_map/dot_general | solution.py:202
  63.8 0.7 collective-permute-start.8
  64.5 1.9 %collective-permute-start.7 = (bf16[256,768]{1,0:T(8,128)(2,1)S(1)}, bf16[256,768]{1,0:T(8,128)(2,1)S(1)}, u32[]{:S(2)}, u32[]{:S(2)}) collective-permute-start(bf16[256,768]{1,0:T(8,128)(2,1)S(1)} %slice.80), channel_id=1, source_target_pairs={{1,0},{2,1},{3,2},{4,3},{5,4},{6,5},{7,6},{8,7},{9,8},{10,9},{11,1... | collective-permute-start | bytes 1179656 | tf_op jit(solution)/shard_map/ppermute | solution.py:26
  66.4 0.1 broadcast_select_fusion
  66.5 2.4 %collective-permute-start.6 = (bf16[256,768]{1,0:T(8,128)(2,1)S(1)}, bf16[256,768]{1,0:T(8,128)(2,1)S(1)}, u32[]{:S(2)}, u32[]{:S(2)}) collective-permute-start(bf16[256,768]{1,0:T(8,128)(2,1)S(1)} %get-tuple-element.14), channel_id=1, source_target_pairs={{0,1},{1,2},{2,3},{3,4},{4,5},{5,6},{6,7},{7,8},{8,9},{9,10},{10,1... | collective-permute-start | bytes 1179656 | tf_op jit(solution)/shard_map/ppermute | solution.py:25
  68.9 0.7 collective-permute-start.9
  70.3 1.4 %collective-permute-done.7 = bf16[256,768]{1,0:T(8,128)(2,1)S(1)} collective-permute-done((bf16[256,768]{1,0:T(8,128)(2,1)S(1)}, bf16[256,768]{1,0:T(8,128)(2,1)S(1)}, u32[]{:S(2)}, u32[]{:S(2)}) %collective-permute-start.7) | collective-permute-done | bytes 393248 | tf_op jit(solution)/shard_map/ppermute | solution.py:26
  71.7 7.2 %collective-permute-done.6 = bf16[256,768]{1,0:T(8,128)(2,1)S(1)} collective-permute-done((bf16[256,768]{1,0:T(8,128)(2,1)S(1)}, bf16[256,768]{1,0:T(8,128)(2,1)S(1)}, u32[]{:S(2)}, u32[]{:S(2)}) %collective-permute-start.6) | collective-permute-done | bytes 393248 | tf_op jit(solution)/shard_map/ppermute | solution.py:25
  78.9 0.3 convert_reduce_fusion
  79.3 1.3 %collective-permute-start.10 = (bf16[256,768]{1,0:T(8,128)(2,1)S(1)}, bf16[256,768]{1,0:T(8,128)(2,1)S(1)}, u32[]{:S(2)}, u32[]{:S(2)}) collective-permute-start(bf16[256,768]{1,0:T(8,128)(2,1)S(1)} %broadcast_select_fusion.2), channel_id=1, source_target_pairs={{0,2},{4,6},{8,10},{12,14},{16,18},{20,22},{24,26},{28,30}} | collective-permute-start | bytes 1179656 | tf_op jit(solution)/shard_map/ppermute | solution.py:52
  80.6 0.6 fusion.4
  81.2 1.9 %fusion.6 = bf16[1024,768]{1,0:T(8,128)(2,1)S(1)} fusion(f32[768]{0:T(1024)S(1)} %get-tuple-element.5, f32[1024]{0:T(1024)S(1)} %add_rsqrt_fusion, f32[1024]{0:T(1024)S(1)} %broadcast_multiply_fusion, bf16[256,768]{1,0:T(8,128)(2,1)S(1)} %collective-permute-done.7, bf16[512,768]{1,0:T(8,128)(2,1)S(1)} %add_convert_fusion.1, ...), kind=kLoop, calls=%fused_computation.14 | loop fusion | flops 7864320 | bytes 3156992 | tf_op jit(solution)/shard_map/convert_element_type | solution.py:68
  83.1 8.3 %collective-permute-done.10 = bf16[256,768]{1,0:T(8,128)(2,1)S(1)} collective-permute-done((bf16[256,768]{1,0:T(8,128)(2,1)S(1)}, bf16[256,768]{1,0:T(8,128)(2,1)S(1)}, u32[]{:S(2)}, u32[]{:S(2)}) %collective-permute-start.10) | collective-permute-done | bytes 393248 | tf_op jit(solution)/shard_map/ppermute | solution.py:52
  91.4 1.5 %collective-permute-start.11 = (bf16[256,768]{1,0:T(8,128)(2,1)S(1)}, bf16[256,768]{1,0:T(8,128)(2,1)S(1)}, u32[]{:S(2)}, u32[]{:S(2)}) collective-permute-start(bf16[256,768]{1,0:T(8,128)(2,1)S(1)} %broadcast_select_fusion.4), channel_id=1, source_target_pairs={{0,1},{2,3},{4,5},{6,7},{8,9},{10,11},{12,13},{14,15},{16,17},{18,... | collective-permute-start | bytes 1179656 | tf_op jit(solution)/shard_map/ppermute | solution.py:52
  93.0 4.0 %convolution_convert_fusion.refs_0_.refs_1_.refs_2_ = bf16[1024,1536]{1,0:T(8,128)(2,1)} fusion(bf16[1024,768]{1,0:T(8,128)(2,1)S(1)} %fusion.6, bf16[768,2304]{1,0:T(8,128)(2,1)S(1)} %copy-done.2), kind=kOutput, calls=%fused_computation.4 | convolution fusion | flops 2417491968 | bytes 7077888 | tf_op jit(solution)/shard_map/dot_general | solution.py:189
  97.0 1.7 %multiply_convert_fusion.q_ref = bf16[512,768]{1,0:T(8,128)(2,1)} fusion(bf16[768,2304]{1,0:T(8,128)(2,1)S(1)} %copy-done.2, bf16[1024,768]{1,0:T(8,128)(2,1)S(1)} %fusion.6), kind=kOutput, calls=%fused_computation.34 | convolution fusion | flops 604766208 | bytes 2752512 | tf_op jit(solution)/shard_map/dot_general | solution.py:194
  98.7 0.2 convert_reduce_fusion.3
  98.9 0.2 fusion.29
  99.1 1.8 %convolution_convert_fusion.2.refs_3_ = bf16[256,1536]{1,0:T(8,128)(2,1)} fusion(bf16[768,2304]{1,0:T(8,128)(2,1)S(1)} %copy-done.2, bf16[256,768]{1,0:T(8,128)(2,1)S(1)} %get-tuple-element.8, f32[768]{0:T(1024)S(1)} %get-tuple-element.5, f32[256]{0:T(256)S(1)} %add_rsqrt_fusion.3, f32[256]{0:T(256)S(1)} %broadcast_multiply_fusion.3), kind=kOutput, calls=%fused_computation.18 | convolution fusion | flops 605356032 | bytes 3545088 | tf_op jit(solution)/shard_map/dot_general | solution.py:196
  100.9 15.6 %shard_map.114 = bf16[512,768]{1,0:T(8,128)(2,1)} custom-call(s32[2]{0:T(128)} %pad_add_fusion.pos_ref, bf16[512,768]{1,0:T(8,128)(2,1)} %multiply_convert_fusion.q_ref, bf16[1024,1536]{1,0:T(8,128)(2,1)} %convolution_convert_fusion.refs_0_.refs_1_.refs_2_, bf16[1024,1536]{1,0:T(8,128)(2,1)} %convolution_convert_fusion.refs_0_.refs_1_.refs_2_, ...), custom_call_target="tpu_custom_call" | custom-call | flops 6442450944 | bytes 7077888 | tf_op jit(solution)/shard_map/pallas_call | solution.py:144
  116.5 2.4 %convert_reduce_fusion.2 = (f32[512]{0:T(512)S(1)}, bf16[512,768]{1,0:T(8,128)(2,1)S(1)}) fusion(bf16[512,768]{1,0:T(8,128)(2,1)} %shard_map.114, bf16[2,768,768]{2,1,0:T(8,128)(2,1)} %param.13, bf16[512,768]{1,0:T(8,128)(2,1)S(1)} %add_convert_fusion.1), kind=kOutput, calls=%fused_computation.25 | convolution fusion | flops 605945344 | bytes 3540992 | tf_op jit(solution)/shard_map/dot_general | solution.py:202
  118.9 0.4 fusion.16
  119.3 0.8 fusion.35
  120.1 0.1 slice_reduce_fusion
  120.2 0.1 fusion.43
  120.3 0.2 select_reduce_fusion
  120.5 0.6 multiply_add_fusion
  (43 shorter events, 0.3 us)
Async XLA Ops:
  0.6 118.7 %copy-start = (bf16[768,512]{1,0:T(8,128)(2,1)S(1)}, bf16[768,512]{1,0:T(8,128)(2,1)}, u32[]{:S(2)}) copy-start(bf16[768,512]{1,0:T(8,128)(2,1)} %param.15) | copy-start | bytes 2359300
  1.7 2.6 %collective-permute-start.2 = (bf16[256,768]{1,0:T(8,128)(2,1)S(1)}, bf16[256,768]{1,0:T(8,128)(2,1)S(1)}, u32[]{:S(2)}, u32[]{:S(2)}) collective-permute-start(bf16[256,768]{1,0:T(8,128)(2,1)S(1)} %slice.59), channel_id=1, source_target_pairs={{0,8},{16,24}} | collective-permute-start | bytes 1179656 | tf_op jit(solution)/shard_map/ppermute | solution.py:52
  2.4 14.2 %collective-permute-start.1 = (bf16[256,768]{1,0:T(8,128)(2,1)S(1)}, bf16[256,768]{1,0:T(8,128)(2,1)S(1)}, u32[]{:S(2)}, u32[]{:S(2)}) collective-permute-start(bf16[256,768]{1,0:T(8,128)(2,1)S(1)} %slice.59), channel_id=1, source_target_pairs={{1,0},{2,1},{3,2},{4,3},{5,4},{6,5},{7,6},{8,7},{9,8},{10,9},{11,1... | collective-permute-start | bytes 1179656 | tf_op jit(solution)/shard_map/ppermute | solution.py:26
  5.6 9.0 %copy-start.5 = (f32[2,768]{1,0:T(2,128)S(1)}, f32[2,768]{1,0:T(2,128)}, u32[]{:S(2)}) copy-start(f32[2,768]{1,0:T(2,128)} %param.11) | copy-start | bytes 18436
  5.6 11.1 %copy-start.1 = (bf16[512,768]{1,0:T(8,128)(2,1)S(1)}, bf16[512,768]{1,0:T(8,128)(2,1)}, u32[]{:S(2)}) copy-start(bf16[512,768]{1,0:T(8,128)(2,1)} %param.10) | copy-start | bytes 2359300
  5.6 11.0 %collective-permute-start = (bf16[256,768]{1,0:T(8,128)(2,1)S(1)}, bf16[256,768]{1,0:T(8,128)(2,1)S(1)}, u32[]{:S(2)}, u32[]{:S(2)}) collective-permute-start(bf16[256,768]{1,0:T(8,128)(2,1)S(1)} %get-tuple-element.16), channel_id=1, source_target_pairs={{0,1},{1,2},{2,3},{3,4},{4,5},{5,6},{6,7},{7,8},{8,9},{9,10},{10,1... | collective-permute-start | bytes 1179656 | tf_op jit(solution)/shard_map/ppermute | solution.py:25
  14.7 2.3 %collective-permute-start.3 = (bf16[256,768]{1,0:T(8,128)(2,1)S(1)}, bf16[256,768]{1,0:T(8,128)(2,1)}, u32[]{:S(2)}, u32[]{:S(2)}) collective-permute-start(bf16[256,768]{1,0:T(8,128)(2,1)S(1)} %get-tuple-element.15), channel_id=1, source_target_pairs={{0,4},{8,12},{16,20},{24,28}} | collective-permute-start | bytes 1179656 | tf_op jit(solution)/shard_map/ppermute | solution.py:52
  17.1 19.2 %collective-permute-start.4 = (bf16[256,768]{1,0:T(8,128)(2,1)S(1)}, bf16[256,768]{1,0:T(8,128)(2,1)S(1)}, u32[]{:S(2)}, u32[]{:S(2)}) collective-permute-start(bf16[256,768]{1,0:T(8,128)(2,1)S(1)} %broadcast_select_fusion.3), channel_id=1, source_target_pairs={{0,2},{4,6},{8,10},{12,14},{16,18},{20,22},{24,26},{28,30}} | collective-permute-start | bytes 1179656 | tf_op jit(solution)/shard_map/ppermute | solution.py:52
  19.0 18.9 %copy-start.3 = (bf16[768,2304]{1,0:T(8,128)(2,1)S(1)}, bf16[768,2304]{1,0:T(8,128)(2,1)}, u32[]{:S(2)}) copy-start(bf16[768,2304]{1,0:T(8,128)(2,1)} %get-tuple-element.12) | copy-start | bytes 10616836
  36.3 7.3 %collective-permute-start.5 = (bf16[256,768]{1,0:T(8,128)(2,1)S(1)}, bf16[256,768]{1,0:T(8,128)(2,1)S(1)}, u32[]{:S(2)}, u32[]{:S(2)}) collective-permute-start(bf16[256,768]{1,0:T(8,128)(2,1)S(1)} %broadcast_select_fusion.5), channel_id=1, source_target_pairs={{0,1},{2,3},{4,5},{6,7},{8,9},{10,11},{12,13},{14,15},{16,17},{18,... | collective-permute-start | bytes 1179656 | tf_op jit(solution)/shard_map/ppermute | solution.py:52
  63.8 2.6 %collective-permute-start.8 = (bf16[256,768]{1,0:T(8,128)(2,1)S(1)}, bf16[256,768]{1,0:T(8,128)(2,1)S(1)}, u32[]{:S(2)}, u32[]{:S(2)}) collective-permute-start(bf16[256,768]{1,0:T(8,128)(2,1)S(1)} %slice.80), channel_id=1, source_target_pairs={{0,8},{16,24}} | collective-permute-start | bytes 1179656 | tf_op jit(solution)/shard_map/ppermute | solution.py:52
  64.5 7.2 %collective-permute-start.7 = (bf16[256,768]{1,0:T(8,128)(2,1)S(1)}, bf16[256,768]{1,0:T(8,128)(2,1)S(1)}, u32[]{:S(2)}, u32[]{:S(2)}) collective-permute-start(bf16[256,768]{1,0:T(8,128)(2,1)S(1)} %slice.80), channel_id=1, source_target_pairs={{1,0},{2,1},{3,2},{4,3},{5,4},{6,5},{7,6},{8,7},{9,8},{10,9},{11,1... | collective-permute-start | bytes 1179656 | tf_op jit(solution)/shard_map/ppermute | solution.py:26
  66.5 12.4 %collective-permute-start.6 = (bf16[256,768]{1,0:T(8,128)(2,1)S(1)}, bf16[256,768]{1,0:T(8,128)(2,1)S(1)}, u32[]{:S(2)}, u32[]{:S(2)}) collective-permute-start(bf16[256,768]{1,0:T(8,128)(2,1)S(1)} %get-tuple-element.14), channel_id=1, source_target_pairs={{0,1},{1,2},{2,3},{3,4},{4,5},{5,6},{6,7},{7,8},{8,9},{9,10},{10,1... | collective-permute-start | bytes 1179656 | tf_op jit(solution)/shard_map/ppermute | solution.py:25
  68.9 10.3 %collective-permute-start.9 = (bf16[256,768]{1,0:T(8,128)(2,1)S(1)}, bf16[256,768]{1,0:T(8,128)(2,1)S(1)}, u32[]{:S(2)}, u32[]{:S(2)}) collective-permute-start(bf16[256,768]{1,0:T(8,128)(2,1)S(1)} %get-tuple-element.13), channel_id=1, source_target_pairs={{0,4},{8,12},{16,20},{24,28}} | collective-permute-start | bytes 1179656 | tf_op jit(solution)/shard_map/ppermute | solution.py:52
  79.3 12.1 %collective-permute-start.10 = (bf16[256,768]{1,0:T(8,128)(2,1)S(1)}, bf16[256,768]{1,0:T(8,128)(2,1)S(1)}, u32[]{:S(2)}, u32[]{:S(2)}) collective-permute-start(bf16[256,768]{1,0:T(8,128)(2,1)S(1)} %broadcast_select_fusion.2), channel_id=1, source_target_pairs={{0,2},{4,6},{8,10},{12,14},{16,18},{20,22},{24,26},{28,30}} | collective-permute-start | bytes 1179656 | tf_op jit(solution)/shard_map/ppermute | solution.py:52
  81.2 11.8 %copy-start.2 = (bf16[768,2304]{1,0:T(8,128)(2,1)S(1)}, bf16[768,2304]{1,0:T(8,128)(2,1)}, u32[]{:S(2)}) copy-start(bf16[768,2304]{1,0:T(8,128)(2,1)} %get-tuple-element.11) | copy-start | bytes 10616836
  91.4 7.2 %collective-permute-start.11 = (bf16[256,768]{1,0:T(8,128)(2,1)S(1)}, bf16[256,768]{1,0:T(8,128)(2,1)S(1)}, u32[]{:S(2)}, u32[]{:S(2)}) collective-permute-start(bf16[256,768]{1,0:T(8,128)(2,1)S(1)} %broadcast_select_fusion.4), channel_id=1, source_target_pairs={{0,1},{2,3},{4,5},{6,7},{8,9},{10,11},{12,13},{14,15},{16,17},{18,... | collective-permute-start | bytes 1179656 | tf_op jit(solution)/shard_map/ppermute | solution.py:52
  116.5 2.8 %copy-start.9 = (f32[768]{0:T(1024)S(1)}, f32[768]{0:T(1024)}, u32[]{:S(2)}) copy-start(f32[768]{0:T(1024)} %param.14) | copy-start | bytes 9220
  118.9 1.4 %copy-start.6 = (s32[512]{0:T(512)S(1)}, s32[512]{0:T(512)}, u32[]{:S(2)}) copy-start(s32[512]{0:T(512)} %param.16) | copy-start | bytes 6148
  119.3 1.2 %copy-start.7 = (f32[512]{0:T(512)S(1)}, f32[512]{0:T(512)}, u32[]{:S(2)}) copy-start(f32[512]{0:T(512)} %param.18) | copy-start | bytes 6148
  119.3 1.2 %copy-start.8 = (s32[512]{0:T(512)S(1)}, s32[512]{0:T(512)}, u32[]{:S(2)}) copy-start(s32[512]{0:T(512)} %param.17) | copy-start | bytes 6148
  120.5 0.6 copy-start.4
